TPU v7x, 32 devices: a whole 2x2x4 slice. The times are simulated.
32 devices in a mesh: groups: 2 (over y), replica: 4 (over z), tensor: 4 (over x, core).
Axes of the slice: x: 2, y: 2, z: 4, core: 2. Of those that a mesh axis runs over, the one named last changes fastest.
Arguments:
- queries: bfloat16 [8, 128, 8192], P(('groups', 'replica'), None, 'tensor'), parts along dimension 0, may hold values from -12 to 12
- suffix_kv: bfloat16 [8, 2, 128, 1024], P(('groups', 'replica'), None, None, 'tensor'), parts along dimension 0, may hold values from -12 to 12
- page_pool: bfloat16 [96, 2, 128, 1024], P(('groups', 'replica'), None, 'tensor'), parts along dimension 0, may hold values from -6 to 6
- offsets: int32 [8, 8], P('groups'), parts along dimension 0, may hold values from 1 to 3, as said below
- slots: int32 [8, 8], P('groups'), parts along dimension 0, may hold values from 0 to 11, as said below
- prefix_len: int32 [8], P('groups'), parts along dimension 0, may hold values from 1 to 1024, 2048 in all
Outputs:
- attended: bfloat16 [8, 128, 8192], P(('groups', 'replica'), None, 'tensor'), parts along dimension 0
There are 2 independent parts, one for each index of `groups`. A program takes and returns all parts, laid end to end along the dimension named above; each array names one. Nothing has to cross between parts.
Inputs may be any that keep to these rules, and one draw needn't show every extreme that they name: Page p of request r is held by replica (r - offsets[r, p]) mod 4; one request takes at most 4 pages from one holder, and exactly 4 from some holder. `slots`: the prefix pages of one request are distinct pool entries. `prefix_len`: the longest prefix fills all 8 pages.
All inputs are finite; a program needn't handle non-finite values.
Results may differ from a plain program's by a relative error of at most 0.0034.
Values may be sent and summed in bfloat16 or wider, within the bound.
No kernel may reach another device: no remote copies, remote signals or barrier semaphores. Data moves between devices by JAX's collectives and lax.ppermute only.
A program may use at most 64 MiB of HBM per device.

v0:
```python
import math

import jax
import jax.numpy as jnp
from jax import lax
from jax.sharding import PartitionSpec as P

HEADS = 64
KV_HEADS = 8
HEAD_DIM = 128


NEG_FILL = -1e30


def passed_along(value, axis, steps):
    count = lax.axis_size(axis)
    pairs = [(source, (source + steps) % count) for source in range(count)]
    return lax.ppermute(value, axis, pairs)


def absorb(state_now, scores, visible, values):
    run_max, run_sum, run_acc = state_now
    masked = jnp.where(visible, scores, NEG_FILL)
    new_max = jnp.maximum(run_max, jnp.max(masked, axis=-1))
    weights = jnp.where(visible, jnp.exp(masked - new_max[..., None]), 0.0)
    rescale = jnp.exp(run_max - new_max)
    run_sum = run_sum * rescale + jnp.sum(weights, axis=-1)
    update = jnp.einsum(
        "kgqc,ckd->kgqd", weights.astype(jnp.bfloat16), values, preferred_element_type=jnp.float32
    )
    run_acc = run_acc * rescale[..., None] + update
    return (new_max, run_sum, run_acc)


def pack_pages(pool_part, offsets, slots, holder, replicas, span_count, slot_cap):
    distances = jnp.arange(1, span_count + 1, dtype=jnp.int32)
    readers = (holder + distances) % replicas
    off_rows = jnp.take(offsets, readers, axis=0)
    slot_rows = jnp.take(slots, readers, axis=0)
    matched = (off_rows == distances[:, None]).astype(jnp.int32)
    ranking = jnp.cumsum(matched, axis=1) - 1
    places = jnp.arange(slot_cap, dtype=jnp.int32)
    picked = matched[:, None, :] * (ranking[:, None, :] == places[None, :, None]).astype(jnp.int32)
    chosen = jnp.sum(picked * slot_rows[:, None, :], axis=2)
    gathered = jnp.take(pool_part, chosen.reshape(-1), axis=0)
    return gathered.reshape((span_count, slot_cap) + pool_part.shape[1:])


def page_index(own_offsets, slot_cap):
    page_count = own_offsets.shape[0]
    same_holder = own_offsets[:, None] == own_offsets[None, :]
    counter = jnp.arange(page_count, dtype=jnp.int32)
    earlier = counter[None, :] < counter[:, None]
    ranking = jnp.sum((same_holder & earlier).astype(jnp.int32), axis=1)
    return (own_offsets - 1) * slot_cap + ranking


def on_device(queries, suffix_kv, page_pool, offsets, slots, prefix_len):
    replicas = lax.axis_size("replica")
    reader = lax.axis_index("replica")
    span_count = min(8, replicas - 1)
    page_count = offsets.shape[1]
    slot_cap = (page_count + span_count - 1) // span_count + 1
    own_offsets = lax.dynamic_index_in_dim(offsets, reader, 0, keepdims=False)
    own_length = lax.dynamic_index_in_dim(prefix_len, reader, 0, keepdims=False)
    source = lax.all_to_all(page_pool, "tensor", split_axis=3, concat_axis=2, tiled=True)
    payload = pack_pages(source, offsets, slots, reader, replicas, span_count, slot_cap)
    arrivals = []
    for distance in range(1, span_count + 1):
        arrivals.append(passed_along(payload[distance - 1], "replica", distance))
    arrived = jnp.stack(arrivals)
    flattened = arrived.reshape((span_count * slot_cap,) + arrived.shape[2:])
    fetched = jnp.take(flattened, page_index(own_offsets, slot_cap), axis=0)
    width = fetched.shape[3]
    kv_local = width // HEAD_DIM
    group = HEADS // KV_HEADS
    suffix_rows = queries.shape[1]
    prefix_rows = page_count * fetched.shape[2]
    scale = HEAD_DIM ** (-0.5)
    query_heads = queries[0].reshape(suffix_rows, kv_local, group, HEAD_DIM)
    suffix_keys = suffix_kv[0, 0].reshape(suffix_rows, kv_local, HEAD_DIM)
    suffix_vals = suffix_kv[0, 1].reshape(suffix_rows, kv_local, HEAD_DIM)
    initial = (
        jnp.full((kv_local, group, suffix_rows), NEG_FILL, jnp.float32),
        jnp.zeros((kv_local, group, suffix_rows), jnp.float32),
        jnp.zeros((kv_local, group, suffix_rows, HEAD_DIM), jnp.float32),
    )
    suffix_scores = (
        jnp.einsum("qkgd,ckd->kgqc", query_heads, suffix_keys, preferred_element_type=jnp.float32)
        * scale
    )
    query_pos = jnp.arange(suffix_rows, dtype=jnp.int32)
    causal = query_pos[:, None] >= query_pos[None, :]
    state_now = absorb(initial, suffix_scores, causal, suffix_vals)
    block_rows = math.gcd(prefix_rows, 512)
    block_count = prefix_rows // block_rows
    prefix_keys = fetched[:, 0].reshape(block_count, block_rows, kv_local, HEAD_DIM)
    prefix_vals = fetched[:, 1].reshape(block_count, block_rows, kv_local, HEAD_DIM)
    block_pos = jnp.arange(block_rows, dtype=jnp.int32)

    def visit(state_in, pieces):
        keys_block, vals_block, first_row = pieces
        block_scores = (
            jnp.einsum(
                "qkgd,ckd->kgqc", query_heads, keys_block, preferred_element_type=jnp.float32
            )
            * scale
        )
        visible = first_row + block_pos < own_length
        return (absorb(state_in, block_scores, visible, vals_block), None)

    starts = jnp.arange(block_count, dtype=jnp.int32) * block_rows
    state_now, unused = lax.scan(visit, state_now, (prefix_keys, prefix_vals, starts))
    run_max, run_sum, run_acc = state_now
    result = run_acc / run_sum[..., None]
    result = result.transpose(2, 0, 1, 3).reshape(1, suffix_rows, kv_local * group * HEAD_DIM)
    return result.astype(jnp.bfloat16)


def solution(mesh):
    in_specs = (
        P(("groups", "replica"), None, "tensor"),
        P(("groups", "replica"), None, None, "tensor"),
        P(("groups", "replica"), None, "tensor", None),
        P("groups", None),
        P("groups", None),
        P("groups"),
    )
    out_specs = P(("groups", "replica"), None, "tensor")
    return jax.shard_map(
        on_device, mesh=mesh, in_specs=in_specs, out_specs=out_specs, check_vma=False
    )
```

profile of v0, /device:TPU:9, one launch (start us, length us, event | category | flops | bytes accessed | tf_op | source)
XLA Modules:
  0.0 132.8 jit_solution(631455684307266697)
XLA Ops:
  0.0 12.7 %copy.73 = bf16[12,2,32,1024]{2,0,1,3:T(8,128)(2,1)} copy(bf16[12,2,32,1024]{3,2,1,0:T(8,128)(2,1)} %param.12) | data formatting | bytes 3145728 | tf_op args[2]
  12.7 8.9 %reshape.178 = bf16[4,2,98304]{2,1,0:T(2,128)(2,1)} reshape(bf16[1024,2,12,32]{3,2,1,0:T(8,128)(2,1)} %bitcast.95) | data formatting | bytes 3145728
  21.6 4.3 %all-to-all-start = ((bf16[4,2,98304]{2,1,0:T(2,128)(2,1)}), bf16[4,2,98304]{2,1,0:T(2,128)(2,1)S(1)}, u32[]{:S(2)}, u32[]{:S(2)}) async-start(bf16[4,2,98304]{2,1,0:T(2,128)(2,1)} %reshape.178), calls=%async_computation | async-start | bytes 3145728 | tf_op jit(solution)/shard_map/all_to_all | solution.py:67
  29.1 16.0 %all-to-all-done = bf16[4,2,98304]{2,1,0:T(2,128)(2,1)S(1)} async-done(((bf16[4,2,98304]{2,1,0:T(2,128)(2,1)}), bf16[4,2,98304]{2,1,0:T(2,128)(2,1)S(1)}, u32[]{:S(2)}, u32[]{:S(2)}) %all-to-all-start) | async-done | bytes 1572896 | tf_op jit(solution)/shard_map/all_to_all | solution.py:67
  45.1 7.1 %reshape.179 = bf16[1024,2,12,32]{3,2,1,0:T(8,128)(2,1)} reshape(bf16[4,2,98304]{2,1,0:T(2,128)(2,1)S(1)} %all-to-all-done) | data formatting | bytes 3145728
  52.2 9.6 %copy.91 = bf16[12,2,32,4,256]{4,3,2,1,0:T(4,128)(2,1)S(1)} copy(bf16[12,2,32,4,256]{2,0,1,4,3:T(8,128)(2,1)} %bitcast.94) | data formatting | bytes 3145728 | tf_op jit(solution)/shard_map/all_to_all | solution.py:67
  61.7 1.5 %copy.75 = bf16[12,2,4,32,256]{4,3,2,1,0:T(8,128)(2,1)} copy(bf16[12,2,4,32,256]{4,2,3,1,0:T(4,128)(2,1)S(1)} %bitcast.96) | data formatting | bytes 3145728 | tf_op jit(solution)/shard_map/all_to_all | solution.py:67
  63.2 2.1 %gather_fusion = bf16[12,2,128,256]{3,2,1,0:T(8,128)(2,1)S(1)} fusion(bf16[12,2,128,256]{3,2,1,0:T(8,128)(2,1)} %bitcast.97, s32[1024]{0:T(1024)S(1)} %pad_clamp_fusion.1), kind=kCustom, calls=%fused_computation.2 | custom fusion | bytes 3145776 | tf_op jit(solution)/shard_map/jit(_take)/gather | solution.py:46
  65.5 1.1 fusion.35
  66.6 1.3 collective-permute-start
  67.9 1.0 collective-permute-start.1
  68.9 1.5 %collective-permute-start.2 = (bf16[4,2,128,256]{3,2,1,0:T(8,128)(2,1)S(1)}, bf16[4,2,128,256]{3,2,1,0:T(8,128)(2,1)}, u32[]{:S(2)}, u32[]{:S(2)}) collective-permute-start(bf16[4,2,128,256]{3,2,1,0:T(8,128)(2,1)S(1)} %get-tuple-element.151), channel_id=1, source_target_pairs={{0,12},{4,0},{8,4},{12,8},{1,13},{5,1},{9,5},{13,9},{2,14},{6,2},{... | collective-permute-start | bytes 1572872 | tf_op jit(solution)/shard_map/ppermute | solution.py:19
  70.8 0.6 dynamic_slice.19
  71.4 1.5 %convolution_add_fusion = f32[2,8,128,128]{3,2,1,0:T(8,128)} fusion(bf16[128,2,128,1]{0,2,3,1:T(8,128)(2,1)S(1)} %bitcast.102, f32[2,8,128,128]{2,3,1,0:T(8,128)S(1)} %get-tuple-element.160, f32[2,8,128]{2,1,0:T(8,128)S(1)} %get-tuple-element.157, f32[2,8,128]{2,1,0:T(8,128)S(1)} %broadcast_maximum_fusion, pred[128,128]{0,1:T(8,128)(4,1)S(1)} %iota_compare_fusion), kind=kOutput, calls=%fused_computation.30 | convolution fusion | flops 68157440 | bytes 2195456 | tf_op jit(solution)/shard_map/kgqc,ckd->kgqd/dot_general | solution.py:29
  72.9 6.5 %collective-permute-done = bf16[4,2,128,256]{3,2,1,0:T(8,128)(2,1)S(1)} collective-permute-done((bf16[4,2,128,256]{3,2,1,0:T(8,128)(2,1)}, bf16[4,2,128,256]{3,2,1,0:T(8,128)(2,1)S(1)}, u32[]{:S(2)}, u32[]{:S(2)}) %collective-permute-start) | collective-permute-done | bytes 524320 | tf_op jit(solution)/shard_map/ppermute | solution.py:19
  79.4 32.9 %collective-permute-done.1 = bf16[4,2,128,256]{3,2,1,0:T(8,128)(2,1)} collective-permute-done((bf16[4,2,128,256]{3,2,1,0:T(8,128)(2,1)}, bf16[4,2,128,256]{3,2,1,0:T(8,128)(2,1)}, u32[]{:S(2)}, u32[]{:S(2)}) %collective-permute-start.1) | collective-permute-done | bytes 524320 | tf_op jit(solution)/shard_map/ppermute | solution.py:19
  112.3 3.1 %collective-permute-done.2 = bf16[4,2,128,256]{3,2,1,0:T(8,128)(2,1)} collective-permute-done((bf16[4,2,128,256]{3,2,1,0:T(8,128)(2,1)S(1)}, bf16[4,2,128,256]{3,2,1,0:T(8,128)(2,1)}, u32[]{:S(2)}, u32[]{:S(2)}) %collective-permute-start.2) | collective-permute-done | bytes 524320 | tf_op jit(solution)/shard_map/ppermute | solution.py:19
  115.4 1.5 %pad_maximum_fusion = bf16[3,4,2,128,256]{4,3,2,1,0:T(8,128)(2,1)S(1)} fusion(bf16[1,4,2,128,256]{4,3,2,1,0:T(8,128)(2,1)} %bitcast.14, bf16[1,4,2,128,256]{4,3,2,1,0:T(8,128)(2,1)} %bitcast.13, bf16[1,4,2,128,256]{4,3,2,1,0:T(8,128)(2,1)} %bitcast.101), kind=kLoop, calls=%fused_computation.28 | loop fusion | flops 1572864 | bytes 3145728 | tf_op jit(solution)/shard_map/stack | solution.py:72
  116.9 0.6 gather_fusion.1
  118.1 0.8 copy-done.1
  118.9 12.1 %while.15 = (s32[]{:T(128)}, f32[2,8,128]{2,1,0:T(8,128)S(1)}, f32[2,8,128]{2,1,0:T(8,128)S(1)}, f32[2,8,128,128]{3,2,1,0:T(8,128)S(1)}, s32[2]{0:T(128)S(1)}, /...) while((s32[]{:T(128)}, f32[2,8,128]{2,1,0:T(8,128)S(1)}, ...), condition=%wide.region_8.10_spmd.clone, body=%wide.region_5.9_spmd.clone.sunk | while | flops 551031808 | bytes 16910460 | solution.py:114
  118.9 0.6 dynamic_slice.36
  119.5 1.2 fusion.50
  121.1 0.8 bitcast_reduce_fusion.2
  121.9 1.1 fusion.51
  123.1 1.9 %fusion.52 = f32[2,8,128,128]{3,2,1,0:T(8,128)S(1)} fusion(f32[2,512,128,8]{2,1,3,0:T(8,128)S(1)} %get-tuple-element.226, f32[2,8,128]{2,1,0:T(8,128)S(1)} %max.5, pred[512]{0:T(512)(128)(4,1)S(1)} %fusion.50, f32[2,8,128,128]{3,2,1,0:T(8,128)S(1)} %get-tuple-element.243, f32[2,8,128]{2,1,0:T(8,128)S(1)} %get-tuple-element.228, ...), kind=kOutput, calls=%fused_computation.15.clone.1 | convolution fusion | flops 274202624 | bytes 6570496 | tf_op jit(solution)/shard_map/while/body/eval_jaxpr/kgqc,ckd->kgqd/dot_general | solution.py:29
  125.0 0.6 dynamic_slice.36
  125.6 1.2 fusion.50
  127.2 0.8 bitcast_reduce_fusion.2
  127.9 1.1 fusion.51
  129.1 1.9 %fusion.52 = f32[2,8,128,128]{3,2,1,0:T(8,128)S(1)} fusion(f32[2,512,128,8]{2,1,3,0:T(8,128)S(1)} %get-tuple-element.226, f32[2,8,128]{2,1,0:T(8,128)S(1)} %max.5, pred[512]{0:T(512)(128)(4,1)S(1)} %fusion.50, f32[2,8,128,128]{3,2,1,0:T(8,128)S(1)} %get-tuple-element.243, f32[2,8,128]{2,1,0:T(8,128)S(1)} %get-tuple-element.228, ...), kind=kOutput, calls=%fused_computation.15.clone.1 | convolution fusion | flops 274202624 | bytes 6570496 | tf_op jit(solution)/shard_map/while/body/eval_jaxpr/kgqc,ckd->kgqd/dot_general | solution.py:29
  131.7 1.0 convert_element_type.35
  (59 shorter events, 5.7 us)
Async XLA Ops:
  0.0 26.5 %copy-start = (s32[4,8]{1,0:T(4,128)S(1)}, s32[4,8]{1,0:T(4,128)}, u32[]{:S(2)}) copy-start(s32[4,8]{1,0:T(4,128)} %param.14) | copy-start | bytes 388
  12.7 13.3 %copy-start.4 = (s32[4,8]{1,0:T(4,128)S(1)}, s32[4,8]{1,0:T(4,128)}, u32[]{:S(2)}) copy-start(s32[4,8]{1,0:T(4,128)} %param.13) | copy-start | bytes 388
  12.7 15.3 %copy-start.2 = (bf16[1,128,2048]{2,1,0:T(8,128)(2,1)S(1)}, bf16[1,128,2048]{2,1,0:T(8,128)(2,1)}, u32[]{:S(2)}) copy-start(bf16[1,128,2048]{2,1,0:T(8,128)(2,1)} %param.10) | copy-start | bytes 1572868
  21.6 6.7 %copy-start.5 = (bf16[1,2,128,256]{3,2,1,0:T(8,128)(2,1)S(1)}, bf16[1,2,128,256]{3,2,1,0:T(8,128)(2,1)}, u32[]{:S(2)}) copy-start(bf16[1,2,128,256]{3,2,1,0:T(8,128)(2,1)} %param.11) | copy-start | bytes 393220
  21.6 23.6 %all-to-all-start = ((bf16[4,2,98304]{2,1,0:T(2,128)(2,1)}), bf16[4,2,98304]{2,1,0:T(2,128)(2,1)S(1)}, u32[]{:S(2)}, u32[]{:S(2)}) async-start(bf16[4,2,98304]{2,1,0:T(2,128)(2,1)} %reshape.178), calls=%async_computation | async-start | bytes 3145728 | tf_op jit(solution)/shard_map/all_to_all | solution.py:67
  65.3 5.5 %copy-start.6 = (s32[4]{0:T(128)S(1)}, s32[4]{0:T(128)}, u32[]{:S(2)}) copy-start(s32[4]{0:T(128)} %param.15) | copy-start | bytes 52
  66.6 12.8 %collective-permute-start = (bf16[4,2,128,256]{3,2,1,0:T(8,128)(2,1)}, bf16[4,2,128,256]{3,2,1,0:T(8,128)(2,1)S(1)}, u32[]{:S(2)}, u32[]{:S(2)}) collective-permute-start(bf16[4,2,128,256]{3,2,1,0:T(8,128)(2,1)} %get-tuple-element.150), channel_id=1, source_target_pairs={{0,4},{4,8},{8,12},{12,0},{1,5},{5,9},{9,13},{13,1},{2,6},{6,10},{... | collective-permute-start | bytes 1572872 | tf_op jit(solution)/shard_map/ppermute | solution.py:19
  67.9 44.4 %collective-permute-start.1 = (bf16[4,2,128,256]{3,2,1,0:T(8,128)(2,1)}, bf16[4,2,128,256]{3,2,1,0:T(8,128)(2,1)}, u32[]{:S(2)}, u32[]{:S(2)}) collective-permute-start(bf16[4,2,128,256]{3,2,1,0:T(8,128)(2,1)} %get-tuple-element.152), channel_id=1, source_target_pairs={{0,8},{4,12},{8,0},{12,4},{1,9},{5,13},{9,1},{13,5},{2,10},{6,14},... | collective-permute-start | bytes 1572872 | tf_op jit(solution)/shard_map/ppermute | solution.py:19
  68.9 46.4 %collective-permute-start.2 = (bf16[4,2,128,256]{3,2,1,0:T(8,128)(2,1)S(1)}, bf16[4,2,128,256]{3,2,1,0:T(8,128)(2,1)}, u32[]{:S(2)}, u32[]{:S(2)}) collective-permute-start(bf16[4,2,128,256]{3,2,1,0:T(8,128)(2,1)S(1)} %get-tuple-element.151), channel_id=1, source_target_pairs={{0,12},{4,0},{8,4},{12,8},{1,13},{5,1},{9,5},{13,9},{2,14},{6,2},{... | collective-permute-start | bytes 1572872 | tf_op jit(solution)/shard_map/ppermute | solution.py:19
  79.4 36.0 %copy-start.3 = (bf16[4,2,128,256]{3,2,1,0:T(8,128)(2,1)}, bf16[4,2,128,256]{3,2,1,0:T(8,128)(2,1)S(1)}, u32[]{:S(2)}) copy-start(bf16[4,2,128,256]{3,2,1,0:T(8,128)(2,1)S(1)} %collective-permute-done) | copy-start | bytes 1572868
  117.7 1.2 copy-start.1
where the time goes:
time: 133 us
  waiting for transfers between devices  58.5 us (44%)
  local copies, waits for them, and re-layouts  50.6 us (38%)
  starting transfers between devices  8.11 us (6%)
  other arithmetic  7.99 us (6%)
  matrix products  7.18 us (5%)
    ppermute x3, waiting for transfers between devices, passed_along(): return lax.ppermute(value, axis, pairs)  42.4 us
    unnamed x21, local copies, waits for them, and re-layouts  30.3 us
    all_to_all x1, waiting for transfers between devices, on_device(): lax.all_to_all(page_pool, 'tensor', split_axis=3, concat_axis=2, tiled=True)  16 us
    all_to_all x2, local copies, waits for them, and re-layouts, on_device(): lax.all_to_all(page_pool, 'tensor', split_axis=3, concat_axis=2, tiled=True)  11 us
    dot_general x3, matrix products, absorb(): jnp.einsum('kgqc,ckd->kgqd', weights.astype(jnp.bfloat16), values, prefer...  5.31 us
    all_to_all x1, starting transfers between devices, on_device(): lax.all_to_all(page_pool, 'tensor', split_axis=3, concat_axis=2, tiled=True)  4.34 us
    ppermute x3, starting transfers between devices, passed_along(): return lax.ppermute(value, axis, pairs)  3.78 us
  transfers between devices with their start and end apart: 4, of which 4 were waited for; matrix products, arithmetic and copies ran while one was open for 4% of the time, Pallas kernels for 0%

commit v1 on v0

v1 whole, which is shorter than its diff:
```python
import math

import jax
import jax.numpy as jnp
from jax import lax
from jax.sharding import PartitionSpec as P

HEADS = 64
KV_HEADS = 8
HEAD_DIM = 128


NEG_FILL = -1e30


def passed_along(value, axis, steps):
    count = lax.axis_size(axis)
    pairs = [(source, (source + steps) % count) for source in range(count)]
    return lax.ppermute(value, axis, pairs)


def absorb(state_now, scores, visible, values):
    run_max, run_sum, run_acc = state_now
    masked = jnp.where(visible, scores, NEG_FILL)
    new_max = jnp.maximum(run_max, jnp.max(masked, axis=-1))
    weights = jnp.where(visible, jnp.exp(masked - new_max[..., None]), 0.0)
    rescale = jnp.exp(run_max - new_max)
    run_sum = run_sum * rescale + jnp.sum(weights, axis=-1)
    update = jnp.einsum(
        "kgqc,kcd->kgqd", weights.astype(jnp.bfloat16), values, preferred_element_type=jnp.float32
    )
    run_acc = run_acc * rescale[..., None] + update
    return (new_max, run_sum, run_acc)


def slot_choice(offsets_rows, distances, slot_cap):
    matched = (offsets_rows == distances[:, None]).astype(jnp.int32)
    ranking = jnp.cumsum(matched, axis=1) - 1
    places = jnp.arange(slot_cap, dtype=jnp.int32)
    picked = matched[:, None, :] * (ranking[:, None, :] == places[None, :, None]).astype(jnp.int32)
    return picked


def pack_pages(pool_part, offsets, slots, holder, replicas, span_count, slot_cap, tensor_count):
    distances = jnp.arange(1, span_count + 1, dtype=jnp.int32)
    readers = (holder + distances) % replicas
    off_rows = jnp.take(offsets, readers, axis=0)
    slot_rows = jnp.take(slots, readers, axis=0)
    picked = slot_choice(off_rows, distances, slot_cap)
    chosen = jnp.sum(picked * slot_rows[:, None, :], axis=2)
    gathered = jnp.take(pool_part, chosen.reshape(-1), axis=0)
    pages, kv, rows, width = gathered.shape
    split = gathered.reshape(span_count, slot_cap, kv, rows, tensor_count, width // tensor_count)
    return split.transpose(0, 4, 1, 2, 3, 5)


def on_device(queries, suffix_kv, page_pool, offsets, slots, prefix_len):
    replicas = lax.axis_size("replica")
    tensor_count = lax.axis_size("tensor")
    reader = lax.axis_index("replica")
    span_count = min(8, replicas - 1)
    page_count = offsets.shape[1]
    slot_cap = (page_count + span_count - 1) // span_count + 1
    own_offsets = lax.dynamic_index_in_dim(offsets, reader, 0, keepdims=False)
    own_length = lax.dynamic_index_in_dim(prefix_len, reader, 0, keepdims=False)
    payload = pack_pages(
        page_pool, offsets, slots, reader, replicas, span_count, slot_cap, tensor_count
    )
    arrivals = []
    for distance in range(1, span_count + 1):
        arrivals.append(passed_along(payload[distance - 1], "replica", distance))

    page_rows = page_pool.shape[2] * tensor_count
    quarter = page_pool.shape[2]
    width = suffix_kv.shape[3]
    kv_local = width // HEAD_DIM
    group = HEADS // KV_HEADS
    suffix_rows = queries.shape[1]
    scale = HEAD_DIM ** (-0.5)
    query_heads = queries[0].reshape(suffix_rows, kv_local, group, HEAD_DIM)
    suffix_keys = suffix_kv[0, 0].reshape(suffix_rows, kv_local, HEAD_DIM).transpose(1, 0, 2)
    suffix_vals = suffix_kv[0, 1].reshape(suffix_rows, kv_local, HEAD_DIM).transpose(1, 0, 2)
    initial = (
        jnp.full((kv_local, group, suffix_rows), NEG_FILL, jnp.float32),
        jnp.zeros((kv_local, group, suffix_rows), jnp.float32),
        jnp.zeros((kv_local, group, suffix_rows, HEAD_DIM), jnp.float32),
    )
    suffix_scores = (
        jnp.einsum("qkgd,kcd->kgqc", query_heads, suffix_keys, preferred_element_type=jnp.float32)
        * scale
    )
    query_pos = jnp.arange(suffix_rows, dtype=jnp.int32)
    causal = query_pos[:, None] >= query_pos[None, :]
    state_now = absorb(initial, suffix_scores, causal, suffix_vals)

    distances = jnp.arange(1, span_count + 1, dtype=jnp.int32)
    own_picked = slot_choice(own_offsets[None, :], distances, slot_cap)
    page_ids = jnp.arange(page_count, dtype=jnp.int32)
    slot_page = jnp.sum(own_picked * page_ids[None, None, :], axis=2)
    slot_used = jnp.sum(own_picked, axis=2) > 0
    chunk_ids = jnp.arange(tensor_count, dtype=jnp.int32)
    row_ids = jnp.arange(quarter, dtype=jnp.int32)
    for distance in range(1, span_count + 1):
        local = lax.all_to_all(
            arrivals[distance - 1], "tensor", split_axis=0, concat_axis=0, tiled=True
        )
        keys_block = local[:, :, 0].reshape(tensor_count * slot_cap * quarter, kv_local, HEAD_DIM)
        vals_block = local[:, :, 1].reshape(tensor_count * slot_cap * quarter, kv_local, HEAD_DIM)
        position = (
            slot_page[distance - 1][None, :, None] * page_rows
            + chunk_ids[:, None, None] * quarter
            + row_ids[None, None, :]
        )
        visible = slot_used[distance - 1][None, :, None] & (position < own_length)
        visible = visible.reshape(-1)
        block_scores = (
            jnp.einsum(
                "qkgd,ckd->kgqc", query_heads, keys_block, preferred_element_type=jnp.float32
            )
            * scale
        )
        state_now = absorb(
            state_now, block_scores, visible[None, None, None, :], vals_block.transpose(1, 0, 2)
        )
    run_max, run_sum, run_acc = state_now
    result = run_acc / run_sum[..., None]
    result = result.transpose(2, 0, 1, 3).reshape(1, suffix_rows, kv_local * group * HEAD_DIM)
    return result.astype(jnp.bfloat16)


def solution(mesh):
    in_specs = (
        P(("groups", "replica"), None, "tensor"),
        P(("groups", "replica"), None, None, "tensor"),
        P(("groups", "replica"), None, "tensor", None),
        P("groups", None),
        P("groups", None),
        P("groups"),
    )
    out_specs = P(("groups", "replica"), None, "tensor")
    return jax.shard_map(
        on_device, mesh=mesh, in_specs=in_specs, out_specs=out_specs, check_vma=False
    )
```

time: 133 us -> 112 us (0.84)
  the two profiles are of different devices: /device:TPU:9 before, /device:TPU:23 now
where the time goes in v1:
time: 112 us; the launch traced here: 111 us
  starting transfers between devices  44.1 us (39%)
  local copies, waits for them, and re-layouts  34.8 us (31%)
  waiting for transfers between devices  16.7 us (15%)
  matrix products  8.02 us (7%)
  other arithmetic  7.49 us (7%)
    all_to_all x3, starting transfers between devices, on_device(): lax.all_to_all(arrivals[distance - 1], 'tensor', split_axis=0, concat_axi...  40.7 us
    another operation x6, local copies, waits for them, and re-layouts, on_device(): local[:, :, 1]  8.97 us
    all_to_all x3, waiting for transfers between devices, on_device(): lax.all_to_all(arrivals[distance - 1], 'tensor', split_axis=0, concat_axi...  8.61 us
    ppermute x3, waiting for transfers between devices, passed_along(): return lax.ppermute(value, axis, pairs)  8.12 us
    slice x3, local copies, waits for them, and re-layouts, on_device(): local[:, :, 1]  5.61 us
    gather x2, local copies, waits for them, and re-layouts, pack_pages(): gathered = jnp.take(pool_part, chosen.reshape(-1), axis=0)  4.75 us
    another operation x3, local copies, waits for them, and re-layouts, on_device(): local[:, :, 0]  4.44 us
    dot_general x4, matrix products, absorb(): jnp.einsum('kgqc,kcd->kgqd', weights.astype(jnp.bfloat16), values, prefer...  4.22 us
  transfers between devices with their start and end apart: 6, of which 3 were waited for; matrix products, arithmetic and copies ran while one was open for 17% of the time, Pallas kernels for 0%

profile of v1, /device:TPU:23, one launch (start us, length us, event | category | flops | bytes accessed | tf_op | source)
XLA Modules:
  0.0 111.5 jit_solution(8072606878463199649)
XLA Ops:
  0.9 1.2 %gather_fusion.1 = s32[3,8]{1,0:T(4,128)S(1)} fusion(s32[4,8]{1,0:T(4,128)} %param.11, s32[1024]{0:T(1024)S(1)} %pad_clamp_fusion.1), kind=kCustom, calls=%fused_computation.clone | custom fusion | bytes 204 | tf_op jit(solution)/shard_map/jit(_take)/gather | solution.py:47
  2.1 1.2 %gather_fusion.2 = s32[3,8]{1,0:T(4,128)S(1)} fusion(s32[4,8]{1,0:T(4,128)} %param.12, s32[1024]{0:T(1024)S(1)} %pad_clamp_fusion.1), kind=kCustom, calls=%fused_computation.1.clone | custom fusion | bytes 204 | tf_op jit(solution)/shard_map/jit(_take)/gather | solution.py:48
  4.3 1.9 %gather_fusion = bf16[12,2,32,1024]{3,2,1,0:T(8,128)(2,1)} fusion(bf16[12,2,32,1024]{3,2,1,0:T(8,128)(2,1)S(1)} %copy-done, s32[1024]{0:T(1024)S(1)} %pad_clamp_fusion), kind=kCustom, calls=%fused_computation.2 | custom fusion | bytes 3145776 | tf_op jit(solution)/shard_map/jit(_take)/gather | solution.py:51
  6.1 2.9 %gather.10 = bf16[3,4,2,32,4,256]{5,4,3,2,1,0:T(4,128)(2,1)S(1)} reshape(bf16[12,2,32,1024]{3,2,1,0:T(8,128)(2,1)} %gather_fusion) | data formatting | bytes 3145728 | tf_op jit(solution)/shard_map/jit(_take)/gather | solution.py:51
  9.8 1.6 %slice_bitcast_fusion.2 = (bf16[4,4,2,32,256]{4,0,3,2,1:T(4,128)(2,1)S(1)}, bf16[4,4,2,32,256]{4,0,3,2,1:T(4,128)(2,1)}, bf16[4,4,2,32,256]{4,0,3,2,1:T(4,128)(2,1)}) fusion(bf16[3,4,4,2,32,256]{5,1,4,3,2,0:T(4,128)(2,1)S(1)} %select_bitcast_fusion), kind=kLoop, calls=%fused_computation.55 | loop fusion | bytes 3145728 | tf_op jit(solution)/shard_map/squeeze | solution.py:71
  11.4 1.3 %collective-permute-start = (bf16[4,4,2,32,256]{4,0,3,2,1:T(4,128)(2,1)S(1)}, bf16[4,4,2,32,256]{4,0,3,2,1:T(4,128)(2,1)S(1)}, u32[]{:S(2)}, u32[]{:S(2)}) collective-permute-start(bf16[4,4,2,32,256]{4,0,3,2,1:T(4,128)(2,1)S(1)} %get-tuple-element.14), channel_id=1, source_target_pairs={{0,4},{4,8},{8,12},{12,0},{1,5},{5,9},{9,13},{13,1},{2,6},{6,10},{... | collective-permute-start | bytes 1572872 | tf_op jit(solution)/shard_map/ppermute | solution.py:19
  12.8 1.9 %collective-permute-start.1 = (bf16[4,4,2,32,256]{4,0,3,2,1:T(4,128)(2,1)}, bf16[4,4,2,32,256]{4,0,3,2,1:T(4,128)(2,1)}, u32[]{:S(2)}, u32[]{:S(2)}) collective-permute-start(bf16[4,4,2,32,256]{4,0,3,2,1:T(4,128)(2,1)} %get-tuple-element.16), channel_id=1, source_target_pairs={{0,8},{4,12},{8,0},{12,4},{1,9},{5,13},{9,1},{13,5},{2,10},{6,14},... | collective-permute-start | bytes 1572872 | tf_op jit(solution)/shard_map/ppermute | solution.py:19
  16.1 8.1 %collective-permute-done = bf16[4,4,2,32,256]{4,0,3,2,1:T(4,128)(2,1)S(1)} collective-permute-done((bf16[4,4,2,32,256]{4,0,3,2,1:T(4,128)(2,1)S(1)}, bf16[4,4,2,32,256]{4,0,3,2,1:T(4,128)(2,1)S(1)}, u32[]{:S(2)}, u32[]{:S(2)}) %collective-permute-start) | collective-permute-done | bytes 524320 | tf_op jit(solution)/shard_map/ppermute | solution.py:19
  25.2 28.7 %all-to-all-start = ((bf16[4,4,2,32,256]{4,3,1,2,0:T(8,128)(2,1)}), bf16[4,4,2,32,256]{4,3,1,2,0:T(8,128)(2,1)S(1)}, u32[]{:S(2)}, u32[]{:S(2)}) async-start(bf16[4,4,2,32,256]{4,3,1,2,0:T(8,128)(2,1)} %copy.81), calls=%async_computation | async-start | bytes 1048576 | tf_op jit(solution)/shard_map/all_to_all | solution.py:104
  55.5 5.3 %all-to-all-done = bf16[4,4,2,32,256]{4,3,1,2,0:T(8,128)(2,1)S(1)} async-done(((bf16[4,4,2,32,256]{4,3,1,2,0:T(8,128)(2,1)}), bf16[4,4,2,32,256]{4,3,1,2,0:T(8,128)(2,1)S(1)}, u32[]{:S(2)}, u32[]{:S(2)}) %all-to-all-start) | async-done | bytes 524320 | tf_op jit(solution)/shard_map/all_to_all | solution.py:104
  60.8 6.0 %all-to-all-start.2 = ((bf16[4,4,2,32,256]{4,3,1,2,0:T(8,128)(2,1)}), bf16[4,4,2,32,256]{4,3,1,2,0:T(8,128)(2,1)}, u32[]{:S(2)}, u32[]{:S(2)}) async-start(bf16[4,4,2,32,256]{4,3,1,2,0:T(8,128)(2,1)} %copy.91), calls=%async_computation.2 | async-start | bytes 1048576 | tf_op jit(solution)/shard_map/all_to_all | solution.py:104
  68.6 1.9 %copy.86 = bf16[4,4,2,32,256]{4,3,1,2,0:T(8,128)(2,1)} copy(bf16[4,4,2,32,256]{4,0,3,2,1:T(4,128)(2,1)} %collective-permute-done.1) | data formatting | bytes 1048576 | tf_op jit(solution)/shard_map/ppermute | solution.py:19
  70.6 3.3 %all-to-all-done.2 = bf16[4,4,2,32,256]{4,3,1,2,0:T(8,128)(2,1)} async-done(((bf16[4,4,2,32,256]{4,3,1,2,0:T(8,128)(2,1)}), bf16[4,4,2,32,256]{4,3,1,2,0:T(8,128)(2,1)}, u32[]{:S(2)}, u32[]{:S(2)}) %all-to-all-start.2) | async-done | bytes 524320 | tf_op jit(solution)/shard_map/all_to_all | solution.py:104
  73.8 6.0 %all-to-all-start.1 = ((bf16[4,4,2,32,256]{4,3,1,2,0:T(8,128)(2,1)}), bf16[4,4,2,32,256]{4,3,1,2,0:T(8,128)(2,1)}, u32[]{:S(2)}, u32[]{:S(2)}) async-start(bf16[4,4,2,32,256]{4,3,1,2,0:T(8,128)(2,1)} %copy.86), calls=%async_computation.1 | async-start | bytes 1048576 | tf_op jit(solution)/shard_map/all_to_all | solution.py:104
  79.8 1.9 %fusion.92 = (bf16[4,4,1,32,256]{4,3,1,2,0:T(8,128)(2,1)}, bf16[4,4,1,32,256]{4,3,1,2,0:T(8,128)(2,1)}) fusion(bf16[4,4,2,32,256]{4,3,1,2,0:T(8,128)(2,1)} %copy-done.1), kind=kLoop, calls=%fused_computation.147 | loop fusion | bytes 1048576 | tf_op jit(solution)/shard_map/slice | solution.py:108
  81.7 1.0 reshape_squeeze.31
  83.6 1.0 reshape_squeeze.30
  84.6 1.9 %fusion.94 = (bf16[4,4,1,32,256]{4,3,1,2,0:T(8,128)(2,1)}, bf16[4,4,1,32,256]{4,3,1,2,0:T(8,128)(2,1)}) fusion(bf16[4,4,2,32,256]{4,3,1,2,0:T(8,128)(2,1)} %all-to-all-done.2), kind=kLoop, calls=%fused_computation.149 | loop fusion | bytes 1048576 | tf_op jit(solution)/shard_map/slice | solution.py:108
  86.5 1.7 %reshape_squeeze.35 = bf16[512,2,128]{2,1,0:T(2,128)(2,1)} reshape(bf16[4,4,1,32,256]{4,3,1,2,0:T(8,128)(2,1)} %get-tuple-element.21) | data formatting | bytes 524288 | tf_op jit(solution)/shard_map/reshape;squeeze | solution.py:108
  88.2 1.8 %copy.94 = bf16[512,2,128]{0,2,1:T(8,128)(2,1)} copy(bf16[512,2,128]{2,1,0:T(2,128)(2,1)} %reshape_squeeze.35) | data formatting | bytes 524288 | tf_op jit(solution)/shard_map/reshape;squeeze | solution.py:108
  90.0 1.7 %reshape_squeeze.34 = bf16[512,2,128]{2,1,0:T(2,128)(2,1)} reshape(bf16[4,4,1,32,256]{4,3,1,2,0:T(8,128)(2,1)} %get-tuple-element.22) | data formatting | bytes 524288 | tf_op jit(solution)/shard_map/reshape;squeeze | solution.py:107
  91.8 1.9 %fusion.93 = (bf16[4,4,1,32,256]{4,3,1,2,0:T(8,128)(2,1)}, bf16[4,4,1,32,256]{4,3,1,2,0:T(8,128)(2,1)}) fusion(bf16[4,4,2,32,256]{4,3,1,2,0:T(8,128)(2,1)} %all-to-all-done.1), kind=kLoop, calls=%fused_computation.148 | loop fusion | bytes 1048576 | tf_op jit(solution)/shard_map/slice | solution.py:108
  93.6 1.7 %reshape_squeeze.33 = bf16[512,2,128]{2,1,0:T(2,128)(2,1)} reshape(bf16[4,4,1,32,256]{4,3,1,2,0:T(8,128)(2,1)} %get-tuple-element.19) | data formatting | bytes 524288 | tf_op jit(solution)/shard_map/reshape;squeeze | solution.py:108
  95.3 1.8 %copy.89 = bf16[512,2,128]{0,2,1:T(8,128)(2,1)} copy(bf16[512,2,128]{2,1,0:T(2,128)(2,1)} %reshape_squeeze.33) | data formatting | bytes 524288 | tf_op jit(solution)/shard_map/reshape;squeeze | solution.py:108
  97.2 1.7 %reshape_squeeze.32 = bf16[512,2,128]{2,1,0:T(2,128)(2,1)} reshape(bf16[4,4,1,32,256]{4,3,1,2,0:T(8,128)(2,1)} %get-tuple-element.20) | data formatting | bytes 524288 | tf_op jit(solution)/shard_map/reshape;squeeze | solution.py:107
  98.9 1.8 %bitcast_reduce_fusion.1 = (f32[2,8,128]{2,1,0:T(8,128)S(1)}, f32[2,512,128,8]{2,1,3,0:T(8,128)S(1)}) fusion(pred[512]{0:T(512)(128)(4,1)S(1)} %and.78, bf16[128,2,8,128]{3,2,1,0:T(8,128)(2,1)S(1)} %bitcast.236, bf16[512,2,128,1]{2,1,0,3:T(2,128)(2,1)} %bitcast.241), kind=kOutput, calls=%fused_computation.8 | convolution fusion | flops 271579136 | bytes 4989440 | tf_op jit(solution)/shard_map/qkgd,ckd->kgqc/dot_general | solution.py:117
  102.4 1.2 %fusion.10 = f32[2,8,128]{2,1,0:T(8,128)S(1)} fusion(f32[2,512,128,8]{2,1,3,0:T(8,128)S(1)} %get-tuple-element.40, f32[2,8,128]{2,1,0:T(8,128)S(1)} %get-tuple-element.11, pred[512]{0:T(512)(128)(4,1)S(1)} %and.82), kind=kLoop, calls=%fused_computation.22 | loop fusion | flops 5240832 | bytes 4211200 | tf_op jit(solution)/shard_map/reduce_sum | solution.py:28
  103.6 1.2 %fusion.30 = f32[128,2,8,128]{0,3,2,1:T(8,128)S(1)} fusion(f32[2,512,128,8]{2,1,3,0:T(8,128)S(1)} %get-tuple-element.40, f32[2,8,128]{2,1,0:T(8,128)S(1)} %get-tuple-element.11, pred[512]{0:T(512)(128)(4,1)S(1)} %and.82, bf16[512,2,128]{0,2,1:T(8,128)(2,1)S(1)} %copy-done.5), kind=kOutput, calls=%fused_computation.37 | convolution fusion | flops 273678336 | bytes 5513728 | tf_op jit(solution)/shard_map/kgqc,kcd->kgqd/dot_general | solution.py:29
  104.8 1.2 %fusion.8 = f32[2,8,128]{2,1,0:T(8,128)S(1)} fusion(f32[2,512,128,8]{2,1,3,0:T(8,128)S(1)} %get-tuple-element.42, f32[2,8,128]{2,1,0:T(8,128)S(1)} %get-tuple-element.12, pred[512]{0:T(512)(128)(4,1)S(1)} %and.78), kind=kLoop, calls=%fused_computation.20 | loop fusion | flops 5240832 | bytes 4211200 | tf_op jit(solution)/shard_map/reduce_sum | solution.py:28
  106.0 1.2 %fusion.27 = f32[128,2,8,128]{0,3,2,1:T(8,128)S(1)} fusion(f32[2,512,128,8]{2,1,3,0:T(8,128)S(1)} %get-tuple-element.42, f32[2,8,128]{2,1,0:T(8,128)S(1)} %get-tuple-element.12, pred[512]{0:T(512)(128)(4,1)S(1)} %and.78, bf16[512,2,128]{0,2,1:T(8,128)(2,1)S(1)} %copy-done.6), kind=kOutput, calls=%fused_computation.36 | convolution fusion | flops 273678336 | bytes 5513728 | tf_op jit(solution)/shard_map/kgqc,kcd->kgqd/dot_general | solution.py:29
  107.2 1.2 %fusion.6 = f32[2,8,128]{2,1,0:T(8,128)S(1)} fusion(f32[2,512,128,8]{2,1,3,0:T(8,128)S(1)} %get-tuple-element.44, f32[2,8,128]{2,1,0:T(8,128)S(1)} %get-tuple-element.13, pred[512]{0:T(512)(128)(4,1)S(1)} %and.72), kind=kLoop, calls=%fused_computation.18 | loop fusion | flops 5240832 | bytes 4211200 | tf_op jit(solution)/shard_map/reduce_sum | solution.py:28
  108.4 1.2 %fusion.24 = f32[128,2,8,128]{0,3,2,1:T(8,128)S(1)} fusion(f32[2,512,128,8]{2,1,3,0:T(8,128)S(1)} %get-tuple-element.44, f32[2,8,128]{2,1,0:T(8,128)S(1)} %get-tuple-element.13, pred[512]{0:T(512)(128)(4,1)S(1)} %and.72, bf16[512,2,128]{0,2,1:T(8,128)(2,1)S(1)} %copy-done.4), kind=kOutput, calls=%fused_computation.35 | convolution fusion | flops 273678336 | bytes 5513728 | tf_op jit(solution)/shard_map/kgqc,kcd->kgqd/dot_general | solution.py:29
  (68 shorter events, 12.6 us)
Async XLA Ops:
  0.0 4.2 %copy-start = (bf16[12,2,32,1024]{3,2,1,0:T(8,128)(2,1)S(1)}, bf16[12,2,32,1024]{3,2,1,0:T(8,128)(2,1)}, u32[]{:S(2)}) copy-start(bf16[12,2,32,1024]{3,2,1,0:T(8,128)(2,1)} %param.10) | copy-start | bytes 4718596
  6.1 8.6 %copy-start.8 = (s32[4]{0:T(128)S(1)}, s32[4]{0:T(128)}, u32[]{:S(2)}) copy-start(s32[4]{0:T(128)} %param.13) | copy-start | bytes 52
  9.0 45.5 %copy-start.7 = (bf16[1,2,128,256]{3,2,1,0:T(8,128)(2,1)S(1)}, bf16[1,2,128,256]{3,2,1,0:T(8,128)(2,1)}, u32[]{:S(2)}) copy-start(bf16[1,2,128,256]{3,2,1,0:T(8,128)(2,1)} %param.9) | copy-start | bytes 393220
  9.8 58.3 %copy-start.3 = (bf16[1,128,2048]{2,1,0:T(8,128)(2,1)S(1)}, bf16[1,128,2048]{2,1,0:T(8,128)(2,1)}, u32[]{:S(2)}) copy-start(bf16[1,128,2048]{2,1,0:T(8,128)(2,1)} %param.8) | copy-start | bytes 1572868
  11.4 12.9 %collective-permute-start = (bf16[4,4,2,32,256]{4,0,3,2,1:T(4,128)(2,1)S(1)}, bf16[4,4,2,32,256]{4,0,3,2,1:T(4,128)(2,1)S(1)}, u32[]{:S(2)}, u32[]{:S(2)}) collective-permute-start(bf16[4,4,2,32,256]{4,0,3,2,1:T(4,128)(2,1)S(1)} %get-tuple-element.14), channel_id=1, source_target_pairs={{0,4},{4,8},{8,12},{12,0},{1,5},{5,9},{9,13},{13,1},{2,6},{6,10},{... | collective-permute-start | bytes 1572872 | tf_op jit(solution)/shard_map/ppermute | solution.py:19
  12.7 41.9 %collective-permute-start.2 = (bf16[4,4,2,32,256]{4,0,3,2,1:T(4,128)(2,1)}, bf16[4,4,2,32,256]{4,0,3,2,1:T(4,128)(2,1)S(1)}, u32[]{:S(2)}, u32[]{:S(2)}) collective-permute-start(bf16[4,4,2,32,256]{4,0,3,2,1:T(4,128)(2,1)} %get-tuple-element.15), channel_id=1, source_target_pairs={{0,12},{4,0},{8,4},{12,8},{1,13},{5,1},{9,5},{13,9},{2,14},{6,2},{... | collective-permute-start | bytes 1572872 | tf_op jit(solution)/shard_map/ppermute | solution.py:19
  12.8 55.8 %collective-permute-start.1 = (bf16[4,4,2,32,256]{4,0,3,2,1:T(4,128)(2,1)}, bf16[4,4,2,32,256]{4,0,3,2,1:T(4,128)(2,1)}, u32[]{:S(2)}, u32[]{:S(2)}) collective-permute-start(bf16[4,4,2,32,256]{4,0,3,2,1:T(4,128)(2,1)} %get-tuple-element.16), channel_id=1, source_target_pairs={{0,8},{4,12},{8,0},{12,4},{1,9},{5,13},{9,1},{13,5},{2,10},{6,14},... | collective-permute-start | bytes 1572872 | tf_op jit(solution)/shard_map/ppermute | solution.py:19
  25.2 35.6 %all-to-all-start = ((bf16[4,4,2,32,256]{4,3,1,2,0:T(8,128)(2,1)}), bf16[4,4,2,32,256]{4,3,1,2,0:T(8,128)(2,1)S(1)}, u32[]{:S(2)}, u32[]{:S(2)}) async-start(bf16[4,4,2,32,256]{4,3,1,2,0:T(8,128)(2,1)} %copy.81), calls=%async_computation | async-start | bytes 1048576 | tf_op jit(solution)/shard_map/all_to_all | solution.py:104
  60.8 7.5 %copy-start.1 = (bf16[4,4,2,32,256]{4,3,1,2,0:T(8,128)(2,1)}, bf16[4,4,2,32,256]{4,3,1,2,0:T(8,128)(2,1)S(1)}, u32[]{:S(2)}) copy-start(bf16[4,4,2,32,256]{4,3,1,2,0:T(8,128)(2,1)S(1)} %all-to-all-done) | copy-start | bytes 1572868
  60.8 13.0 %all-to-all-start.2 = ((bf16[4,4,2,32,256]{4,3,1,2,0:T(8,128)(2,1)}), bf16[4,4,2,32,256]{4,3,1,2,0:T(8,128)(2,1)}, u32[]{:S(2)}, u32[]{:S(2)}) async-start(bf16[4,4,2,32,256]{4,3,1,2,0:T(8,128)(2,1)} %copy.91), calls=%async_computation.2 | async-start | bytes 1048576 | tf_op jit(solution)/shard_map/all_to_all | solution.py:104
  73.8 17.9 %all-to-all-start.1 = ((bf16[4,4,2,32,256]{4,3,1,2,0:T(8,128)(2,1)}), bf16[4,4,2,32,256]{4,3,1,2,0:T(8,128)(2,1)}, u32[]{:S(2)}, u32[]{:S(2)}) async-start(bf16[4,4,2,32,256]{4,3,1,2,0:T(8,128)(2,1)} %copy.86), calls=%async_computation.1 | async-start | bytes 1048576 | tf_op jit(solution)/shard_map/all_to_all | solution.py:104
  98.9 1.9 %copy-start.2 = (bf16[512,2,128]{2,1,0:T(2,128)(2,1)S(1)}, bf16[512,2,128]{2,1,0:T(2,128)(2,1)}, u32[]{:S(2)}) copy-start(bf16[512,2,128]{2,1,0:T(2,128)(2,1)} %reshape_squeeze.34) | copy-start | bytes 786436
  101.6 2.0 %copy-start.5 = (bf16[512,2,128]{0,2,1:T(8,128)(2,1)S(1)}, bf16[512,2,128]{0,2,1:T(8,128)(2,1)}, u32[]{:S(2)}) copy-start(bf16[512,2,128]{0,2,1:T(8,128)(2,1)} %copy.94) | copy-start | bytes 786436
  103.6 2.4 %copy-start.6 = (bf16[512,2,128]{0,2,1:T(8,128)(2,1)S(1)}, bf16[512,2,128]{0,2,1:T(8,128)(2,1)}, u32[]{:S(2)}) copy-start(bf16[512,2,128]{0,2,1:T(8,128)(2,1)} %copy.89) | copy-start | bytes 786436
  106.0 2.4 %copy-start.4 = (bf16[512,2,128]{0,2,1:T(8,128)(2,1)S(1)}, bf16[512,2,128]{0,2,1:T(8,128)(2,1)}, u32[]{:S(2)}) copy-start(bf16[512,2,128]{0,2,1:T(8,128)(2,1)} %copy.84) | copy-start | bytes 786436

commit v2 on v1

--- a/solution.py
+++ b/solution.py
@@ -1,8 +1,10 @@
+import functools
 import math
 
 import jax
 import jax.numpy as jnp
 from jax import lax
+from jax.experimental import pallas as pl
 from jax.sharding import PartitionSpec as P
 
 HEADS = 64
@@ -72,26 +74,7 @@
 
     page_rows = page_pool.shape[2] * tensor_count
     quarter = page_pool.shape[2]
-    width = suffix_kv.shape[3]
-    kv_local = width // HEAD_DIM
-    group = HEADS // KV_HEADS
     suffix_rows = queries.shape[1]
-    scale = HEAD_DIM ** (-0.5)
-    query_heads = queries[0].reshape(suffix_rows, kv_local, group, HEAD_DIM)
-    suffix_keys = suffix_kv[0, 0].reshape(suffix_rows, kv_local, HEAD_DIM).transpose(1, 0, 2)
-    suffix_vals = suffix_kv[0, 1].reshape(suffix_rows, kv_local, HEAD_DIM).transpose(1, 0, 2)
-    initial = (
-        jnp.full((kv_local, group, suffix_rows), NEG_FILL, jnp.float32),
-        jnp.zeros((kv_local, group, suffix_rows), jnp.float32),
-        jnp.zeros((kv_local, group, suffix_rows, HEAD_DIM), jnp.float32),
-    )
-    suffix_scores = (
-        jnp.einsum("qkgd,kcd->kgqc", query_heads, suffix_keys, preferred_element_type=jnp.float32)
-        * scale
-    )
-    query_pos = jnp.arange(suffix_rows, dtype=jnp.int32)
-    causal = query_pos[:, None] >= query_pos[None, :]
-    state_now = absorb(initial, suffix_scores, causal, suffix_vals)
 
     distances = jnp.arange(1, span_count + 1, dtype=jnp.int32)
     own_picked = slot_choice(own_offsets[None, :], distances, slot_cap)
@@ -100,32 +83,78 @@
     slot_used = jnp.sum(own_picked, axis=2) > 0
     chunk_ids = jnp.arange(tensor_count, dtype=jnp.int32)
     row_ids = jnp.arange(quarter, dtype=jnp.int32)
+    position = (
+        slot_page[:, None, :, None] * page_rows
+        + chunk_ids[None, :, None, None] * quarter
+        + row_ids[None, None, None, :]
+    )
+    visible = slot_used[:, None, :, None] & (position < own_length)
+    visible = visible.astype(jnp.int32).reshape(span_count, 1, -1)
+    chunks = []
     for distance in range(1, span_count + 1):
-        local = lax.all_to_all(
-            arrivals[distance - 1], "tensor", split_axis=0, concat_axis=0, tiled=True
+        chunks.append(
+            lax.all_to_all(arrivals[distance - 1], "tensor", split_axis=0, concat_axis=0, tiled=True)
         )
-        keys_block = local[:, :, 0].reshape(tensor_count * slot_cap * quarter, kv_local, HEAD_DIM)
-        vals_block = local[:, :, 1].reshape(tensor_count * slot_cap * quarter, kv_local, HEAD_DIM)
-        position = (
-            slot_page[distance - 1][None, :, None] * page_rows
-            + chunk_ids[:, None, None] * quarter
-            + row_ids[None, None, :]
+    result = attend(queries[0], suffix_kv[0], visible, chunks)
+    return result.reshape(1, suffix_rows, result.shape[1])
+
+
+def attention_kernel(chunk_count, q_ref, suf_ref, vis_ref, *rest):
+    chunk_refs, o_ref = rest[:chunk_count], rest[chunk_count]
+    rows, width = q_ref.shape
+    kv_local = suf_ref.shape[2] // HEAD_DIM
+    group = width // (kv_local * HEAD_DIM)
+    scale = HEAD_DIM ** (-0.5)
+    dims = (((1,), (1,)), ((), ()))
+    row_pos = lax.broadcasted_iota(jnp.int32, (group * rows, rows), 0) % rows
+    col_pos = lax.broadcasted_iota(jnp.int32, (group * rows, rows), 1)
+    causal = col_pos <= row_pos
+    for head in range(kv_local):
+        lanes = pl.ds(head * HEAD_DIM, HEAD_DIM)
+        q_all = jnp.concatenate(
+            [q_ref[:, pl.ds((head * group + g) * HEAD_DIM, HEAD_DIM)] for g in range(group)], axis=0
         )
-        visible = slot_used[distance - 1][None, :, None] & (position < own_length)
-        visible = visible.reshape(-1)
-        block_scores = (
-            jnp.einsum(
-                "qkgd,ckd->kgqc", query_heads, keys_block, preferred_element_type=jnp.float32
-            )
-            * scale
-        )
-        state_now = absorb(
-            state_now, block_scores, visible[None, None, None, :], vals_block.transpose(1, 0, 2)
-        )
-    run_max, run_sum, run_acc = state_now
-    result = run_acc / run_sum[..., None]
-    result = result.transpose(2, 0, 1, 3).reshape(1, suffix_rows, kv_local * group * HEAD_DIM)
-    return result.astype(jnp.bfloat16)
+        keys = [suf_ref[0, :, lanes]]
+        vals = [suf_ref[1, :, lanes]]
+        masks = [causal]
+        for c in range(chunk_count):
+            ref = chunk_refs[c]
+            keys.append(ref[:, :, 0, :, lanes].reshape(-1, HEAD_DIM))
+            vals.append(ref[:, :, 1, :, lanes].reshape(-1, HEAD_DIM))
+            masks.append(vis_ref[c] > 0)
+        scores = []
+        top = None
+        for key, mask in zip(keys, masks):
+            s = lax.dot_general(q_all, key, dims, preferred_element_type=jnp.float32) * scale
+            s = jnp.where(mask, s, NEG_FILL)
+            scores.append(s)
+            part = jnp.max(s, axis=-1, keepdims=True)
+            top = part if top is None else jnp.maximum(top, part)
+        total = None
+        acc = None
+        for s, val, mask in zip(scores, vals, masks):
+            w = jnp.where(mask, jnp.exp(s - top), 0.0)
+            part = jnp.sum(w, axis=-1, keepdims=True)
+            total = part if total is None else total + part
+            pv = jnp.dot(w.astype(jnp.bfloat16), val, preferred_element_type=jnp.float32)
+            acc = pv if acc is None else acc + pv
+        out = (acc / total).astype(o_ref.dtype)
+        for g in range(group):
+            o_ref[:, pl.ds((head * group + g) * HEAD_DIM, HEAD_DIM)] = out[g * rows:(g + 1) * rows]
+
+
+def attend(q, suf, visible, chunks):
+    rows, width = q.shape
+    keys_total = suf.shape[1] + sum(c.size // (2 * suf.shape[2]) for c in chunks)
+    flops = 4 * rows * width * keys_total
+    nbytes = 2 * (q.size * 2 + suf.size + sum(c.size for c in chunks))
+    return pl.pallas_call(
+        functools.partial(attention_kernel, len(chunks)),
+        out_shape=jax.ShapeDtypeStruct((rows, width), jnp.bfloat16),
+        cost_estimate=pl.CostEstimate(
+            flops=flops, transcendentals=rows * (width // HEAD_DIM) * keys_total, bytes_accessed=nbytes
+        ),
+    )(q, suf, visible, *chunks)
 
 
 def solution(mesh):

time: 112 us -> 93.6 us (0.84)
  the two profiles are of different devices: /device:TPU:23 before, /device:TPU:1 now
where the time goes in v2:
time: 93.6 us; the launch traced here: 92.4 us
  starting transfers between devices  42.3 us (45%)
  waiting for transfers between devices  29.1 us (31%)
  local copies, waits for them, and re-layouts  10.1 us (11%)
  Pallas kernels  8.36 us (9%)
  other arithmetic  2.43 us (3%)
    ppermute x3, starting transfers between devices, passed_along(): return lax.ppermute(value, axis, pairs)  27 us
    ppermute x3, waiting for transfers between devices, passed_along(): return lax.ppermute(value, axis, pairs)  16.1 us
    all_to_all x3, starting transfers between devices, on_device(): lax.all_to_all(arrivals[distance - 1], 'tensor', split_axis=0, concat_axi...  15.3 us
    all_to_all x3, waiting for transfers between devices, on_device(): lax.all_to_all(arrivals[distance - 1], 'tensor', split_axis=0, concat_axi...  13 us
    pallas_call x1, Pallas kernels, attend(): pl.pallas_call(functools.partial(attention_kernel, len(chunks)), out_shap...  8.36 us
    gather x2, local copies, waits for them, and re-layouts, pack_pages(): gathered = jnp.take(pool_part, chosen.reshape(-1), axis=0)  4.76 us
  transfers between devices with their start and end apart: 6, of which 5 were waited for; matrix products, arithmetic and copies ran while one was open for 3% of the time, Pallas kernels for 0%

profile of v2, /device:TPU:1, one launch (start us, length us, event | category | flops | bytes accessed | tf_op | source)
XLA Modules:
  0.0 92.4 jit_solution(14700315608299357381)
XLA Ops:
  0.1 0.8 dynamic-slice_bitcast_fusion
  0.9 1.2 %gather_fusion.1 = s32[3,8]{1,0:T(4,128)S(1)} fusion(s32[4,8]{1,0:T(4,128)} %param.11, s32[1024]{0:T(1024)S(1)} %pad_clamp_fusion.1), kind=kCustom, calls=%fused_computation.clone | custom fusion | bytes 204 | tf_op jit(solution)/shard_map/jit(_take)/gather | solution.py:49
  2.1 1.2 %gather_fusion.2 = s32[3,8]{1,0:T(4,128)S(1)} fusion(s32[4,8]{1,0:T(4,128)} %param.12, s32[1024]{0:T(1024)S(1)} %pad_clamp_fusion.1), kind=kCustom, calls=%fused_computation.1.clone | custom fusion | bytes 204 | tf_op jit(solution)/shard_map/jit(_take)/gather | solution.py:50
  3.4 0.1 broadcast_select_fusion
  3.4 0.1 fusion.2
  3.5 0.2 reduce_window_sum.18
  3.7 0.2 reduce_window_sum.17
  3.9 0.3 fusion.1
  4.1 0.1 reshape.186
  4.3 1.9 %gather_fusion = bf16[12,2,32,1024]{3,2,1,0:T(8,128)(2,1)} fusion(bf16[12,2,32,1024]{3,2,1,0:T(8,128)(2,1)S(1)} %copy-done, s32[1024]{0:T(1024)S(1)} %pad_clamp_fusion), kind=kCustom, calls=%fused_computation.2 | custom fusion | bytes 3145776 | tf_op jit(solution)/shard_map/jit(_take)/gather | solution.py:53
  6.1 2.9 %gather.10 = bf16[3,4,2,32,4,256]{5,4,3,2,1,0:T(4,128)(2,1)S(1)} reshape(bf16[12,2,32,1024]{3,2,1,0:T(8,128)(2,1)} %gather_fusion) | data formatting | bytes 3145728 | tf_op jit(solution)/shard_map/jit(_take)/gather | solution.py:53
  9.0 0.2 fusion
  9.3 0.2 slice_bitcast_fusion
  9.5 4.2 %collective-permute-start.2 = (bf16[4,4,2,32,256]{4,3,2,1,0:T(8,128)(2,1)S(1)}, bf16[4,4,2,32,256]{4,3,2,1,0:T(8,128)(2,1)}, u32[]{:S(2)}, u32[]{:S(2)}) collective-permute-start(bf16[4,4,2,32,256]{4,3,2,1,0:T(8,128)(2,1)S(1)} %get-tuple-element.8), channel_id=1, source_target_pairs={{0,12},{4,0},{8,4},{12,8},{1,13},{5,1},{9,5},{13,9},{2,14},{6,2},{... | collective-permute-start | bytes 1572872 | tf_op jit(solution)/shard_map/ppermute | solution.py:21
  13.7 10.7 %collective-permute-done.2 = bf16[4,4,2,32,256]{4,3,2,1,0:T(8,128)(2,1)} collective-permute-done((bf16[4,4,2,32,256]{4,3,2,1,0:T(8,128)(2,1)S(1)}, bf16[4,4,2,32,256]{4,3,2,1,0:T(8,128)(2,1)}, u32[]{:S(2)}, u32[]{:S(2)}) %collective-permute-start.2) | collective-permute-done | bytes 524320 | tf_op jit(solution)/shard_map/ppermute | solution.py:21
  24.3 6.0 %all-to-all-start.2 = ((bf16[4,4,2,32,256]{4,3,2,1,0:T(8,128)(2,1)}), bf16[4,4,2,32,256]{4,3,2,1,0:T(8,128)(2,1)S(1)}, u32[]{:S(2)}, u32[]{:S(2)}) async-start(bf16[4,4,2,32,256]{4,3,2,1,0:T(8,128)(2,1)} %collective-permute-done.2), calls=%async_computation.2 | async-start | bytes 1048576 | tf_op jit(solution)/shard_map/all_to_all | solution.py:96
  30.4 22.8 %collective-permute-start = (bf16[4,4,2,32,256]{4,3,2,1,0:T(8,128)(2,1)S(1)}, bf16[4,4,2,32,256]{4,3,2,1,0:T(8,128)(2,1)}, u32[]{:S(2)}, u32[]{:S(2)}) collective-permute-start(bf16[4,4,2,32,256]{4,3,2,1,0:T(8,128)(2,1)S(1)} %get-tuple-element.10), channel_id=1, source_target_pairs={{0,4},{4,8},{8,12},{12,0},{1,5},{5,9},{9,13},{13,1},{2,6},{6,10},{... | collective-permute-start | bytes 1572872 | tf_op jit(solution)/shard_map/ppermute | solution.py:21
  53.1 4.8 %collective-permute-done.1 = bf16[4,4,2,32,256]{4,3,2,1,0:T(8,128)(2,1)} collective-permute-done((bf16[4,4,2,32,256]{4,3,2,1,0:T(8,128)(2,1)S(1)}, bf16[4,4,2,32,256]{4,3,2,1,0:T(8,128)(2,1)}, u32[]{:S(2)}, u32[]{:S(2)}) %collective-permute-start.1) | collective-permute-done | bytes 524320 | tf_op jit(solution)/shard_map/ppermute | solution.py:21
  58.0 5.0 %all-to-all-start.1 = ((bf16[4,4,2,32,256]{4,3,2,1,0:T(8,128)(2,1)}), bf16[4,4,2,32,256]{4,3,2,1,0:T(8,128)(2,1)S(1)}, u32[]{:S(2)}, u32[]{:S(2)}) async-start(bf16[4,4,2,32,256]{4,3,2,1,0:T(8,128)(2,1)} %collective-permute-done.1), calls=%async_computation.1 | async-start | bytes 1048576 | tf_op jit(solution)/shard_map/all_to_all | solution.py:96
  63.0 0.6 dynamic_slice.9
  63.5 0.1 and.35
  63.6 0.1 and.43
  63.7 0.1 add.111
  63.8 0.6 collective-permute-done
  64.4 6.5 %all-to-all-done.1.rest_1_ = bf16[4,4,2,32,256]{4,3,2,1,0:T(8,128)(2,1)S(1)} async-done(((bf16[4,4,2,32,256]{4,3,2,1,0:T(8,128)(2,1)}), bf16[4,4,2,32,256]{4,3,2,1,0:T(8,128)(2,1)S(1)}, u32[]{:S(2)}, u32[]{:S(2)}) %all-to-all-start.1) | async-done | bytes 524320 | tf_op jit(solution)/shard_map/all_to_all | solution.py:96
  70.9 4.3 %all-to-all-start = ((bf16[4,4,2,32,256]{4,3,2,1,0:T(8,128)(2,1)}), bf16[4,4,2,32,256]{4,3,2,1,0:T(8,128)(2,1)S(1)}, u32[]{:S(2)}, u32[]{:S(2)}) async-start(bf16[4,4,2,32,256]{4,3,2,1,0:T(8,128)(2,1)} %collective-permute-done), calls=%async_computation | async-start | bytes 1048576 | tf_op jit(solution)/shard_map/all_to_all | solution.py:96
  75.3 0.1 add.108
  75.4 0.1 add.109
  75.5 1.3 %and_convert_fusion.vis_ref = s32[3,1,512]{2,1,0:T(1,128)} fusion(pred[3,1,512]{2,1,0:T(4,128)(4,1)S(1)} %and.43, s32[3,1,512]{2,1,0:T(1,128)S(1)} %add.109, s32[]{:T(128)} %bitcast.3, s32[512]{0:T(512)S(1)} %add.111), kind=kLoop, calls=%fused_computation.8 | loop fusion | flops 6144 | bytes 15876 | tf_op jit(solution)/shard_map/convert_element_type | solution.py:92
  76.7 6.5 %all-to-all-done.rest_0_ = bf16[4,4,2,32,256]{4,3,2,1,0:T(8,128)(2,1)S(1)} async-done(((bf16[4,4,2,32,256]{4,3,2,1,0:T(8,128)(2,1)}), bf16[4,4,2,32,256]{4,3,2,1,0:T(8,128)(2,1)S(1)}, u32[]{:S(2)}, u32[]{:S(2)}) %all-to-all-start) | async-done | bytes 524320 | tf_op jit(solution)/shard_map/all_to_all | solution.py:96
  83.2 0.8 copy-done.3
  84.0 8.4 %shard_map.64 = bf16[128,2048]{1,0:T(8,128)(2,1)} custom-call(bf16[128,2048]{1,0:T(8,128)(2,1)} %bitcast.18, bf16[2,128,256]{2,1,0:T(8,128)(2,1)} %bitcast.19, s32[3,1,512]{2,1,0:T(1,128)} %and_convert_fusion.vis_ref, bf16[4,4,2,32,256]{4,3,2,1,0:T(8,128)(2,1)} %copy-done.3, bf16[4,4,2,32,256]{4,3,2,1,0:T(8,128)(2,1)} %copy-done.2, ...), custom_call_target="tpu_custom_call" | custom-call | flops 1744830464 | bytes 2752512 | tf_op jit(solution)/shard_map/pallas_call | solution.py:151
  (25 shorter events, 0.2 us)
Async XLA Ops:
  0.0 4.3 %copy-start = (bf16[12,2,32,1024]{3,2,1,0:T(8,128)(2,1)S(1)}, bf16[12,2,32,1024]{3,2,1,0:T(8,128)(2,1)}, u32[]{:S(2)}) copy-start(bf16[12,2,32,1024]{3,2,1,0:T(8,128)(2,1)} %param.10) | copy-start | bytes 4718596
  9.4 53.5 %copy-start.4 = (s32[4]{0:T(128)S(1)}, s32[4]{0:T(128)}, u32[]{:S(2)}) copy-start(s32[4]{0:T(128)} %param.13) | copy-start | bytes 52
  9.5 14.9 %collective-permute-start.2 = (bf16[4,4,2,32,256]{4,3,2,1,0:T(8,128)(2,1)S(1)}, bf16[4,4,2,32,256]{4,3,2,1,0:T(8,128)(2,1)}, u32[]{:S(2)}, u32[]{:S(2)}) collective-permute-start(bf16[4,4,2,32,256]{4,3,2,1,0:T(8,128)(2,1)S(1)} %get-tuple-element.8), channel_id=1, source_target_pairs={{0,12},{4,0},{8,4},{12,8},{1,13},{5,1},{9,5},{13,9},{2,14},{6,2},{... | collective-permute-start | bytes 1572872 | tf_op jit(solution)/shard_map/ppermute | solution.py:21
  13.7 44.3 %collective-permute-start.1 = (bf16[4,4,2,32,256]{4,3,2,1,0:T(8,128)(2,1)S(1)}, bf16[4,4,2,32,256]{4,3,2,1,0:T(8,128)(2,1)}, u32[]{:S(2)}, u32[]{:S(2)}) collective-permute-start(bf16[4,4,2,32,256]{4,3,2,1,0:T(8,128)(2,1)S(1)} %get-tuple-element.9), channel_id=1, source_target_pairs={{0,8},{4,12},{8,0},{12,4},{1,9},{5,13},{9,1},{13,5},{2,10},{6,14},... | collective-permute-start | bytes 1572872 | tf_op jit(solution)/shard_map/ppermute | solution.py:21
  24.3 33.6 %all-to-all-start.2 = ((bf16[4,4,2,32,256]{4,3,2,1,0:T(8,128)(2,1)}), bf16[4,4,2,32,256]{4,3,2,1,0:T(8,128)(2,1)S(1)}, u32[]{:S(2)}, u32[]{:S(2)}) async-start(bf16[4,4,2,32,256]{4,3,2,1,0:T(8,128)(2,1)} %collective-permute-done.2), calls=%async_computation.2 | async-start | bytes 1048576 | tf_op jit(solution)/shard_map/all_to_all | solution.py:96
  30.4 34.0 %collective-permute-start = (bf16[4,4,2,32,256]{4,3,2,1,0:T(8,128)(2,1)S(1)}, bf16[4,4,2,32,256]{4,3,2,1,0:T(8,128)(2,1)}, u32[]{:S(2)}, u32[]{:S(2)}) collective-permute-start(bf16[4,4,2,32,256]{4,3,2,1,0:T(8,128)(2,1)S(1)} %get-tuple-element.10), channel_id=1, source_target_pairs={{0,4},{4,8},{8,12},{12,0},{1,5},{5,9},{9,13},{13,1},{2,6},{6,10},{... | collective-permute-start | bytes 1572872 | tf_op jit(solution)/shard_map/ppermute | solution.py:21
  58.0 25.3 %copy-start.1 = (bf16[4,4,2,32,256]{4,3,2,1,0:T(8,128)(2,1)}, bf16[4,4,2,32,256]{4,3,2,1,0:T(8,128)(2,1)S(1)}, u32[]{:S(2)}) copy-start(bf16[4,4,2,32,256]{4,3,2,1,0:T(8,128)(2,1)S(1)} %all-to-all-done.2.rest_2_) | copy-start | bytes 1572868
  58.0 13.0 %all-to-all-start.1 = ((bf16[4,4,2,32,256]{4,3,2,1,0:T(8,128)(2,1)}), bf16[4,4,2,32,256]{4,3,2,1,0:T(8,128)(2,1)S(1)}, u32[]{:S(2)}, u32[]{:S(2)}) async-start(bf16[4,4,2,32,256]{4,3,2,1,0:T(8,128)(2,1)} %collective-permute-done.1), calls=%async_computation.1 | async-start | bytes 1048576 | tf_op jit(solution)/shard_map/all_to_all | solution.py:96
  70.9 12.3 %copy-start.2 = (bf16[4,4,2,32,256]{4,3,2,1,0:T(8,128)(2,1)}, bf16[4,4,2,32,256]{4,3,2,1,0:T(8,128)(2,1)S(1)}, u32[]{:S(2)}) copy-start(bf16[4,4,2,32,256]{4,3,2,1,0:T(8,128)(2,1)S(1)} %all-to-all-done.1.rest_1_) | copy-start | bytes 1572868
  70.9 12.3 %all-to-all-start = ((bf16[4,4,2,32,256]{4,3,2,1,0:T(8,128)(2,1)}), bf16[4,4,2,32,256]{4,3,2,1,0:T(8,128)(2,1)S(1)}, u32[]{:S(2)}, u32[]{:S(2)}) async-start(bf16[4,4,2,32,256]{4,3,2,1,0:T(8,128)(2,1)} %collective-permute-done), calls=%async_computation | async-start | bytes 1048576 | tf_op jit(solution)/shard_map/all_to_all | solution.py:96
  83.2 0.8 copy-start.3

commit v3 on v2

v3 whole, which is shorter than its diff:
```python
import functools

import jax
import jax.numpy as jnp
from jax import lax
from jax.experimental import pallas as pl
from jax.experimental.pallas import tpu as pltpu
from jax.sharding import PartitionSpec as P

HEADS = 64
KV_HEADS = 8
HEAD_DIM = 128


NEG_FILL = -1e30


def slot_choice(offsets_rows, distances, slot_cap):
    matched = (offsets_rows == distances[:, None]).astype(jnp.int32)
    page_count = offsets_rows.shape[1]
    page_ids = jnp.arange(page_count, dtype=jnp.int32)
    earlier = (page_ids[None, :] < page_ids[:, None]).astype(jnp.int32)
    ranking = jnp.sum(matched[:, None, :] * earlier[None, :, :], axis=2)
    places = jnp.arange(slot_cap, dtype=jnp.int32)
    return matched[:, None, :] * (ranking[:, None, :] == places[None, :, None]).astype(jnp.int32)


def gather_kernel(cap, tensor_count, idx_ref, pool_ref, o_ref):
    me = idx_ref[idx_ref.shape[0] - 1]
    lanes = o_ref.shape[-1]
    for shift in range(tensor_count):
        start = pl.multiple_of(((me + shift) % tensor_count) * lanes, lanes)
        o_ref[0, shift, 0] = pool_ref[0, :, :, pl.ds(start, lanes)]


def pack_pages(pool_part, chosen, me, span_count, slot_cap, tensor_count):
    pages, kv, rows, width = pool_part.shape
    lanes = width // tensor_count
    table = jnp.concatenate([chosen.reshape(-1), me.reshape(1)]).astype(jnp.int32)
    grid_spec = pltpu.PrefetchScalarGridSpec(
        num_scalar_prefetch=1,
        grid=(span_count * slot_cap,),
        in_specs=[pl.BlockSpec((1, kv, rows, width), lambda i, idx: (idx[i], 0, 0, 0))],
        out_specs=pl.BlockSpec(
            (1, tensor_count, 1, kv, rows, lanes),
            lambda i, idx: (i // slot_cap, 0, i % slot_cap, 0, 0, 0),
        ),
    )
    nbytes = 2 * 2 * span_count * slot_cap * kv * rows * width
    return pl.pallas_call(
        functools.partial(gather_kernel, slot_cap, tensor_count),
        grid_spec=grid_spec,
        out_shape=jax.ShapeDtypeStruct(
            (span_count, tensor_count, slot_cap, kv, rows, lanes), pool_part.dtype
        ),
        cost_estimate=pl.CostEstimate(flops=0, transcendentals=0, bytes_accessed=nbytes),
    )(table, pool_part)


def on_device(queries, suffix_kv, page_pool, offsets, slots, prefix_len):
    replicas = lax.axis_size("replica")
    tensor_count = lax.axis_size("tensor")
    reader = lax.axis_index("replica")
    me = lax.axis_index("tensor")
    span_count = min(8, replicas - 1)
    page_count = offsets.shape[1]
    slot_cap = (page_count + span_count - 1) // span_count + 1
    distances = jnp.arange(1, span_count + 1, dtype=jnp.int32)

    off_twice = jnp.concatenate([offsets, offsets], axis=0)
    slots_twice = jnp.concatenate([slots, slots], axis=0)
    off_rows = lax.dynamic_slice_in_dim(off_twice, reader + 1, span_count, 0)
    slot_rows = lax.dynamic_slice_in_dim(slots_twice, reader + 1, span_count, 0)
    picked = slot_choice(off_rows, distances, slot_cap)
    chosen = jnp.sum(picked * slot_rows[:, None, :], axis=2)
    payload = pack_pages(page_pool, chosen, me, span_count, slot_cap, tensor_count)

    arrivals = []
    for distance in range(1, span_count + 1):
        for shift in range(tensor_count):
            pairs = []
            for source in range(replicas):
                for peer in range(tensor_count):
                    target = ((source + distance) % replicas) * tensor_count + (peer + shift) % tensor_count
                    pairs.append((source * tensor_count + peer, target))
            arrivals.append(lax.ppermute(payload[distance - 1, shift], ("replica", "tensor"), pairs))

    quarter = page_pool.shape[2]
    page_rows = quarter * tensor_count
    suffix_rows = queries.shape[1]
    own_offsets = lax.dynamic_index_in_dim(offsets, reader, 0, keepdims=False)
    own_length = lax.dynamic_index_in_dim(prefix_len, reader, 0, keepdims=False)
    own_picked = slot_choice(own_offsets[None, :], distances, slot_cap)
    page_ids = jnp.arange(page_count, dtype=jnp.int32)
    slot_page = jnp.sum(own_picked * page_ids[None, None, :], axis=2)
    slot_used = jnp.sum(own_picked, axis=2) > 0
    shifts = jnp.arange(tensor_count, dtype=jnp.int32)
    row_ids = jnp.arange(quarter, dtype=jnp.int32)
    position = (
        slot_page[:, None, :, None] * page_rows
        + ((me - shifts + tensor_count) % tensor_count)[None, :, None, None] * quarter
        + row_ids[None, None, None, :]
    )
    visible = slot_used[:, None, :, None] & (position < own_length)
    visible = visible.astype(jnp.int32).reshape(span_count * tensor_count, 1, -1)
    result = attend(queries[0], suffix_kv[0], visible, arrivals)
    return result.reshape(1, suffix_rows, result.shape[1])


def attention_kernel(chunk_count, q_ref, suf_ref, vis_ref, *rest):
    chunk_refs, o_ref = rest[:chunk_count], rest[chunk_count]
    rows, width = q_ref.shape
    kv_local = suf_ref.shape[2] // HEAD_DIM
    group = width // (kv_local * HEAD_DIM)
    scale = HEAD_DIM ** (-0.5)
    dims = (((1,), (1,)), ((), ()))
    row_pos = lax.broadcasted_iota(jnp.int32, (group * rows, rows), 0) % rows
    col_pos = lax.broadcasted_iota(jnp.int32, (group * rows, rows), 1)
    causal = col_pos <= row_pos
    for head in range(kv_local):
        lanes = pl.ds(head * HEAD_DIM, HEAD_DIM)
        q_all = jnp.concatenate(
            [q_ref[:, pl.ds((head * group + g) * HEAD_DIM, HEAD_DIM)] for g in range(group)], axis=0
        )
        keys = [suf_ref[0, :, lanes]]
        vals = [suf_ref[1, :, lanes]]
        masks = [causal]
        for c in range(chunk_count):
            ref = chunk_refs[c]
            keys.append(ref[:, 0, :, lanes].reshape(-1, HEAD_DIM))
            vals.append(ref[:, 1, :, lanes].reshape(-1, HEAD_DIM))
            masks.append(vis_ref[c] > 0)
        scores = []
        top = None
        for key, mask in zip(keys, masks):
            s = lax.dot_general(q_all, key, dims, preferred_element_type=jnp.float32) * scale
            s = jnp.where(mask, s, NEG_FILL)
            scores.append(s)
            part = jnp.max(s, axis=-1, keepdims=True)
            top = part if top is None else jnp.maximum(top, part)
        total = None
        acc = None
        for s, val, mask in zip(scores, vals, masks):
            w = jnp.where(mask, jnp.exp(s - top), 0.0)
            part = jnp.sum(w, axis=-1, keepdims=True)
            total = part if total is None else total + part
            pv = jnp.dot(w.astype(jnp.bfloat16), val, preferred_element_type=jnp.float32)
            acc = pv if acc is None else acc + pv
        out = (acc / total).astype(o_ref.dtype)
        for g in range(group):
            o_ref[:, pl.ds((head * group + g) * HEAD_DIM, HEAD_DIM)] = out[g * rows:(g + 1) * rows]


def attend(q, suf, visible, chunks):
    rows, width = q.shape
    keys_total = suf.shape[1] + sum(c.size // (2 * suf.shape[2]) for c in chunks)
    flops = 4 * rows * width * keys_total
    nbytes = 2 * (q.size * 2 + suf.size + sum(c.size for c in chunks))
    return pl.pallas_call(
        functools.partial(attention_kernel, len(chunks)),
        out_shape=jax.ShapeDtypeStruct((rows, width), jnp.bfloat16),
        cost_estimate=pl.CostEstimate(
            flops=flops, transcendentals=rows * (width // HEAD_DIM) * keys_total, bytes_accessed=nbytes
        ),
    )(q, suf, visible, *chunks)


def solution(mesh):
    in_specs = (
        P(("groups", "replica"), None, "tensor"),
        P(("groups", "replica"), None, None, "tensor"),
        P(("groups", "replica"), None, "tensor", None),
        P("groups", None),
        P("groups", None),
        P("groups"),
    )
    out_specs = P(("groups", "replica"), None, "tensor")
    return jax.shard_map(
        on_device, mesh=mesh, in_specs=in_specs, out_specs=out_specs, check_vma=False
    )
```

time: 93.6 us -> 73.4 us (0.78)
  the two profiles are of different devices: /device:TPU:1 before, /device:TPU:12 now
where the time goes in v3:
time: 73.4 us; the launch traced here: 73 us
  waiting for transfers between devices  27.2 us (37%)
  starting transfers between devices  19.9 us (27%)
  Pallas kernels  17.8 us (24%)
  other arithmetic  4 us (5%)
  local copies, waits for them, and re-layouts  3.99 us (5%)
    ppermute x12, waiting for transfers between devices, on_device(): lax.ppermute(payload[distance - 1, shift], ('replica', 'tensor'), pairs)  27.2 us
    ppermute x12, starting transfers between devices, on_device(): lax.ppermute(payload[distance - 1, shift], ('replica', 'tensor'), pairs)  19.9 us
    pallas_call x1, Pallas kernels, attend(): pl.pallas_call(functools.partial(attention_kernel, len(chunks)), out_shap...  9.99 us
    pallas_call x1, Pallas kernels, pack_pages(): pl.pallas_call(functools.partial(gather_kernel, slot_cap, tensor_count),...  7.8 us
    squeeze x1, local copies, waits for them, and re-layouts, on_device(): payload[distance - 1, shift]  1.58 us
  transfers between devices with their start and end apart: 12, of which 7 were waited for; matrix products, arithmetic and copies ran while one was open for 3% of the time, Pallas kernels for 0%

profile of v3, /device:TPU:12, one launch (start us, length us, event | category | flops | bytes accessed | tf_op | source)
XLA Modules:
  0.0 73.0 jit_solution(3793209212756775368)
XLA Ops:
  0.0 0.8 %pad_add_fusion = s32[8,8]{1,0:T(8,128)S(1)} fusion(s32[4,8]{1,0:T(4,128)} %param.9), kind=kLoop, calls=%fused_computation.21 | loop fusion | flops 64 | bytes 384 | tf_op jit(solution)/shard_map/concatenate | solution.py:70
  0.8 0.7 fusion.3
  1.5 0.8 %pad_add_fusion.1 = s32[8,8]{1,0:T(8,128)S(1)} fusion(s32[4,8]{1,0:T(4,128)} %param.10), kind=kLoop, calls=%fused_computation.22 | loop fusion | flops 64 | bytes 384 | tf_op jit(solution)/shard_map/concatenate | solution.py:71
  2.3 0.2 multiply_reduce_fusion
  2.5 0.3 fusion
  2.8 0.6 pad_add_fusion.2.idx_ref
  3.4 7.8 %shard_map.64 = bf16[3,4,4,2,32,256]{5,4,3,2,1,0:T(8,128)(2,1)} custom-call(s32[13]{0:T(128)} %pad_add_fusion.2.idx_ref, bf16[12,2,32,1024]{3,2,1,0:T(8,128)(2,1)} %pool_ref.1), custom_call_target="tpu_custom_call" | custom-call | bytes 3145728 | tf_op jit(solution)/shard_map/pallas_call | solution.py:50
  11.2 1.6 %slice_bitcast_fusion = (bf16[4,2,32,256]{3,2,1,0:T(8,128)(2,1)S(1)}, bf16[4,2,32,256]{3,2,1,0:T(8,128)(2,1)S(1)}, bf16[4,2,32,256]{3,2,1,0:T(8,128)(2,1)S(1)}, ...) fusion(bf16[3,4,4,2,32,256]{5,4,3,2,1,0:T(8,128)(2,1)} %shard_m, ...), kind=kLoop, calls=%fused_computation | loop fusion | bytes 3145728 | tf_op jit(solution)/shard_map/squeeze | solution.py:86
  12.8 1.5 %collective-permute-start = (bf16[4,2,32,256]{3,2,1,0:T(8,128)(2,1)S(1)}, bf16[4,2,32,256]{3,2,1,0:T(8,128)(2,1)S(1)}, u32[]{:S(2)}, u32[]{:S(2)}) collective-permute-start(bf16[4,2,32,256]{3,2,1,0:T(8,128)(2,1)S(1)} %get-tuple-element.20), channel_id=1, source_target_pairs={{0,4},{1,5},{2,6},{3,7},{4,8},{5,9},{6,10},{7,11},{8,12},{9,13},{1... | collective-permute-start | bytes 393224 | tf_op jit(solution)/shard_map/ppermute | solution.py:86
  14.3 0.9 %collective-permute-start.1 = (bf16[4,2,32,256]{3,2,1,0:T(8,128)(2,1)S(1)}, bf16[4,2,32,256]{3,2,1,0:T(8,128)(2,1)S(1)}, u32[]{:S(2)}, u32[]{:S(2)}) collective-permute-start(bf16[4,2,32,256]{3,2,1,0:T(8,128)(2,1)S(1)} %get-tuple-element.19), channel_id=1, source_target_pairs={{0,5},{1,6},{2,7},{3,4},{4,9},{5,10},{6,11},{7,8},{8,13},{9,14},{1... | collective-permute-start | bytes 393224 | tf_op jit(solution)/shard_map/ppermute | solution.py:86
  15.2 1.3 %collective-permute-start.10 = (bf16[4,2,32,256]{3,2,1,0:T(8,128)(2,1)S(1)}, bf16[4,2,32,256]{3,2,1,0:T(8,128)(2,1)S(1)}, u32[]{:S(2)}, u32[]{:S(2)}) collective-permute-start(bf16[4,2,32,256]{3,2,1,0:T(8,128)(2,1)S(1)} %get-tuple-element.10), channel_id=1, source_target_pairs={{0,14},{1,15},{2,12},{3,13},{4,2},{5,3},{6,0},{7,1},{8,6},{9,7},{1... | collective-permute-start | bytes 393224 | tf_op jit(solution)/shard_map/ppermute | solution.py:86
  16.5 3.5 %collective-permute-start.11 = (bf16[4,2,32,256]{3,2,1,0:T(8,128)(2,1)S(1)}, bf16[4,2,32,256]{3,2,1,0:T(8,128)(2,1)S(1)}, u32[]{:S(2)}, u32[]{:S(2)}) collective-permute-start(bf16[4,2,32,256]{3,2,1,0:T(8,128)(2,1)S(1)} %get-tuple-element.9), channel_id=1, source_target_pairs={{0,15},{1,12},{2,13},{3,14},{4,3},{5,0},{6,1},{7,2},{8,7},{9,4},{1... | collective-permute-start | bytes 393224 | tf_op jit(solution)/shard_map/ppermute | solution.py:86
  20.2 0.1 add.94
  20.3 0.6 collective-permute-start.3
  20.9 0.2 collective-permute-done.1.rest_1_
  21.0 2.9 %collective-permute-start.4 = (bf16[4,2,32,256]{3,2,1,0:T(8,128)(2,1)S(1)}, bf16[4,2,32,256]{3,2,1,0:T(8,128)(2,1)S(1)}, u32[]{:S(2)}, u32[]{:S(2)}) collective-permute-start(bf16[4,2,32,256]{3,2,1,0:T(8,128)(2,1)S(1)} %get-tuple-element.16), channel_id=1, source_target_pairs={{0,8},{1,9},{2,10},{3,11},{4,12},{5,13},{6,14},{7,15},{8,0},{9,1},... | collective-permute-start | bytes 393224 | tf_op jit(solution)/shard_map/ppermute | solution.py:86
  24.0 0.1 and.35
  24.1 0.6 dynamic_slice.15
  24.7 0.1 add.96
  24.8 1.0 %collective-permute-done.10.rest_10_ = bf16[4,2,32,256]{3,2,1,0:T(8,128)(2,1)S(1)} collective-permute-done((bf16[4,2,32,256]{3,2,1,0:T(8,128)(2,1)S(1)}, bf16[4,2,32,256]{3,2,1,0:T(8,128)(2,1)S(1)}, u32[]{:S(2)}, u32[]{:S(2)}) %collective-permute-start.10) | collective-permute-done | bytes 131104 | tf_op jit(solution)/shard_map/ppermute | solution.py:86
  25.7 4.5 %collective-permute-start.5 = (bf16[4,2,32,256]{3,2,1,0:T(8,128)(2,1)S(1)}, bf16[4,2,32,256]{3,2,1,0:T(8,128)(2,1)S(1)}, u32[]{:S(2)}, u32[]{:S(2)}) collective-permute-start(bf16[4,2,32,256]{3,2,1,0:T(8,128)(2,1)S(1)} %get-tuple-element.15), channel_id=1, source_target_pairs={{0,9},{1,10},{2,11},{3,8},{4,13},{5,14},{6,15},{7,12},{8,1},{9,2},... | collective-permute-start | bytes 393224 | tf_op jit(solution)/shard_map/ppermute | solution.py:86
  30.2 4.3 %collective-permute-start.6 = (bf16[4,2,32,256]{3,2,1,0:T(8,128)(2,1)S(1)}, bf16[4,2,32,256]{3,2,1,0:T(8,128)(2,1)S(1)}, u32[]{:S(2)}, u32[]{:S(2)}) collective-permute-start(bf16[4,2,32,256]{3,2,1,0:T(8,128)(2,1)S(1)} %get-tuple-element.14), channel_id=1, source_target_pairs={{0,10},{1,11},{2,8},{3,9},{4,14},{5,15},{6,12},{7,13},{8,2},{9,3},... | collective-permute-start | bytes 393224 | tf_op jit(solution)/shard_map/ppermute | solution.py:86
  34.5 0.4 collective-permute-start.8
  34.9 13.3 %collective-permute-done.4.rest_4_ = bf16[4,2,32,256]{3,2,1,0:T(8,128)(2,1)S(1)} collective-permute-done((bf16[4,2,32,256]{3,2,1,0:T(8,128)(2,1)S(1)}, bf16[4,2,32,256]{3,2,1,0:T(8,128)(2,1)S(1)}, u32[]{:S(2)}, u32[]{:S(2)}) %collective-permute-start.4) | collective-permute-done | bytes 131104 | tf_op jit(solution)/shard_map/ppermute | solution.py:86
  48.2 0.2 collective-permute-start.9
  48.3 1.2 %and_convert_fusion.vis_ref = s32[12,1,128]{2,1,0:T(1,128)} fusion(pred[12,1,128]{2,1,0:T(4,128)(4,1)S(1)} %and.35, s32[12,1,128]{2,1,0:T(1,128)S(1)} %add.94, s32[]{:T(128)} %bitcast.3, s32[128]{0:T(128)S(1)} %add.96), kind=kLoop, calls=%fused_computation.12 | loop fusion | flops 6144 | bytes 14340 | tf_op jit(solution)/shard_map/convert_element_type | solution.py:105
  49.6 1.4 %collective-permute-done.5.rest_5_ = bf16[4,2,32,256]{3,2,1,0:T(8,128)(2,1)S(1)} collective-permute-done((bf16[4,2,32,256]{3,2,1,0:T(8,128)(2,1)S(1)}, bf16[4,2,32,256]{3,2,1,0:T(8,128)(2,1)S(1)}, u32[]{:S(2)}, u32[]{:S(2)}) %collective-permute-start.5) | collective-permute-done | bytes 131104 | tf_op jit(solution)/shard_map/ppermute | solution.py:86
  51.0 5.5 %collective-permute-done.6.rest_6_ = bf16[4,2,32,256]{3,2,1,0:T(8,128)(2,1)S(1)} collective-permute-done((bf16[4,2,32,256]{3,2,1,0:T(8,128)(2,1)S(1)}, bf16[4,2,32,256]{3,2,1,0:T(8,128)(2,1)S(1)}, u32[]{:S(2)}, u32[]{:S(2)}) %collective-permute-start.6) | collective-permute-done | bytes 131104 | tf_op jit(solution)/shard_map/ppermute | solution.py:86
  56.5 2.8 %collective-permute-done.7.rest_7_ = bf16[4,2,32,256]{3,2,1,0:T(8,128)(2,1)S(1)} collective-permute-done((bf16[4,2,32,256]{3,2,1,0:T(8,128)(2,1)S(1)}, bf16[4,2,32,256]{3,2,1,0:T(8,128)(2,1)S(1)}, u32[]{:S(2)}, u32[]{:S(2)}) %collective-permute-start.7) | collective-permute-done | bytes 131104 | tf_op jit(solution)/shard_map/ppermute | solution.py:86
  59.2 3.1 %collective-permute-done.9.rest_9_ = bf16[4,2,32,256]{3,2,1,0:T(8,128)(2,1)S(1)} collective-permute-done((bf16[4,2,32,256]{3,2,1,0:T(8,128)(2,1)S(1)}, bf16[4,2,32,256]{3,2,1,0:T(8,128)(2,1)S(1)}, u32[]{:S(2)}, u32[]{:S(2)}) %collective-permute-start.9) | collective-permute-done | bytes 131104 | tf_op jit(solution)/shard_map/ppermute | solution.py:86
  62.5 0.6 copy-done.11
  63.0 10.0 %shard_map.65 = bf16[128,2048]{1,0:T(8,128)(2,1)} custom-call(bf16[128,2048]{1,0:T(8,128)(2,1)} %bitcast.31, bf16[2,128,256]{2,1,0:T(8,128)(2,1)} %bitcast.32, s32[12,1,128]{2,1,0:T(1,128)} %and_convert_fusion.vis_ref, bf16[4,2,32,256]{3,2,1,0:T(8,128)(2,1)} %copy-done, bf16[4,2,32,256]{3,2,1,0:T(8,128)(2,1)} %copy-done.1, ...), custom_call_target="tpu_custom_call" | custom-call | flops 1744830464 | bytes 2752512 | tf_op jit(solution)/shard_map/pallas_call | solution.py:159
  (44 shorter events, 0.5 us)
Async XLA Ops:
  11.2 12.8 %copy-start.12 = (s32[4]{0:T(128)S(1)}, s32[4]{0:T(128)}, u32[]{:S(2)}) copy-start(s32[4]{0:T(128)} %param.11) | copy-start | bytes 52
  12.8 7.4 %collective-permute-start = (bf16[4,2,32,256]{3,2,1,0:T(8,128)(2,1)S(1)}, bf16[4,2,32,256]{3,2,1,0:T(8,128)(2,1)S(1)}, u32[]{:S(2)}, u32[]{:S(2)}) collective-permute-start(bf16[4,2,32,256]{3,2,1,0:T(8,128)(2,1)S(1)} %get-tuple-element.20), channel_id=1, source_target_pairs={{0,4},{1,5},{2,6},{3,7},{4,8},{5,9},{6,10},{7,11},{8,12},{9,13},{1... | collective-permute-start | bytes 393224 | tf_op jit(solution)/shard_map/ppermute | solution.py:86
  14.3 6.7 %collective-permute-start.1 = (bf16[4,2,32,256]{3,2,1,0:T(8,128)(2,1)S(1)}, bf16[4,2,32,256]{3,2,1,0:T(8,128)(2,1)S(1)}, u32[]{:S(2)}, u32[]{:S(2)}) collective-permute-start(bf16[4,2,32,256]{3,2,1,0:T(8,128)(2,1)S(1)} %get-tuple-element.19), channel_id=1, source_target_pairs={{0,5},{1,6},{2,7},{3,4},{4,9},{5,10},{6,11},{7,8},{8,13},{9,14},{1... | collective-permute-start | bytes 393224 | tf_op jit(solution)/shard_map/ppermute | solution.py:86
  15.2 10.5 %collective-permute-start.10 = (bf16[4,2,32,256]{3,2,1,0:T(8,128)(2,1)S(1)}, bf16[4,2,32,256]{3,2,1,0:T(8,128)(2,1)S(1)}, u32[]{:S(2)}, u32[]{:S(2)}) collective-permute-start(bf16[4,2,32,256]{3,2,1,0:T(8,128)(2,1)S(1)} %get-tuple-element.10), channel_id=1, source_target_pairs={{0,14},{1,15},{2,12},{3,13},{4,2},{5,3},{6,0},{7,1},{8,6},{9,7},{1... | collective-permute-start | bytes 393224 | tf_op jit(solution)/shard_map/ppermute | solution.py:86
  16.5 13.8 %collective-permute-start.11 = (bf16[4,2,32,256]{3,2,1,0:T(8,128)(2,1)S(1)}, bf16[4,2,32,256]{3,2,1,0:T(8,128)(2,1)S(1)}, u32[]{:S(2)}, u32[]{:S(2)}) collective-permute-start(bf16[4,2,32,256]{3,2,1,0:T(8,128)(2,1)S(1)} %get-tuple-element.9), channel_id=1, source_target_pairs={{0,15},{1,12},{2,13},{3,14},{4,3},{5,0},{6,1},{7,2},{8,7},{9,4},{1... | collective-permute-start | bytes 393224 | tf_op jit(solution)/shard_map/ppermute | solution.py:86
  20.0 14.5 %collective-permute-start.2 = (bf16[4,2,32,256]{3,2,1,0:T(8,128)(2,1)S(1)}, bf16[4,2,32,256]{3,2,1,0:T(8,128)(2,1)S(1)}, u32[]{:S(2)}, u32[]{:S(2)}) collective-permute-start(bf16[4,2,32,256]{3,2,1,0:T(8,128)(2,1)S(1)} %get-tuple-element.18), channel_id=1, source_target_pairs={{0,6},{1,7},{2,4},{3,5},{4,10},{5,11},{6,8},{7,9},{8,14},{9,15},{1... | collective-permute-start | bytes 393224 | tf_op jit(solution)/shard_map/ppermute | solution.py:86
  20.3 42.1 %copy-start = (bf16[4,2,32,256]{3,2,1,0:T(8,128)(2,1)}, bf16[4,2,32,256]{3,2,1,0:T(8,128)(2,1)S(1)}, u32[]{:S(2)}) copy-start(bf16[4,2,32,256]{3,2,1,0:T(8,128)(2,1)S(1)} %collective-permute-done.rest_0_) | copy-start | bytes 393220
  20.3 14.2 %collective-permute-start.3 = (bf16[4,2,32,256]{3,2,1,0:T(8,128)(2,1)S(1)}, bf16[4,2,32,256]{3,2,1,0:T(8,128)(2,1)S(1)}, u32[]{:S(2)}, u32[]{:S(2)}) collective-permute-start(bf16[4,2,32,256]{3,2,1,0:T(8,128)(2,1)S(1)} %get-tuple-element.17), channel_id=1, source_target_pairs={{0,7},{1,4},{2,5},{3,6},{4,11},{5,8},{6,9},{7,10},{8,15},{9,12},{1... | collective-permute-start | bytes 393224 | tf_op jit(solution)/shard_map/ppermute | solution.py:86
  21.0 41.4 %copy-start.1 = (bf16[4,2,32,256]{3,2,1,0:T(8,128)(2,1)}, bf16[4,2,32,256]{3,2,1,0:T(8,128)(2,1)S(1)}, u32[]{:S(2)}) copy-start(bf16[4,2,32,256]{3,2,1,0:T(8,128)(2,1)S(1)} %collective-permute-done.1.rest_1_) | copy-start | bytes 393220
  21.0 27.1 %collective-permute-start.4 = (bf16[4,2,32,256]{3,2,1,0:T(8,128)(2,1)S(1)}, bf16[4,2,32,256]{3,2,1,0:T(8,128)(2,1)S(1)}, u32[]{:S(2)}, u32[]{:S(2)}) collective-permute-start(bf16[4,2,32,256]{3,2,1,0:T(8,128)(2,1)S(1)} %get-tuple-element.16), channel_id=1, source_target_pairs={{0,8},{1,9},{2,10},{3,11},{4,12},{5,13},{6,14},{7,15},{8,0},{9,1},... | collective-permute-start | bytes 393224 | tf_op jit(solution)/shard_map/ppermute | solution.py:86
  25.7 36.7 %copy-start.2 = (bf16[4,2,32,256]{3,2,1,0:T(8,128)(2,1)}, bf16[4,2,32,256]{3,2,1,0:T(8,128)(2,1)S(1)}, u32[]{:S(2)}) copy-start(bf16[4,2,32,256]{3,2,1,0:T(8,128)(2,1)S(1)} %collective-permute-done.10.rest_10_) | copy-start | bytes 393220
  25.7 25.3 %collective-permute-start.5 = (bf16[4,2,32,256]{3,2,1,0:T(8,128)(2,1)S(1)}, bf16[4,2,32,256]{3,2,1,0:T(8,128)(2,1)S(1)}, u32[]{:S(2)}, u32[]{:S(2)}) collective-permute-start(bf16[4,2,32,256]{3,2,1,0:T(8,128)(2,1)S(1)} %get-tuple-element.15), channel_id=1, source_target_pairs={{0,9},{1,10},{2,11},{3,8},{4,13},{5,14},{6,15},{7,12},{8,1},{9,2},... | collective-permute-start | bytes 393224 | tf_op jit(solution)/shard_map/ppermute | solution.py:86
  30.2 32.2 %copy-start.3 = (bf16[4,2,32,256]{3,2,1,0:T(8,128)(2,1)}, bf16[4,2,32,256]{3,2,1,0:T(8,128)(2,1)S(1)}, u32[]{:S(2)}) copy-start(bf16[4,2,32,256]{3,2,1,0:T(8,128)(2,1)S(1)} %collective-permute-done.11.rest_11_) | copy-start | bytes 393220
  30.2 26.2 %collective-permute-start.6 = (bf16[4,2,32,256]{3,2,1,0:T(8,128)(2,1)S(1)}, bf16[4,2,32,256]{3,2,1,0:T(8,128)(2,1)S(1)}, u32[]{:S(2)}, u32[]{:S(2)}) collective-permute-start(bf16[4,2,32,256]{3,2,1,0:T(8,128)(2,1)S(1)} %get-tuple-element.14), channel_id=1, source_target_pairs={{0,10},{1,11},{2,8},{3,9},{4,14},{5,15},{6,12},{7,13},{8,2},{9,3},... | collective-permute-start | bytes 393224 | tf_op jit(solution)/shard_map/ppermute | solution.py:86
  34.5 27.9 %copy-start.4 = (bf16[4,2,32,256]{3,2,1,0:T(8,128)(2,1)}, bf16[4,2,32,256]{3,2,1,0:T(8,128)(2,1)S(1)}, u32[]{:S(2)}) copy-start(bf16[4,2,32,256]{3,2,1,0:T(8,128)(2,1)S(1)} %collective-permute-done.2.rest_2_) | copy-start | bytes 393220
  34.5 24.7 %collective-permute-start.7 = (bf16[4,2,32,256]{3,2,1,0:T(8,128)(2,1)S(1)}, bf16[4,2,32,256]{3,2,1,0:T(8,128)(2,1)S(1)}, u32[]{:S(2)}, u32[]{:S(2)}) collective-permute-start(bf16[4,2,32,256]{3,2,1,0:T(8,128)(2,1)S(1)} %get-tuple-element.13), channel_id=1, source_target_pairs={{0,11},{1,8},{2,9},{3,10},{4,15},{5,12},{6,13},{7,14},{8,3},{9,0},... | collective-permute-start | bytes 393224 | tf_op jit(solution)/shard_map/ppermute | solution.py:86
  34.5 27.9 %copy-start.5 = (bf16[4,2,32,256]{3,2,1,0:T(8,128)(2,1)}, bf16[4,2,32,256]{3,2,1,0:T(8,128)(2,1)S(1)}, u32[]{:S(2)}) copy-start(bf16[4,2,32,256]{3,2,1,0:T(8,128)(2,1)S(1)} %collective-permute-done.3.rest_3_) | copy-start | bytes 393220
  34.5 24.7 %collective-permute-start.8 = (bf16[4,2,32,256]{3,2,1,0:T(8,128)(2,1)S(1)}, bf16[4,2,32,256]{3,2,1,0:T(8,128)(2,1)S(1)}, u32[]{:S(2)}, u32[]{:S(2)}) collective-permute-start(bf16[4,2,32,256]{3,2,1,0:T(8,128)(2,1)S(1)} %get-tuple-element.12), channel_id=1, source_target_pairs={{0,12},{1,13},{2,14},{3,15},{4,0},{5,1},{6,2},{7,3},{8,4},{9,5},{1... | collective-permute-start | bytes 393224 | tf_op jit(solution)/shard_map/ppermute | solution.py:86
  48.2 14.3 %copy-start.6 = (bf16[4,2,32,256]{3,2,1,0:T(8,128)(2,1)}, bf16[4,2,32,256]{3,2,1,0:T(8,128)(2,1)S(1)}, u32[]{:S(2)}) copy-start(bf16[4,2,32,256]{3,2,1,0:T(8,128)(2,1)S(1)} %collective-permute-done.4.rest_4_) | copy-start | bytes 393220
  48.2 14.2 %collective-permute-start.9 = (bf16[4,2,32,256]{3,2,1,0:T(8,128)(2,1)S(1)}, bf16[4,2,32,256]{3,2,1,0:T(8,128)(2,1)S(1)}, u32[]{:S(2)}, u32[]{:S(2)}) collective-permute-start(bf16[4,2,32,256]{3,2,1,0:T(8,128)(2,1)S(1)} %get-tuple-element.11), channel_id=1, source_target_pairs={{0,13},{1,14},{2,15},{3,12},{4,1},{5,2},{6,3},{7,0},{8,5},{9,6},{1... | collective-permute-start | bytes 393224 | tf_op jit(solution)/shard_map/ppermute | solution.py:86
  51.0 11.5 %copy-start.7 = (bf16[4,2,32,256]{3,2,1,0:T(8,128)(2,1)}, bf16[4,2,32,256]{3,2,1,0:T(8,128)(2,1)S(1)}, u32[]{:S(2)}) copy-start(bf16[4,2,32,256]{3,2,1,0:T(8,128)(2,1)S(1)} %collective-permute-done.5.rest_5_) | copy-start | bytes 393220
  56.5 6.0 %copy-start.8 = (bf16[4,2,32,256]{3,2,1,0:T(8,128)(2,1)}, bf16[4,2,32,256]{3,2,1,0:T(8,128)(2,1)S(1)}, u32[]{:S(2)}) copy-start(bf16[4,2,32,256]{3,2,1,0:T(8,128)(2,1)S(1)} %collective-permute-done.6.rest_6_) | copy-start | bytes 393220
  59.2 3.2 %copy-start.9 = (bf16[4,2,32,256]{3,2,1,0:T(8,128)(2,1)}, bf16[4,2,32,256]{3,2,1,0:T(8,128)(2,1)S(1)}, u32[]{:S(2)}) copy-start(bf16[4,2,32,256]{3,2,1,0:T(8,128)(2,1)S(1)} %collective-permute-done.7.rest_7_) | copy-start | bytes 393220
  59.2 3.2 %copy-start.10 = (bf16[4,2,32,256]{3,2,1,0:T(8,128)(2,1)}, bf16[4,2,32,256]{3,2,1,0:T(8,128)(2,1)S(1)}, u32[]{:S(2)}) copy-start(bf16[4,2,32,256]{3,2,1,0:T(8,128)(2,1)S(1)} %collective-permute-done.8.rest_8_) | copy-start | bytes 393220
  62.4 0.7 copy-start.11

commit v4 on v3

--- a/solution.py
+++ b/solution.py
@@ -25,34 +25,38 @@
     return matched[:, None, :] * (ranking[:, None, :] == places[None, :, None]).astype(jnp.int32)
 
 
-def gather_kernel(cap, tensor_count, idx_ref, pool_ref, o_ref):
-    me = idx_ref[idx_ref.shape[0] - 1]
-    lanes = o_ref.shape[-1]
-    for shift in range(tensor_count):
-        start = pl.multiple_of(((me + shift) % tensor_count) * lanes, lanes)
-        o_ref[0, shift, 0] = pool_ref[0, :, :, pl.ds(start, lanes)]
+def gather_kernel(span_count, slot_cap, tensor_count, idx_ref, pool_ref, *out_refs):
+    me = idx_ref[span_count * slot_cap]
+    lanes = out_refs[0].shape[-1]
+    starts = [
+        pl.multiple_of(((me + shift) % tensor_count) * lanes, lanes) for shift in range(tensor_count)
+    ]
+    for distance in range(span_count):
+        for slot in range(slot_cap):
+            page = idx_ref[distance * slot_cap + slot]
+            for shift in range(tensor_count):
+                out_refs[distance * tensor_count + shift][slot] = pool_ref[
+                    page, :, :, pl.ds(starts[shift], lanes)
+                ]
 
 
 def pack_pages(pool_part, chosen, me, span_count, slot_cap, tensor_count):
     pages, kv, rows, width = pool_part.shape
     lanes = width // tensor_count
     table = jnp.concatenate([chosen.reshape(-1), me.reshape(1)]).astype(jnp.int32)
+    piece = (slot_cap, kv, rows, lanes)
+    count = span_count * tensor_count
     grid_spec = pltpu.PrefetchScalarGridSpec(
         num_scalar_prefetch=1,
-        grid=(span_count * slot_cap,),
-        in_specs=[pl.BlockSpec((1, kv, rows, width), lambda i, idx: (idx[i], 0, 0, 0))],
-        out_specs=pl.BlockSpec(
-            (1, tensor_count, 1, kv, rows, lanes),
-            lambda i, idx: (i // slot_cap, 0, i % slot_cap, 0, 0, 0),
-        ),
+        grid=(1,),
+        in_specs=[pl.BlockSpec((pages, kv, rows, width), lambda i, idx: (0, 0, 0, 0))],
+        out_specs=[pl.BlockSpec(piece, lambda i, idx: (0, 0, 0, 0)) for _ in range(count)],
     )
-    nbytes = 2 * 2 * span_count * slot_cap * kv * rows * width
+    nbytes = 2 * (pool_part.size + span_count * slot_cap * kv * rows * width)
     return pl.pallas_call(
-        functools.partial(gather_kernel, slot_cap, tensor_count),
+        functools.partial(gather_kernel, span_count, slot_cap, tensor_count),
         grid_spec=grid_spec,
-        out_shape=jax.ShapeDtypeStruct(
-            (span_count, tensor_count, slot_cap, kv, rows, lanes), pool_part.dtype
-        ),
+        out_shape=[jax.ShapeDtypeStruct(piece, pool_part.dtype) for _ in range(count)],
         cost_estimate=pl.CostEstimate(flops=0, transcendentals=0, bytes_accessed=nbytes),
     )(table, pool_part)
 
@@ -83,7 +87,7 @@
                 for peer in range(tensor_count):
                     target = ((source + distance) % replicas) * tensor_count + (peer + shift) % tensor_count
                     pairs.append((source * tensor_count + peer, target))
-            arrivals.append(lax.ppermute(payload[distance - 1, shift], ("replica", "tensor"), pairs))
+            arrivals.append(lax.ppermute(payload[(distance - 1) * tensor_count + shift], ("replica", "tensor"), pairs))
 
     quarter = page_pool.shape[2]
     page_rows = quarter * tensor_count

time: 73.4 us -> 69.6 us (0.948)
  the two profiles are of different devices: /device:TPU:12 before, /device:TPU:1 now
where the time goes in v4:
time: 69.6 us; the launch traced here: 69.3 us
  starting transfers between devices  35.2 us (51%)
  waiting for transfers between devices  14.3 us (21%)
  Pallas kernels  13.4 us (19%)
  other arithmetic  3.92 us (6%)
  local copies, waits for them, and re-layouts  2.4 us (3%)
    ppermute x12, starting transfers between devices, on_device(): lax.ppermute(payload[(distance - 1) * tensor_count + shift], ('replica',...  35.2 us
    ppermute x12, waiting for transfers between devices, on_device(): lax.ppermute(payload[(distance - 1) * tensor_count + shift], ('replica',...  14.3 us
    pallas_call x1, Pallas kernels, attend(): pl.pallas_call(functools.partial(attention_kernel, len(chunks)), out_shap...  9.99 us
    pallas_call x1, Pallas kernels, pack_pages(): pl.pallas_call(functools.partial(gather_kernel, span_count, slot_cap, ten...  3.4 us
  transfers between devices with their start and end apart: 12, of which 3 were waited for; matrix products, arithmetic and copies ran while one was open for 3% of the time, Pallas kernels for 0%

profile of v4, /device:TPU:1, one launch (start us, length us, event | category | flops | bytes accessed | tf_op | source)
XLA Modules:
  0.0 69.3 jit_solution(9656825522955392534)
XLA Ops:
  0.0 0.8 %pad_add_fusion = s32[8,8]{1,0:T(8,128)S(1)} fusion(s32[4,8]{1,0:T(4,128)} %param.9), kind=kLoop, calls=%fused_computation.9 | loop fusion | flops 64 | bytes 384 | tf_op jit(solution)/shard_map/concatenate | solution.py:74
  0.8 0.7 fusion.3
  1.5 0.8 %pad_add_fusion.1 = s32[8,8]{1,0:T(8,128)S(1)} fusion(s32[4,8]{1,0:T(4,128)} %param.10), kind=kLoop, calls=%fused_computation.10 | loop fusion | flops 64 | bytes 384 | tf_op jit(solution)/shard_map/concatenate | solution.py:75
  2.2 0.1 fusion.2
  2.3 0.2 multiply_reduce_fusion
  2.5 0.3 fusion
  2.8 0.1 reshape.139
  2.8 0.6 pad_add_fusion.2.idx_ref
  3.4 3.4 %shard_map.64 = (bf16[4,2,32,256]{3,2,1,0:T(8,128)(2,1)}, bf16[4,2,32,256]{3,2,1,0:T(8,128)(2,1)}, bf16[4,2,32,256]{3,2,1,0:T(8,128)(2,1)}, bf16[4,2,32,256]{3,2...) custom-call(s32[13]{0:T(128)} %pad_add_fusion.2.idx_ref, ...), custom_call_target="tpu_custom_call" | custom-call | bytes 3145728 | tf_op jit(solution)/shard_map/pallas_call | solution.py:56
  6.8 2.1 %collective-permute-start = (bf16[4,2,32,256]{3,2,1,0:T(8,128)(2,1)}, bf16[4,2,32,256]{3,2,1,0:T(8,128)(2,1)S(1)}, u32[]{:S(2)}, u32[]{:S(2)}) collective-permute-start(bf16[4,2,32,256]{3,2,1,0:T(8,128)(2,1)} %get-tuple-element.17), channel_id=1, source_target_pairs={{0,4},{1,5},{2,6},{3,7},{4,8},{5,9},{6,10},{7,11},{8,12},{9,13},{1... | collective-permute-start | bytes 393224 | tf_op jit(solution)/shard_map/ppermute | solution.py:90
  9.0 3.1 %collective-permute-start.1 = (bf16[4,2,32,256]{3,2,1,0:T(8,128)(2,1)}, bf16[4,2,32,256]{3,2,1,0:T(8,128)(2,1)S(1)}, u32[]{:S(2)}, u32[]{:S(2)}) collective-permute-start(bf16[4,2,32,256]{3,2,1,0:T(8,128)(2,1)} %get-tuple-element.18), channel_id=1, source_target_pairs={{0,5},{1,6},{2,7},{3,4},{4,9},{5,10},{6,11},{7,8},{8,13},{9,14},{1... | collective-permute-start | bytes 393224 | tf_op jit(solution)/shard_map/ppermute | solution.py:90
  12.0 1.3 %collective-permute-start.2 = (bf16[4,2,32,256]{3,2,1,0:T(8,128)(2,1)}, bf16[4,2,32,256]{3,2,1,0:T(8,128)(2,1)S(1)}, u32[]{:S(2)}, u32[]{:S(2)}) collective-permute-start(bf16[4,2,32,256]{3,2,1,0:T(8,128)(2,1)} %get-tuple-element.19), channel_id=1, source_target_pairs={{0,6},{1,7},{2,4},{3,5},{4,10},{5,11},{6,8},{7,9},{8,14},{9,15},{1... | collective-permute-start | bytes 393224 | tf_op jit(solution)/shard_map/ppermute | solution.py:90
  13.3 0.3 collective-permute-start.3
  13.6 1.7 %collective-permute-start.4 = (bf16[4,2,32,256]{3,2,1,0:T(8,128)(2,1)}, bf16[4,2,32,256]{3,2,1,0:T(8,128)(2,1)S(1)}, u32[]{:S(2)}, u32[]{:S(2)}) collective-permute-start(bf16[4,2,32,256]{3,2,1,0:T(8,128)(2,1)} %get-tuple-element.21), channel_id=1, source_target_pairs={{0,8},{1,9},{2,10},{3,11},{4,12},{5,13},{6,14},{7,15},{8,0},{9,1},... | collective-permute-start | bytes 393224 | tf_op jit(solution)/shard_map/ppermute | solution.py:90
  15.3 0.6 dynamic_slice.15
  15.9 0.1 add.96
  16.1 0.1 and.35
  16.2 1.9 %collective-permute-start.5 = (bf16[4,2,32,256]{3,2,1,0:T(8,128)(2,1)}, bf16[4,2,32,256]{3,2,1,0:T(8,128)(2,1)S(1)}, u32[]{:S(2)}, u32[]{:S(2)}) collective-permute-start(bf16[4,2,32,256]{3,2,1,0:T(8,128)(2,1)} %get-tuple-element.22), channel_id=1, source_target_pairs={{0,9},{1,10},{2,11},{3,8},{4,13},{5,14},{6,15},{7,12},{8,1},{9,2},... | collective-permute-start | bytes 393224 | tf_op jit(solution)/shard_map/ppermute | solution.py:90
  18.1 3.1 %collective-permute-start.6 = (bf16[4,2,32,256]{3,2,1,0:T(8,128)(2,1)}, bf16[4,2,32,256]{3,2,1,0:T(8,128)(2,1)S(1)}, u32[]{:S(2)}, u32[]{:S(2)}) collective-permute-start(bf16[4,2,32,256]{3,2,1,0:T(8,128)(2,1)} %get-tuple-element.23), channel_id=1, source_target_pairs={{0,10},{1,11},{2,8},{3,9},{4,14},{5,15},{6,12},{7,13},{8,2},{9,3},... | collective-permute-start | bytes 393224 | tf_op jit(solution)/shard_map/ppermute | solution.py:90
  21.3 0.1 add.93
  21.4 0.1 add.94
  21.5 1.7 %collective-permute-start.7 = (bf16[4,2,32,256]{3,2,1,0:T(8,128)(2,1)}, bf16[4,2,32,256]{3,2,1,0:T(8,128)(2,1)S(1)}, u32[]{:S(2)}, u32[]{:S(2)}) collective-permute-start(bf16[4,2,32,256]{3,2,1,0:T(8,128)(2,1)} %get-tuple-element.24), channel_id=1, source_target_pairs={{0,11},{1,8},{2,9},{3,10},{4,15},{5,12},{6,13},{7,14},{8,3},{9,0},... | collective-permute-start | bytes 393224 | tf_op jit(solution)/shard_map/ppermute | solution.py:90
  23.2 1.9 %collective-permute-done.3.rest_3_ = bf16[4,2,32,256]{3,2,1,0:T(8,128)(2,1)S(1)} collective-permute-done((bf16[4,2,32,256]{3,2,1,0:T(8,128)(2,1)}, bf16[4,2,32,256]{3,2,1,0:T(8,128)(2,1)S(1)}, u32[]{:S(2)}, u32[]{:S(2)}) %collective-permute-start.3) | collective-permute-done | bytes 131104 | tf_op jit(solution)/shard_map/ppermute | solution.py:90
  25.2 1.1 %collective-permute-start.8 = (bf16[4,2,32,256]{3,2,1,0:T(8,128)(2,1)}, bf16[4,2,32,256]{3,2,1,0:T(8,128)(2,1)S(1)}, u32[]{:S(2)}, u32[]{:S(2)}) collective-permute-start(bf16[4,2,32,256]{3,2,1,0:T(8,128)(2,1)} %get-tuple-element.25), channel_id=1, source_target_pairs={{0,12},{1,13},{2,14},{3,15},{4,0},{5,1},{6,2},{7,3},{8,4},{9,5},{1... | collective-permute-start | bytes 393224 | tf_op jit(solution)/shard_map/ppermute | solution.py:90
  26.3 11.3 %collective-permute-done.4.rest_4_ = bf16[4,2,32,256]{3,2,1,0:T(8,128)(2,1)S(1)} collective-permute-done((bf16[4,2,32,256]{3,2,1,0:T(8,128)(2,1)}, bf16[4,2,32,256]{3,2,1,0:T(8,128)(2,1)S(1)}, u32[]{:S(2)}, u32[]{:S(2)}) %collective-permute-start.4) | collective-permute-done | bytes 131104 | tf_op jit(solution)/shard_map/ppermute | solution.py:90
  37.6 6.2 %collective-permute-start.9 = (bf16[4,2,32,256]{3,2,1,0:T(8,128)(2,1)}, bf16[4,2,32,256]{3,2,1,0:T(8,128)(2,1)S(1)}, u32[]{:S(2)}, u32[]{:S(2)}) collective-permute-start(bf16[4,2,32,256]{3,2,1,0:T(8,128)(2,1)} %get-tuple-element.26), channel_id=1, source_target_pairs={{0,13},{1,14},{2,15},{3,12},{4,1},{5,2},{6,3},{7,0},{8,5},{9,6},{1... | collective-permute-start | bytes 393224 | tf_op jit(solution)/shard_map/ppermute | solution.py:90
  43.8 2.5 %collective-permute-start.10 = (bf16[4,2,32,256]{3,2,1,0:T(8,128)(2,1)}, bf16[4,2,32,256]{3,2,1,0:T(8,128)(2,1)S(1)}, u32[]{:S(2)}, u32[]{:S(2)}) collective-permute-start(bf16[4,2,32,256]{3,2,1,0:T(8,128)(2,1)} %get-tuple-element.27), channel_id=1, source_target_pairs={{0,14},{1,15},{2,12},{3,13},{4,2},{5,3},{6,0},{7,1},{8,6},{9,7},{1... | collective-permute-start | bytes 393224 | tf_op jit(solution)/shard_map/ppermute | solution.py:90
  46.3 10.1 %collective-permute-start.11 = (bf16[4,2,32,256]{3,2,1,0:T(8,128)(2,1)}, bf16[4,2,32,256]{3,2,1,0:T(8,128)(2,1)S(1)}, u32[]{:S(2)}, u32[]{:S(2)}) collective-permute-start(bf16[4,2,32,256]{3,2,1,0:T(8,128)(2,1)} %get-tuple-element.28), channel_id=1, source_target_pairs={{0,15},{1,12},{2,13},{3,14},{4,3},{5,0},{6,1},{7,2},{8,7},{9,4},{1... | collective-permute-start | bytes 393224 | tf_op jit(solution)/shard_map/ppermute | solution.py:90
  56.4 1.2 %and_convert_fusion.vis_ref = s32[12,1,128]{2,1,0:T(1,128)} fusion(pred[12,1,128]{2,1,0:T(4,128)(4,1)S(1)} %and.35, s32[12,1,128]{2,1,0:T(1,128)S(1)} %add.94, s32[]{:T(128)} %bitcast.3, s32[128]{0:T(128)S(1)} %add.96), kind=kLoop, calls=%fused_computation | loop fusion | flops 6144 | bytes 14340 | tf_op jit(solution)/shard_map/convert_element_type | solution.py:109
  57.7 1.0 %collective-permute-done.11.rest_11_ = bf16[4,2,32,256]{3,2,1,0:T(8,128)(2,1)S(1)} collective-permute-done((bf16[4,2,32,256]{3,2,1,0:T(8,128)(2,1)}, bf16[4,2,32,256]{3,2,1,0:T(8,128)(2,1)S(1)}, u32[]{:S(2)}, u32[]{:S(2)}) %collective-permute-start.11) | collective-permute-done | bytes 131104 | tf_op jit(solution)/shard_map/ppermute | solution.py:90
  58.8 0.6 copy-done.11
  59.3 10.0 %shard_map.65 = bf16[128,2048]{1,0:T(8,128)(2,1)} custom-call(bf16[128,2048]{1,0:T(8,128)(2,1)} %bitcast.7, bf16[2,128,256]{2,1,0:T(8,128)(2,1)} %bitcast.8, s32[12,1,128]{2,1,0:T(1,128)} %and_convert_fusion.vis_ref, bf16[4,2,32,256]{3,2,1,0:T(8,128)(2,1)} %copy-done, bf16[4,2,32,256]{3,2,1,0:T(8,128)(2,1)} %copy-done.1, bf16[4,2,32,256]{3,2,1,0:T(8,128)(2,1)} %copy-done.2, ...), custom_call_target="tpu_custom_call" | custom-call | flops 1744830464 | bytes 2752512 | tf_op jit(solution)/shard_map/pallas_call | solution.py:163
  (43 shorter events, 0.3 us)
Async XLA Ops:
  0.0 15.3 %copy-start.12 = (s32[4]{0:T(128)S(1)}, s32[4]{0:T(128)}, u32[]{:S(2)}) copy-start(s32[4]{0:T(128)} %param.11) | copy-start | bytes 52
  6.8 9.3 %collective-permute-start = (bf16[4,2,32,256]{3,2,1,0:T(8,128)(2,1)}, bf16[4,2,32,256]{3,2,1,0:T(8,128)(2,1)S(1)}, u32[]{:S(2)}, u32[]{:S(2)}) collective-permute-start(bf16[4,2,32,256]{3,2,1,0:T(8,128)(2,1)} %get-tuple-element.17), channel_id=1, source_target_pairs={{0,4},{1,5},{2,6},{3,7},{4,8},{5,9},{6,10},{7,11},{8,12},{9,13},{1... | collective-permute-start | bytes 393224 | tf_op jit(solution)/shard_map/ppermute | solution.py:90
  9.0 9.2 %collective-permute-start.1 = (bf16[4,2,32,256]{3,2,1,0:T(8,128)(2,1)}, bf16[4,2,32,256]{3,2,1,0:T(8,128)(2,1)S(1)}, u32[]{:S(2)}, u32[]{:S(2)}) collective-permute-start(bf16[4,2,32,256]{3,2,1,0:T(8,128)(2,1)} %get-tuple-element.18), channel_id=1, source_target_pairs={{0,5},{1,6},{2,7},{3,4},{4,9},{5,10},{6,11},{7,8},{8,13},{9,14},{1... | collective-permute-start | bytes 393224 | tf_op jit(solution)/shard_map/ppermute | solution.py:90
  12.0 9.5 %collective-permute-start.2 = (bf16[4,2,32,256]{3,2,1,0:T(8,128)(2,1)}, bf16[4,2,32,256]{3,2,1,0:T(8,128)(2,1)S(1)}, u32[]{:S(2)}, u32[]{:S(2)}) collective-permute-start(bf16[4,2,32,256]{3,2,1,0:T(8,128)(2,1)} %get-tuple-element.19), channel_id=1, source_target_pairs={{0,6},{1,7},{2,4},{3,5},{4,10},{5,11},{6,8},{7,9},{8,14},{9,15},{1... | collective-permute-start | bytes 393224 | tf_op jit(solution)/shard_map/ppermute | solution.py:90
  13.3 11.9 %collective-permute-start.3 = (bf16[4,2,32,256]{3,2,1,0:T(8,128)(2,1)}, bf16[4,2,32,256]{3,2,1,0:T(8,128)(2,1)S(1)}, u32[]{:S(2)}, u32[]{:S(2)}) collective-permute-start(bf16[4,2,32,256]{3,2,1,0:T(8,128)(2,1)} %get-tuple-element.20), channel_id=1, source_target_pairs={{0,7},{1,4},{2,5},{3,6},{4,11},{5,8},{6,9},{7,10},{8,15},{9,12},{1... | collective-permute-start | bytes 393224 | tf_op jit(solution)/shard_map/ppermute | solution.py:90
  13.6 24.0 %collective-permute-start.4 = (bf16[4,2,32,256]{3,2,1,0:T(8,128)(2,1)}, bf16[4,2,32,256]{3,2,1,0:T(8,128)(2,1)S(1)}, u32[]{:S(2)}, u32[]{:S(2)}) collective-permute-start(bf16[4,2,32,256]{3,2,1,0:T(8,128)(2,1)} %get-tuple-element.21), channel_id=1, source_target_pairs={{0,8},{1,9},{2,10},{3,11},{4,12},{5,13},{6,14},{7,15},{8,0},{9,1},... | collective-permute-start | bytes 393224 | tf_op jit(solution)/shard_map/ppermute | solution.py:90
  16.2 42.5 %copy-start = (bf16[4,2,32,256]{3,2,1,0:T(8,128)(2,1)}, bf16[4,2,32,256]{3,2,1,0:T(8,128)(2,1)S(1)}, u32[]{:S(2)}) copy-start(bf16[4,2,32,256]{3,2,1,0:T(8,128)(2,1)S(1)} %collective-permute-done.rest_0_) | copy-start | bytes 393220
  16.2 27.6 %collective-permute-start.5 = (bf16[4,2,32,256]{3,2,1,0:T(8,128)(2,1)}, bf16[4,2,32,256]{3,2,1,0:T(8,128)(2,1)S(1)}, u32[]{:S(2)}, u32[]{:S(2)}) collective-permute-start(bf16[4,2,32,256]{3,2,1,0:T(8,128)(2,1)} %get-tuple-element.22), channel_id=1, source_target_pairs={{0,9},{1,10},{2,11},{3,8},{4,13},{5,14},{6,15},{7,12},{8,1},{9,2},... | collective-permute-start | bytes 393224 | tf_op jit(solution)/shard_map/ppermute | solution.py:90
  18.1 40.6 %copy-start.1 = (bf16[4,2,32,256]{3,2,1,0:T(8,128)(2,1)}, bf16[4,2,32,256]{3,2,1,0:T(8,128)(2,1)S(1)}, u32[]{:S(2)}) copy-start(bf16[4,2,32,256]{3,2,1,0:T(8,128)(2,1)S(1)} %collective-permute-done.1.rest_1_) | copy-start | bytes 393220
  18.1 28.2 %collective-permute-start.6 = (bf16[4,2,32,256]{3,2,1,0:T(8,128)(2,1)}, bf16[4,2,32,256]{3,2,1,0:T(8,128)(2,1)S(1)}, u32[]{:S(2)}, u32[]{:S(2)}) collective-permute-start(bf16[4,2,32,256]{3,2,1,0:T(8,128)(2,1)} %get-tuple-element.23), channel_id=1, source_target_pairs={{0,10},{1,11},{2,8},{3,9},{4,14},{5,15},{6,12},{7,13},{8,2},{9,3},... | collective-permute-start | bytes 393224 | tf_op jit(solution)/shard_map/ppermute | solution.py:90
  21.5 37.2 %copy-start.2 = (bf16[4,2,32,256]{3,2,1,0:T(8,128)(2,1)}, bf16[4,2,32,256]{3,2,1,0:T(8,128)(2,1)S(1)}, u32[]{:S(2)}) copy-start(bf16[4,2,32,256]{3,2,1,0:T(8,128)(2,1)S(1)} %collective-permute-done.2.rest_2_) | copy-start | bytes 393220
  21.5 36.1 %collective-permute-start.7 = (bf16[4,2,32,256]{3,2,1,0:T(8,128)(2,1)}, bf16[4,2,32,256]{3,2,1,0:T(8,128)(2,1)S(1)}, u32[]{:S(2)}, u32[]{:S(2)}) collective-permute-start(bf16[4,2,32,256]{3,2,1,0:T(8,128)(2,1)} %get-tuple-element.24), channel_id=1, source_target_pairs={{0,11},{1,8},{2,9},{3,10},{4,15},{5,12},{6,13},{7,14},{8,3},{9,0},... | collective-permute-start | bytes 393224 | tf_op jit(solution)/shard_map/ppermute | solution.py:90
  25.2 33.5 %copy-start.3 = (bf16[4,2,32,256]{3,2,1,0:T(8,128)(2,1)}, bf16[4,2,32,256]{3,2,1,0:T(8,128)(2,1)S(1)}, u32[]{:S(2)}) copy-start(bf16[4,2,32,256]{3,2,1,0:T(8,128)(2,1)S(1)} %collective-permute-done.3.rest_3_) | copy-start | bytes 393220
  25.2 32.4 %collective-permute-start.8 = (bf16[4,2,32,256]{3,2,1,0:T(8,128)(2,1)}, bf16[4,2,32,256]{3,2,1,0:T(8,128)(2,1)S(1)}, u32[]{:S(2)}, u32[]{:S(2)}) collective-permute-start(bf16[4,2,32,256]{3,2,1,0:T(8,128)(2,1)} %get-tuple-element.25), channel_id=1, source_target_pairs={{0,12},{1,13},{2,14},{3,15},{4,0},{5,1},{6,2},{7,3},{8,4},{9,5},{1... | collective-permute-start | bytes 393224 | tf_op jit(solution)/shard_map/ppermute | solution.py:90
  37.6 21.1 %copy-start.4 = (bf16[4,2,32,256]{3,2,1,0:T(8,128)(2,1)}, bf16[4,2,32,256]{3,2,1,0:T(8,128)(2,1)S(1)}, u32[]{:S(2)}) copy-start(bf16[4,2,32,256]{3,2,1,0:T(8,128)(2,1)S(1)} %collective-permute-done.4.rest_4_) | copy-start | bytes 393220
  37.6 20.0 %collective-permute-start.9 = (bf16[4,2,32,256]{3,2,1,0:T(8,128)(2,1)}, bf16[4,2,32,256]{3,2,1,0:T(8,128)(2,1)S(1)}, u32[]{:S(2)}, u32[]{:S(2)}) collective-permute-start(bf16[4,2,32,256]{3,2,1,0:T(8,128)(2,1)} %get-tuple-element.26), channel_id=1, source_target_pairs={{0,13},{1,14},{2,15},{3,12},{4,1},{5,2},{6,3},{7,0},{8,5},{9,6},{1... | collective-permute-start | bytes 393224 | tf_op jit(solution)/shard_map/ppermute | solution.py:90
  43.8 14.9 %copy-start.5 = (bf16[4,2,32,256]{3,2,1,0:T(8,128)(2,1)}, bf16[4,2,32,256]{3,2,1,0:T(8,128)(2,1)S(1)}, u32[]{:S(2)}) copy-start(bf16[4,2,32,256]{3,2,1,0:T(8,128)(2,1)S(1)} %collective-permute-done.5.rest_5_) | copy-start | bytes 393220
  43.8 13.9 %collective-permute-start.10 = (bf16[4,2,32,256]{3,2,1,0:T(8,128)(2,1)}, bf16[4,2,32,256]{3,2,1,0:T(8,128)(2,1)S(1)}, u32[]{:S(2)}, u32[]{:S(2)}) collective-permute-start(bf16[4,2,32,256]{3,2,1,0:T(8,128)(2,1)} %get-tuple-element.27), channel_id=1, source_target_pairs={{0,14},{1,15},{2,12},{3,13},{4,2},{5,3},{6,0},{7,1},{8,6},{9,7},{1... | collective-permute-start | bytes 393224 | tf_op jit(solution)/shard_map/ppermute | solution.py:90
  46.3 12.4 %copy-start.6 = (bf16[4,2,32,256]{3,2,1,0:T(8,128)(2,1)}, bf16[4,2,32,256]{3,2,1,0:T(8,128)(2,1)S(1)}, u32[]{:S(2)}) copy-start(bf16[4,2,32,256]{3,2,1,0:T(8,128)(2,1)S(1)} %collective-permute-done.6.rest_6_) | copy-start | bytes 393220
  46.3 12.4 %collective-permute-start.11 = (bf16[4,2,32,256]{3,2,1,0:T(8,128)(2,1)}, bf16[4,2,32,256]{3,2,1,0:T(8,128)(2,1)S(1)}, u32[]{:S(2)}, u32[]{:S(2)}) collective-permute-start(bf16[4,2,32,256]{3,2,1,0:T(8,128)(2,1)} %get-tuple-element.28), channel_id=1, source_target_pairs={{0,15},{1,12},{2,13},{3,14},{4,3},{5,0},{6,1},{7,2},{8,7},{9,4},{1... | collective-permute-start | bytes 393224 | tf_op jit(solution)/shard_map/ppermute | solution.py:90
  57.6 1.1 %copy-start.7 = (bf16[4,2,32,256]{3,2,1,0:T(8,128)(2,1)}, bf16[4,2,32,256]{3,2,1,0:T(8,128)(2,1)S(1)}, u32[]{:S(2)}) copy-start(bf16[4,2,32,256]{3,2,1,0:T(8,128)(2,1)S(1)} %collective-permute-done.7.rest_7_) | copy-start | bytes 393220
  57.6 1.1 %copy-start.8 = (bf16[4,2,32,256]{3,2,1,0:T(8,128)(2,1)}, bf16[4,2,32,256]{3,2,1,0:T(8,128)(2,1)S(1)}, u32[]{:S(2)}) copy-start(bf16[4,2,32,256]{3,2,1,0:T(8,128)(2,1)S(1)} %collective-permute-done.8.rest_8_) | copy-start | bytes 393220
  57.6 1.1 %copy-start.9 = (bf16[4,2,32,256]{3,2,1,0:T(8,128)(2,1)}, bf16[4,2,32,256]{3,2,1,0:T(8,128)(2,1)S(1)}, u32[]{:S(2)}) copy-start(bf16[4,2,32,256]{3,2,1,0:T(8,128)(2,1)S(1)} %collective-permute-done.9.rest_9_) | copy-start | bytes 393220
  57.7 1.1 %copy-start.10 = (bf16[4,2,32,256]{3,2,1,0:T(8,128)(2,1)}, bf16[4,2,32,256]{3,2,1,0:T(8,128)(2,1)S(1)}, u32[]{:S(2)}) copy-start(bf16[4,2,32,256]{3,2,1,0:T(8,128)(2,1)S(1)} %collective-permute-done.10.rest_10_) | copy-start | bytes 393220
  58.7 0.6 copy-start.11

commit v5 on v4

--- a/solution.py
+++ b/solution.py
@@ -101,18 +101,22 @@
     shifts = jnp.arange(tensor_count, dtype=jnp.int32)
     row_ids = jnp.arange(quarter, dtype=jnp.int32)
     position = (
-        slot_page[:, None, :, None] * page_rows
-        + ((me - shifts + tensor_count) % tensor_count)[None, :, None, None] * quarter
+        slot_page[:, :, None, None] * page_rows
+        + ((me - shifts + tensor_count) % tensor_count)[None, None, :, None] * quarter
         + row_ids[None, None, None, :]
     )
-    visible = slot_used[:, None, :, None] & (position < own_length)
-    visible = visible.astype(jnp.int32).reshape(span_count * tensor_count, 1, -1)
-    result = attend(queries[0], suffix_kv[0], visible, arrivals)
+    visible = slot_used[:, :, None, None] & (position < own_length)
+    visible = visible.astype(jnp.int32).reshape(span_count * slot_cap, 1, -1)
+    live = (slot_used & (slot_page * page_rows < own_length)).astype(jnp.int32).reshape(-1)
+    result = attend(queries[0], suffix_kv[0], live, visible, arrivals, slot_cap, tensor_count)
     return result.reshape(1, suffix_rows, result.shape[1])
 
 
-def attention_kernel(chunk_count, q_ref, suf_ref, vis_ref, *rest):
-    chunk_refs, o_ref = rest[:chunk_count], rest[chunk_count]
+def attention_kernel(
+    chunk_count, slot_cap, tensor_count, live_ref, q_ref, suf_ref, vis_ref, *rest
+):
+    chunk_refs = rest[:chunk_count]
+    o_ref, top_ref, sum_ref, acc_ref = rest[chunk_count:]
     rows, width = q_ref.shape
     kv_local = suf_ref.shape[2] // HEAD_DIM
     group = width // (kv_local * HEAD_DIM)
@@ -121,52 +125,87 @@
     row_pos = lax.broadcasted_iota(jnp.int32, (group * rows, rows), 0) % rows
     col_pos = lax.broadcasted_iota(jnp.int32, (group * rows, rows), 1)
     causal = col_pos <= row_pos
+    tile_count = chunk_count // tensor_count * slot_cap
     for head in range(kv_local):
         lanes = pl.ds(head * HEAD_DIM, HEAD_DIM)
         q_all = jnp.concatenate(
             [q_ref[:, pl.ds((head * group + g) * HEAD_DIM, HEAD_DIM)] for g in range(group)], axis=0
         )
-        keys = [suf_ref[0, :, lanes]]
-        vals = [suf_ref[1, :, lanes]]
-        masks = [causal]
-        for c in range(chunk_count):
-            ref = chunk_refs[c]
-            keys.append(ref[:, 0, :, lanes].reshape(-1, HEAD_DIM))
-            vals.append(ref[:, 1, :, lanes].reshape(-1, HEAD_DIM))
-            masks.append(vis_ref[c] > 0)
-        scores = []
-        top = None
-        for key, mask in zip(keys, masks):
-            s = lax.dot_general(q_all, key, dims, preferred_element_type=jnp.float32) * scale
-            s = jnp.where(mask, s, NEG_FILL)
-            scores.append(s)
-            part = jnp.max(s, axis=-1, keepdims=True)
-            top = part if top is None else jnp.maximum(top, part)
-        total = None
-        acc = None
-        for s, val, mask in zip(scores, vals, masks):
-            w = jnp.where(mask, jnp.exp(s - top), 0.0)
-            part = jnp.sum(w, axis=-1, keepdims=True)
-            total = part if total is None else total + part
-            pv = jnp.dot(w.astype(jnp.bfloat16), val, preferred_element_type=jnp.float32)
-            acc = pv if acc is None else acc + pv
-        out = (acc / total).astype(o_ref.dtype)
+
+        def tile(c, part):
+            distance, slot = c // slot_cap, c % slot_cap
+            return jnp.concatenate(
+                [
+                    chunk_refs[distance * tensor_count + s][slot, part, :, lanes]
+                    for s in range(tensor_count)
+                ],
+                axis=0,
+            )
+
+        def raw_scores(key):
+            return lax.dot_general(q_all, key, dims, preferred_element_type=jnp.float32)
+
+        top_ref[...] = jnp.where(causal, raw_scores(suf_ref[0, :, lanes]), NEG_FILL)
+        for c in range(tile_count):
+
+            @pl.when(live_ref[c] > 0)
+            def _():
+                s = jnp.where(vis_ref[c] > 0, raw_scores(tile(c, 0)), NEG_FILL)
+                top_ref[...] = jnp.maximum(top_ref[...], s)
+
+        top = jnp.max(top_ref[...], axis=-1, keepdims=True) * scale
+
+        def weights(raw, mask):
+            return jnp.where(mask, jnp.exp(raw * scale - top), 0.0)
+
+        w = weights(raw_scores(suf_ref[0, :, lanes]), causal)
+        sum_ref[...] = w
+        acc_ref[...] = jnp.dot(
+            w.astype(jnp.bfloat16), suf_ref[1, :, lanes], preferred_element_type=jnp.float32
+        )
+        for c in range(tile_count):
+
+            @pl.when(live_ref[c] > 0)
+            def _():
+                w = weights(raw_scores(tile(c, 0)), vis_ref[c] > 0)
+                sum_ref[...] += w
+                acc_ref[...] += jnp.dot(
+                    w.astype(jnp.bfloat16), tile(c, 1), preferred_element_type=jnp.float32
+                )
+
+        total = jnp.sum(sum_ref[...], axis=-1, keepdims=True)
+        out = (acc_ref[...] / total).astype(o_ref.dtype)
         for g in range(group):
             o_ref[:, pl.ds((head * group + g) * HEAD_DIM, HEAD_DIM)] = out[g * rows:(g + 1) * rows]
 
 
-def attend(q, suf, visible, chunks):
+def attend(q, suf, live, visible, chunks, slot_cap, tensor_count):
     rows, width = q.shape
+    kv_local = suf.shape[2] // HEAD_DIM
+    group = width // (kv_local * HEAD_DIM)
     keys_total = suf.shape[1] + sum(c.size // (2 * suf.shape[2]) for c in chunks)
-    flops = 4 * rows * width * keys_total
+    flops = 6 * rows * width * keys_total
     nbytes = 2 * (q.size * 2 + suf.size + sum(c.size for c in chunks))
+
+    def whole(a):
+        return pl.BlockSpec(a.shape, lambda i, flags: (0,) * a.ndim)
+
+    grid_spec = pltpu.PrefetchScalarGridSpec(
+        num_scalar_prefetch=1,
+        grid=(1,),
+        in_specs=[whole(q), whole(suf), whole(visible)] + [whole(c) for c in chunks],
+        out_specs=pl.BlockSpec((rows, width), lambda i, flags: (0, 0)),
+        scratch_shapes=[pltpu.VMEM((group * rows, rows), jnp.float32)] * 2
+        + [pltpu.VMEM((group * rows, HEAD_DIM), jnp.float32)],
+    )
     return pl.pallas_call(
-        functools.partial(attention_kernel, len(chunks)),
+        functools.partial(attention_kernel, len(chunks), slot_cap, tensor_count),
+        grid_spec=grid_spec,
         out_shape=jax.ShapeDtypeStruct((rows, width), jnp.bfloat16),
         cost_estimate=pl.CostEstimate(
             flops=flops, transcendentals=rows * (width // HEAD_DIM) * keys_total, bytes_accessed=nbytes
         ),
-    )(q, suf, visible, *chunks)
+    )(live, q, suf, visible, *chunks)
 
 
 def solution(mesh):

time: 69.6 us -> 73.3 us (1.053)
  the two profiles are of different devices: /device:TPU:1 before, /device:TPU:23 now
where the time goes in v5:
time: 73.3 us; the launch traced here: 72.1 us
  starting transfers between devices  29.3 us (40%)
  Pallas kernels  18.4 us (25%)
  waiting for transfers between devices  16.7 us (23%)
  other arithmetic  5.11 us (7%)
  local copies, waits for them, and re-layouts  2.41 us (3%)
    ppermute x12, starting transfers between devices, on_device(): lax.ppermute(payload[(distance - 1) * tensor_count + shift], ('replica',...  29.3 us
    ppermute x12, waiting for transfers between devices, on_device(): lax.ppermute(payload[(distance - 1) * tensor_count + shift], ('replica',...  16.7 us
    pallas_call x1, Pallas kernels, attend(): pl.pallas_call(functools.partial(attention_kernel, len(chunks), slot_cap,...  15 us
    pallas_call x1, Pallas kernels, pack_pages(): pl.pallas_call(functools.partial(gather_kernel, span_count, slot_cap, ten...  3.4 us
  transfers between devices with their start and end apart: 12, of which 2 were waited for; matrix products, arithmetic and copies ran while one was open for 5% of the time, Pallas kernels for 0%

profile of v5, /device:TPU:23, one launch (start us, length us, event | category | flops | bytes accessed | tf_op | source)
XLA Modules:
  0.0 72.1 jit_solution(9045898102975809649)
XLA Ops:
  0.0 0.8 %pad_add_fusion = s32[8,8]{1,0:T(8,128)S(1)} fusion(s32[4,8]{1,0:T(4,128)} %param.9), kind=kLoop, calls=%fused_computation.9 | loop fusion | flops 64 | bytes 384 | tf_op jit(solution)/shard_map/concatenate | solution.py:74
  0.8 0.7 fusion.3
  1.5 0.8 %pad_add_fusion.1 = s32[8,8]{1,0:T(8,128)S(1)} fusion(s32[4,8]{1,0:T(4,128)} %param.10), kind=kLoop, calls=%fused_computation.10 | loop fusion | flops 64 | bytes 384 | tf_op jit(solution)/shard_map/concatenate | solution.py:75
  2.3 0.2 multiply_reduce_fusion
  2.5 0.3 fusion
  2.8 0.1 reshape.154
  2.8 0.6 pad_add_fusion.2.idx_ref
  3.5 3.4 %shard_map.64 = (bf16[4,2,32,256]{3,2,1,0:T(8,128)(2,1)}, bf16[4,2,32,256]{3,2,1,0:T(8,128)(2,1)}, bf16[4,2,32,256]{3,2,1,0:T(8,128)(2,1)}, bf16[4,2,32,256]{3,2...) custom-call(s32[13]{0:T(128)} %pad_add_fusion.2.idx_ref, ...), custom_call_target="tpu_custom_call" | custom-call | bytes 3145728 | tf_op jit(solution)/shard_map/pallas_call | solution.py:56
  6.9 1.3 %collective-permute-start = (bf16[4,2,32,256]{3,2,1,0:T(8,128)(2,1)}, bf16[4,2,32,256]{3,2,1,0:T(8,128)(2,1)S(1)}, u32[]{:S(2)}, u32[]{:S(2)}) collective-permute-start(bf16[4,2,32,256]{3,2,1,0:T(8,128)(2,1)} %get-tuple-element.17), channel_id=1, source_target_pairs={{0,4},{1,5},{2,6},{3,7},{4,8},{5,9},{6,10},{7,11},{8,12},{9,13},{1... | collective-permute-start | bytes 393224 | tf_op jit(solution)/shard_map/ppermute | solution.py:90
  8.2 0.8 %collective-permute-start.1 = (bf16[4,2,32,256]{3,2,1,0:T(8,128)(2,1)}, bf16[4,2,32,256]{3,2,1,0:T(8,128)(2,1)S(1)}, u32[]{:S(2)}, u32[]{:S(2)}) collective-permute-start(bf16[4,2,32,256]{3,2,1,0:T(8,128)(2,1)} %get-tuple-element.18), channel_id=1, source_target_pairs={{0,5},{1,6},{2,7},{3,4},{4,9},{5,10},{6,11},{7,8},{8,13},{9,14},{1... | collective-permute-start | bytes 393224 | tf_op jit(solution)/shard_map/ppermute | solution.py:90
  8.9 2.2 %collective-permute-start.2 = (bf16[4,2,32,256]{3,2,1,0:T(8,128)(2,1)}, bf16[4,2,32,256]{3,2,1,0:T(8,128)(2,1)S(1)}, u32[]{:S(2)}, u32[]{:S(2)}) collective-permute-start(bf16[4,2,32,256]{3,2,1,0:T(8,128)(2,1)} %get-tuple-element.19), channel_id=1, source_target_pairs={{0,6},{1,7},{2,4},{3,5},{4,10},{5,11},{6,8},{7,9},{8,14},{9,15},{1... | collective-permute-start | bytes 393224 | tf_op jit(solution)/shard_map/ppermute | solution.py:90
  11.1 0.1 collective-permute-start.3
  11.2 1.3 %collective-permute-start.4 = (bf16[4,2,32,256]{3,2,1,0:T(8,128)(2,1)}, bf16[4,2,32,256]{3,2,1,0:T(8,128)(2,1)S(1)}, u32[]{:S(2)}, u32[]{:S(2)}) collective-permute-start(bf16[4,2,32,256]{3,2,1,0:T(8,128)(2,1)} %get-tuple-element.21), channel_id=1, source_target_pairs={{0,8},{1,9},{2,10},{3,11},{4,12},{5,13},{6,14},{7,15},{8,0},{9,1},... | collective-permute-start | bytes 393224 | tf_op jit(solution)/shard_map/ppermute | solution.py:90
  12.6 0.6 dynamic_slice.15
  13.2 0.1 add.96
  13.3 0.1 gt.12
  13.3 0.6 broadcast_compare_fusion
  13.9 0.1 lt.75
  14.2 0.1 add.94
  14.3 3.8 %collective-permute-start.5 = (bf16[4,2,32,256]{3,2,1,0:T(8,128)(2,1)}, bf16[4,2,32,256]{3,2,1,0:T(8,128)(2,1)S(1)}, u32[]{:S(2)}, u32[]{:S(2)}) collective-permute-start(bf16[4,2,32,256]{3,2,1,0:T(8,128)(2,1)} %get-tuple-element.22), channel_id=1, source_target_pairs={{0,9},{1,10},{2,11},{3,8},{4,13},{5,14},{6,15},{7,12},{8,1},{9,2},... | collective-permute-start | bytes 393224 | tf_op jit(solution)/shard_map/ppermute | solution.py:90
  18.1 0.1 collective-permute-start.6
  18.2 1.2 %and_convert_fusion.vis_ref = s32[12,1,128]{2,1,0:T(1,128)} fusion(pred[12]{0:T(512)(128)(4,1)S(1)} %gt.12, s32[12,1,128]{2,1,0:T(1,128)S(1)} %add.94, s32[]{:T(128)} %bitcast.1, s32[128]{0:T(128)S(1)} %add.96), kind=kLoop, calls=%fused_computation | loop fusion | flops 6144 | bytes 12816 | tf_op jit(solution)/shard_map/convert_element_type | solution.py:109
  19.5 1.0 %collective-permute-start.7 = (bf16[4,2,32,256]{3,2,1,0:T(8,128)(2,1)}, bf16[4,2,32,256]{3,2,1,0:T(8,128)(2,1)S(1)}, u32[]{:S(2)}, u32[]{:S(2)}) collective-permute-start(bf16[4,2,32,256]{3,2,1,0:T(8,128)(2,1)} %get-tuple-element.24), channel_id=1, source_target_pairs={{0,11},{1,8},{2,9},{3,10},{4,15},{5,12},{6,13},{7,14},{8,3},{9,0},... | collective-permute-start | bytes 393224 | tf_op jit(solution)/shard_map/ppermute | solution.py:90
  20.5 1.7 %collective-permute-start.8 = (bf16[4,2,32,256]{3,2,1,0:T(8,128)(2,1)}, bf16[4,2,32,256]{3,2,1,0:T(8,128)(2,1)S(1)}, u32[]{:S(2)}, u32[]{:S(2)}) collective-permute-start(bf16[4,2,32,256]{3,2,1,0:T(8,128)(2,1)} %get-tuple-element.25), channel_id=1, source_target_pairs={{0,12},{1,13},{2,14},{3,15},{4,0},{5,1},{6,2},{7,3},{8,4},{9,5},{1... | collective-permute-start | bytes 393224 | tf_op jit(solution)/shard_map/ppermute | solution.py:90
  22.2 11.7 %collective-permute-done.4.rest_4_ = bf16[4,2,32,256]{3,2,1,0:T(8,128)(2,1)S(1)} collective-permute-done((bf16[4,2,32,256]{3,2,1,0:T(8,128)(2,1)}, bf16[4,2,32,256]{3,2,1,0:T(8,128)(2,1)S(1)}, u32[]{:S(2)}, u32[]{:S(2)}) %collective-permute-start.4) | collective-permute-done | bytes 131104 | tf_op jit(solution)/shard_map/ppermute | solution.py:90
  33.9 3.3 %collective-permute-start.9 = (bf16[4,2,32,256]{3,2,1,0:T(8,128)(2,1)}, bf16[4,2,32,256]{3,2,1,0:T(8,128)(2,1)S(1)}, u32[]{:S(2)}, u32[]{:S(2)}) collective-permute-start(bf16[4,2,32,256]{3,2,1,0:T(8,128)(2,1)} %get-tuple-element.26), channel_id=1, source_target_pairs={{0,13},{1,14},{2,15},{3,12},{4,1},{5,2},{6,3},{7,0},{8,5},{9,6},{1... | collective-permute-start | bytes 393224 | tf_op jit(solution)/shard_map/ppermute | solution.py:90
  37.2 3.2 %collective-permute-start.10 = (bf16[4,2,32,256]{3,2,1,0:T(8,128)(2,1)}, bf16[4,2,32,256]{3,2,1,0:T(8,128)(2,1)S(1)}, u32[]{:S(2)}, u32[]{:S(2)}) collective-permute-start(bf16[4,2,32,256]{3,2,1,0:T(8,128)(2,1)} %get-tuple-element.27), channel_id=1, source_target_pairs={{0,14},{1,15},{2,12},{3,13},{4,2},{5,3},{6,0},{7,1},{8,6},{9,7},{1... | collective-permute-start | bytes 393224 | tf_op jit(solution)/shard_map/ppermute | solution.py:90
  40.3 10.5 %collective-permute-start.11 = (bf16[4,2,32,256]{3,2,1,0:T(8,128)(2,1)}, bf16[4,2,32,256]{3,2,1,0:T(8,128)(2,1)S(1)}, u32[]{:S(2)}, u32[]{:S(2)}) collective-permute-start(bf16[4,2,32,256]{3,2,1,0:T(8,128)(2,1)} %get-tuple-element.28), channel_id=1, source_target_pairs={{0,15},{1,12},{2,13},{3,14},{4,3},{5,0},{6,1},{7,2},{8,7},{9,4},{1... | collective-permute-start | bytes 393224 | tf_op jit(solution)/shard_map/ppermute | solution.py:90
  50.9 0.5 and_convert_fusion.1.live_ref
  51.4 5.0 %collective-permute-done.11.rest_11_ = bf16[4,2,32,256]{3,2,1,0:T(8,128)(2,1)S(1)} collective-permute-done((bf16[4,2,32,256]{3,2,1,0:T(8,128)(2,1)}, bf16[4,2,32,256]{3,2,1,0:T(8,128)(2,1)S(1)}, u32[]{:S(2)}, u32[]{:S(2)}) %collective-permute-start.11) | collective-permute-done | bytes 131104 | tf_op jit(solution)/shard_map/ppermute | solution.py:90
  56.5 0.6 copy-done.11
  57.1 15.0 %shard_map.65 = bf16[128,2048]{1,0:T(8,128)(2,1)} custom-call(s32[12]{0:T(128)} %and_convert_fusion.1.live_ref, bf16[128,2048]{1,0:T(8,128)(2,1)} %bitcast.7, bf16[2,128,256]{2,1,0:T(8,128)(2,1)} %bitcast.8, s32[12,1,128]{2,1,0:T(1,128)} %and_convert_fusion.vis_ref, bf16[4,2,32,256]{3,2,1,0:T(8,128)(2,1)} %copy-done, bf16[4,2,32,256]{3,2,1,0:T(8,128)(2,1)} %copy-done.1, ...), custom_call_target="tpu_custom_call" | custom-call | flops 2617245696 | bytes 2752512 | tf_op jit(solution)/shard_map/pallas_call | solution.py:201
  (45 shorter events, 0.3 us)
Async XLA Ops:
  0.0 12.6 %copy-start.12 = (s32[4]{0:T(128)S(1)}, s32[4]{0:T(128)}, u32[]{:S(2)}) copy-start(s32[4]{0:T(128)} %param.11) | copy-start | bytes 52
  6.9 7.4 %collective-permute-start = (bf16[4,2,32,256]{3,2,1,0:T(8,128)(2,1)}, bf16[4,2,32,256]{3,2,1,0:T(8,128)(2,1)S(1)}, u32[]{:S(2)}, u32[]{:S(2)}) collective-permute-start(bf16[4,2,32,256]{3,2,1,0:T(8,128)(2,1)} %get-tuple-element.17), channel_id=1, source_target_pairs={{0,4},{1,5},{2,6},{3,7},{4,8},{5,9},{6,10},{7,11},{8,12},{9,13},{1... | collective-permute-start | bytes 393224 | tf_op jit(solution)/shard_map/ppermute | solution.py:90
  8.2 9.9 %collective-permute-start.1 = (bf16[4,2,32,256]{3,2,1,0:T(8,128)(2,1)}, bf16[4,2,32,256]{3,2,1,0:T(8,128)(2,1)S(1)}, u32[]{:S(2)}, u32[]{:S(2)}) collective-permute-start(bf16[4,2,32,256]{3,2,1,0:T(8,128)(2,1)} %get-tuple-element.18), channel_id=1, source_target_pairs={{0,5},{1,6},{2,7},{3,4},{4,9},{5,10},{6,11},{7,8},{8,13},{9,14},{1... | collective-permute-start | bytes 393224 | tf_op jit(solution)/shard_map/ppermute | solution.py:90
  8.9 10.5 %collective-permute-start.2 = (bf16[4,2,32,256]{3,2,1,0:T(8,128)(2,1)}, bf16[4,2,32,256]{3,2,1,0:T(8,128)(2,1)S(1)}, u32[]{:S(2)}, u32[]{:S(2)}) collective-permute-start(bf16[4,2,32,256]{3,2,1,0:T(8,128)(2,1)} %get-tuple-element.19), channel_id=1, source_target_pairs={{0,6},{1,7},{2,4},{3,5},{4,10},{5,11},{6,8},{7,9},{8,14},{9,15},{1... | collective-permute-start | bytes 393224 | tf_op jit(solution)/shard_map/ppermute | solution.py:90
  11.1 9.4 %collective-permute-start.3 = (bf16[4,2,32,256]{3,2,1,0:T(8,128)(2,1)}, bf16[4,2,32,256]{3,2,1,0:T(8,128)(2,1)S(1)}, u32[]{:S(2)}, u32[]{:S(2)}) collective-permute-start(bf16[4,2,32,256]{3,2,1,0:T(8,128)(2,1)} %get-tuple-element.20), channel_id=1, source_target_pairs={{0,7},{1,4},{2,5},{3,6},{4,11},{5,8},{6,9},{7,10},{8,15},{9,12},{1... | collective-permute-start | bytes 393224 | tf_op jit(solution)/shard_map/ppermute | solution.py:90
  11.2 22.7 %collective-permute-start.4 = (bf16[4,2,32,256]{3,2,1,0:T(8,128)(2,1)}, bf16[4,2,32,256]{3,2,1,0:T(8,128)(2,1)S(1)}, u32[]{:S(2)}, u32[]{:S(2)}) collective-permute-start(bf16[4,2,32,256]{3,2,1,0:T(8,128)(2,1)} %get-tuple-element.21), channel_id=1, source_target_pairs={{0,8},{1,9},{2,10},{3,11},{4,12},{5,13},{6,14},{7,15},{8,0},{9,1},... | collective-permute-start | bytes 393224 | tf_op jit(solution)/shard_map/ppermute | solution.py:90
  14.3 42.2 %copy-start = (bf16[4,2,32,256]{3,2,1,0:T(8,128)(2,1)}, bf16[4,2,32,256]{3,2,1,0:T(8,128)(2,1)S(1)}, u32[]{:S(2)}) copy-start(bf16[4,2,32,256]{3,2,1,0:T(8,128)(2,1)S(1)} %collective-permute-done.rest_0_) | copy-start | bytes 393220
  14.3 22.9 %collective-permute-start.5 = (bf16[4,2,32,256]{3,2,1,0:T(8,128)(2,1)}, bf16[4,2,32,256]{3,2,1,0:T(8,128)(2,1)S(1)}, u32[]{:S(2)}, u32[]{:S(2)}) collective-permute-start(bf16[4,2,32,256]{3,2,1,0:T(8,128)(2,1)} %get-tuple-element.22), channel_id=1, source_target_pairs={{0,9},{1,10},{2,11},{3,8},{4,13},{5,14},{6,15},{7,12},{8,1},{9,2},... | collective-permute-start | bytes 393224 | tf_op jit(solution)/shard_map/ppermute | solution.py:90
  18.0 38.4 %copy-start.1 = (bf16[4,2,32,256]{3,2,1,0:T(8,128)(2,1)}, bf16[4,2,32,256]{3,2,1,0:T(8,128)(2,1)S(1)}, u32[]{:S(2)}) copy-start(bf16[4,2,32,256]{3,2,1,0:T(8,128)(2,1)S(1)} %collective-permute-done.1.rest_1_) | copy-start | bytes 393220
  18.1 22.3 %collective-permute-start.6 = (bf16[4,2,32,256]{3,2,1,0:T(8,128)(2,1)}, bf16[4,2,32,256]{3,2,1,0:T(8,128)(2,1)S(1)}, u32[]{:S(2)}, u32[]{:S(2)}) collective-permute-start(bf16[4,2,32,256]{3,2,1,0:T(8,128)(2,1)} %get-tuple-element.23), channel_id=1, source_target_pairs={{0,10},{1,11},{2,8},{3,9},{4,14},{5,15},{6,12},{7,13},{8,2},{9,3},... | collective-permute-start | bytes 393224 | tf_op jit(solution)/shard_map/ppermute | solution.py:90
  19.4 37.0 %copy-start.2 = (bf16[4,2,32,256]{3,2,1,0:T(8,128)(2,1)}, bf16[4,2,32,256]{3,2,1,0:T(8,128)(2,1)S(1)}, u32[]{:S(2)}) copy-start(bf16[4,2,32,256]{3,2,1,0:T(8,128)(2,1)S(1)} %collective-permute-done.2.rest_2_) | copy-start | bytes 393220
  19.5 31.9 %collective-permute-start.7 = (bf16[4,2,32,256]{3,2,1,0:T(8,128)(2,1)}, bf16[4,2,32,256]{3,2,1,0:T(8,128)(2,1)S(1)}, u32[]{:S(2)}, u32[]{:S(2)}) collective-permute-start(bf16[4,2,32,256]{3,2,1,0:T(8,128)(2,1)} %get-tuple-element.24), channel_id=1, source_target_pairs={{0,11},{1,8},{2,9},{3,10},{4,15},{5,12},{6,13},{7,14},{8,3},{9,0},... | collective-permute-start | bytes 393224 | tf_op jit(solution)/shard_map/ppermute | solution.py:90
  20.5 35.9 %copy-start.3 = (bf16[4,2,32,256]{3,2,1,0:T(8,128)(2,1)}, bf16[4,2,32,256]{3,2,1,0:T(8,128)(2,1)S(1)}, u32[]{:S(2)}) copy-start(bf16[4,2,32,256]{3,2,1,0:T(8,128)(2,1)S(1)} %collective-permute-done.3.rest_3_) | copy-start | bytes 393220
  20.5 30.9 %collective-permute-start.8 = (bf16[4,2,32,256]{3,2,1,0:T(8,128)(2,1)}, bf16[4,2,32,256]{3,2,1,0:T(8,128)(2,1)S(1)}, u32[]{:S(2)}, u32[]{:S(2)}) collective-permute-start(bf16[4,2,32,256]{3,2,1,0:T(8,128)(2,1)} %get-tuple-element.25), channel_id=1, source_target_pairs={{0,12},{1,13},{2,14},{3,15},{4,0},{5,1},{6,2},{7,3},{8,4},{9,5},{1... | collective-permute-start | bytes 393224 | tf_op jit(solution)/shard_map/ppermute | solution.py:90
  33.9 22.6 %copy-start.4 = (bf16[4,2,32,256]{3,2,1,0:T(8,128)(2,1)}, bf16[4,2,32,256]{3,2,1,0:T(8,128)(2,1)S(1)}, u32[]{:S(2)}) copy-start(bf16[4,2,32,256]{3,2,1,0:T(8,128)(2,1)S(1)} %collective-permute-done.4.rest_4_) | copy-start | bytes 393220
  33.9 17.5 %collective-permute-start.9 = (bf16[4,2,32,256]{3,2,1,0:T(8,128)(2,1)}, bf16[4,2,32,256]{3,2,1,0:T(8,128)(2,1)S(1)}, u32[]{:S(2)}, u32[]{:S(2)}) collective-permute-start(bf16[4,2,32,256]{3,2,1,0:T(8,128)(2,1)} %get-tuple-element.26), channel_id=1, source_target_pairs={{0,13},{1,14},{2,15},{3,12},{4,1},{5,2},{6,3},{7,0},{8,5},{9,6},{1... | collective-permute-start | bytes 393224 | tf_op jit(solution)/shard_map/ppermute | solution.py:90
  37.2 19.3 %copy-start.5 = (bf16[4,2,32,256]{3,2,1,0:T(8,128)(2,1)}, bf16[4,2,32,256]{3,2,1,0:T(8,128)(2,1)S(1)}, u32[]{:S(2)}) copy-start(bf16[4,2,32,256]{3,2,1,0:T(8,128)(2,1)S(1)} %collective-permute-done.5.rest_5_) | copy-start | bytes 393220
  37.2 14.3 %collective-permute-start.10 = (bf16[4,2,32,256]{3,2,1,0:T(8,128)(2,1)}, bf16[4,2,32,256]{3,2,1,0:T(8,128)(2,1)S(1)}, u32[]{:S(2)}, u32[]{:S(2)}) collective-permute-start(bf16[4,2,32,256]{3,2,1,0:T(8,128)(2,1)} %get-tuple-element.27), channel_id=1, source_target_pairs={{0,14},{1,15},{2,12},{3,13},{4,2},{5,3},{6,0},{7,1},{8,6},{9,7},{1... | collective-permute-start | bytes 393224 | tf_op jit(solution)/shard_map/ppermute | solution.py:90
  40.3 16.1 %copy-start.6 = (bf16[4,2,32,256]{3,2,1,0:T(8,128)(2,1)}, bf16[4,2,32,256]{3,2,1,0:T(8,128)(2,1)S(1)}, u32[]{:S(2)}) copy-start(bf16[4,2,32,256]{3,2,1,0:T(8,128)(2,1)S(1)} %collective-permute-done.6.rest_6_) | copy-start | bytes 393220
  40.3 16.1 %collective-permute-start.11 = (bf16[4,2,32,256]{3,2,1,0:T(8,128)(2,1)}, bf16[4,2,32,256]{3,2,1,0:T(8,128)(2,1)S(1)}, u32[]{:S(2)}, u32[]{:S(2)}) collective-permute-start(bf16[4,2,32,256]{3,2,1,0:T(8,128)(2,1)} %get-tuple-element.28), channel_id=1, source_target_pairs={{0,15},{1,12},{2,13},{3,14},{4,3},{5,0},{6,1},{7,2},{8,7},{9,4},{1... | collective-permute-start | bytes 393224 | tf_op jit(solution)/shard_map/ppermute | solution.py:90
  51.4 5.1 %copy-start.7 = (bf16[4,2,32,256]{3,2,1,0:T(8,128)(2,1)}, bf16[4,2,32,256]{3,2,1,0:T(8,128)(2,1)S(1)}, u32[]{:S(2)}) copy-start(bf16[4,2,32,256]{3,2,1,0:T(8,128)(2,1)S(1)} %collective-permute-done.7.rest_7_) | copy-start | bytes 393220
  51.4 5.1 %copy-start.8 = (bf16[4,2,32,256]{3,2,1,0:T(8,128)(2,1)}, bf16[4,2,32,256]{3,2,1,0:T(8,128)(2,1)S(1)}, u32[]{:S(2)}) copy-start(bf16[4,2,32,256]{3,2,1,0:T(8,128)(2,1)S(1)} %collective-permute-done.8.rest_8_) | copy-start | bytes 393220
  51.4 5.1 %copy-start.9 = (bf16[4,2,32,256]{3,2,1,0:T(8,128)(2,1)}, bf16[4,2,32,256]{3,2,1,0:T(8,128)(2,1)S(1)}, u32[]{:S(2)}) copy-start(bf16[4,2,32,256]{3,2,1,0:T(8,128)(2,1)S(1)} %collective-permute-done.9.rest_9_) | copy-start | bytes 393220
  51.4 5.1 %copy-start.10 = (bf16[4,2,32,256]{3,2,1,0:T(8,128)(2,1)}, bf16[4,2,32,256]{3,2,1,0:T(8,128)(2,1)S(1)}, u32[]{:S(2)}) copy-start(bf16[4,2,32,256]{3,2,1,0:T(8,128)(2,1)S(1)} %collective-permute-done.10.rest_10_) | copy-start | bytes 393220
  56.4 0.7 copy-start.11

commit v6 on v4

--- a/solution.py
+++ b/solution.py
@@ -25,32 +25,42 @@
     return matched[:, None, :] * (ranking[:, None, :] == places[None, :, None]).astype(jnp.int32)
 
 
-def gather_kernel(span_count, slot_cap, tensor_count, idx_ref, pool_ref, *out_refs):
-    me = idx_ref[span_count * slot_cap]
+def gather_kernel(span_count, slot_cap, tensor_count, off_ref, slot_ref, pool_ref, *out_refs):
+    replicas, page_count = off_ref.shape
+    holder = lax.axis_index("replica")
+    me = lax.axis_index("tensor")
     lanes = out_refs[0].shape[-1]
     starts = [
         pl.multiple_of(((me + shift) % tensor_count) * lanes, lanes) for shift in range(tensor_count)
     ]
-    for distance in range(span_count):
+    for distance in range(1, span_count + 1):
+        reader = (holder + distance) % replicas
+        chosen = [jnp.int32(0)] * slot_cap
+        count = jnp.int32(0)
+        for page in range(page_count):
+            matched = off_ref[reader, page] == distance
+            place = slot_ref[reader, page]
+            chosen = [
+                jnp.where(matched & (count == slot), place, chosen[slot]) for slot in range(slot_cap)
+            ]
+            count = count + matched.astype(jnp.int32)
         for slot in range(slot_cap):
-            page = idx_ref[distance * slot_cap + slot]
             for shift in range(tensor_count):
-                out_refs[distance * tensor_count + shift][slot] = pool_ref[
-                    page, :, :, pl.ds(starts[shift], lanes)
+                out_refs[(distance - 1) * tensor_count + shift][slot] = pool_ref[
+                    chosen[slot], :, :, pl.ds(starts[shift], lanes)
                 ]
 
 
-def pack_pages(pool_part, chosen, me, span_count, slot_cap, tensor_count):
+def pack_pages(pool_part, offsets, slots, span_count, slot_cap, tensor_count):
     pages, kv, rows, width = pool_part.shape
     lanes = width // tensor_count
-    table = jnp.concatenate([chosen.reshape(-1), me.reshape(1)]).astype(jnp.int32)
     piece = (slot_cap, kv, rows, lanes)
     count = span_count * tensor_count
     grid_spec = pltpu.PrefetchScalarGridSpec(
-        num_scalar_prefetch=1,
+        num_scalar_prefetch=2,
         grid=(1,),
-        in_specs=[pl.BlockSpec((pages, kv, rows, width), lambda i, idx: (0, 0, 0, 0))],
-        out_specs=[pl.BlockSpec(piece, lambda i, idx: (0, 0, 0, 0)) for _ in range(count)],
+        in_specs=[pl.BlockSpec((pages, kv, rows, width), lambda i, o, s: (0, 0, 0, 0))],
+        out_specs=[pl.BlockSpec(piece, lambda i, o, s: (0, 0, 0, 0)) for _ in range(count)],
     )
     nbytes = 2 * (pool_part.size + span_count * slot_cap * kv * rows * width)
     return pl.pallas_call(
@@ -58,7 +68,7 @@
         grid_spec=grid_spec,
         out_shape=[jax.ShapeDtypeStruct(piece, pool_part.dtype) for _ in range(count)],
         cost_estimate=pl.CostEstimate(flops=0, transcendentals=0, bytes_accessed=nbytes),
-    )(table, pool_part)
+    )(offsets, slots, pool_part)
 
 
 def on_device(queries, suffix_kv, page_pool, offsets, slots, prefix_len):
@@ -71,13 +81,7 @@
     slot_cap = (page_count + span_count - 1) // span_count + 1
     distances = jnp.arange(1, span_count + 1, dtype=jnp.int32)
 
-    off_twice = jnp.concatenate([offsets, offsets], axis=0)
-    slots_twice = jnp.concatenate([slots, slots], axis=0)
-    off_rows = lax.dynamic_slice_in_dim(off_twice, reader + 1, span_count, 0)
-    slot_rows = lax.dynamic_slice_in_dim(slots_twice, reader + 1, span_count, 0)
-    picked = slot_choice(off_rows, distances, slot_cap)
-    chosen = jnp.sum(picked * slot_rows[:, None, :], axis=2)
-    payload = pack_pages(page_pool, chosen, me, span_count, slot_cap, tensor_count)
+    payload = pack_pages(page_pool, offsets, slots, span_count, slot_cap, tensor_count)
 
     arrivals = []
     for distance in range(1, span_count + 1):
@@ -135,21 +139,27 @@
             vals.append(ref[:, 1, :, lanes].reshape(-1, HEAD_DIM))
             masks.append(vis_ref[c] > 0)
         scores = []
-        top = None
         for key, mask in zip(keys, masks):
             s = lax.dot_general(q_all, key, dims, preferred_element_type=jnp.float32) * scale
-            s = jnp.where(mask, s, NEG_FILL)
-            scores.append(s)
-            part = jnp.max(s, axis=-1, keepdims=True)
-            top = part if top is None else jnp.maximum(top, part)
+            scores.append(jnp.where(mask, s, NEG_FILL))
+        even = all(s.shape == scores[0].shape for s in scores)
+        if even:
+            running = scores[0]
+            for s in scores[1:]:
+                running = jnp.maximum(running, s)
+            top = jnp.max(running, axis=-1, keepdims=True)
+        else:
+            top = functools.reduce(jnp.maximum, [jnp.max(s, axis=-1, keepdims=True) for s in scores])
         total = None
         acc = None
         for s, val, mask in zip(scores, vals, masks):
             w = jnp.where(mask, jnp.exp(s - top), 0.0)
-            part = jnp.sum(w, axis=-1, keepdims=True)
+            part = w if even else jnp.sum(w, axis=-1, keepdims=True)
             total = part if total is None else total + part
             pv = jnp.dot(w.astype(jnp.bfloat16), val, preferred_element_type=jnp.float32)
             acc = pv if acc is None else acc + pv
+        if even:
+            total = jnp.sum(total, axis=-1, keepdims=True)
         out = (acc / total).astype(o_ref.dtype)
         for g in range(group):
             o_ref[:, pl.ds((head * group + g) * HEAD_DIM, HEAD_DIM)] = out[g * rows:(g + 1) * rows]

time: 69.6 us -> 66.6 us (0.957)
  other arithmetic: 3.92 us -> 1.78 us
  starting transfers between devices: 35.2 us -> 34 us
    concatenate x3 -> x0, other arithmetic: 2.12 us -> none  [the longest x1 0.77 us: on_device(): off_twice = jnp.concatenate([offsets, offsets], axis=0)]
    ppermute x12, starting transfers between devices: 35.2 us -> 34 us  [on_device(): lax.ppermute(payload[(distance - 1) * tensor_count + shift], ('replica',...]
  transfers between devices with their start and end apart: 12 -> 12, of which waited for: 3 -> 3; matrix products, arithmetic and copies ran while one was open for 3% -> 5% of each run, Pallas kernels for 0% -> 0%
where the time goes in v6:
time: 66.6 us; the launch traced here: 66.4 us
  starting transfers between devices  34 us (51%)
  waiting for transfers between devices  14.2 us (21%)
  Pallas kernels  13.8 us (21%)
  local copies, waits for them, and re-layouts  2.39 us (4%)
  other arithmetic  1.78 us (3%)
    ppermute x12, starting transfers between devices, on_device(): lax.ppermute(payload[(distance - 1) * tensor_count + shift], ('replica',...  34 us
    ppermute x12, waiting for transfers between devices, on_device(): lax.ppermute(payload[(distance - 1) * tensor_count + shift], ('replica',...  14.2 us
    pallas_call x1, Pallas kernels, attend(): pl.pallas_call(functools.partial(attention_kernel, len(chunks)), out_shap...  10.2 us
    pallas_call x1, Pallas kernels, pack_pages(): pl.pallas_call(functools.partial(gather_kernel, span_count, slot_cap, ten...  3.63 us
  transfers between devices with their start and end apart: 12, of which 3 were waited for; matrix products, arithmetic and copies ran while one was open for 5% of the time, Pallas kernels for 0%

profile of v6, /device:TPU:1, one launch (start us, length us, event | category | flops | bytes accessed | tf_op | source)
XLA Modules:
  0.0 66.4 jit_solution(16420098283749009886)
XLA Ops:
  0.0 3.6 %shard_map.64 = (bf16[4,2,32,256]{3,2,1,0:T(8,128)(2,1)}, bf16[4,2,32,256]{3,2,1,0:T(8,128)(2,1)}, bf16[4,2,32,256]{3,2,1,0:T(8,128)(2,1)}, bf16[4,2,32,256]{3,2...) custom-call(s32[4,8]{1,0:T(4,128)} %off_ref.1, ...), custom_call_target="tpu_custom_call" | custom-call | bytes 3145728 | tf_op jit(solution)/shard_map/pallas_call | solution.py:66
  3.6 2.1 %collective-permute-start = (bf16[4,2,32,256]{3,2,1,0:T(8,128)(2,1)}, bf16[4,2,32,256]{3,2,1,0:T(8,128)(2,1)S(1)}, u32[]{:S(2)}, u32[]{:S(2)}) collective-permute-start(bf16[4,2,32,256]{3,2,1,0:T(8,128)(2,1)} %get-tuple-element.17), channel_id=1, source_target_pairs={{0,4},{1,5},{2,6},{3,7},{4,8},{5,9},{6,10},{7,11},{8,12},{9,13},{1... | collective-permute-start | bytes 393224 | tf_op jit(solution)/shard_map/ppermute | solution.py:94
  5.8 3.1 %collective-permute-start.1 = (bf16[4,2,32,256]{3,2,1,0:T(8,128)(2,1)}, bf16[4,2,32,256]{3,2,1,0:T(8,128)(2,1)S(1)}, u32[]{:S(2)}, u32[]{:S(2)}) collective-permute-start(bf16[4,2,32,256]{3,2,1,0:T(8,128)(2,1)} %get-tuple-element.18), channel_id=1, source_target_pairs={{0,5},{1,6},{2,7},{3,4},{4,9},{5,10},{6,11},{7,8},{8,13},{9,14},{1... | collective-permute-start | bytes 393224 | tf_op jit(solution)/shard_map/ppermute | solution.py:94
  8.8 1.3 %collective-permute-start.2 = (bf16[4,2,32,256]{3,2,1,0:T(8,128)(2,1)}, bf16[4,2,32,256]{3,2,1,0:T(8,128)(2,1)S(1)}, u32[]{:S(2)}, u32[]{:S(2)}) collective-permute-start(bf16[4,2,32,256]{3,2,1,0:T(8,128)(2,1)} %get-tuple-element.19), channel_id=1, source_target_pairs={{0,6},{1,7},{2,4},{3,5},{4,10},{5,11},{6,8},{7,9},{8,14},{9,15},{1... | collective-permute-start | bytes 393224 | tf_op jit(solution)/shard_map/ppermute | solution.py:94
  10.1 0.3 collective-permute-start.3
  10.4 1.7 %collective-permute-start.4 = (bf16[4,2,32,256]{3,2,1,0:T(8,128)(2,1)}, bf16[4,2,32,256]{3,2,1,0:T(8,128)(2,1)S(1)}, u32[]{:S(2)}, u32[]{:S(2)}) collective-permute-start(bf16[4,2,32,256]{3,2,1,0:T(8,128)(2,1)} %get-tuple-element.21), channel_id=1, source_target_pairs={{0,8},{1,9},{2,10},{3,11},{4,12},{5,13},{6,14},{7,15},{8,0},{9,1},... | collective-permute-start | bytes 393224 | tf_op jit(solution)/shard_map/ppermute | solution.py:94
  12.1 0.7 %dynamic-slice_bitcast_fusion = s32[8]{0:T(128)S(1)} fusion(s32[4,8]{1,0:T(4,128)} %off_ref.1, s32[]{:T(128)S(6)} %select_n.17), kind=kLoop, calls=%fused_computation.18 | loop fusion | bytes 68 | tf_op jit(solution)/shard_map/eq | solution.py:19
  12.8 0.1 compare_convert_fusion
  12.9 0.1 multiply_reduce_fusion
  13.0 0.2 fusion
  13.2 0.7 dynamic_slice.9
  13.9 0.1 add.84
  14.0 0.1 and.31
  14.1 0.1 and.35
  14.2 0.0 collective-permute-done.rest_0_
  14.2 1.9 %collective-permute-start.5 = (bf16[4,2,32,256]{3,2,1,0:T(8,128)(2,1)}, bf16[4,2,32,256]{3,2,1,0:T(8,128)(2,1)S(1)}, u32[]{:S(2)}, u32[]{:S(2)}) collective-permute-start(bf16[4,2,32,256]{3,2,1,0:T(8,128)(2,1)} %get-tuple-element.22), channel_id=1, source_target_pairs={{0,9},{1,10},{2,11},{3,8},{4,13},{5,14},{6,15},{7,12},{8,1},{9,2},... | collective-permute-start | bytes 393224 | tf_op jit(solution)/shard_map/ppermute | solution.py:94
  16.1 0.0 collective-permute-done.1.rest_1_
  16.1 3.1 %collective-permute-start.6 = (bf16[4,2,32,256]{3,2,1,0:T(8,128)(2,1)}, bf16[4,2,32,256]{3,2,1,0:T(8,128)(2,1)S(1)}, u32[]{:S(2)}, u32[]{:S(2)}) collective-permute-start(bf16[4,2,32,256]{3,2,1,0:T(8,128)(2,1)} %get-tuple-element.23), channel_id=1, source_target_pairs={{0,10},{1,11},{2,8},{3,9},{4,14},{5,15},{6,12},{7,13},{8,2},{9,3},... | collective-permute-start | bytes 393224 | tf_op jit(solution)/shard_map/ppermute | solution.py:94
  19.2 0.1 broadcast_add_fusion
  19.3 0.1 add.81
  19.4 0.1 add.82
  19.5 0.5 collective-permute-start.7
  20.0 1.9 %collective-permute-done.3.rest_3_ = bf16[4,2,32,256]{3,2,1,0:T(8,128)(2,1)S(1)} collective-permute-done((bf16[4,2,32,256]{3,2,1,0:T(8,128)(2,1)}, bf16[4,2,32,256]{3,2,1,0:T(8,128)(2,1)S(1)}, u32[]{:S(2)}, u32[]{:S(2)}) %collective-permute-start.3) | collective-permute-done | bytes 131104 | tf_op jit(solution)/shard_map/ppermute | solution.py:94
  22.0 1.1 %collective-permute-start.8 = (bf16[4,2,32,256]{3,2,1,0:T(8,128)(2,1)}, bf16[4,2,32,256]{3,2,1,0:T(8,128)(2,1)S(1)}, u32[]{:S(2)}, u32[]{:S(2)}) collective-permute-start(bf16[4,2,32,256]{3,2,1,0:T(8,128)(2,1)} %get-tuple-element.25), channel_id=1, source_target_pairs={{0,12},{1,13},{2,14},{3,15},{4,0},{5,1},{6,2},{7,3},{8,4},{9,5},{1... | collective-permute-start | bytes 393224 | tf_op jit(solution)/shard_map/ppermute | solution.py:94
  23.1 11.3 %collective-permute-done.4.rest_4_ = bf16[4,2,32,256]{3,2,1,0:T(8,128)(2,1)S(1)} collective-permute-done((bf16[4,2,32,256]{3,2,1,0:T(8,128)(2,1)}, bf16[4,2,32,256]{3,2,1,0:T(8,128)(2,1)S(1)}, u32[]{:S(2)}, u32[]{:S(2)}) %collective-permute-start.4) | collective-permute-done | bytes 131104 | tf_op jit(solution)/shard_map/ppermute | solution.py:94
  34.4 6.2 %collective-permute-start.9 = (bf16[4,2,32,256]{3,2,1,0:T(8,128)(2,1)}, bf16[4,2,32,256]{3,2,1,0:T(8,128)(2,1)S(1)}, u32[]{:S(2)}, u32[]{:S(2)}) collective-permute-start(bf16[4,2,32,256]{3,2,1,0:T(8,128)(2,1)} %get-tuple-element.26), channel_id=1, source_target_pairs={{0,13},{1,14},{2,15},{3,12},{4,1},{5,2},{6,3},{7,0},{8,5},{9,6},{1... | collective-permute-start | bytes 393224 | tf_op jit(solution)/shard_map/ppermute | solution.py:94
  40.6 2.5 %collective-permute-start.10 = (bf16[4,2,32,256]{3,2,1,0:T(8,128)(2,1)}, bf16[4,2,32,256]{3,2,1,0:T(8,128)(2,1)S(1)}, u32[]{:S(2)}, u32[]{:S(2)}) collective-permute-start(bf16[4,2,32,256]{3,2,1,0:T(8,128)(2,1)} %get-tuple-element.27), channel_id=1, source_target_pairs={{0,14},{1,15},{2,12},{3,13},{4,2},{5,3},{6,0},{7,1},{8,6},{9,7},{1... | collective-permute-start | bytes 393224 | tf_op jit(solution)/shard_map/ppermute | solution.py:94
  43.1 10.1 %collective-permute-start.11 = (bf16[4,2,32,256]{3,2,1,0:T(8,128)(2,1)}, bf16[4,2,32,256]{3,2,1,0:T(8,128)(2,1)S(1)}, u32[]{:S(2)}, u32[]{:S(2)}) collective-permute-start(bf16[4,2,32,256]{3,2,1,0:T(8,128)(2,1)} %get-tuple-element.28), channel_id=1, source_target_pairs={{0,15},{1,12},{2,13},{3,14},{4,3},{5,0},{6,1},{7,2},{8,7},{9,4},{1... | collective-permute-start | bytes 393224 | tf_op jit(solution)/shard_map/ppermute | solution.py:94
  53.2 1.3 %and_convert_fusion.vis_ref = s32[12,1,128]{2,1,0:T(1,128)} fusion(pred[12,1,128]{2,1,0:T(4,128)(4,1)S(1)} %and.35, s32[12,1,128]{2,1,0:T(1,128)S(1)} %add.82, s32[]{:T(128)} %bitcast.3, s32[128]{0:T(128)S(1)} %add.84), kind=kLoop, calls=%fused_computation | loop fusion | flops 6144 | bytes 14340 | tf_op jit(solution)/shard_map/convert_element_type | solution.py:113
  54.6 0.9 %collective-permute-done.11.rest_11_ = bf16[4,2,32,256]{3,2,1,0:T(8,128)(2,1)S(1)} collective-permute-done((bf16[4,2,32,256]{3,2,1,0:T(8,128)(2,1)}, bf16[4,2,32,256]{3,2,1,0:T(8,128)(2,1)S(1)}, u32[]{:S(2)}, u32[]{:S(2)}) %collective-permute-start.11) | collective-permute-done | bytes 131104 | tf_op jit(solution)/shard_map/ppermute | solution.py:94
  55.6 0.6 copy-done.11
  56.2 10.2 %shard_map.65 = bf16[128,2048]{1,0:T(8,128)(2,1)} custom-call(bf16[128,2048]{1,0:T(8,128)(2,1)} %bitcast.6, bf16[2,128,256]{2,1,0:T(8,128)(2,1)} %bitcast.7, s32[12,1,128]{2,1,0:T(1,128)} %and_convert_fusion.vis_ref, bf16[4,2,32,256]{3,2,1,0:T(8,128)(2,1)} %copy-done, bf16[4,2,32,256]{3,2,1,0:T(8,128)(2,1)} %copy-done.1, bf16[4,2,32,256]{3,2,1,0:T(8,128)(2,1)} %copy-done.2, ...), custom_call_target="tpu_custom_call" | custom-call | flops 1744830464 | bytes 2752512 | tf_op jit(solution)/shard_map/pallas_call | solution.py:173
  (38 shorter events, 0.1 us)
Async XLA Ops:
  0.0 13.2 %copy-start.12 = (s32[4]{0:T(128)S(1)}, s32[4]{0:T(128)}, u32[]{:S(2)}) copy-start(s32[4]{0:T(128)} %param.11) | copy-start | bytes 52
  3.6 10.5 %collective-permute-start = (bf16[4,2,32,256]{3,2,1,0:T(8,128)(2,1)}, bf16[4,2,32,256]{3,2,1,0:T(8,128)(2,1)S(1)}, u32[]{:S(2)}, u32[]{:S(2)}) collective-permute-start(bf16[4,2,32,256]{3,2,1,0:T(8,128)(2,1)} %get-tuple-element.17), channel_id=1, source_target_pairs={{0,4},{1,5},{2,6},{3,7},{4,8},{5,9},{6,10},{7,11},{8,12},{9,13},{1... | collective-permute-start | bytes 393224 | tf_op jit(solution)/shard_map/ppermute | solution.py:94
  5.8 10.4 %collective-permute-start.1 = (bf16[4,2,32,256]{3,2,1,0:T(8,128)(2,1)}, bf16[4,2,32,256]{3,2,1,0:T(8,128)(2,1)S(1)}, u32[]{:S(2)}, u32[]{:S(2)}) collective-permute-start(bf16[4,2,32,256]{3,2,1,0:T(8,128)(2,1)} %get-tuple-element.18), channel_id=1, source_target_pairs={{0,5},{1,6},{2,7},{3,4},{4,9},{5,10},{6,11},{7,8},{8,13},{9,14},{1... | collective-permute-start | bytes 393224 | tf_op jit(solution)/shard_map/ppermute | solution.py:94
  8.8 10.7 %collective-permute-start.2 = (bf16[4,2,32,256]{3,2,1,0:T(8,128)(2,1)}, bf16[4,2,32,256]{3,2,1,0:T(8,128)(2,1)S(1)}, u32[]{:S(2)}, u32[]{:S(2)}) collective-permute-start(bf16[4,2,32,256]{3,2,1,0:T(8,128)(2,1)} %get-tuple-element.19), channel_id=1, source_target_pairs={{0,6},{1,7},{2,4},{3,5},{4,10},{5,11},{6,8},{7,9},{8,14},{9,15},{1... | collective-permute-start | bytes 393224 | tf_op jit(solution)/shard_map/ppermute | solution.py:94
  10.1 11.9 %collective-permute-start.3 = (bf16[4,2,32,256]{3,2,1,0:T(8,128)(2,1)}, bf16[4,2,32,256]{3,2,1,0:T(8,128)(2,1)S(1)}, u32[]{:S(2)}, u32[]{:S(2)}) collective-permute-start(bf16[4,2,32,256]{3,2,1,0:T(8,128)(2,1)} %get-tuple-element.20), channel_id=1, source_target_pairs={{0,7},{1,4},{2,5},{3,6},{4,11},{5,8},{6,9},{7,10},{8,15},{9,12},{1... | collective-permute-start | bytes 393224 | tf_op jit(solution)/shard_map/ppermute | solution.py:94
  10.4 24.0 %collective-permute-start.4 = (bf16[4,2,32,256]{3,2,1,0:T(8,128)(2,1)}, bf16[4,2,32,256]{3,2,1,0:T(8,128)(2,1)S(1)}, u32[]{:S(2)}, u32[]{:S(2)}) collective-permute-start(bf16[4,2,32,256]{3,2,1,0:T(8,128)(2,1)} %get-tuple-element.21), channel_id=1, source_target_pairs={{0,8},{1,9},{2,10},{3,11},{4,12},{5,13},{6,14},{7,15},{8,0},{9,1},... | collective-permute-start | bytes 393224 | tf_op jit(solution)/shard_map/ppermute | solution.py:94
  14.2 41.3 %copy-start = (bf16[4,2,32,256]{3,2,1,0:T(8,128)(2,1)}, bf16[4,2,32,256]{3,2,1,0:T(8,128)(2,1)S(1)}, u32[]{:S(2)}) copy-start(bf16[4,2,32,256]{3,2,1,0:T(8,128)(2,1)S(1)} %collective-permute-done.rest_0_) | copy-start | bytes 393220
  14.2 26.4 %collective-permute-start.5 = (bf16[4,2,32,256]{3,2,1,0:T(8,128)(2,1)}, bf16[4,2,32,256]{3,2,1,0:T(8,128)(2,1)S(1)}, u32[]{:S(2)}, u32[]{:S(2)}) collective-permute-start(bf16[4,2,32,256]{3,2,1,0:T(8,128)(2,1)} %get-tuple-element.22), channel_id=1, source_target_pairs={{0,9},{1,10},{2,11},{3,8},{4,13},{5,14},{6,15},{7,12},{8,1},{9,2},... | collective-permute-start | bytes 393224 | tf_op jit(solution)/shard_map/ppermute | solution.py:94
  16.1 39.4 %copy-start.1 = (bf16[4,2,32,256]{3,2,1,0:T(8,128)(2,1)}, bf16[4,2,32,256]{3,2,1,0:T(8,128)(2,1)S(1)}, u32[]{:S(2)}) copy-start(bf16[4,2,32,256]{3,2,1,0:T(8,128)(2,1)S(1)} %collective-permute-done.1.rest_1_) | copy-start | bytes 393220
  16.1 27.0 %collective-permute-start.6 = (bf16[4,2,32,256]{3,2,1,0:T(8,128)(2,1)}, bf16[4,2,32,256]{3,2,1,0:T(8,128)(2,1)S(1)}, u32[]{:S(2)}, u32[]{:S(2)}) collective-permute-start(bf16[4,2,32,256]{3,2,1,0:T(8,128)(2,1)} %get-tuple-element.23), channel_id=1, source_target_pairs={{0,10},{1,11},{2,8},{3,9},{4,14},{5,15},{6,12},{7,13},{8,2},{9,3},... | collective-permute-start | bytes 393224 | tf_op jit(solution)/shard_map/ppermute | solution.py:94
  19.5 36.0 %copy-start.2 = (bf16[4,2,32,256]{3,2,1,0:T(8,128)(2,1)}, bf16[4,2,32,256]{3,2,1,0:T(8,128)(2,1)S(1)}, u32[]{:S(2)}) copy-start(bf16[4,2,32,256]{3,2,1,0:T(8,128)(2,1)S(1)} %collective-permute-done.2.rest_2_) | copy-start | bytes 393220
  19.5 35.0 %collective-permute-start.7 = (bf16[4,2,32,256]{3,2,1,0:T(8,128)(2,1)}, bf16[4,2,32,256]{3,2,1,0:T(8,128)(2,1)S(1)}, u32[]{:S(2)}, u32[]{:S(2)}) collective-permute-start(bf16[4,2,32,256]{3,2,1,0:T(8,128)(2,1)} %get-tuple-element.24), channel_id=1, source_target_pairs={{0,11},{1,8},{2,9},{3,10},{4,15},{5,12},{6,13},{7,14},{8,3},{9,0},... | collective-permute-start | bytes 393224 | tf_op jit(solution)/shard_map/ppermute | solution.py:94
  22.0 33.5 %copy-start.3 = (bf16[4,2,32,256]{3,2,1,0:T(8,128)(2,1)}, bf16[4,2,32,256]{3,2,1,0:T(8,128)(2,1)S(1)}, u32[]{:S(2)}) copy-start(bf16[4,2,32,256]{3,2,1,0:T(8,128)(2,1)S(1)} %collective-permute-done.3.rest_3_) | copy-start | bytes 393220
  22.0 32.5 %collective-permute-start.8 = (bf16[4,2,32,256]{3,2,1,0:T(8,128)(2,1)}, bf16[4,2,32,256]{3,2,1,0:T(8,128)(2,1)S(1)}, u32[]{:S(2)}, u32[]{:S(2)}) collective-permute-start(bf16[4,2,32,256]{3,2,1,0:T(8,128)(2,1)} %get-tuple-element.25), channel_id=1, source_target_pairs={{0,12},{1,13},{2,14},{3,15},{4,0},{5,1},{6,2},{7,3},{8,4},{9,5},{1... | collective-permute-start | bytes 393224 | tf_op jit(solution)/shard_map/ppermute | solution.py:94
  34.4 21.1 %copy-start.4 = (bf16[4,2,32,256]{3,2,1,0:T(8,128)(2,1)}, bf16[4,2,32,256]{3,2,1,0:T(8,128)(2,1)S(1)}, u32[]{:S(2)}) copy-start(bf16[4,2,32,256]{3,2,1,0:T(8,128)(2,1)S(1)} %collective-permute-done.4.rest_4_) | copy-start | bytes 393220
  34.4 20.1 %collective-permute-start.9 = (bf16[4,2,32,256]{3,2,1,0:T(8,128)(2,1)}, bf16[4,2,32,256]{3,2,1,0:T(8,128)(2,1)S(1)}, u32[]{:S(2)}, u32[]{:S(2)}) collective-permute-start(bf16[4,2,32,256]{3,2,1,0:T(8,128)(2,1)} %get-tuple-element.26), channel_id=1, source_target_pairs={{0,13},{1,14},{2,15},{3,12},{4,1},{5,2},{6,3},{7,0},{8,5},{9,6},{1... | collective-permute-start | bytes 393224 | tf_op jit(solution)/shard_map/ppermute | solution.py:94
  40.6 14.9 %copy-start.5 = (bf16[4,2,32,256]{3,2,1,0:T(8,128)(2,1)}, bf16[4,2,32,256]{3,2,1,0:T(8,128)(2,1)S(1)}, u32[]{:S(2)}) copy-start(bf16[4,2,32,256]{3,2,1,0:T(8,128)(2,1)S(1)} %collective-permute-done.5.rest_5_) | copy-start | bytes 393220
  40.6 14.0 %collective-permute-start.10 = (bf16[4,2,32,256]{3,2,1,0:T(8,128)(2,1)}, bf16[4,2,32,256]{3,2,1,0:T(8,128)(2,1)S(1)}, u32[]{:S(2)}, u32[]{:S(2)}) collective-permute-start(bf16[4,2,32,256]{3,2,1,0:T(8,128)(2,1)} %get-tuple-element.27), channel_id=1, source_target_pairs={{0,14},{1,15},{2,12},{3,13},{4,2},{5,3},{6,0},{7,1},{8,6},{9,7},{1... | collective-permute-start | bytes 393224 | tf_op jit(solution)/shard_map/ppermute | solution.py:94
  43.1 12.4 %copy-start.6 = (bf16[4,2,32,256]{3,2,1,0:T(8,128)(2,1)}, bf16[4,2,32,256]{3,2,1,0:T(8,128)(2,1)S(1)}, u32[]{:S(2)}) copy-start(bf16[4,2,32,256]{3,2,1,0:T(8,128)(2,1)S(1)} %collective-permute-done.6.rest_6_) | copy-start | bytes 393220
  43.1 12.4 %collective-permute-start.11 = (bf16[4,2,32,256]{3,2,1,0:T(8,128)(2,1)}, bf16[4,2,32,256]{3,2,1,0:T(8,128)(2,1)S(1)}, u32[]{:S(2)}, u32[]{:S(2)}) collective-permute-start(bf16[4,2,32,256]{3,2,1,0:T(8,128)(2,1)} %get-tuple-element.28), channel_id=1, source_target_pairs={{0,15},{1,12},{2,13},{3,14},{4,3},{5,0},{6,1},{7,2},{8,7},{9,4},{1... | collective-permute-start | bytes 393224 | tf_op jit(solution)/shard_map/ppermute | solution.py:94
  54.5 1.0 %copy-start.7 = (bf16[4,2,32,256]{3,2,1,0:T(8,128)(2,1)}, bf16[4,2,32,256]{3,2,1,0:T(8,128)(2,1)S(1)}, u32[]{:S(2)}) copy-start(bf16[4,2,32,256]{3,2,1,0:T(8,128)(2,1)S(1)} %collective-permute-done.7.rest_7_) | copy-start | bytes 393220
  54.5 1.0 %copy-start.8 = (bf16[4,2,32,256]{3,2,1,0:T(8,128)(2,1)}, bf16[4,2,32,256]{3,2,1,0:T(8,128)(2,1)S(1)}, u32[]{:S(2)}) copy-start(bf16[4,2,32,256]{3,2,1,0:T(8,128)(2,1)S(1)} %collective-permute-done.8.rest_8_) | copy-start | bytes 393220
  54.5 1.0 %copy-start.9 = (bf16[4,2,32,256]{3,2,1,0:T(8,128)(2,1)}, bf16[4,2,32,256]{3,2,1,0:T(8,128)(2,1)S(1)}, u32[]{:S(2)}) copy-start(bf16[4,2,32,256]{3,2,1,0:T(8,128)(2,1)S(1)} %collective-permute-done.9.rest_9_) | copy-start | bytes 393220
  54.6 1.0 %copy-start.10 = (bf16[4,2,32,256]{3,2,1,0:T(8,128)(2,1)}, bf16[4,2,32,256]{3,2,1,0:T(8,128)(2,1)S(1)}, u32[]{:S(2)}) copy-start(bf16[4,2,32,256]{3,2,1,0:T(8,128)(2,1)S(1)} %collective-permute-done.10.rest_10_) | copy-start | bytes 393220
  55.5 0.7 %copy-start.11 = (bf16[4,2,32,256]{3,2,1,0:T(8,128)(2,1)}, bf16[4,2,32,256]{3,2,1,0:T(8,128)(2,1)S(1)}, u32[]{:S(2)}) copy-start(bf16[4,2,32,256]{3,2,1,0:T(8,128)(2,1)S(1)} %collective-permute-done.11.rest_11_) | copy-start | bytes 393220

commit v7 on v6

--- a/solution.py
+++ b/solution.py
@@ -111,15 +111,21 @@
     )
     visible = slot_used[:, None, :, None] & (position < own_length)
     visible = visible.astype(jnp.int32).reshape(span_count * tensor_count, 1, -1)
-    result = attend(queries[0], suffix_kv[0], visible, arrivals)
+    result = attend(queries[0], suffix_kv[0], visible, arrivals, tensor_count)
     return result.reshape(1, suffix_rows, result.shape[1])
 
 
-def attention_kernel(chunk_count, q_ref, suf_ref, vis_ref, *rest):
-    chunk_refs, o_ref = rest[:chunk_count], rest[chunk_count]
+def attention_kernel(chunk_count, with_suffix, carry_in, final, *refs):
+    refs = list(refs)
+    q_ref = refs.pop(0)
+    suf_ref = refs.pop(0) if with_suffix else None
+    vis_ref = refs.pop(0)
+    chunk_refs = [refs.pop(0) for _ in range(chunk_count)]
+    if carry_in:
+        top_in, sum_in, acc_in = refs.pop(0), refs.pop(0), refs.pop(0)
     rows, width = q_ref.shape
-    kv_local = suf_ref.shape[2] // HEAD_DIM
-    group = width // (kv_local * HEAD_DIM)
+    group = HEADS // KV_HEADS
+    kv_local = width // (group * HEAD_DIM)
     scale = HEAD_DIM ** (-0.5)
     dims = (((1,), (1,)), ((), ()))
     row_pos = lax.broadcasted_iota(jnp.int32, (group * rows, rows), 0) % rows
@@ -130,9 +136,11 @@
         q_all = jnp.concatenate(
             [q_ref[:, pl.ds((head * group + g) * HEAD_DIM, HEAD_DIM)] for g in range(group)], axis=0
         )
-        keys = [suf_ref[0, :, lanes]]
-        vals = [suf_ref[1, :, lanes]]
-        masks = [causal]
+        keys, vals, masks = [], [], []
+        if with_suffix:
+            keys.append(suf_ref[0, :, lanes])
+            vals.append(suf_ref[1, :, lanes])
+            masks.append(causal)
         for c in range(chunk_count):
             ref = chunk_refs[c]
             keys.append(ref[:, 0, :, lanes].reshape(-1, HEAD_DIM))
@@ -150,6 +158,9 @@
             top = jnp.max(running, axis=-1, keepdims=True)
         else:
             top = functools.reduce(jnp.maximum, [jnp.max(s, axis=-1, keepdims=True) for s in scores])
+        if carry_in:
+            before = top_in[head]
+            top = jnp.maximum(top, before)
         total = None
         acc = None
         for s, val, mask in zip(scores, vals, masks):
@@ -160,23 +171,49 @@
             acc = pv if acc is None else acc + pv
         if even:
             total = jnp.sum(total, axis=-1, keepdims=True)
-        out = (acc / total).astype(o_ref.dtype)
-        for g in range(group):
-            o_ref[:, pl.ds((head * group + g) * HEAD_DIM, HEAD_DIM)] = out[g * rows:(g + 1) * rows]
-
-
-def attend(q, suf, visible, chunks):
+        if carry_in:
+            rescale = jnp.exp(before - top)
+            total = total + sum_in[head] * rescale
+            acc = acc + acc_in[head] * rescale
+        if final:
+            o_ref = refs[0]
+            out = (acc / total).astype(o_ref.dtype)
+            for g in range(group):
+                o_ref[:, pl.ds((head * group + g) * HEAD_DIM, HEAD_DIM)] = out[g * rows:(g + 1) * rows]
+        else:
+            top_out, sum_out, acc_out = refs
+            top_out[head] = top
+            sum_out[head] = total
+            acc_out[head] = acc
+
+
+def attend_part(q, suf, visible, chunks, carry, final):
     rows, width = q.shape
-    keys_total = suf.shape[1] + sum(c.size // (2 * suf.shape[2]) for c in chunks)
+    group = HEADS // KV_HEADS
+    kv_local = width // (group * HEAD_DIM)
+    lanes = kv_local * HEAD_DIM
+    keys_total = sum(c.size // (2 * lanes) for c in chunks) + (0 if suf is None else suf.shape[1])
     flops = 4 * rows * width * keys_total
-    nbytes = 2 * (q.size * 2 + suf.size + sum(c.size for c in chunks))
+    nbytes = 2 * (q.size * 2 + sum(c.size for c in chunks)) + (0 if suf is None else 2 * suf.size)
+    state = [
+        jax.ShapeDtypeStruct((kv_local, group * rows, 1), jnp.float32),
+        jax.ShapeDtypeStruct((kv_local, group * rows, 1), jnp.float32),
+        jax.ShapeDtypeStruct((kv_local, group * rows, HEAD_DIM), jnp.float32),
+    ]
+    out_shape = jax.ShapeDtypeStruct((rows, width), jnp.bfloat16) if final else state
+    operands = [q] + ([] if suf is None else [suf]) + [visible] + list(chunks) + list(carry)
     return pl.pallas_call(
-        functools.partial(attention_kernel, len(chunks)),
-        out_shape=jax.ShapeDtypeStruct((rows, width), jnp.bfloat16),
+        functools.partial(attention_kernel, len(chunks), suf is not None, len(carry) > 0, final),
+        out_shape=out_shape,
         cost_estimate=pl.CostEstimate(
             flops=flops, transcendentals=rows * (width // HEAD_DIM) * keys_total, bytes_accessed=nbytes
         ),
-    )(q, suf, visible, *chunks)
+    )(*operands)
+
+
+def attend(q, suf, visible, chunks, first_count):
+    carry = attend_part(q, suf, visible[:first_count], chunks[:first_count], (), False)
+    return attend_part(q, None, visible[first_count:], chunks[first_count:], carry, True)
 
 
 def solution(mesh):

time: 66.6 us -> 67 us (level)
  the two profiles are of different devices: /device:TPU:1 before, /device:TPU:21 now
where the time goes in v7:
time: 67 us; the launch traced here: 66.8 us
  starting transfers between devices  25.5 us (38%)
  waiting for transfers between devices  19.4 us (29%)
  Pallas kernels  17.1 us (26%)
  local copies, waits for them, and re-layouts  3.42 us (5%)
  other arithmetic  1.22 us (2%)
    ppermute x12, starting transfers between devices, on_device(): lax.ppermute(payload[(distance - 1) * tensor_count + shift], ('replica',...  25.5 us
    ppermute x12, waiting for transfers between devices, on_device(): lax.ppermute(payload[(distance - 1) * tensor_count + shift], ('replica',...  19.4 us
    pallas_call x2, Pallas kernels, attend_part(): pl.pallas_call(functools.partial(attention_kernel, len(chunks), suf is no...  13.5 us
    pallas_call x1, Pallas kernels, pack_pages(): pl.pallas_call(functools.partial(gather_kernel, span_count, slot_cap, ten...  3.63 us
  transfers between devices with their start and end apart: 12, of which 3 were waited for; matrix products, arithmetic and copies ran while one was open for 6% of the time, Pallas kernels for 8%

profile of v7, /device:TPU:21, one launch (start us, length us, event | category | flops | bytes accessed | tf_op | source)
XLA Modules:
  0.0 66.8 jit_solution(16644191111802159994)
XLA Ops:
  0.0 3.6 %shard_map.64 = (bf16[4,2,32,256]{3,2,1,0:T(8,128)(2,1)}, bf16[4,2,32,256]{3,2,1,0:T(8,128)(2,1)}, bf16[4,2,32,256]{3,2,1,0:T(8,128)(2,1)}, bf16[4,2,32,256]{3,2...) custom-call(s32[4,8]{1,0:T(4,128)} %off_ref.1, ...), custom_call_target="tpu_custom_call" | custom-call | bytes 3145728 | tf_op jit(solution)/shard_map/pallas_call | solution.py:66
  3.6 0.1 collective-permute-start
  3.7 4.1 %collective-permute-start.1 = (bf16[4,2,32,256]{3,2,1,0:T(8,128)(2,1)}, bf16[4,2,32,256]{3,2,1,0:T(8,128)(2,1)S(1)}, u32[]{:S(2)}, u32[]{:S(2)}) collective-permute-start(bf16[4,2,32,256]{3,2,1,0:T(8,128)(2,1)} %get-tuple-element.21), channel_id=1, source_target_pairs={{0,9},{1,10},{2,11},{3,8},{4,13},{5,14},{6,15},{7,12},{8,1},{9,2},... | collective-permute-start | bytes 393224 | tf_op jit(solution)/shard_map/ppermute | solution.py:94
  7.8 0.1 collective-permute-start.2
  7.8 1.3 %collective-permute-start.8 = (bf16[4,2,32,256]{3,2,1,0:T(8,128)(2,1)}, bf16[4,2,32,256]{3,2,1,0:T(8,128)(2,1)S(1)}, u32[]{:S(2)}, u32[]{:S(2)}) collective-permute-start(bf16[4,2,32,256]{3,2,1,0:T(8,128)(2,1)} %get-tuple-element.28), channel_id=1, source_target_pairs={{0,4},{1,5},{2,6},{3,7},{4,8},{5,9},{6,10},{7,11},{8,12},{9,13},{1... | collective-permute-start | bytes 393224 | tf_op jit(solution)/shard_map/ppermute | solution.py:94
  9.1 2.2 %collective-permute-start.9 = (bf16[4,2,32,256]{3,2,1,0:T(8,128)(2,1)}, bf16[4,2,32,256]{3,2,1,0:T(8,128)(2,1)S(1)}, u32[]{:S(2)}, u32[]{:S(2)}) collective-permute-start(bf16[4,2,32,256]{3,2,1,0:T(8,128)(2,1)} %get-tuple-element.29), channel_id=1, source_target_pairs={{0,5},{1,6},{2,7},{3,4},{4,9},{5,10},{6,11},{7,8},{8,13},{9,14},{1... | collective-permute-start | bytes 393224 | tf_op jit(solution)/shard_map/ppermute | solution.py:94
  11.3 0.7 %dynamic-slice_bitcast_fusion = s32[8]{0:T(128)S(1)} fusion(s32[4,8]{1,0:T(4,128)} %off_ref.1, s32[]{:T(128)S(6)} %select_n.17), kind=kLoop, calls=%fused_computation.20 | loop fusion | bytes 68 | tf_op jit(solution)/shard_map/eq | solution.py:19
  12.0 0.6 dynamic_slice.9
  12.6 0.1 compare_convert_fusion
  12.7 0.1 multiply_reduce_fusion
  12.8 0.2 select_reduce_fusion
  13.0 0.1 broadcast_add_fusion
  13.1 7.0 %collective-permute-done.refs_2_ = bf16[4,2,32,256]{3,2,1,0:T(8,128)(2,1)S(1)} collective-permute-done((bf16[4,2,32,256]{3,2,1,0:T(8,128)(2,1)}, bf16[4,2,32,256]{3,2,1,0:T(8,128)(2,1)S(1)}, u32[]{:S(2)}, u32[]{:S(2)}) %collective-permute-start) | collective-permute-done | bytes 131104 | tf_op jit(solution)/shard_map/ppermute | solution.py:94
  20.1 0.6 collective-permute-start.10
  20.7 2.3 %collective-permute-done.1.refs_3_ = bf16[4,2,32,256]{3,2,1,0:T(8,128)(2,1)S(1)} collective-permute-done((bf16[4,2,32,256]{3,2,1,0:T(8,128)(2,1)}, bf16[4,2,32,256]{3,2,1,0:T(8,128)(2,1)S(1)}, u32[]{:S(2)}, u32[]{:S(2)}) %collective-permute-start.1) | collective-permute-done | bytes 131104 | tf_op jit(solution)/shard_map/ppermute | solution.py:94
  23.1 5.1 %collective-permute-start.11 = (bf16[4,2,32,256]{3,2,1,0:T(8,128)(2,1)}, bf16[4,2,32,256]{3,2,1,0:T(8,128)(2,1)S(1)}, u32[]{:S(2)}, u32[]{:S(2)}) collective-permute-start(bf16[4,2,32,256]{3,2,1,0:T(8,128)(2,1)} %get-tuple-element.31), channel_id=1, source_target_pairs={{0,7},{1,4},{2,5},{3,6},{4,11},{5,8},{6,9},{7,10},{8,15},{9,12},{1... | collective-permute-start | bytes 393224 | tf_op jit(solution)/shard_map/ppermute | solution.py:94
  28.2 10.7 %collective-permute-start.3 = (bf16[4,2,32,256]{3,2,1,0:T(8,128)(2,1)}, bf16[4,2,32,256]{3,2,1,0:T(8,128)(2,1)S(1)}, u32[]{:S(2)}, u32[]{:S(2)}) collective-permute-start(bf16[4,2,32,256]{3,2,1,0:T(8,128)(2,1)} %get-tuple-element.23), channel_id=1, source_target_pairs={{0,11},{1,8},{2,9},{3,10},{4,15},{5,12},{6,13},{7,14},{8,3},{9,0},... | collective-permute-start | bytes 393224 | tf_op jit(solution)/shard_map/ppermute | solution.py:94
  38.9 0.0 collective-permute-start.4
  38.9 0.0 collective-permute-done.9.refs_4_
  39.0 0.1 collective-permute-start.5
  39.0 1.2 %collective-permute-start.6 = (bf16[4,2,32,256]{3,2,1,0:T(8,128)(2,1)}, bf16[4,2,32,256]{3,2,1,0:T(8,128)(2,1)S(1)}, u32[]{:S(2)}, u32[]{:S(2)}) collective-permute-start(bf16[4,2,32,256]{3,2,1,0:T(8,128)(2,1)} %get-tuple-element.26), channel_id=1, source_target_pairs={{0,14},{1,15},{2,12},{3,13},{4,2},{5,3},{6,0},{7,1},{8,6},{9,7},{1... | collective-permute-start | bytes 393224 | tf_op jit(solution)/shard_map/ppermute | solution.py:94
  40.3 10.1 %collective-permute-done.11.refs_6_ = bf16[4,2,32,256]{3,2,1,0:T(8,128)(2,1)S(1)} collective-permute-done((bf16[4,2,32,256]{3,2,1,0:T(8,128)(2,1)}, bf16[4,2,32,256]{3,2,1,0:T(8,128)(2,1)S(1)}, u32[]{:S(2)}, u32[]{:S(2)}) %collective-permute-start.11) | collective-permute-done | bytes 131104 | tf_op jit(solution)/shard_map/ppermute | solution.py:94
  50.4 0.7 %fusion.1 = s32[3,4,4,32]{3,2,1,0:T(4,128)S(1)} fusion(s32[]{:T(128)} %bitcast.2, s32[3,4,4]{2,1,0:T(4,128)S(1)} %broadcast_add_fusion, pred[3,4]{1,0:T(4,128)(4,1)S(1)} %broadcast_compare_fusion), kind=kLoop, calls=%fused_computation.2 | loop fusion | flops 6144 | bytes 6352 | tf_op jit(solution)/shard_map/convert_element_type | solution.py:113
  51.1 0.7 %slice.13.refs_1_ = s32[8,1,128]{2,1,0:T(1,128)} reshape(s32[2,4,4,32]{3,2,1,0:T(4,128)S(1)} %slice.16) | data formatting | bytes 8192 | tf_op jit(solution)/shard_map/slice | solution.py:216
  51.8 0.7 %slice.15.refs_2_ = s32[4,1,128]{2,1,0:T(1,128)} reshape(s32[1,4,4,32]{3,2,1,0:T(4,128)S(1)} %slice.17) | data formatting | bytes 4096 | tf_op jit(solution)/shard_map/slice | solution.py:215
  52.5 5.4 %shard_map.65 = (f32[2,1024,1]{2,1,0:T(8,128)}, f32[2,1024,1]{2,1,0:T(8,128)}, f32[2,1024,128]{2,1,0:T(8,128)}) custom-call(bf16[128,2048]{1,0:T(8,128)(2,1)} %bitcast.6, bf16[2,128,256]{2,1,0:T(8,128)(2,1)} %bitcast.8, s32[4,1,128]{2,1,0:T(1,128)} %slice.15.refs_2_, bf16[4,2,32,256]{3,2,1,0:T(8,128)(2,1)} %copy-done.8, bf16[4,2,32,256]{3,2,1,0:T(8,128)(2,1)} %copy-done.9, ...), custom_call_target="tpu_custom_call" | custom-call | flops 671088640 | bytes 1703936 | tf_op jit(solution)/shard_map/pallas_call | solution.py:205
  57.9 0.5 copy-done.3
  58.5 0.0 copy-done.4
  58.5 0.1 copy-done.5
  58.6 0.0 copy-done.6
  58.6 0.0 copy-done.7
  58.7 8.1 %shard_map.66 = bf16[128,2048]{1,0:T(8,128)(2,1)} custom-call(bf16[128,2048]{1,0:T(8,128)(2,1)} %bitcast.7, s32[8,1,128]{2,1,0:T(1,128)} %slice.13.refs_1_, bf16[4,2,32,256]{3,2,1,0:T(8,128)(2,1)} %copy-done, bf16[4,2,32,256]{3,2,1,0:T(8,128)(2,1)} %copy-done.1, bf16[4,2,32,256]{3,2,1,0:T(8,128)(2,1)} %copy-done.2, bf16[4,2,32,256]{3,2,1,0:T(8,128)(2,1)} %copy-done.3, ...), custom_call_target="tpu_custom_call" | custom-call | flops 1073741824 | bytes 2097152 | tf_op jit(solution)/shard_map/pallas_call | solution.py:205
  (37 shorter events, 0.1 us)
Async XLA Ops:
  0.0 12.0 %copy-start.12 = (s32[4]{0:T(128)S(1)}, s32[4]{0:T(128)}, u32[]{:S(2)}) copy-start(s32[4]{0:T(128)} %param.11) | copy-start | bytes 52
  3.6 16.5 %collective-permute-start = (bf16[4,2,32,256]{3,2,1,0:T(8,128)(2,1)}, bf16[4,2,32,256]{3,2,1,0:T(8,128)(2,1)S(1)}, u32[]{:S(2)}, u32[]{:S(2)}) collective-permute-start(bf16[4,2,32,256]{3,2,1,0:T(8,128)(2,1)} %get-tuple-element.20), channel_id=1, source_target_pairs={{0,8},{1,9},{2,10},{3,11},{4,12},{5,13},{6,14},{7,15},{8,0},{9,1},... | collective-permute-start | bytes 393224 | tf_op jit(solution)/shard_map/ppermute | solution.py:94
  3.7 19.4 %collective-permute-start.1 = (bf16[4,2,32,256]{3,2,1,0:T(8,128)(2,1)}, bf16[4,2,32,256]{3,2,1,0:T(8,128)(2,1)S(1)}, u32[]{:S(2)}, u32[]{:S(2)}) collective-permute-start(bf16[4,2,32,256]{3,2,1,0:T(8,128)(2,1)} %get-tuple-element.21), channel_id=1, source_target_pairs={{0,9},{1,10},{2,11},{3,8},{4,13},{5,14},{6,15},{7,12},{8,1},{9,2},... | collective-permute-start | bytes 393224 | tf_op jit(solution)/shard_map/ppermute | solution.py:94
  7.8 20.4 %collective-permute-start.2 = (bf16[4,2,32,256]{3,2,1,0:T(8,128)(2,1)}, bf16[4,2,32,256]{3,2,1,0:T(8,128)(2,1)S(1)}, u32[]{:S(2)}, u32[]{:S(2)}) collective-permute-start(bf16[4,2,32,256]{3,2,1,0:T(8,128)(2,1)} %get-tuple-element.22), channel_id=1, source_target_pairs={{0,10},{1,11},{2,8},{3,9},{4,14},{5,15},{6,12},{7,13},{8,2},{9,3},... | collective-permute-start | bytes 393224 | tf_op jit(solution)/shard_map/ppermute | solution.py:94
  7.8 31.1 %collective-permute-start.8 = (bf16[4,2,32,256]{3,2,1,0:T(8,128)(2,1)}, bf16[4,2,32,256]{3,2,1,0:T(8,128)(2,1)S(1)}, u32[]{:S(2)}, u32[]{:S(2)}) collective-permute-start(bf16[4,2,32,256]{3,2,1,0:T(8,128)(2,1)} %get-tuple-element.28), channel_id=1, source_target_pairs={{0,4},{1,5},{2,6},{3,7},{4,8},{5,9},{6,10},{7,11},{8,12},{9,13},{1... | collective-permute-start | bytes 393224 | tf_op jit(solution)/shard_map/ppermute | solution.py:94
  9.1 29.8 %collective-permute-start.9 = (bf16[4,2,32,256]{3,2,1,0:T(8,128)(2,1)}, bf16[4,2,32,256]{3,2,1,0:T(8,128)(2,1)S(1)}, u32[]{:S(2)}, u32[]{:S(2)}) collective-permute-start(bf16[4,2,32,256]{3,2,1,0:T(8,128)(2,1)} %get-tuple-element.29), channel_id=1, source_target_pairs={{0,5},{1,6},{2,7},{3,4},{4,9},{5,10},{6,11},{7,8},{8,13},{9,14},{1... | collective-permute-start | bytes 393224 | tf_op jit(solution)/shard_map/ppermute | solution.py:94
  20.1 37.8 %copy-start = (bf16[4,2,32,256]{3,2,1,0:T(8,128)(2,1)}, bf16[4,2,32,256]{3,2,1,0:T(8,128)(2,1)S(1)}, u32[]{:S(2)}) copy-start(bf16[4,2,32,256]{3,2,1,0:T(8,128)(2,1)S(1)} %collective-permute-done.refs_2_) | copy-start | bytes 393220
  20.1 18.9 %collective-permute-start.10 = (bf16[4,2,32,256]{3,2,1,0:T(8,128)(2,1)}, bf16[4,2,32,256]{3,2,1,0:T(8,128)(2,1)S(1)}, u32[]{:S(2)}, u32[]{:S(2)}) collective-permute-start(bf16[4,2,32,256]{3,2,1,0:T(8,128)(2,1)} %get-tuple-element.30), channel_id=1, source_target_pairs={{0,6},{1,7},{2,4},{3,5},{4,10},{5,11},{6,8},{7,9},{8,14},{9,15},{1... | collective-permute-start | bytes 393224 | tf_op jit(solution)/shard_map/ppermute | solution.py:94
  23.0 34.9 %copy-start.1 = (bf16[4,2,32,256]{3,2,1,0:T(8,128)(2,1)}, bf16[4,2,32,256]{3,2,1,0:T(8,128)(2,1)S(1)}, u32[]{:S(2)}) copy-start(bf16[4,2,32,256]{3,2,1,0:T(8,128)(2,1)S(1)} %collective-permute-done.1.refs_3_) | copy-start | bytes 393220
  23.1 27.3 %collective-permute-start.11 = (bf16[4,2,32,256]{3,2,1,0:T(8,128)(2,1)}, bf16[4,2,32,256]{3,2,1,0:T(8,128)(2,1)S(1)}, u32[]{:S(2)}, u32[]{:S(2)}) collective-permute-start(bf16[4,2,32,256]{3,2,1,0:T(8,128)(2,1)} %get-tuple-element.31), channel_id=1, source_target_pairs={{0,7},{1,4},{2,5},{3,6},{4,11},{5,8},{6,9},{7,10},{8,15},{9,12},{1... | collective-permute-start | bytes 393224 | tf_op jit(solution)/shard_map/ppermute | solution.py:94
  28.2 29.8 %copy-start.2 = (bf16[4,2,32,256]{3,2,1,0:T(8,128)(2,1)}, bf16[4,2,32,256]{3,2,1,0:T(8,128)(2,1)S(1)}, u32[]{:S(2)}) copy-start(bf16[4,2,32,256]{3,2,1,0:T(8,128)(2,1)S(1)} %collective-permute-done.2.refs_4_) | copy-start | bytes 393220
  28.2 29.7 %collective-permute-start.3 = (bf16[4,2,32,256]{3,2,1,0:T(8,128)(2,1)}, bf16[4,2,32,256]{3,2,1,0:T(8,128)(2,1)S(1)}, u32[]{:S(2)}, u32[]{:S(2)}) collective-permute-start(bf16[4,2,32,256]{3,2,1,0:T(8,128)(2,1)} %get-tuple-element.23), channel_id=1, source_target_pairs={{0,11},{1,8},{2,9},{3,10},{4,15},{5,12},{6,13},{7,14},{8,3},{9,0},... | collective-permute-start | bytes 393224 | tf_op jit(solution)/shard_map/ppermute | solution.py:94
  38.9 13.5 %copy-start.8 = (bf16[4,2,32,256]{3,2,1,0:T(8,128)(2,1)}, bf16[4,2,32,256]{3,2,1,0:T(8,128)(2,1)S(1)}, u32[]{:S(2)}) copy-start(bf16[4,2,32,256]{3,2,1,0:T(8,128)(2,1)S(1)} %collective-permute-done.8.refs_3_) | copy-start | bytes 393220
  38.9 18.9 %collective-permute-start.4 = (bf16[4,2,32,256]{3,2,1,0:T(8,128)(2,1)}, bf16[4,2,32,256]{3,2,1,0:T(8,128)(2,1)S(1)}, u32[]{:S(2)}, u32[]{:S(2)}) collective-permute-start(bf16[4,2,32,256]{3,2,1,0:T(8,128)(2,1)} %get-tuple-element.24), channel_id=1, source_target_pairs={{0,12},{1,13},{2,14},{3,15},{4,0},{5,1},{6,2},{7,3},{8,4},{9,5},{1... | collective-permute-start | bytes 393224 | tf_op jit(solution)/shard_map/ppermute | solution.py:94
  38.9 13.5 %copy-start.9 = (bf16[4,2,32,256]{3,2,1,0:T(8,128)(2,1)}, bf16[4,2,32,256]{3,2,1,0:T(8,128)(2,1)S(1)}, u32[]{:S(2)}) copy-start(bf16[4,2,32,256]{3,2,1,0:T(8,128)(2,1)S(1)} %collective-permute-done.9.refs_4_) | copy-start | bytes 393220
  39.0 18.9 %collective-permute-start.5 = (bf16[4,2,32,256]{3,2,1,0:T(8,128)(2,1)}, bf16[4,2,32,256]{3,2,1,0:T(8,128)(2,1)S(1)}, u32[]{:S(2)}, u32[]{:S(2)}) collective-permute-start(bf16[4,2,32,256]{3,2,1,0:T(8,128)(2,1)} %get-tuple-element.25), channel_id=1, source_target_pairs={{0,13},{1,14},{2,15},{3,12},{4,1},{5,2},{6,3},{7,0},{8,5},{9,6},{1... | collective-permute-start | bytes 393224 | tf_op jit(solution)/shard_map/ppermute | solution.py:94
  39.0 13.4 %copy-start.10 = (bf16[4,2,32,256]{3,2,1,0:T(8,128)(2,1)}, bf16[4,2,32,256]{3,2,1,0:T(8,128)(2,1)S(1)}, u32[]{:S(2)}) copy-start(bf16[4,2,32,256]{3,2,1,0:T(8,128)(2,1)S(1)} %collective-permute-done.10.refs_5_) | copy-start | bytes 393220
  39.0 18.8 %collective-permute-start.6 = (bf16[4,2,32,256]{3,2,1,0:T(8,128)(2,1)}, bf16[4,2,32,256]{3,2,1,0:T(8,128)(2,1)S(1)}, u32[]{:S(2)}, u32[]{:S(2)}) collective-permute-start(bf16[4,2,32,256]{3,2,1,0:T(8,128)(2,1)} %get-tuple-element.26), channel_id=1, source_target_pairs={{0,14},{1,15},{2,12},{3,13},{4,2},{5,3},{6,0},{7,1},{8,6},{9,7},{1... | collective-permute-start | bytes 393224 | tf_op jit(solution)/shard_map/ppermute | solution.py:94
  50.4 2.1 %copy-start.11 = (bf16[4,2,32,256]{3,2,1,0:T(8,128)(2,1)}, bf16[4,2,32,256]{3,2,1,0:T(8,128)(2,1)S(1)}, u32[]{:S(2)}) copy-start(bf16[4,2,32,256]{3,2,1,0:T(8,128)(2,1)S(1)} %collective-permute-done.11.refs_6_) | copy-start | bytes 393220
  50.4 7.5 %collective-permute-start.7 = (bf16[4,2,32,256]{3,2,1,0:T(8,128)(2,1)}, bf16[4,2,32,256]{3,2,1,0:T(8,128)(2,1)S(1)}, u32[]{:S(2)}, u32[]{:S(2)}) collective-permute-start(bf16[4,2,32,256]{3,2,1,0:T(8,128)(2,1)} %get-tuple-element.27), channel_id=1, source_target_pairs={{0,15},{1,12},{2,13},{3,14},{4,3},{5,0},{6,1},{7,2},{8,7},{9,4},{1... | collective-permute-start | bytes 393224 | tf_op jit(solution)/shard_map/ppermute | solution.py:94
  57.8 0.7 copy-start.3
  57.8 0.7 %copy-start.4 = (bf16[4,2,32,256]{3,2,1,0:T(8,128)(2,1)}, bf16[4,2,32,256]{3,2,1,0:T(8,128)(2,1)S(1)}, u32[]{:S(2)}) copy-start(bf16[4,2,32,256]{3,2,1,0:T(8,128)(2,1)S(1)} %collective-permute-done.4.refs_6_) | copy-start | bytes 393220
  57.9 0.7 %copy-start.5 = (bf16[4,2,32,256]{3,2,1,0:T(8,128)(2,1)}, bf16[4,2,32,256]{3,2,1,0:T(8,128)(2,1)S(1)}, u32[]{:S(2)}) copy-start(bf16[4,2,32,256]{3,2,1,0:T(8,128)(2,1)S(1)} %collective-permute-done.5.refs_7_) | copy-start | bytes 393220
  57.9 0.7 %copy-start.6 = (bf16[4,2,32,256]{3,2,1,0:T(8,128)(2,1)}, bf16[4,2,32,256]{3,2,1,0:T(8,128)(2,1)S(1)}, u32[]{:S(2)}) copy-start(bf16[4,2,32,256]{3,2,1,0:T(8,128)(2,1)S(1)} %collective-permute-done.6.refs_8_) | copy-start | bytes 393220
  57.9 0.8 %copy-start.7 = (bf16[4,2,32,256]{3,2,1,0:T(8,128)(2,1)}, bf16[4,2,32,256]{3,2,1,0:T(8,128)(2,1)S(1)}, u32[]{:S(2)}) copy-start(bf16[4,2,32,256]{3,2,1,0:T(8,128)(2,1)S(1)} %collective-permute-done.7.refs_9_) | copy-start | bytes 393220

commit v8 on v6

--- a/solution.py
+++ b/solution.py
@@ -133,33 +133,43 @@
         keys = [suf_ref[0, :, lanes]]
         vals = [suf_ref[1, :, lanes]]
         masks = [causal]
-        for c in range(chunk_count):
-            ref = chunk_refs[c]
-            keys.append(ref[:, 0, :, lanes].reshape(-1, HEAD_DIM))
-            vals.append(ref[:, 1, :, lanes].reshape(-1, HEAD_DIM))
-            masks.append(vis_ref[c] > 0)
+        pieces = [
+            (
+                chunk_refs[c][:, 0, :, lanes].reshape(-1, HEAD_DIM),
+                chunk_refs[c][:, 1, :, lanes].reshape(-1, HEAD_DIM),
+                vis_ref[c],
+            )
+            for c in range(chunk_count)
+        ]
+        join = 2 if chunk_count % 2 == 0 else 1
+        for c in range(0, chunk_count, join):
+            part = pieces[c:c + join]
+            keys.append(jnp.concatenate([p[0] for p in part], axis=0))
+            vals.append(jnp.concatenate([p[1] for p in part], axis=0))
+            masks.append(jnp.concatenate([p[2] for p in part], axis=-1) > 0)
         scores = []
         for key, mask in zip(keys, masks):
             s = lax.dot_general(q_all, key, dims, preferred_element_type=jnp.float32) * scale
             scores.append(jnp.where(mask, s, NEG_FILL))
-        even = all(s.shape == scores[0].shape for s in scores)
-        if even:
-            running = scores[0]
-            for s in scores[1:]:
-                running = jnp.maximum(running, s)
-            top = jnp.max(running, axis=-1, keepdims=True)
-        else:
-            top = functools.reduce(jnp.maximum, [jnp.max(s, axis=-1, keepdims=True) for s in scores])
-        total = None
+        widths = sorted(set(s.shape[-1] for s in scores))
+        top = None
+        for width_now in widths:
+            same = [s for s in scores if s.shape[-1] == width_now]
+            part = functools.reduce(jnp.maximum, same)
+            part = jnp.max(part, axis=-1, keepdims=True)
+            top = part if top is None else jnp.maximum(top, part)
+        sums = {}
         acc = None
         for s, val, mask in zip(scores, vals, masks):
             w = jnp.where(mask, jnp.exp(s - top), 0.0)
-            part = w if even else jnp.sum(w, axis=-1, keepdims=True)
-            total = part if total is None else total + part
+            width_now = s.shape[-1]
+            sums[width_now] = w if width_now not in sums else sums[width_now] + w
             pv = jnp.dot(w.astype(jnp.bfloat16), val, preferred_element_type=jnp.float32)
             acc = pv if acc is None else acc + pv
-        if even:
-            total = jnp.sum(total, axis=-1, keepdims=True)
+        total = None
+        for width_now in widths:
+            part = jnp.sum(sums[width_now], axis=-1, keepdims=True)
+            total = part if total is None else total + part
         out = (acc / total).astype(o_ref.dtype)
         for g in range(group):
             o_ref[:, pl.ds((head * group + g) * HEAD_DIM, HEAD_DIM)] = out[g * rows:(g + 1) * rows]

time: 66.6 us -> 65.7 us (0.986)
  Pallas kernels: 13.8 us -> 13 us
    pallas_call x1, Pallas kernels: 10.2 us -> 9.34 us  [attend(): pl.pallas_call(functools.partial(attention_kernel, len(chunks)), out_shap...]
where the time goes in v8:
time: 65.7 us; the launch traced here: 65.5 us
  starting transfers between devices  34 us (52%)
  waiting for transfers between devices  14.2 us (22%)
  Pallas kernels  13 us (20%)
  local copies, waits for them, and re-layouts  2.39 us (4%)
  other arithmetic  1.78 us (3%)
    ppermute x12, starting transfers between devices, on_device(): lax.ppermute(payload[(distance - 1) * tensor_count + shift], ('replica',...  34 us
    ppermute x12, waiting for transfers between devices, on_device(): lax.ppermute(payload[(distance - 1) * tensor_count + shift], ('replica',...  14.2 us
    pallas_call x1, Pallas kernels, attend(): pl.pallas_call(functools.partial(attention_kernel, len(chunks)), out_shap...  9.34 us
    pallas_call x1, Pallas kernels, pack_pages(): pl.pallas_call(functools.partial(gather_kernel, span_count, slot_cap, ten...  3.63 us
  transfers between devices with their start and end apart: 12, of which 3 were waited for; matrix products, arithmetic and copies ran while one was open for 5% of the time, Pallas kernels for 0%

profile of v8, /device:TPU:1, one launch (start us, length us, event | category | flops | bytes accessed | tf_op | source)
XLA Modules:
  0.0 65.5 jit_solution(4176426563318925072)
XLA Ops:
  0.0 3.6 %shard_map.64 = (bf16[4,2,32,256]{3,2,1,0:T(8,128)(2,1)}, bf16[4,2,32,256]{3,2,1,0:T(8,128)(2,1)}, bf16[4,2,32,256]{3,2,1,0:T(8,128)(2,1)}, bf16[4,2,32,256]{3,2...) custom-call(s32[4,8]{1,0:T(4,128)} %off_ref.1, ...), custom_call_target="tpu_custom_call" | custom-call | bytes 3145728 | tf_op jit(solution)/shard_map/pallas_call | solution.py:66
  3.6 2.1 %collective-permute-start = (bf16[4,2,32,256]{3,2,1,0:T(8,128)(2,1)}, bf16[4,2,32,256]{3,2,1,0:T(8,128)(2,1)S(1)}, u32[]{:S(2)}, u32[]{:S(2)}) collective-permute-start(bf16[4,2,32,256]{3,2,1,0:T(8,128)(2,1)} %get-tuple-element.17), channel_id=1, source_target_pairs={{0,4},{1,5},{2,6},{3,7},{4,8},{5,9},{6,10},{7,11},{8,12},{9,13},{1... | collective-permute-start | bytes 393224 | tf_op jit(solution)/shard_map/ppermute | solution.py:94
  5.8 3.1 %collective-permute-start.1 = (bf16[4,2,32,256]{3,2,1,0:T(8,128)(2,1)}, bf16[4,2,32,256]{3,2,1,0:T(8,128)(2,1)S(1)}, u32[]{:S(2)}, u32[]{:S(2)}) collective-permute-start(bf16[4,2,32,256]{3,2,1,0:T(8,128)(2,1)} %get-tuple-element.18), channel_id=1, source_target_pairs={{0,5},{1,6},{2,7},{3,4},{4,9},{5,10},{6,11},{7,8},{8,13},{9,14},{1... | collective-permute-start | bytes 393224 | tf_op jit(solution)/shard_map/ppermute | solution.py:94
  8.8 1.3 %collective-permute-start.2 = (bf16[4,2,32,256]{3,2,1,0:T(8,128)(2,1)}, bf16[4,2,32,256]{3,2,1,0:T(8,128)(2,1)S(1)}, u32[]{:S(2)}, u32[]{:S(2)}) collective-permute-start(bf16[4,2,32,256]{3,2,1,0:T(8,128)(2,1)} %get-tuple-element.19), channel_id=1, source_target_pairs={{0,6},{1,7},{2,4},{3,5},{4,10},{5,11},{6,8},{7,9},{8,14},{9,15},{1... | collective-permute-start | bytes 393224 | tf_op jit(solution)/shard_map/ppermute | solution.py:94
  10.1 0.3 collective-permute-start.3
  10.4 1.7 %collective-permute-start.4 = (bf16[4,2,32,256]{3,2,1,0:T(8,128)(2,1)}, bf16[4,2,32,256]{3,2,1,0:T(8,128)(2,1)S(1)}, u32[]{:S(2)}, u32[]{:S(2)}) collective-permute-start(bf16[4,2,32,256]{3,2,1,0:T(8,128)(2,1)} %get-tuple-element.21), channel_id=1, source_target_pairs={{0,8},{1,9},{2,10},{3,11},{4,12},{5,13},{6,14},{7,15},{8,0},{9,1},... | collective-permute-start | bytes 393224 | tf_op jit(solution)/shard_map/ppermute | solution.py:94
  12.1 0.7 %dynamic-slice_bitcast_fusion = s32[8]{0:T(128)S(1)} fusion(s32[4,8]{1,0:T(4,128)} %off_ref.1, s32[]{:T(128)S(6)} %select_n.17), kind=kLoop, calls=%fused_computation.18 | loop fusion | bytes 68 | tf_op jit(solution)/shard_map/eq | solution.py:19
  12.8 0.1 compare_convert_fusion
  12.9 0.1 multiply_reduce_fusion
  13.0 0.2 fusion
  13.2 0.7 %dynamic_slice.9 = s32[1]{0:T(128)} dynamic-slice(s32[4]{0:T(128)S(1)} %copy-done.12, s32[]{:T(128)S(6)} %select_n.17), dynamic_slice_sizes={1} | dynamic-slice | bytes 12 | tf_op jit(solution)/shard_map/jit(dynamic_index_in_dim)/dynamic_slice | solution.py:100
  13.9 0.1 add.84
  14.0 0.1 and.31
  14.1 0.1 and.35
  14.2 1.9 %collective-permute-start.5 = (bf16[4,2,32,256]{3,2,1,0:T(8,128)(2,1)}, bf16[4,2,32,256]{3,2,1,0:T(8,128)(2,1)S(1)}, u32[]{:S(2)}, u32[]{:S(2)}) collective-permute-start(bf16[4,2,32,256]{3,2,1,0:T(8,128)(2,1)} %get-tuple-element.22), channel_id=1, source_target_pairs={{0,9},{1,10},{2,11},{3,8},{4,13},{5,14},{6,15},{7,12},{8,1},{9,2},... | collective-permute-start | bytes 393224 | tf_op jit(solution)/shard_map/ppermute | solution.py:94
  16.1 3.1 %collective-permute-start.6 = (bf16[4,2,32,256]{3,2,1,0:T(8,128)(2,1)}, bf16[4,2,32,256]{3,2,1,0:T(8,128)(2,1)S(1)}, u32[]{:S(2)}, u32[]{:S(2)}) collective-permute-start(bf16[4,2,32,256]{3,2,1,0:T(8,128)(2,1)} %get-tuple-element.23), channel_id=1, source_target_pairs={{0,10},{1,11},{2,8},{3,9},{4,14},{5,15},{6,12},{7,13},{8,2},{9,3},... | collective-permute-start | bytes 393224 | tf_op jit(solution)/shard_map/ppermute | solution.py:94
  19.2 0.1 broadcast_add_fusion
  19.3 0.1 add.81
  19.4 0.1 add.82
  19.5 0.5 collective-permute-start.7
  20.0 1.9 %collective-permute-done.3.rest_3_ = bf16[4,2,32,256]{3,2,1,0:T(8,128)(2,1)S(1)} collective-permute-done((bf16[4,2,32,256]{3,2,1,0:T(8,128)(2,1)}, bf16[4,2,32,256]{3,2,1,0:T(8,128)(2,1)S(1)}, u32[]{:S(2)}, u32[]{:S(2)}) %collective-permute-start.3) | collective-permute-done | bytes 131104 | tf_op jit(solution)/shard_map/ppermute | solution.py:94
  22.0 1.1 %collective-permute-start.8 = (bf16[4,2,32,256]{3,2,1,0:T(8,128)(2,1)}, bf16[4,2,32,256]{3,2,1,0:T(8,128)(2,1)S(1)}, u32[]{:S(2)}, u32[]{:S(2)}) collective-permute-start(bf16[4,2,32,256]{3,2,1,0:T(8,128)(2,1)} %get-tuple-element.25), channel_id=1, source_target_pairs={{0,12},{1,13},{2,14},{3,15},{4,0},{5,1},{6,2},{7,3},{8,4},{9,5},{1... | collective-permute-start | bytes 393224 | tf_op jit(solution)/shard_map/ppermute | solution.py:94
  23.1 11.3 %collective-permute-done.4.rest_4_ = bf16[4,2,32,256]{3,2,1,0:T(8,128)(2,1)S(1)} collective-permute-done((bf16[4,2,32,256]{3,2,1,0:T(8,128)(2,1)}, bf16[4,2,32,256]{3,2,1,0:T(8,128)(2,1)S(1)}, u32[]{:S(2)}, u32[]{:S(2)}) %collective-permute-start.4) | collective-permute-done | bytes 131104 | tf_op jit(solution)/shard_map/ppermute | solution.py:94
  34.4 6.2 %collective-permute-start.9 = (bf16[4,2,32,256]{3,2,1,0:T(8,128)(2,1)}, bf16[4,2,32,256]{3,2,1,0:T(8,128)(2,1)S(1)}, u32[]{:S(2)}, u32[]{:S(2)}) collective-permute-start(bf16[4,2,32,256]{3,2,1,0:T(8,128)(2,1)} %get-tuple-element.26), channel_id=1, source_target_pairs={{0,13},{1,14},{2,15},{3,12},{4,1},{5,2},{6,3},{7,0},{8,5},{9,6},{1... | collective-permute-start | bytes 393224 | tf_op jit(solution)/shard_map/ppermute | solution.py:94
  40.6 2.5 %collective-permute-start.10 = (bf16[4,2,32,256]{3,2,1,0:T(8,128)(2,1)}, bf16[4,2,32,256]{3,2,1,0:T(8,128)(2,1)S(1)}, u32[]{:S(2)}, u32[]{:S(2)}) collective-permute-start(bf16[4,2,32,256]{3,2,1,0:T(8,128)(2,1)} %get-tuple-element.27), channel_id=1, source_target_pairs={{0,14},{1,15},{2,12},{3,13},{4,2},{5,3},{6,0},{7,1},{8,6},{9,7},{1... | collective-permute-start | bytes 393224 | tf_op jit(solution)/shard_map/ppermute | solution.py:94
  43.1 0.0 collective-permute-done.6.rest_6_
  43.1 10.1 %collective-permute-start.11 = (bf16[4,2,32,256]{3,2,1,0:T(8,128)(2,1)}, bf16[4,2,32,256]{3,2,1,0:T(8,128)(2,1)S(1)}, u32[]{:S(2)}, u32[]{:S(2)}) collective-permute-start(bf16[4,2,32,256]{3,2,1,0:T(8,128)(2,1)} %get-tuple-element.28), channel_id=1, source_target_pairs={{0,15},{1,12},{2,13},{3,14},{4,3},{5,0},{6,1},{7,2},{8,7},{9,4},{1... | collective-permute-start | bytes 393224 | tf_op jit(solution)/shard_map/ppermute | solution.py:94
  53.2 1.3 %and_convert_fusion.vis_ref = s32[12,1,128]{2,1,0:T(1,128)} fusion(pred[12,1,128]{2,1,0:T(4,128)(4,1)S(1)} %and.35, s32[12,1,128]{2,1,0:T(1,128)S(1)} %add.82, s32[]{:T(128)} %bitcast.3, s32[128]{0:T(128)S(1)} %add.84), kind=kLoop, calls=%fused_computation | loop fusion | flops 6144 | bytes 14340 | tf_op jit(solution)/shard_map/convert_element_type | solution.py:113
  54.5 0.0 collective-permute-done.7.rest_7_
  54.6 0.9 %collective-permute-done.11.rest_11_ = bf16[4,2,32,256]{3,2,1,0:T(8,128)(2,1)S(1)} collective-permute-done((bf16[4,2,32,256]{3,2,1,0:T(8,128)(2,1)}, bf16[4,2,32,256]{3,2,1,0:T(8,128)(2,1)S(1)}, u32[]{:S(2)}, u32[]{:S(2)}) %collective-permute-start.11) | collective-permute-done | bytes 131104 | tf_op jit(solution)/shard_map/ppermute | solution.py:94
  55.6 0.6 copy-done.11
  56.2 9.3 %shard_map.65 = bf16[128,2048]{1,0:T(8,128)(2,1)} custom-call(bf16[128,2048]{1,0:T(8,128)(2,1)} %bitcast.6, bf16[2,128,256]{2,1,0:T(8,128)(2,1)} %bitcast.7, s32[12,1,128]{2,1,0:T(1,128)} %and_convert_fusion.vis_ref, bf16[4,2,32,256]{3,2,1,0:T(8,128)(2,1)} %copy-done, bf16[4,2,32,256]{3,2,1,0:T(8,128)(2,1)} %copy-done.1, bf16[4,2,32,256]{3,2,1,0:T(8,128)(2,1)} %copy-done.2, ...), custom_call_target="tpu_custom_call" | custom-call | flops 1744830464 | bytes 2752512 | tf_op jit(solution)/shard_map/pallas_call | solution.py:183
  (38 shorter events, 0.1 us)
Async XLA Ops:
  0.0 13.2 %copy-start.12 = (s32[4]{0:T(128)S(1)}, s32[4]{0:T(128)}, u32[]{:S(2)}) copy-start(s32[4]{0:T(128)} %param.11) | copy-start | bytes 52
  3.6 10.5 %collective-permute-start = (bf16[4,2,32,256]{3,2,1,0:T(8,128)(2,1)}, bf16[4,2,32,256]{3,2,1,0:T(8,128)(2,1)S(1)}, u32[]{:S(2)}, u32[]{:S(2)}) collective-permute-start(bf16[4,2,32,256]{3,2,1,0:T(8,128)(2,1)} %get-tuple-element.17), channel_id=1, source_target_pairs={{0,4},{1,5},{2,6},{3,7},{4,8},{5,9},{6,10},{7,11},{8,12},{9,13},{1... | collective-permute-start | bytes 393224 | tf_op jit(solution)/shard_map/ppermute | solution.py:94
  5.8 10.4 %collective-permute-start.1 = (bf16[4,2,32,256]{3,2,1,0:T(8,128)(2,1)}, bf16[4,2,32,256]{3,2,1,0:T(8,128)(2,1)S(1)}, u32[]{:S(2)}, u32[]{:S(2)}) collective-permute-start(bf16[4,2,32,256]{3,2,1,0:T(8,128)(2,1)} %get-tuple-element.18), channel_id=1, source_target_pairs={{0,5},{1,6},{2,7},{3,4},{4,9},{5,10},{6,11},{7,8},{8,13},{9,14},{1... | collective-permute-start | bytes 393224 | tf_op jit(solution)/shard_map/ppermute | solution.py:94
  8.8 10.7 %collective-permute-start.2 = (bf16[4,2,32,256]{3,2,1,0:T(8,128)(2,1)}, bf16[4,2,32,256]{3,2,1,0:T(8,128)(2,1)S(1)}, u32[]{:S(2)}, u32[]{:S(2)}) collective-permute-start(bf16[4,2,32,256]{3,2,1,0:T(8,128)(2,1)} %get-tuple-element.19), channel_id=1, source_target_pairs={{0,6},{1,7},{2,4},{3,5},{4,10},{5,11},{6,8},{7,9},{8,14},{9,15},{1... | collective-permute-start | bytes 393224 | tf_op jit(solution)/shard_map/ppermute | solution.py:94
  10.1 11.9 %collective-permute-start.3 = (bf16[4,2,32,256]{3,2,1,0:T(8,128)(2,1)}, bf16[4,2,32,256]{3,2,1,0:T(8,128)(2,1)S(1)}, u32[]{:S(2)}, u32[]{:S(2)}) collective-permute-start(bf16[4,2,32,256]{3,2,1,0:T(8,128)(2,1)} %get-tuple-element.20), channel_id=1, source_target_pairs={{0,7},{1,4},{2,5},{3,6},{4,11},{5,8},{6,9},{7,10},{8,15},{9,12},{1... | collective-permute-start | bytes 393224 | tf_op jit(solution)/shard_map/ppermute | solution.py:94
  10.4 24.0 %collective-permute-start.4 = (bf16[4,2,32,256]{3,2,1,0:T(8,128)(2,1)}, bf16[4,2,32,256]{3,2,1,0:T(8,128)(2,1)S(1)}, u32[]{:S(2)}, u32[]{:S(2)}) collective-permute-start(bf16[4,2,32,256]{3,2,1,0:T(8,128)(2,1)} %get-tuple-element.21), channel_id=1, source_target_pairs={{0,8},{1,9},{2,10},{3,11},{4,12},{5,13},{6,14},{7,15},{8,0},{9,1},... | collective-permute-start | bytes 393224 | tf_op jit(solution)/shard_map/ppermute | solution.py:94
  14.2 41.3 %copy-start = (bf16[4,2,32,256]{3,2,1,0:T(8,128)(2,1)}, bf16[4,2,32,256]{3,2,1,0:T(8,128)(2,1)S(1)}, u32[]{:S(2)}) copy-start(bf16[4,2,32,256]{3,2,1,0:T(8,128)(2,1)S(1)} %collective-permute-done.rest_0_) | copy-start | bytes 393220
  14.2 26.4 %collective-permute-start.5 = (bf16[4,2,32,256]{3,2,1,0:T(8,128)(2,1)}, bf16[4,2,32,256]{3,2,1,0:T(8,128)(2,1)S(1)}, u32[]{:S(2)}, u32[]{:S(2)}) collective-permute-start(bf16[4,2,32,256]{3,2,1,0:T(8,128)(2,1)} %get-tuple-element.22), channel_id=1, source_target_pairs={{0,9},{1,10},{2,11},{3,8},{4,13},{5,14},{6,15},{7,12},{8,1},{9,2},... | collective-permute-start | bytes 393224 | tf_op jit(solution)/shard_map/ppermute | solution.py:94
  16.1 39.4 %copy-start.1 = (bf16[4,2,32,256]{3,2,1,0:T(8,128)(2,1)}, bf16[4,2,32,256]{3,2,1,0:T(8,128)(2,1)S(1)}, u32[]{:S(2)}) copy-start(bf16[4,2,32,256]{3,2,1,0:T(8,128)(2,1)S(1)} %collective-permute-done.1.rest_1_) | copy-start | bytes 393220
  16.1 27.0 %collective-permute-start.6 = (bf16[4,2,32,256]{3,2,1,0:T(8,128)(2,1)}, bf16[4,2,32,256]{3,2,1,0:T(8,128)(2,1)S(1)}, u32[]{:S(2)}, u32[]{:S(2)}) collective-permute-start(bf16[4,2,32,256]{3,2,1,0:T(8,128)(2,1)} %get-tuple-element.23), channel_id=1, source_target_pairs={{0,10},{1,11},{2,8},{3,9},{4,14},{5,15},{6,12},{7,13},{8,2},{9,3},... | collective-permute-start | bytes 393224 | tf_op jit(solution)/shard_map/ppermute | solution.py:94
  19.5 36.0 %copy-start.2 = (bf16[4,2,32,256]{3,2,1,0:T(8,128)(2,1)}, bf16[4,2,32,256]{3,2,1,0:T(8,128)(2,1)S(1)}, u32[]{:S(2)}) copy-start(bf16[4,2,32,256]{3,2,1,0:T(8,128)(2,1)S(1)} %collective-permute-done.2.rest_2_) | copy-start | bytes 393220
  19.5 35.0 %collective-permute-start.7 = (bf16[4,2,32,256]{3,2,1,0:T(8,128)(2,1)}, bf16[4,2,32,256]{3,2,1,0:T(8,128)(2,1)S(1)}, u32[]{:S(2)}, u32[]{:S(2)}) collective-permute-start(bf16[4,2,32,256]{3,2,1,0:T(8,128)(2,1)} %get-tuple-element.24), channel_id=1, source_target_pairs={{0,11},{1,8},{2,9},{3,10},{4,15},{5,12},{6,13},{7,14},{8,3},{9,0},... | collective-permute-start | bytes 393224 | tf_op jit(solution)/shard_map/ppermute | solution.py:94
  22.0 33.5 %copy-start.3 = (bf16[4,2,32,256]{3,2,1,0:T(8,128)(2,1)}, bf16[4,2,32,256]{3,2,1,0:T(8,128)(2,1)S(1)}, u32[]{:S(2)}) copy-start(bf16[4,2,32,256]{3,2,1,0:T(8,128)(2,1)S(1)} %collective-permute-done.3.rest_3_) | copy-start | bytes 393220
  22.0 32.5 %collective-permute-start.8 = (bf16[4,2,32,256]{3,2,1,0:T(8,128)(2,1)}, bf16[4,2,32,256]{3,2,1,0:T(8,128)(2,1)S(1)}, u32[]{:S(2)}, u32[]{:S(2)}) collective-permute-start(bf16[4,2,32,256]{3,2,1,0:T(8,128)(2,1)} %get-tuple-element.25), channel_id=1, source_target_pairs={{0,12},{1,13},{2,14},{3,15},{4,0},{5,1},{6,2},{7,3},{8,4},{9,5},{1... | collective-permute-start | bytes 393224 | tf_op jit(solution)/shard_map/ppermute | solution.py:94
  34.4 21.1 %copy-start.4 = (bf16[4,2,32,256]{3,2,1,0:T(8,128)(2,1)}, bf16[4,2,32,256]{3,2,1,0:T(8,128)(2,1)S(1)}, u32[]{:S(2)}) copy-start(bf16[4,2,32,256]{3,2,1,0:T(8,128)(2,1)S(1)} %collective-permute-done.4.rest_4_) | copy-start | bytes 393220
  34.4 20.1 %collective-permute-start.9 = (bf16[4,2,32,256]{3,2,1,0:T(8,128)(2,1)}, bf16[4,2,32,256]{3,2,1,0:T(8,128)(2,1)S(1)}, u32[]{:S(2)}, u32[]{:S(2)}) collective-permute-start(bf16[4,2,32,256]{3,2,1,0:T(8,128)(2,1)} %get-tuple-element.26), channel_id=1, source_target_pairs={{0,13},{1,14},{2,15},{3,12},{4,1},{5,2},{6,3},{7,0},{8,5},{9,6},{1... | collective-permute-start | bytes 393224 | tf_op jit(solution)/shard_map/ppermute | solution.py:94
  40.6 14.9 %copy-start.5 = (bf16[4,2,32,256]{3,2,1,0:T(8,128)(2,1)}, bf16[4,2,32,256]{3,2,1,0:T(8,128)(2,1)S(1)}, u32[]{:S(2)}) copy-start(bf16[4,2,32,256]{3,2,1,0:T(8,128)(2,1)S(1)} %collective-permute-done.5.rest_5_) | copy-start | bytes 393220
  40.6 14.0 %collective-permute-start.10 = (bf16[4,2,32,256]{3,2,1,0:T(8,128)(2,1)}, bf16[4,2,32,256]{3,2,1,0:T(8,128)(2,1)S(1)}, u32[]{:S(2)}, u32[]{:S(2)}) collective-permute-start(bf16[4,2,32,256]{3,2,1,0:T(8,128)(2,1)} %get-tuple-element.27), channel_id=1, source_target_pairs={{0,14},{1,15},{2,12},{3,13},{4,2},{5,3},{6,0},{7,1},{8,6},{9,7},{1... | collective-permute-start | bytes 393224 | tf_op jit(solution)/shard_map/ppermute | solution.py:94
  43.1 12.4 %copy-start.6 = (bf16[4,2,32,256]{3,2,1,0:T(8,128)(2,1)}, bf16[4,2,32,256]{3,2,1,0:T(8,128)(2,1)S(1)}, u32[]{:S(2)}) copy-start(bf16[4,2,32,256]{3,2,1,0:T(8,128)(2,1)S(1)} %collective-permute-done.6.rest_6_) | copy-start | bytes 393220
  43.1 12.4 %collective-permute-start.11 = (bf16[4,2,32,256]{3,2,1,0:T(8,128)(2,1)}, bf16[4,2,32,256]{3,2,1,0:T(8,128)(2,1)S(1)}, u32[]{:S(2)}, u32[]{:S(2)}) collective-permute-start(bf16[4,2,32,256]{3,2,1,0:T(8,128)(2,1)} %get-tuple-element.28), channel_id=1, source_target_pairs={{0,15},{1,12},{2,13},{3,14},{4,3},{5,0},{6,1},{7,2},{8,7},{9,4},{1... | collective-permute-start | bytes 393224 | tf_op jit(solution)/shard_map/ppermute | solution.py:94
  54.5 1.0 %copy-start.7 = (bf16[4,2,32,256]{3,2,1,0:T(8,128)(2,1)}, bf16[4,2,32,256]{3,2,1,0:T(8,128)(2,1)S(1)}, u32[]{:S(2)}) copy-start(bf16[4,2,32,256]{3,2,1,0:T(8,128)(2,1)S(1)} %collective-permute-done.7.rest_7_) | copy-start | bytes 393220
  54.5 1.0 %copy-start.8 = (bf16[4,2,32,256]{3,2,1,0:T(8,128)(2,1)}, bf16[4,2,32,256]{3,2,1,0:T(8,128)(2,1)S(1)}, u32[]{:S(2)}) copy-start(bf16[4,2,32,256]{3,2,1,0:T(8,128)(2,1)S(1)} %collective-permute-done.8.rest_8_) | copy-start | bytes 393220
  54.5 1.0 %copy-start.9 = (bf16[4,2,32,256]{3,2,1,0:T(8,128)(2,1)}, bf16[4,2,32,256]{3,2,1,0:T(8,128)(2,1)S(1)}, u32[]{:S(2)}) copy-start(bf16[4,2,32,256]{3,2,1,0:T(8,128)(2,1)S(1)} %collective-permute-done.9.rest_9_) | copy-start | bytes 393220
  54.6 1.0 %copy-start.10 = (bf16[4,2,32,256]{3,2,1,0:T(8,128)(2,1)}, bf16[4,2,32,256]{3,2,1,0:T(8,128)(2,1)S(1)}, u32[]{:S(2)}) copy-start(bf16[4,2,32,256]{3,2,1,0:T(8,128)(2,1)S(1)} %collective-permute-done.10.rest_10_) | copy-start | bytes 393220
  55.5 0.7 %copy-start.11 = (bf16[4,2,32,256]{3,2,1,0:T(8,128)(2,1)}, bf16[4,2,32,256]{3,2,1,0:T(8,128)(2,1)S(1)}, u32[]{:S(2)}) copy-start(bf16[4,2,32,256]{3,2,1,0:T(8,128)(2,1)S(1)} %collective-permute-done.11.rest_11_) | copy-start | bytes 393220

commit v9 on v8

--- a/solution.py
+++ b/solution.py
@@ -29,7 +29,8 @@
     replicas, page_count = off_ref.shape
     holder = lax.axis_index("replica")
     me = lax.axis_index("tensor")
-    lanes = out_refs[0].shape[-1]
+    (out_ref,) = out_refs
+    lanes = out_ref.shape[-1]
     starts = [
         pl.multiple_of(((me + shift) % tensor_count) * lanes, lanes) for shift in range(tensor_count)
     ]
@@ -46,27 +47,25 @@
             count = count + matched.astype(jnp.int32)
         for slot in range(slot_cap):
             for shift in range(tensor_count):
-                out_refs[(distance - 1) * tensor_count + shift][slot] = pool_ref[
-                    chosen[slot], :, :, pl.ds(starts[shift], lanes)
-                ]
+                target = reader * tensor_count + (me + shift) % tensor_count
+                out_ref[target, slot] = pool_ref[chosen[slot], :, :, pl.ds(starts[shift], lanes)]
 
 
 def pack_pages(pool_part, offsets, slots, span_count, slot_cap, tensor_count):
     pages, kv, rows, width = pool_part.shape
     lanes = width // tensor_count
-    piece = (slot_cap, kv, rows, lanes)
-    count = span_count * tensor_count
+    piece = (offsets.shape[0] * tensor_count, slot_cap, kv, rows, lanes)
     grid_spec = pltpu.PrefetchScalarGridSpec(
         num_scalar_prefetch=2,
         grid=(1,),
         in_specs=[pl.BlockSpec((pages, kv, rows, width), lambda i, o, s: (0, 0, 0, 0))],
-        out_specs=[pl.BlockSpec(piece, lambda i, o, s: (0, 0, 0, 0)) for _ in range(count)],
+        out_specs=pl.BlockSpec(piece, lambda i, o, s: (0, 0, 0, 0, 0)),
     )
     nbytes = 2 * (pool_part.size + span_count * slot_cap * kv * rows * width)
     return pl.pallas_call(
         functools.partial(gather_kernel, span_count, slot_cap, tensor_count),
         grid_spec=grid_spec,
-        out_shape=[jax.ShapeDtypeStruct(piece, pool_part.dtype) for _ in range(count)],
+        out_shape=jax.ShapeDtypeStruct(piece, pool_part.dtype),
         cost_estimate=pl.CostEstimate(flops=0, transcendentals=0, bytes_accessed=nbytes),
     )(offsets, slots, pool_part)
 
@@ -83,15 +82,7 @@
 
     payload = pack_pages(page_pool, offsets, slots, span_count, slot_cap, tensor_count)
 
-    arrivals = []
-    for distance in range(1, span_count + 1):
-        for shift in range(tensor_count):
-            pairs = []
-            for source in range(replicas):
-                for peer in range(tensor_count):
-                    target = ((source + distance) % replicas) * tensor_count + (peer + shift) % tensor_count
-                    pairs.append((source * tensor_count + peer, target))
-            arrivals.append(lax.ppermute(payload[(distance - 1) * tensor_count + shift], ("replica", "tensor"), pairs))
+    got = lax.all_to_all(payload, ("replica", "tensor"), split_axis=0, concat_axis=0, tiled=True)
 
     quarter = page_pool.shape[2]
     page_rows = quarter * tensor_count
@@ -106,17 +97,24 @@
     row_ids = jnp.arange(quarter, dtype=jnp.int32)
     position = (
         slot_page[:, None, :, None] * page_rows
-        + ((me - shifts + tensor_count) % tensor_count)[None, :, None, None] * quarter
+        + shifts[None, :, None, None] * quarter
         + row_ids[None, None, None, :]
     )
     visible = slot_used[:, None, :, None] & (position < own_length)
     visible = visible.astype(jnp.int32).reshape(span_count * tensor_count, 1, -1)
-    result = attend(queries[0], suffix_kv[0], visible, arrivals)
+    result = attend(queries[0], suffix_kv[0], visible, got, span_count, tensor_count)
     return result.reshape(1, suffix_rows, result.shape[1])
 
 
-def attention_kernel(chunk_count, q_ref, suf_ref, vis_ref, *rest):
-    chunk_refs, o_ref = rest[:chunk_count], rest[chunk_count]
+def attention_kernel(span_count, tensor_count, q_ref, suf_ref, vis_ref, got_ref, o_ref):
+    chunk_count = span_count * tensor_count
+    replicas = got_ref.shape[0] // tensor_count
+    reader = lax.axis_index("replica")
+    blocks = [
+        ((reader - distance + replicas) % replicas) * tensor_count + peer
+        for distance in range(1, span_count + 1)
+        for peer in range(tensor_count)
+    ]
     rows, width = q_ref.shape
     kv_local = suf_ref.shape[2] // HEAD_DIM
     group = width // (kv_local * HEAD_DIM)
@@ -135,8 +133,8 @@
         masks = [causal]
         pieces = [
             (
-                chunk_refs[c][:, 0, :, lanes].reshape(-1, HEAD_DIM),
-                chunk_refs[c][:, 1, :, lanes].reshape(-1, HEAD_DIM),
+                got_ref[blocks[c], :, 0, :, lanes].reshape(-1, HEAD_DIM),
+                got_ref[blocks[c], :, 1, :, lanes].reshape(-1, HEAD_DIM),
                 vis_ref[c],
             )
             for c in range(chunk_count)
@@ -175,18 +173,19 @@
             o_ref[:, pl.ds((head * group + g) * HEAD_DIM, HEAD_DIM)] = out[g * rows:(g + 1) * rows]
 
 
-def attend(q, suf, visible, chunks):
+def attend(q, suf, visible, got, span_count, tensor_count):
     rows, width = q.shape
-    keys_total = suf.shape[1] + sum(c.size // (2 * suf.shape[2]) for c in chunks)
+    chunk_keys = got.shape[1] * got.shape[3]
+    keys_total = suf.shape[1] + span_count * tensor_count * chunk_keys
     flops = 4 * rows * width * keys_total
-    nbytes = 2 * (q.size * 2 + suf.size + sum(c.size for c in chunks))
+    nbytes = 2 * (q.size * 2 + suf.size + got.size)
     return pl.pallas_call(
-        functools.partial(attention_kernel, len(chunks)),
+        functools.partial(attention_kernel, span_count, tensor_count),
         out_shape=jax.ShapeDtypeStruct((rows, width), jnp.bfloat16),
         cost_estimate=pl.CostEstimate(
             flops=flops, transcendentals=rows * (width // HEAD_DIM) * keys_total, bytes_accessed=nbytes
         ),
-    )(q, suf, visible, *chunks)
+    )(q, suf, visible, got)
 
 
 def solution(mesh):

time: 65.7 us -> 69 us (1.050)
  the two profiles are of different devices: /device:TPU:1 before, /device:TPU:11 now
where the time goes in v9:
time: 69 us; the launch traced here: 68.8 us
  waiting for transfers between devices  43.9 us (64%)
  Pallas kernels  13.3 us (19%)
  starting transfers between devices  6.69 us (10%)
  local copies, waits for them, and re-layouts  3.05 us (4%)
  other arithmetic  1.76 us (3%)
    all_to_all x1, waiting for transfers between devices, on_device(): lax.all_to_all(payload, ('replica', 'tensor'), split_axis=0, concat_axis=...  43.9 us
    pallas_call x1, Pallas kernels, attend(): pl.pallas_call(functools.partial(attention_kernel, span_count, tensor_cou...  9.6 us
    all_to_all x1, starting transfers between devices, on_device(): lax.all_to_all(payload, ('replica', 'tensor'), split_axis=0, concat_axis=...  6.69 us
    pallas_call x1, Pallas kernels, pack_pages(): pl.pallas_call(functools.partial(gather_kernel, span_count, slot_cap, ten...  3.7 us
  transfers between devices with their start and end apart: 1, of which 1 were waited for; matrix products, arithmetic and copies ran while one was open for 5% of the time, Pallas kernels for 0%

profile of v9, /device:TPU:11, one launch (start us, length us, event | category | flops | bytes accessed | tf_op | source)
XLA Modules:
  0.0 68.8 jit_solution(9551444141875642887)
XLA Ops:
  0.0 3.7 %shard_map.64 = bf16[16,4,2,32,256]{4,3,2,1,0:T(8,128)(2,1)} custom-call(s32[4,8]{1,0:T(4,128)} %off_ref.1, s32[4,8]{1,0:T(4,128)} %slot_ref.1, bf16[12,2,32,1024]{3,2,1,0:T(8,128)(2,1)} %pool_ref.1), custom_call_target="tpu_custom_call" | custom-call | bytes 3145728 | tf_op jit(solution)/shard_map/pallas_call | solution.py:65
  3.7 0.0 copy-start.1
  3.7 6.7 %all-to-all-start = ((bf16[16,4,2,32,256]{4,3,2,1,0:T(8,128)(2,1)}), bf16[16,4,2,32,256]{4,3,2,1,0:T(8,128)(2,1)S(1)}, u32[]{:S(2)}, u32[]{:S(2)}) async-start(bf16[16,4,2,32,256]{4,3,2,1,0:T(8,128)(2,1)} %shard_map.64), calls=%async_computation | async-start | bytes 4194304 | tf_op jit(solution)/shard_map/all_to_all | solution.py:85
  10.4 0.1 add.65
  10.5 0.0 copy-done.1
  10.5 0.6 dynamic_slice.9
  11.1 0.7 dynamic-slice_bitcast_fusion
  11.8 0.1 compare_convert_fusion
  11.8 0.1 multiply_reduce_fusion
  12.0 0.2 fusion
  12.2 0.1 and.18
  12.3 0.1 and.21
  12.4 0.1 broadcast_add_fusion
  12.4 0.1 add.62
  12.5 0.1 add.63
  12.6 1.3 %and_convert_fusion.vis_ref = s32[12,1,128]{2,1,0:T(1,128)} fusion(pred[12,1,128]{2,1,0:T(4,128)(4,1)S(1)} %and.21, s32[12,1,128]{2,1,0:T(1,128)S(1)} %add.63, s32[]{:T(128)} %bitcast.3, s32[128]{0:T(128)S(1)} %add.65), kind=kLoop, calls=%fused_computation | loop fusion | flops 6144 | bytes 14340 | tf_op jit(solution)/shard_map/convert_element_type | solution.py:104
  13.9 43.9 %all-to-all-done.got_ref = bf16[16,4,2,32,256]{4,3,2,1,0:T(8,128)(2,1)S(1)} async-done(((bf16[16,4,2,32,256]{4,3,2,1,0:T(8,128)(2,1)}), bf16[16,4,2,32,256]{4,3,2,1,0:T(8,128)(2,1)S(1)}, u32[]{:S(2)}, u32[]{:S(2)}) %all-to-all-start) | async-done | bytes 2097184 | tf_op jit(solution)/shard_map/all_to_all | solution.py:85
  57.8 0.0 copy-start
  57.8 1.3 %copy-done = bf16[16,4,2,32,256]{4,3,2,1,0:T(8,128)(2,1)} copy-done((bf16[16,4,2,32,256]{4,3,2,1,0:T(8,128)(2,1)}, bf16[16,4,2,32,256]{4,3,2,1,0:T(8,128)(2,1)S(1)}, u32[]{:S(2)}) %copy-start) | copy-done | bytes 2097176
  59.2 9.6 %shard_map.65 = bf16[128,2048]{1,0:T(8,128)(2,1)} custom-call(bf16[128,2048]{1,0:T(8,128)(2,1)} %bitcast.6, bf16[2,128,256]{2,1,0:T(8,128)(2,1)} %bitcast.7, s32[12,1,128]{2,1,0:T(1,128)} %and_convert_fusion.vis_ref, bf16[16,4,2,32,256]{4,3,2,1,0:T(8,128)(2,1)} %copy-done), custom_call_target="tpu_custom_call" | custom-call | flops 1744830464 | bytes 3276800 | tf_op jit(solution)/shard_map/pallas_call | solution.py:182
  (6 shorter events, 0.0 us)
Async XLA Ops:
  3.7 6.8 %copy-start.1 = (s32[4]{0:T(128)S(1)}, s32[4]{0:T(128)}, u32[]{:S(2)}) copy-start(s32[4]{0:T(128)} %param.11) | copy-start | bytes 52
  3.7 54.1 %all-to-all-start = ((bf16[16,4,2,32,256]{4,3,2,1,0:T(8,128)(2,1)}), bf16[16,4,2,32,256]{4,3,2,1,0:T(8,128)(2,1)S(1)}, u32[]{:S(2)}, u32[]{:S(2)}) async-start(bf16[16,4,2,32,256]{4,3,2,1,0:T(8,128)(2,1)} %shard_map.64), calls=%async_computation | async-start | bytes 4194304 | tf_op jit(solution)/shard_map/all_to_all | solution.py:85
  57.8 1.4 %copy-start = (bf16[16,4,2,32,256]{4,3,2,1,0:T(8,128)(2,1)}, bf16[16,4,2,32,256]{4,3,2,1,0:T(8,128)(2,1)S(1)}, u32[]{:S(2)}) copy-start(bf16[16,4,2,32,256]{4,3,2,1,0:T(8,128)(2,1)S(1)} %all-to-all-done.got_ref) | copy-start | bytes 6291460

commit v10 on v8

--- a/solution.py
+++ b/solution.py
@@ -149,7 +149,7 @@
             masks.append(jnp.concatenate([p[2] for p in part], axis=-1) > 0)
         scores = []
         for key, mask in zip(keys, masks):
-            s = lax.dot_general(q_all, key, dims, preferred_element_type=jnp.float32) * scale
+            s = lax.dot_general(q_all, key, dims, preferred_element_type=jnp.float32)
             scores.append(jnp.where(mask, s, NEG_FILL))
         widths = sorted(set(s.shape[-1] for s in scores))
         top = None
@@ -158,10 +158,11 @@
             part = functools.reduce(jnp.maximum, same)
             part = jnp.max(part, axis=-1, keepdims=True)
             top = part if top is None else jnp.maximum(top, part)
+        top = top * scale
         sums = {}
         acc = None
         for s, val, mask in zip(scores, vals, masks):
-            w = jnp.where(mask, jnp.exp(s - top), 0.0)
+            w = jnp.exp(s * scale - top)
             width_now = s.shape[-1]
             sums[width_now] = w if width_now not in sums else sums[width_now] + w
             pv = jnp.dot(w.astype(jnp.bfloat16), val, preferred_element_type=jnp.float32)

time: 65.7 us -> 65.2 us (level)
  no operation moved by 1% of the time
where the time goes in v10:
time: 65.2 us; the launch traced here: 65 us
  starting transfers between devices  34 us (52%)
  waiting for transfers between devices  14.2 us (22%)
  Pallas kernels  12.4 us (19%)
  local copies, waits for them, and re-layouts  2.39 us (4%)
  other arithmetic  1.78 us (3%)
    ppermute x12, starting transfers between devices, on_device(): lax.ppermute(payload[(distance - 1) * tensor_count + shift], ('replica',...  34 us
    ppermute x12, waiting for transfers between devices, on_device(): lax.ppermute(payload[(distance - 1) * tensor_count + shift], ('replica',...  14.2 us
    pallas_call x1, Pallas kernels, attend(): pl.pallas_call(functools.partial(attention_kernel, len(chunks)), out_shap...  8.79 us
    pallas_call x1, Pallas kernels, pack_pages(): pl.pallas_call(functools.partial(gather_kernel, span_count, slot_cap, ten...  3.63 us
  transfers between devices with their start and end apart: 12, of which 3 were waited for; matrix products, arithmetic and copies ran while one was open for 5% of the time, Pallas kernels for 0%

profile of v10, /device:TPU:1, one launch (start us, length us, event | category | flops | bytes accessed | tf_op | source)
XLA Modules:
  0.0 65.0 jit_solution(9848352830774462524)
XLA Ops:
  0.0 3.6 %shard_map.64 = (bf16[4,2,32,256]{3,2,1,0:T(8,128)(2,1)}, bf16[4,2,32,256]{3,2,1,0:T(8,128)(2,1)}, bf16[4,2,32,256]{3,2,1,0:T(8,128)(2,1)}, bf16[4,2,32,256]{3,2...) custom-call(s32[4,8]{1,0:T(4,128)} %off_ref.1, ...), custom_call_target="tpu_custom_call" | custom-call | bytes 3145728 | tf_op jit(solution)/shard_map/pallas_call | solution.py:66
  3.6 2.1 %collective-permute-start = (bf16[4,2,32,256]{3,2,1,0:T(8,128)(2,1)}, bf16[4,2,32,256]{3,2,1,0:T(8,128)(2,1)S(1)}, u32[]{:S(2)}, u32[]{:S(2)}) collective-permute-start(bf16[4,2,32,256]{3,2,1,0:T(8,128)(2,1)} %get-tuple-element.17), channel_id=1, source_target_pairs={{0,4},{1,5},{2,6},{3,7},{4,8},{5,9},{6,10},{7,11},{8,12},{9,13},{1... | collective-permute-start | bytes 393224 | tf_op jit(solution)/shard_map/ppermute | solution.py:94
  5.8 3.1 %collective-permute-start.1 = (bf16[4,2,32,256]{3,2,1,0:T(8,128)(2,1)}, bf16[4,2,32,256]{3,2,1,0:T(8,128)(2,1)S(1)}, u32[]{:S(2)}, u32[]{:S(2)}) collective-permute-start(bf16[4,2,32,256]{3,2,1,0:T(8,128)(2,1)} %get-tuple-element.18), channel_id=1, source_target_pairs={{0,5},{1,6},{2,7},{3,4},{4,9},{5,10},{6,11},{7,8},{8,13},{9,14},{1... | collective-permute-start | bytes 393224 | tf_op jit(solution)/shard_map/ppermute | solution.py:94
  8.8 1.3 %collective-permute-start.2 = (bf16[4,2,32,256]{3,2,1,0:T(8,128)(2,1)}, bf16[4,2,32,256]{3,2,1,0:T(8,128)(2,1)S(1)}, u32[]{:S(2)}, u32[]{:S(2)}) collective-permute-start(bf16[4,2,32,256]{3,2,1,0:T(8,128)(2,1)} %get-tuple-element.19), channel_id=1, source_target_pairs={{0,6},{1,7},{2,4},{3,5},{4,10},{5,11},{6,8},{7,9},{8,14},{9,15},{1... | collective-permute-start | bytes 393224 | tf_op jit(solution)/shard_map/ppermute | solution.py:94
  10.1 0.3 collective-permute-start.3
  10.4 1.7 %collective-permute-start.4 = (bf16[4,2,32,256]{3,2,1,0:T(8,128)(2,1)}, bf16[4,2,32,256]{3,2,1,0:T(8,128)(2,1)S(1)}, u32[]{:S(2)}, u32[]{:S(2)}) collective-permute-start(bf16[4,2,32,256]{3,2,1,0:T(8,128)(2,1)} %get-tuple-element.21), channel_id=1, source_target_pairs={{0,8},{1,9},{2,10},{3,11},{4,12},{5,13},{6,14},{7,15},{8,0},{9,1},... | collective-permute-start | bytes 393224 | tf_op jit(solution)/shard_map/ppermute | solution.py:94
  12.1 0.7 %dynamic-slice_bitcast_fusion = s32[8]{0:T(128)S(1)} fusion(s32[4,8]{1,0:T(4,128)} %off_ref.1, s32[]{:T(128)S(6)} %select_n.17), kind=kLoop, calls=%fused_computation.18 | loop fusion | bytes 68 | tf_op jit(solution)/shard_map/eq | solution.py:19
  12.8 0.1 compare_convert_fusion
  12.9 0.1 multiply_reduce_fusion
  13.0 0.2 fusion
  13.2 0.7 %dynamic_slice.9 = s32[1]{0:T(128)} dynamic-slice(s32[4]{0:T(128)S(1)} %copy-done.12, s32[]{:T(128)S(6)} %select_n.17), dynamic_slice_sizes={1} | dynamic-slice | bytes 12 | tf_op jit(solution)/shard_map/jit(dynamic_index_in_dim)/dynamic_slice | solution.py:100
  13.9 0.1 add.84
  14.0 0.1 and.31
  14.1 0.1 and.35
  14.2 1.9 %collective-permute-start.5 = (bf16[4,2,32,256]{3,2,1,0:T(8,128)(2,1)}, bf16[4,2,32,256]{3,2,1,0:T(8,128)(2,1)S(1)}, u32[]{:S(2)}, u32[]{:S(2)}) collective-permute-start(bf16[4,2,32,256]{3,2,1,0:T(8,128)(2,1)} %get-tuple-element.22), channel_id=1, source_target_pairs={{0,9},{1,10},{2,11},{3,8},{4,13},{5,14},{6,15},{7,12},{8,1},{9,2},... | collective-permute-start | bytes 393224 | tf_op jit(solution)/shard_map/ppermute | solution.py:94
  16.1 0.0 collective-permute-done.1.rest_1_
  16.1 3.1 %collective-permute-start.6 = (bf16[4,2,32,256]{3,2,1,0:T(8,128)(2,1)}, bf16[4,2,32,256]{3,2,1,0:T(8,128)(2,1)S(1)}, u32[]{:S(2)}, u32[]{:S(2)}) collective-permute-start(bf16[4,2,32,256]{3,2,1,0:T(8,128)(2,1)} %get-tuple-element.23), channel_id=1, source_target_pairs={{0,10},{1,11},{2,8},{3,9},{4,14},{5,15},{6,12},{7,13},{8,2},{9,3},... | collective-permute-start | bytes 393224 | tf_op jit(solution)/shard_map/ppermute | solution.py:94
  19.2 0.1 broadcast_add_fusion
  19.3 0.1 add.81
  19.4 0.1 add.82
  19.5 0.0 collective-permute-done.2.rest_2_
  19.5 0.5 collective-permute-start.7
  20.0 1.9 %collective-permute-done.3.rest_3_ = bf16[4,2,32,256]{3,2,1,0:T(8,128)(2,1)S(1)} collective-permute-done((bf16[4,2,32,256]{3,2,1,0:T(8,128)(2,1)}, bf16[4,2,32,256]{3,2,1,0:T(8,128)(2,1)S(1)}, u32[]{:S(2)}, u32[]{:S(2)}) %collective-permute-start.3) | collective-permute-done | bytes 131104 | tf_op jit(solution)/shard_map/ppermute | solution.py:94
  22.0 1.1 %collective-permute-start.8 = (bf16[4,2,32,256]{3,2,1,0:T(8,128)(2,1)}, bf16[4,2,32,256]{3,2,1,0:T(8,128)(2,1)S(1)}, u32[]{:S(2)}, u32[]{:S(2)}) collective-permute-start(bf16[4,2,32,256]{3,2,1,0:T(8,128)(2,1)} %get-tuple-element.25), channel_id=1, source_target_pairs={{0,12},{1,13},{2,14},{3,15},{4,0},{5,1},{6,2},{7,3},{8,4},{9,5},{1... | collective-permute-start | bytes 393224 | tf_op jit(solution)/shard_map/ppermute | solution.py:94
  23.1 11.3 %collective-permute-done.4.rest_4_ = bf16[4,2,32,256]{3,2,1,0:T(8,128)(2,1)S(1)} collective-permute-done((bf16[4,2,32,256]{3,2,1,0:T(8,128)(2,1)}, bf16[4,2,32,256]{3,2,1,0:T(8,128)(2,1)S(1)}, u32[]{:S(2)}, u32[]{:S(2)}) %collective-permute-start.4) | collective-permute-done | bytes 131104 | tf_op jit(solution)/shard_map/ppermute | solution.py:94
  34.4 6.2 %collective-permute-start.9 = (bf16[4,2,32,256]{3,2,1,0:T(8,128)(2,1)}, bf16[4,2,32,256]{3,2,1,0:T(8,128)(2,1)S(1)}, u32[]{:S(2)}, u32[]{:S(2)}) collective-permute-start(bf16[4,2,32,256]{3,2,1,0:T(8,128)(2,1)} %get-tuple-element.26), channel_id=1, source_target_pairs={{0,13},{1,14},{2,15},{3,12},{4,1},{5,2},{6,3},{7,0},{8,5},{9,6},{1... | collective-permute-start | bytes 393224 | tf_op jit(solution)/shard_map/ppermute | solution.py:94
  40.6 2.5 %collective-permute-start.10 = (bf16[4,2,32,256]{3,2,1,0:T(8,128)(2,1)}, bf16[4,2,32,256]{3,2,1,0:T(8,128)(2,1)S(1)}, u32[]{:S(2)}, u32[]{:S(2)}) collective-permute-start(bf16[4,2,32,256]{3,2,1,0:T(8,128)(2,1)} %get-tuple-element.27), channel_id=1, source_target_pairs={{0,14},{1,15},{2,12},{3,13},{4,2},{5,3},{6,0},{7,1},{8,6},{9,7},{1... | collective-permute-start | bytes 393224 | tf_op jit(solution)/shard_map/ppermute | solution.py:94
  43.1 10.1 %collective-permute-start.11 = (bf16[4,2,32,256]{3,2,1,0:T(8,128)(2,1)}, bf16[4,2,32,256]{3,2,1,0:T(8,128)(2,1)S(1)}, u32[]{:S(2)}, u32[]{:S(2)}) collective-permute-start(bf16[4,2,32,256]{3,2,1,0:T(8,128)(2,1)} %get-tuple-element.28), channel_id=1, source_target_pairs={{0,15},{1,12},{2,13},{3,14},{4,3},{5,0},{6,1},{7,2},{8,7},{9,4},{1... | collective-permute-start | bytes 393224 | tf_op jit(solution)/shard_map/ppermute | solution.py:94
  53.2 1.3 %and_convert_fusion.vis_ref = s32[12,1,128]{2,1,0:T(1,128)} fusion(pred[12,1,128]{2,1,0:T(4,128)(4,1)S(1)} %and.35, s32[12,1,128]{2,1,0:T(1,128)S(1)} %add.82, s32[]{:T(128)} %bitcast.3, s32[128]{0:T(128)S(1)} %add.84), kind=kLoop, calls=%fused_computation | loop fusion | flops 6144 | bytes 14340 | tf_op jit(solution)/shard_map/convert_element_type | solution.py:113
  54.6 0.9 %collective-permute-done.11.rest_11_ = bf16[4,2,32,256]{3,2,1,0:T(8,128)(2,1)S(1)} collective-permute-done((bf16[4,2,32,256]{3,2,1,0:T(8,128)(2,1)}, bf16[4,2,32,256]{3,2,1,0:T(8,128)(2,1)S(1)}, u32[]{:S(2)}, u32[]{:S(2)}) %collective-permute-start.11) | collective-permute-done | bytes 131104 | tf_op jit(solution)/shard_map/ppermute | solution.py:94
  55.6 0.6 copy-done.11
  56.2 8.8 %shard_map.65 = bf16[128,2048]{1,0:T(8,128)(2,1)} custom-call(bf16[128,2048]{1,0:T(8,128)(2,1)} %bitcast.6, bf16[2,128,256]{2,1,0:T(8,128)(2,1)} %bitcast.7, s32[12,1,128]{2,1,0:T(1,128)} %and_convert_fusion.vis_ref, bf16[4,2,32,256]{3,2,1,0:T(8,128)(2,1)} %copy-done, bf16[4,2,32,256]{3,2,1,0:T(8,128)(2,1)} %copy-done.1, bf16[4,2,32,256]{3,2,1,0:T(8,128)(2,1)} %copy-done.2, ...), custom_call_target="tpu_custom_call" | custom-call | flops 1744830464 | bytes 2752512 | tf_op jit(solution)/shard_map/pallas_call | solution.py:184
  (38 shorter events, 0.1 us)
Async XLA Ops:
  0.0 13.2 %copy-start.12 = (s32[4]{0:T(128)S(1)}, s32[4]{0:T(128)}, u32[]{:S(2)}) copy-start(s32[4]{0:T(128)} %param.11) | copy-start | bytes 52
  3.6 10.5 %collective-permute-start = (bf16[4,2,32,256]{3,2,1,0:T(8,128)(2,1)}, bf16[4,2,32,256]{3,2,1,0:T(8,128)(2,1)S(1)}, u32[]{:S(2)}, u32[]{:S(2)}) collective-permute-start(bf16[4,2,32,256]{3,2,1,0:T(8,128)(2,1)} %get-tuple-element.17), channel_id=1, source_target_pairs={{0,4},{1,5},{2,6},{3,7},{4,8},{5,9},{6,10},{7,11},{8,12},{9,13},{1... | collective-permute-start | bytes 393224 | tf_op jit(solution)/shard_map/ppermute | solution.py:94
  5.8 10.4 %collective-permute-start.1 = (bf16[4,2,32,256]{3,2,1,0:T(8,128)(2,1)}, bf16[4,2,32,256]{3,2,1,0:T(8,128)(2,1)S(1)}, u32[]{:S(2)}, u32[]{:S(2)}) collective-permute-start(bf16[4,2,32,256]{3,2,1,0:T(8,128)(2,1)} %get-tuple-element.18), channel_id=1, source_target_pairs={{0,5},{1,6},{2,7},{3,4},{4,9},{5,10},{6,11},{7,8},{8,13},{9,14},{1... | collective-permute-start | bytes 393224 | tf_op jit(solution)/shard_map/ppermute | solution.py:94
  8.8 10.7 %collective-permute-start.2 = (bf16[4,2,32,256]{3,2,1,0:T(8,128)(2,1)}, bf16[4,2,32,256]{3,2,1,0:T(8,128)(2,1)S(1)}, u32[]{:S(2)}, u32[]{:S(2)}) collective-permute-start(bf16[4,2,32,256]{3,2,1,0:T(8,128)(2,1)} %get-tuple-element.19), channel_id=1, source_target_pairs={{0,6},{1,7},{2,4},{3,5},{4,10},{5,11},{6,8},{7,9},{8,14},{9,15},{1... | collective-permute-start | bytes 393224 | tf_op jit(solution)/shard_map/ppermute | solution.py:94
  10.1 11.9 %collective-permute-start.3 = (bf16[4,2,32,256]{3,2,1,0:T(8,128)(2,1)}, bf16[4,2,32,256]{3,2,1,0:T(8,128)(2,1)S(1)}, u32[]{:S(2)}, u32[]{:S(2)}) collective-permute-start(bf16[4,2,32,256]{3,2,1,0:T(8,128)(2,1)} %get-tuple-element.20), channel_id=1, source_target_pairs={{0,7},{1,4},{2,5},{3,6},{4,11},{5,8},{6,9},{7,10},{8,15},{9,12},{1... | collective-permute-start | bytes 393224 | tf_op jit(solution)/shard_map/ppermute | solution.py:94
  10.4 24.0 %collective-permute-start.4 = (bf16[4,2,32,256]{3,2,1,0:T(8,128)(2,1)}, bf16[4,2,32,256]{3,2,1,0:T(8,128)(2,1)S(1)}, u32[]{:S(2)}, u32[]{:S(2)}) collective-permute-start(bf16[4,2,32,256]{3,2,1,0:T(8,128)(2,1)} %get-tuple-element.21), channel_id=1, source_target_pairs={{0,8},{1,9},{2,10},{3,11},{4,12},{5,13},{6,14},{7,15},{8,0},{9,1},... | collective-permute-start | bytes 393224 | tf_op jit(solution)/shard_map/ppermute | solution.py:94
  14.2 41.3 %copy-start = (bf16[4,2,32,256]{3,2,1,0:T(8,128)(2,1)}, bf16[4,2,32,256]{3,2,1,0:T(8,128)(2,1)S(1)}, u32[]{:S(2)}) copy-start(bf16[4,2,32,256]{3,2,1,0:T(8,128)(2,1)S(1)} %collective-permute-done.rest_0_) | copy-start | bytes 393220
  14.2 26.4 %collective-permute-start.5 = (bf16[4,2,32,256]{3,2,1,0:T(8,128)(2,1)}, bf16[4,2,32,256]{3,2,1,0:T(8,128)(2,1)S(1)}, u32[]{:S(2)}, u32[]{:S(2)}) collective-permute-start(bf16[4,2,32,256]{3,2,1,0:T(8,128)(2,1)} %get-tuple-element.22), channel_id=1, source_target_pairs={{0,9},{1,10},{2,11},{3,8},{4,13},{5,14},{6,15},{7,12},{8,1},{9,2},... | collective-permute-start | bytes 393224 | tf_op jit(solution)/shard_map/ppermute | solution.py:94
  16.1 39.4 %copy-start.1 = (bf16[4,2,32,256]{3,2,1,0:T(8,128)(2,1)}, bf16[4,2,32,256]{3,2,1,0:T(8,128)(2,1)S(1)}, u32[]{:S(2)}) copy-start(bf16[4,2,32,256]{3,2,1,0:T(8,128)(2,1)S(1)} %collective-permute-done.1.rest_1_) | copy-start | bytes 393220
  16.1 27.0 %collective-permute-start.6 = (bf16[4,2,32,256]{3,2,1,0:T(8,128)(2,1)}, bf16[4,2,32,256]{3,2,1,0:T(8,128)(2,1)S(1)}, u32[]{:S(2)}, u32[]{:S(2)}) collective-permute-start(bf16[4,2,32,256]{3,2,1,0:T(8,128)(2,1)} %get-tuple-element.23), channel_id=1, source_target_pairs={{0,10},{1,11},{2,8},{3,9},{4,14},{5,15},{6,12},{7,13},{8,2},{9,3},... | collective-permute-start | bytes 393224 | tf_op jit(solution)/shard_map/ppermute | solution.py:94
  19.5 36.0 %copy-start.2 = (bf16[4,2,32,256]{3,2,1,0:T(8,128)(2,1)}, bf16[4,2,32,256]{3,2,1,0:T(8,128)(2,1)S(1)}, u32[]{:S(2)}) copy-start(bf16[4,2,32,256]{3,2,1,0:T(8,128)(2,1)S(1)} %collective-permute-done.2.rest_2_) | copy-start | bytes 393220
  19.5 35.0 %collective-permute-start.7 = (bf16[4,2,32,256]{3,2,1,0:T(8,128)(2,1)}, bf16[4,2,32,256]{3,2,1,0:T(8,128)(2,1)S(1)}, u32[]{:S(2)}, u32[]{:S(2)}) collective-permute-start(bf16[4,2,32,256]{3,2,1,0:T(8,128)(2,1)} %get-tuple-element.24), channel_id=1, source_target_pairs={{0,11},{1,8},{2,9},{3,10},{4,15},{5,12},{6,13},{7,14},{8,3},{9,0},... | collective-permute-start | bytes 393224 | tf_op jit(solution)/shard_map/ppermute | solution.py:94
  22.0 33.5 %copy-start.3 = (bf16[4,2,32,256]{3,2,1,0:T(8,128)(2,1)}, bf16[4,2,32,256]{3,2,1,0:T(8,128)(2,1)S(1)}, u32[]{:S(2)}) copy-start(bf16[4,2,32,256]{3,2,1,0:T(8,128)(2,1)S(1)} %collective-permute-done.3.rest_3_) | copy-start | bytes 393220
  22.0 32.5 %collective-permute-start.8 = (bf16[4,2,32,256]{3,2,1,0:T(8,128)(2,1)}, bf16[4,2,32,256]{3,2,1,0:T(8,128)(2,1)S(1)}, u32[]{:S(2)}, u32[]{:S(2)}) collective-permute-start(bf16[4,2,32,256]{3,2,1,0:T(8,128)(2,1)} %get-tuple-element.25), channel_id=1, source_target_pairs={{0,12},{1,13},{2,14},{3,15},{4,0},{5,1},{6,2},{7,3},{8,4},{9,5},{1... | collective-permute-start | bytes 393224 | tf_op jit(solution)/shard_map/ppermute | solution.py:94
  34.4 21.1 %copy-start.4 = (bf16[4,2,32,256]{3,2,1,0:T(8,128)(2,1)}, bf16[4,2,32,256]{3,2,1,0:T(8,128)(2,1)S(1)}, u32[]{:S(2)}) copy-start(bf16[4,2,32,256]{3,2,1,0:T(8,128)(2,1)S(1)} %collective-permute-done.4.rest_4_) | copy-start | bytes 393220
  34.4 20.1 %collective-permute-start.9 = (bf16[4,2,32,256]{3,2,1,0:T(8,128)(2,1)}, bf16[4,2,32,256]{3,2,1,0:T(8,128)(2,1)S(1)}, u32[]{:S(2)}, u32[]{:S(2)}) collective-permute-start(bf16[4,2,32,256]{3,2,1,0:T(8,128)(2,1)} %get-tuple-element.26), channel_id=1, source_target_pairs={{0,13},{1,14},{2,15},{3,12},{4,1},{5,2},{6,3},{7,0},{8,5},{9,6},{1... | collective-permute-start | bytes 393224 | tf_op jit(solution)/shard_map/ppermute | solution.py:94
  40.6 14.9 %copy-start.5 = (bf16[4,2,32,256]{3,2,1,0:T(8,128)(2,1)}, bf16[4,2,32,256]{3,2,1,0:T(8,128)(2,1)S(1)}, u32[]{:S(2)}) copy-start(bf16[4,2,32,256]{3,2,1,0:T(8,128)(2,1)S(1)} %collective-permute-done.5.rest_5_) | copy-start | bytes 393220
  40.6 14.0 %collective-permute-start.10 = (bf16[4,2,32,256]{3,2,1,0:T(8,128)(2,1)}, bf16[4,2,32,256]{3,2,1,0:T(8,128)(2,1)S(1)}, u32[]{:S(2)}, u32[]{:S(2)}) collective-permute-start(bf16[4,2,32,256]{3,2,1,0:T(8,128)(2,1)} %get-tuple-element.27), channel_id=1, source_target_pairs={{0,14},{1,15},{2,12},{3,13},{4,2},{5,3},{6,0},{7,1},{8,6},{9,7},{1... | collective-permute-start | bytes 393224 | tf_op jit(solution)/shard_map/ppermute | solution.py:94
  43.1 12.4 %copy-start.6 = (bf16[4,2,32,256]{3,2,1,0:T(8,128)(2,1)}, bf16[4,2,32,256]{3,2,1,0:T(8,128)(2,1)S(1)}, u32[]{:S(2)}) copy-start(bf16[4,2,32,256]{3,2,1,0:T(8,128)(2,1)S(1)} %collective-permute-done.6.rest_6_) | copy-start | bytes 393220
  43.1 12.4 %collective-permute-start.11 = (bf16[4,2,32,256]{3,2,1,0:T(8,128)(2,1)}, bf16[4,2,32,256]{3,2,1,0:T(8,128)(2,1)S(1)}, u32[]{:S(2)}, u32[]{:S(2)}) collective-permute-start(bf16[4,2,32,256]{3,2,1,0:T(8,128)(2,1)} %get-tuple-element.28), channel_id=1, source_target_pairs={{0,15},{1,12},{2,13},{3,14},{4,3},{5,0},{6,1},{7,2},{8,7},{9,4},{1... | collective-permute-start | bytes 393224 | tf_op jit(solution)/shard_map/ppermute | solution.py:94
  54.5 1.0 %copy-start.7 = (bf16[4,2,32,256]{3,2,1,0:T(8,128)(2,1)}, bf16[4,2,32,256]{3,2,1,0:T(8,128)(2,1)S(1)}, u32[]{:S(2)}) copy-start(bf16[4,2,32,256]{3,2,1,0:T(8,128)(2,1)S(1)} %collective-permute-done.7.rest_7_) | copy-start | bytes 393220
  54.5 1.0 %copy-start.8 = (bf16[4,2,32,256]{3,2,1,0:T(8,128)(2,1)}, bf16[4,2,32,256]{3,2,1,0:T(8,128)(2,1)S(1)}, u32[]{:S(2)}) copy-start(bf16[4,2,32,256]{3,2,1,0:T(8,128)(2,1)S(1)} %collective-permute-done.8.rest_8_) | copy-start | bytes 393220
  54.5 1.0 %copy-start.9 = (bf16[4,2,32,256]{3,2,1,0:T(8,128)(2,1)}, bf16[4,2,32,256]{3,2,1,0:T(8,128)(2,1)S(1)}, u32[]{:S(2)}) copy-start(bf16[4,2,32,256]{3,2,1,0:T(8,128)(2,1)S(1)} %collective-permute-done.9.rest_9_) | copy-start | bytes 393220
  54.6 1.0 %copy-start.10 = (bf16[4,2,32,256]{3,2,1,0:T(8,128)(2,1)}, bf16[4,2,32,256]{3,2,1,0:T(8,128)(2,1)S(1)}, u32[]{:S(2)}) copy-start(bf16[4,2,32,256]{3,2,1,0:T(8,128)(2,1)S(1)} %collective-permute-done.10.rest_10_) | copy-start | bytes 393220
  55.5 0.7 %copy-start.11 = (bf16[4,2,32,256]{3,2,1,0:T(8,128)(2,1)}, bf16[4,2,32,256]{3,2,1,0:T(8,128)(2,1)S(1)}, u32[]{:S(2)}) copy-start(bf16[4,2,32,256]{3,2,1,0:T(8,128)(2,1)S(1)} %collective-permute-done.11.rest_11_) | copy-start | bytes 393220

commit v11 on v10

--- a/solution.py
+++ b/solution.py
@@ -98,28 +98,29 @@
     suffix_rows = queries.shape[1]
     own_offsets = lax.dynamic_index_in_dim(offsets, reader, 0, keepdims=False)
     own_length = lax.dynamic_index_in_dim(prefix_len, reader, 0, keepdims=False)
-    own_picked = slot_choice(own_offsets[None, :], distances, slot_cap)
     page_ids = jnp.arange(page_count, dtype=jnp.int32)
-    slot_page = jnp.sum(own_picked * page_ids[None, None, :], axis=2)
-    slot_used = jnp.sum(own_picked, axis=2) > 0
+    earlier = (page_ids[None, :] < page_ids[:, None]).astype(jnp.int32)
+    same = (own_offsets[:, None] == own_offsets[None, :]).astype(jnp.int32)
+    rank = jnp.sum(same * earlier, axis=1)
+    table = jnp.concatenate([own_offsets, rank]).astype(jnp.int32)
     shifts = jnp.arange(tensor_count, dtype=jnp.int32)
     row_ids = jnp.arange(quarter, dtype=jnp.int32)
     position = (
-        slot_page[:, None, :, None] * page_rows
-        + ((me - shifts + tensor_count) % tensor_count)[None, :, None, None] * quarter
-        + row_ids[None, None, None, :]
-    )
-    visible = slot_used[:, None, :, None] & (position < own_length)
-    visible = visible.astype(jnp.int32).reshape(span_count * tensor_count, 1, -1)
-    result = attend(queries[0], suffix_kv[0], visible, arrivals)
+        page_ids[:, None, None] * page_rows
+        + ((me - shifts + tensor_count) % tensor_count)[None, :, None] * quarter
+        + row_ids[None, None, :]
+    )
+    visible = (position < own_length).astype(jnp.int32).reshape(page_count, 1, -1)
+    result = attend(queries[0], suffix_kv[0], table, visible, arrivals, span_count, tensor_count)
     return result.reshape(1, suffix_rows, result.shape[1])
 
 
-def attention_kernel(chunk_count, q_ref, suf_ref, vis_ref, *rest):
-    chunk_refs, o_ref = rest[:chunk_count], rest[chunk_count]
+def attention_kernel(span_count, tensor_count, tab_ref, q_ref, suf_ref, vis_ref, *rest):
+    chunk_refs, o_ref = rest[:-1], rest[-1]
+    page_count = vis_ref.shape[0]
     rows, width = q_ref.shape
-    kv_local = suf_ref.shape[2] // HEAD_DIM
-    group = width // (kv_local * HEAD_DIM)
+    group = HEADS // KV_HEADS
+    kv_local = width // (group * HEAD_DIM)
     scale = HEAD_DIM ** (-0.5)
     dims = (((1,), (1,)), ((), ()))
     row_pos = lax.broadcasted_iota(jnp.int32, (group * rows, rows), 0) % rows
@@ -130,23 +131,28 @@
         q_all = jnp.concatenate(
             [q_ref[:, pl.ds((head * group + g) * HEAD_DIM, HEAD_DIM)] for g in range(group)], axis=0
         )
+
+        def page_part(page, part):
+            distance, slot = tab_ref[page], tab_ref[page_count + page]
+            pieces = []
+            for shift in range(tensor_count):
+                piece = chunk_refs[shift][slot, part, :, lanes]
+                for d in range(2, span_count + 1):
+                    other = chunk_refs[(d - 1) * tensor_count + shift][slot, part, :, lanes]
+                    piece = jnp.where(distance == d, other, piece)
+                pieces.append(piece)
+            return jnp.concatenate(pieces, axis=0)
+
         keys = [suf_ref[0, :, lanes]]
         vals = [suf_ref[1, :, lanes]]
         masks = [causal]
-        pieces = [
-            (
-                chunk_refs[c][:, 0, :, lanes].reshape(-1, HEAD_DIM),
-                chunk_refs[c][:, 1, :, lanes].reshape(-1, HEAD_DIM),
-                vis_ref[c],
+        join = 2 if page_count % 2 == 0 else 1
+        for page in range(0, page_count, join):
+            keys.append(jnp.concatenate([page_part(p, 0) for p in range(page, page + join)], axis=0))
+            vals.append(jnp.concatenate([page_part(p, 1) for p in range(page, page + join)], axis=0))
+            masks.append(
+                jnp.concatenate([vis_ref[p] for p in range(page, page + join)], axis=-1) > 0
             )
-            for c in range(chunk_count)
-        ]
-        join = 2 if chunk_count % 2 == 0 else 1
-        for c in range(0, chunk_count, join):
-            part = pieces[c:c + join]
-            keys.append(jnp.concatenate([p[0] for p in part], axis=0))
-            vals.append(jnp.concatenate([p[1] for p in part], axis=0))
-            masks.append(jnp.concatenate([p[2] for p in part], axis=-1) > 0)
         scores = []
         for key, mask in zip(keys, masks):
             s = lax.dot_general(q_all, key, dims, preferred_element_type=jnp.float32)
@@ -161,7 +167,7 @@
         top = top * scale
         sums = {}
         acc = None
-        for s, val, mask in zip(scores, vals, masks):
+        for s, val in zip(scores, vals):
             w = jnp.exp(s * scale - top)
             width_now = s.shape[-1]
             sums[width_now] = w if width_now not in sums else sums[width_now] + w
@@ -176,18 +182,29 @@
             o_ref[:, pl.ds((head * group + g) * HEAD_DIM, HEAD_DIM)] = out[g * rows:(g + 1) * rows]
 
 
-def attend(q, suf, visible, chunks):
+def attend(q, suf, table, visible, chunks, span_count, tensor_count):
     rows, width = q.shape
-    keys_total = suf.shape[1] + sum(c.size // (2 * suf.shape[2]) for c in chunks)
+    keys_total = suf.shape[1] + visible.shape[0] * visible.shape[2]
     flops = 4 * rows * width * keys_total
     nbytes = 2 * (q.size * 2 + suf.size + sum(c.size for c in chunks))
+
+    def whole(a):
+        return pl.BlockSpec(a.shape, lambda i, t: (0,) * a.ndim)
+
+    grid_spec = pltpu.PrefetchScalarGridSpec(
+        num_scalar_prefetch=1,
+        grid=(1,),
+        in_specs=[whole(q), whole(suf), whole(visible)] + [whole(c) for c in chunks],
+        out_specs=pl.BlockSpec((rows, width), lambda i, t: (0, 0)),
+    )
     return pl.pallas_call(
-        functools.partial(attention_kernel, len(chunks)),
+        functools.partial(attention_kernel, span_count, tensor_count),
+        grid_spec=grid_spec,
         out_shape=jax.ShapeDtypeStruct((rows, width), jnp.bfloat16),
         cost_estimate=pl.CostEstimate(
             flops=flops, transcendentals=rows * (width // HEAD_DIM) * keys_total, bytes_accessed=nbytes
         ),
-    )(q, suf, visible, *chunks)
+    )(table, q, suf, visible, *chunks)
 
 
 def solution(mesh):

time: 65.2 us -> 64.2 us (0.985)
  Pallas kernels: 12.4 us -> 11.5 us
    pallas_call x1, Pallas kernels: 8.79 us -> 7.83 us  [attend(): pl.pallas_call(functools.partial(attention_kernel, span_count, tensor_cou...]
    squeeze x0 -> x1, local copies, waits for them, and re-layouts: none -> 0.69 us  [on_device(): own_offsets = lax.dynamic_index_in_dim(offsets, reader, 0, keepdims=False)]
    eq x1 -> x0, local copies, waits for them, and re-layouts: 0.69 us -> none  [slot_choice(): matched = (offsets_rows == distances[:, None]).astype(jnp.int32)]
    concatenate x0 -> x1, other arithmetic: none -> 0.65 us  [on_device(): table = jnp.concatenate([own_offsets, rank]).astype(jnp.int32)]
    convert_element_type x3 -> x1, other arithmetic: 1.35 us -> 1.22 us  [on_device(): (position < own_length).astype(jnp.int32).reshape(page_count, 1, -1)]
  transfers between devices with their start and end apart: 12 -> 12, of which waited for: 3 -> 3; matrix products, arithmetic and copies ran while one was open for 5% -> 6% of each run, Pallas kernels for 0% -> 0%
where the time goes in v11:
time: 64.2 us; the launch traced here: 64 us
  starting transfers between devices  34.4 us (54%)
  waiting for transfers between devices  13.7 us (21%)
  Pallas kernels  11.5 us (18%)
  local copies, waits for them, and re-layouts  2.2 us (3%)
  other arithmetic  2.14 us (3%)
    ppermute x12, starting transfers between devices, on_device(): lax.ppermute(payload[(distance - 1) * tensor_count + shift], ('replica',...  34.4 us
    ppermute x12, waiting for transfers between devices, on_device(): lax.ppermute(payload[(distance - 1) * tensor_count + shift], ('replica',...  13.7 us
    pallas_call x1, Pallas kernels, attend(): pl.pallas_call(functools.partial(attention_kernel, span_count, tensor_cou...  7.83 us
    pallas_call x1, Pallas kernels, pack_pages(): pl.pallas_call(functools.partial(gather_kernel, span_count, slot_cap, ten...  3.63 us
  transfers between devices with their start and end apart: 12, of which 3 were waited for; matrix products, arithmetic and copies ran while one was open for 6% of the time, Pallas kernels for 0%

profile of v11, /device:TPU:1, one launch (start us, length us, event | category | flops | bytes accessed | tf_op | source)
XLA Modules:
  0.0 64.0 jit_solution(2897087213404842472)
XLA Ops:
  0.0 3.6 %shard_map.64 = (bf16[4,2,32,256]{3,2,1,0:T(8,128)(2,1)}, bf16[4,2,32,256]{3,2,1,0:T(8,128)(2,1)}, bf16[4,2,32,256]{3,2,1,0:T(8,128)(2,1)}, bf16[4,2,32,256]{3,2...) custom-call(s32[4,8]{1,0:T(4,128)} %off_ref.1, ...), custom_call_target="tpu_custom_call" | custom-call | bytes 3145728 | tf_op jit(solution)/shard_map/pallas_call | solution.py:66
  3.6 2.1 %collective-permute-start = (bf16[4,2,32,256]{3,2,1,0:T(8,128)(2,1)}, bf16[4,2,32,256]{3,2,1,0:T(8,128)(2,1)S(1)}, u32[]{:S(2)}, u32[]{:S(2)}) collective-permute-start(bf16[4,2,32,256]{3,2,1,0:T(8,128)(2,1)} %get-tuple-element.17), channel_id=1, source_target_pairs={{0,4},{1,5},{2,6},{3,7},{4,8},{5,9},{6,10},{7,11},{8,12},{9,13},{1... | collective-permute-start | bytes 393224 | tf_op jit(solution)/shard_map/ppermute | solution.py:94
  5.8 3.1 %collective-permute-start.1 = (bf16[4,2,32,256]{3,2,1,0:T(8,128)(2,1)}, bf16[4,2,32,256]{3,2,1,0:T(8,128)(2,1)S(1)}, u32[]{:S(2)}, u32[]{:S(2)}) collective-permute-start(bf16[4,2,32,256]{3,2,1,0:T(8,128)(2,1)} %get-tuple-element.18), channel_id=1, source_target_pairs={{0,5},{1,6},{2,7},{3,4},{4,9},{5,10},{6,11},{7,8},{8,13},{9,14},{1... | collective-permute-start | bytes 393224 | tf_op jit(solution)/shard_map/ppermute | solution.py:94
  8.8 1.3 %collective-permute-start.2 = (bf16[4,2,32,256]{3,2,1,0:T(8,128)(2,1)}, bf16[4,2,32,256]{3,2,1,0:T(8,128)(2,1)S(1)}, u32[]{:S(2)}, u32[]{:S(2)}) collective-permute-start(bf16[4,2,32,256]{3,2,1,0:T(8,128)(2,1)} %get-tuple-element.19), channel_id=1, source_target_pairs={{0,6},{1,7},{2,4},{3,5},{4,10},{5,11},{6,8},{7,9},{8,14},{9,15},{1... | collective-permute-start | bytes 393224 | tf_op jit(solution)/shard_map/ppermute | solution.py:94
  10.1 0.3 collective-permute-start.3
  10.4 1.7 %collective-permute-start.4 = (bf16[4,2,32,256]{3,2,1,0:T(8,128)(2,1)}, bf16[4,2,32,256]{3,2,1,0:T(8,128)(2,1)S(1)}, u32[]{:S(2)}, u32[]{:S(2)}) collective-permute-start(bf16[4,2,32,256]{3,2,1,0:T(8,128)(2,1)} %get-tuple-element.21), channel_id=1, source_target_pairs={{0,8},{1,9},{2,10},{3,11},{4,12},{5,13},{6,14},{7,15},{8,0},{9,1},... | collective-permute-start | bytes 393224 | tf_op jit(solution)/shard_map/ppermute | solution.py:94
  12.1 0.1 add.76
  12.2 0.1 broadcast_add_fusion
  12.3 0.1 add.73
  12.3 0.1 add.74
  12.4 0.7 %dynamic_slice.9 = s32[1]{0:T(128)} dynamic-slice(s32[4]{0:T(128)S(1)} %copy-done.12, s32[]{:T(128)S(6)} %select_n.17), dynamic_slice_sizes={1} | dynamic-slice | bytes 12 | tf_op jit(solution)/shard_map/jit(dynamic_index_in_dim)/dynamic_slice | solution.py:100
  13.1 0.0 collective-permute-done.rest_0_
  13.1 1.9 %collective-permute-start.5 = (bf16[4,2,32,256]{3,2,1,0:T(8,128)(2,1)}, bf16[4,2,32,256]{3,2,1,0:T(8,128)(2,1)S(1)}, u32[]{:S(2)}, u32[]{:S(2)}) collective-permute-start(bf16[4,2,32,256]{3,2,1,0:T(8,128)(2,1)} %get-tuple-element.22), channel_id=1, source_target_pairs={{0,9},{1,10},{2,11},{3,8},{4,13},{5,14},{6,15},{7,12},{8,1},{9,2},... | collective-permute-start | bytes 393224 | tf_op jit(solution)/shard_map/ppermute | solution.py:94
  15.0 0.0 collective-permute-done.1.rest_1_
  15.0 3.1 %collective-permute-start.6 = (bf16[4,2,32,256]{3,2,1,0:T(8,128)(2,1)}, bf16[4,2,32,256]{3,2,1,0:T(8,128)(2,1)S(1)}, u32[]{:S(2)}, u32[]{:S(2)}) collective-permute-start(bf16[4,2,32,256]{3,2,1,0:T(8,128)(2,1)} %get-tuple-element.23), channel_id=1, source_target_pairs={{0,10},{1,11},{2,8},{3,9},{4,14},{5,15},{6,12},{7,13},{8,2},{9,3},... | collective-permute-start | bytes 393224 | tf_op jit(solution)/shard_map/ppermute | solution.py:94
  18.1 1.2 %compare_convert_fusion.vis_ref = s32[8,1,128]{2,1,0:T(1,128)} fusion(s32[8,1,128]{2,1,0:T(1,128)S(1)} %add.74, s32[]{:T(128)} %bitcast.3, s32[128]{0:T(128)S(1)} %add.76), kind=kLoop, calls=%fused_computation | loop fusion | flops 3072 | bytes 8708 | tf_op jit(solution)/shard_map/convert_element_type | solution.py:113
  19.3 0.7 %dynamic-slice_bitcast_fusion = s32[8]{0:T(128)S(1)} fusion(s32[4,8]{1,0:T(4,128)} %off_ref.1, s32[]{:T(128)S(6)} %select_n.17), kind=kLoop, calls=%fused_computation.11 | loop fusion | bytes 68 | tf_op jit(solution)/shard_map/jit(dynamic_index_in_dim)/squeeze | solution.py:99
  20.0 1.0 %collective-permute-start.7 = (bf16[4,2,32,256]{3,2,1,0:T(8,128)(2,1)}, bf16[4,2,32,256]{3,2,1,0:T(8,128)(2,1)S(1)}, u32[]{:S(2)}, u32[]{:S(2)}) collective-permute-start(bf16[4,2,32,256]{3,2,1,0:T(8,128)(2,1)} %get-tuple-element.24), channel_id=1, source_target_pairs={{0,11},{1,8},{2,9},{3,10},{4,15},{5,12},{6,13},{7,14},{8,3},{9,0},... | collective-permute-start | bytes 393224 | tf_op jit(solution)/shard_map/ppermute | solution.py:94
  21.0 1.0 %collective-permute-done.3.rest_3_ = bf16[4,2,32,256]{3,2,1,0:T(8,128)(2,1)S(1)} collective-permute-done((bf16[4,2,32,256]{3,2,1,0:T(8,128)(2,1)}, bf16[4,2,32,256]{3,2,1,0:T(8,128)(2,1)S(1)}, u32[]{:S(2)}, u32[]{:S(2)}) %collective-permute-start.3) | collective-permute-done | bytes 131104 | tf_op jit(solution)/shard_map/ppermute | solution.py:94
  22.0 1.1 %collective-permute-start.8 = (bf16[4,2,32,256]{3,2,1,0:T(8,128)(2,1)}, bf16[4,2,32,256]{3,2,1,0:T(8,128)(2,1)S(1)}, u32[]{:S(2)}, u32[]{:S(2)}) collective-permute-start(bf16[4,2,32,256]{3,2,1,0:T(8,128)(2,1)} %get-tuple-element.25), channel_id=1, source_target_pairs={{0,12},{1,13},{2,14},{3,15},{4,0},{5,1},{6,2},{7,3},{8,4},{9,5},{1... | collective-permute-start | bytes 393224 | tf_op jit(solution)/shard_map/ppermute | solution.py:94
  23.1 11.3 %collective-permute-done.4.rest_4_ = bf16[4,2,32,256]{3,2,1,0:T(8,128)(2,1)S(1)} collective-permute-done((bf16[4,2,32,256]{3,2,1,0:T(8,128)(2,1)}, bf16[4,2,32,256]{3,2,1,0:T(8,128)(2,1)S(1)}, u32[]{:S(2)}, u32[]{:S(2)}) %collective-permute-start.4) | collective-permute-done | bytes 131104 | tf_op jit(solution)/shard_map/ppermute | solution.py:94
  34.4 6.2 %collective-permute-start.9 = (bf16[4,2,32,256]{3,2,1,0:T(8,128)(2,1)}, bf16[4,2,32,256]{3,2,1,0:T(8,128)(2,1)S(1)}, u32[]{:S(2)}, u32[]{:S(2)}) collective-permute-start(bf16[4,2,32,256]{3,2,1,0:T(8,128)(2,1)} %get-tuple-element.26), channel_id=1, source_target_pairs={{0,13},{1,14},{2,15},{3,12},{4,1},{5,2},{6,3},{7,0},{8,5},{9,6},{1... | collective-permute-start | bytes 393224 | tf_op jit(solution)/shard_map/ppermute | solution.py:94
  40.6 2.5 %collective-permute-start.10 = (bf16[4,2,32,256]{3,2,1,0:T(8,128)(2,1)}, bf16[4,2,32,256]{3,2,1,0:T(8,128)(2,1)S(1)}, u32[]{:S(2)}, u32[]{:S(2)}) collective-permute-start(bf16[4,2,32,256]{3,2,1,0:T(8,128)(2,1)} %get-tuple-element.27), channel_id=1, source_target_pairs={{0,14},{1,15},{2,12},{3,13},{4,2},{5,3},{6,0},{7,1},{8,6},{9,7},{1... | collective-permute-start | bytes 393224 | tf_op jit(solution)/shard_map/ppermute | solution.py:94
  43.1 0.0 collective-permute-done.6.rest_6_
  43.1 10.1 %collective-permute-start.11 = (bf16[4,2,32,256]{3,2,1,0:T(8,128)(2,1)}, bf16[4,2,32,256]{3,2,1,0:T(8,128)(2,1)S(1)}, u32[]{:S(2)}, u32[]{:S(2)}) collective-permute-start(bf16[4,2,32,256]{3,2,1,0:T(8,128)(2,1)} %get-tuple-element.28), channel_id=1, source_target_pairs={{0,15},{1,12},{2,13},{3,14},{4,3},{5,0},{6,1},{7,2},{8,7},{9,4},{1... | collective-permute-start | bytes 393224 | tf_op jit(solution)/shard_map/ppermute | solution.py:94
  53.2 0.2 select_reduce_fusion
  53.4 0.7 %pad_add_fusion.tab_ref = s32[16]{0:T(128)} fusion(s32[8]{0:T(128)S(1)} %select_reduce_fusion, s32[8]{0:T(128)S(1)} %dynamic-slice_bitcast_fusion), kind=kLoop, calls=%fused_computation.9 | loop fusion | flops 16 | bytes 128 | tf_op jit(solution)/shard_map/concatenate | solution.py:105
  54.1 0.0 collective-permute-done.9.rest_9_
  54.1 0.0 collective-permute-done.10.rest_10_
  54.1 1.4 %collective-permute-done.11.rest_11_ = bf16[4,2,32,256]{3,2,1,0:T(8,128)(2,1)S(1)} collective-permute-done((bf16[4,2,32,256]{3,2,1,0:T(8,128)(2,1)}, bf16[4,2,32,256]{3,2,1,0:T(8,128)(2,1)S(1)}, u32[]{:S(2)}, u32[]{:S(2)}) %collective-permute-start.11) | collective-permute-done | bytes 131104 | tf_op jit(solution)/shard_map/ppermute | solution.py:94
  55.6 0.6 copy-done.11
  56.1 7.8 %shard_map.65 = bf16[128,2048]{1,0:T(8,128)(2,1)} custom-call(s32[16]{0:T(128)} %pad_add_fusion.tab_ref, bf16[128,2048]{1,0:T(8,128)(2,1)} %bitcast.6, bf16[2,128,256]{2,1,0:T(8,128)(2,1)} %bitcast.7, s32[8,1,128]{2,1,0:T(1,128)} %compare_convert_fusion.vis_ref, bf16[4,2,32,256]{3,2,1,0:T(8,128)(2,1)} %copy-done, bf16[4,2,32,256]{3,2,1,0:T(8,128)(2,1)} %copy-done.1, ...), custom_call_target="tpu_custom_call" | custom-call | flops 1207959552 | bytes 2752512 | tf_op jit(solution)/shard_map/pallas_call | solution.py:200
  (32 shorter events, 0.1 us)
Async XLA Ops:
  0.0 12.4 %copy-start.12 = (s32[4]{0:T(128)S(1)}, s32[4]{0:T(128)}, u32[]{:S(2)}) copy-start(s32[4]{0:T(128)} %param.11) | copy-start | bytes 52
  3.6 9.5 %collective-permute-start = (bf16[4,2,32,256]{3,2,1,0:T(8,128)(2,1)}, bf16[4,2,32,256]{3,2,1,0:T(8,128)(2,1)S(1)}, u32[]{:S(2)}, u32[]{:S(2)}) collective-permute-start(bf16[4,2,32,256]{3,2,1,0:T(8,128)(2,1)} %get-tuple-element.17), channel_id=1, source_target_pairs={{0,4},{1,5},{2,6},{3,7},{4,8},{5,9},{6,10},{7,11},{8,12},{9,13},{1... | collective-permute-start | bytes 393224 | tf_op jit(solution)/shard_map/ppermute | solution.py:94
  5.8 9.2 %collective-permute-start.1 = (bf16[4,2,32,256]{3,2,1,0:T(8,128)(2,1)}, bf16[4,2,32,256]{3,2,1,0:T(8,128)(2,1)S(1)}, u32[]{:S(2)}, u32[]{:S(2)}) collective-permute-start(bf16[4,2,32,256]{3,2,1,0:T(8,128)(2,1)} %get-tuple-element.18), channel_id=1, source_target_pairs={{0,5},{1,6},{2,7},{3,4},{4,9},{5,10},{6,11},{7,8},{8,13},{9,14},{1... | collective-permute-start | bytes 393224 | tf_op jit(solution)/shard_map/ppermute | solution.py:94
  8.8 11.2 %collective-permute-start.2 = (bf16[4,2,32,256]{3,2,1,0:T(8,128)(2,1)}, bf16[4,2,32,256]{3,2,1,0:T(8,128)(2,1)S(1)}, u32[]{:S(2)}, u32[]{:S(2)}) collective-permute-start(bf16[4,2,32,256]{3,2,1,0:T(8,128)(2,1)} %get-tuple-element.19), channel_id=1, source_target_pairs={{0,6},{1,7},{2,4},{3,5},{4,10},{5,11},{6,8},{7,9},{8,14},{9,15},{1... | collective-permute-start | bytes 393224 | tf_op jit(solution)/shard_map/ppermute | solution.py:94
  10.1 11.9 %collective-permute-start.3 = (bf16[4,2,32,256]{3,2,1,0:T(8,128)(2,1)}, bf16[4,2,32,256]{3,2,1,0:T(8,128)(2,1)S(1)}, u32[]{:S(2)}, u32[]{:S(2)}) collective-permute-start(bf16[4,2,32,256]{3,2,1,0:T(8,128)(2,1)} %get-tuple-element.20), channel_id=1, source_target_pairs={{0,7},{1,4},{2,5},{3,6},{4,11},{5,8},{6,9},{7,10},{8,15},{9,12},{1... | collective-permute-start | bytes 393224 | tf_op jit(solution)/shard_map/ppermute | solution.py:94
  10.4 24.0 %collective-permute-start.4 = (bf16[4,2,32,256]{3,2,1,0:T(8,128)(2,1)}, bf16[4,2,32,256]{3,2,1,0:T(8,128)(2,1)S(1)}, u32[]{:S(2)}, u32[]{:S(2)}) collective-permute-start(bf16[4,2,32,256]{3,2,1,0:T(8,128)(2,1)} %get-tuple-element.21), channel_id=1, source_target_pairs={{0,8},{1,9},{2,10},{3,11},{4,12},{5,13},{6,14},{7,15},{8,0},{9,1},... | collective-permute-start | bytes 393224 | tf_op jit(solution)/shard_map/ppermute | solution.py:94
  13.1 42.4 %copy-start = (bf16[4,2,32,256]{3,2,1,0:T(8,128)(2,1)}, bf16[4,2,32,256]{3,2,1,0:T(8,128)(2,1)S(1)}, u32[]{:S(2)}) copy-start(bf16[4,2,32,256]{3,2,1,0:T(8,128)(2,1)S(1)} %collective-permute-done.rest_0_) | copy-start | bytes 393220
  13.1 27.5 %collective-permute-start.5 = (bf16[4,2,32,256]{3,2,1,0:T(8,128)(2,1)}, bf16[4,2,32,256]{3,2,1,0:T(8,128)(2,1)S(1)}, u32[]{:S(2)}, u32[]{:S(2)}) collective-permute-start(bf16[4,2,32,256]{3,2,1,0:T(8,128)(2,1)} %get-tuple-element.22), channel_id=1, source_target_pairs={{0,9},{1,10},{2,11},{3,8},{4,13},{5,14},{6,15},{7,12},{8,1},{9,2},... | collective-permute-start | bytes 393224 | tf_op jit(solution)/shard_map/ppermute | solution.py:94
  15.0 40.5 %copy-start.1 = (bf16[4,2,32,256]{3,2,1,0:T(8,128)(2,1)}, bf16[4,2,32,256]{3,2,1,0:T(8,128)(2,1)S(1)}, u32[]{:S(2)}) copy-start(bf16[4,2,32,256]{3,2,1,0:T(8,128)(2,1)S(1)} %collective-permute-done.1.rest_1_) | copy-start | bytes 393220
  15.0 28.1 %collective-permute-start.6 = (bf16[4,2,32,256]{3,2,1,0:T(8,128)(2,1)}, bf16[4,2,32,256]{3,2,1,0:T(8,128)(2,1)S(1)}, u32[]{:S(2)}, u32[]{:S(2)}) collective-permute-start(bf16[4,2,32,256]{3,2,1,0:T(8,128)(2,1)} %get-tuple-element.23), channel_id=1, source_target_pairs={{0,10},{1,11},{2,8},{3,9},{4,14},{5,15},{6,12},{7,13},{8,2},{9,3},... | collective-permute-start | bytes 393224 | tf_op jit(solution)/shard_map/ppermute | solution.py:94
  20.0 35.5 %copy-start.2 = (bf16[4,2,32,256]{3,2,1,0:T(8,128)(2,1)}, bf16[4,2,32,256]{3,2,1,0:T(8,128)(2,1)S(1)}, u32[]{:S(2)}) copy-start(bf16[4,2,32,256]{3,2,1,0:T(8,128)(2,1)S(1)} %collective-permute-done.2.rest_2_) | copy-start | bytes 393220
  20.0 34.0 %collective-permute-start.7 = (bf16[4,2,32,256]{3,2,1,0:T(8,128)(2,1)}, bf16[4,2,32,256]{3,2,1,0:T(8,128)(2,1)S(1)}, u32[]{:S(2)}, u32[]{:S(2)}) collective-permute-start(bf16[4,2,32,256]{3,2,1,0:T(8,128)(2,1)} %get-tuple-element.24), channel_id=1, source_target_pairs={{0,11},{1,8},{2,9},{3,10},{4,15},{5,12},{6,13},{7,14},{8,3},{9,0},... | collective-permute-start | bytes 393224 | tf_op jit(solution)/shard_map/ppermute | solution.py:94
  22.0 33.5 %copy-start.3 = (bf16[4,2,32,256]{3,2,1,0:T(8,128)(2,1)}, bf16[4,2,32,256]{3,2,1,0:T(8,128)(2,1)S(1)}, u32[]{:S(2)}) copy-start(bf16[4,2,32,256]{3,2,1,0:T(8,128)(2,1)S(1)} %collective-permute-done.3.rest_3_) | copy-start | bytes 393220
  22.0 32.1 %collective-permute-start.8 = (bf16[4,2,32,256]{3,2,1,0:T(8,128)(2,1)}, bf16[4,2,32,256]{3,2,1,0:T(8,128)(2,1)S(1)}, u32[]{:S(2)}, u32[]{:S(2)}) collective-permute-start(bf16[4,2,32,256]{3,2,1,0:T(8,128)(2,1)} %get-tuple-element.25), channel_id=1, source_target_pairs={{0,12},{1,13},{2,14},{3,15},{4,0},{5,1},{6,2},{7,3},{8,4},{9,5},{1... | collective-permute-start | bytes 393224 | tf_op jit(solution)/shard_map/ppermute | solution.py:94
  34.4 21.1 %copy-start.4 = (bf16[4,2,32,256]{3,2,1,0:T(8,128)(2,1)}, bf16[4,2,32,256]{3,2,1,0:T(8,128)(2,1)S(1)}, u32[]{:S(2)}) copy-start(bf16[4,2,32,256]{3,2,1,0:T(8,128)(2,1)S(1)} %collective-permute-done.4.rest_4_) | copy-start | bytes 393220
  34.4 19.7 %collective-permute-start.9 = (bf16[4,2,32,256]{3,2,1,0:T(8,128)(2,1)}, bf16[4,2,32,256]{3,2,1,0:T(8,128)(2,1)S(1)}, u32[]{:S(2)}, u32[]{:S(2)}) collective-permute-start(bf16[4,2,32,256]{3,2,1,0:T(8,128)(2,1)} %get-tuple-element.26), channel_id=1, source_target_pairs={{0,13},{1,14},{2,15},{3,12},{4,1},{5,2},{6,3},{7,0},{8,5},{9,6},{1... | collective-permute-start | bytes 393224 | tf_op jit(solution)/shard_map/ppermute | solution.py:94
  40.6 14.9 %copy-start.5 = (bf16[4,2,32,256]{3,2,1,0:T(8,128)(2,1)}, bf16[4,2,32,256]{3,2,1,0:T(8,128)(2,1)S(1)}, u32[]{:S(2)}) copy-start(bf16[4,2,32,256]{3,2,1,0:T(8,128)(2,1)S(1)} %collective-permute-done.5.rest_5_) | copy-start | bytes 393220
  40.6 13.5 %collective-permute-start.10 = (bf16[4,2,32,256]{3,2,1,0:T(8,128)(2,1)}, bf16[4,2,32,256]{3,2,1,0:T(8,128)(2,1)S(1)}, u32[]{:S(2)}, u32[]{:S(2)}) collective-permute-start(bf16[4,2,32,256]{3,2,1,0:T(8,128)(2,1)} %get-tuple-element.27), channel_id=1, source_target_pairs={{0,14},{1,15},{2,12},{3,13},{4,2},{5,3},{6,0},{7,1},{8,6},{9,7},{1... | collective-permute-start | bytes 393224 | tf_op jit(solution)/shard_map/ppermute | solution.py:94
  43.1 12.4 %copy-start.6 = (bf16[4,2,32,256]{3,2,1,0:T(8,128)(2,1)}, bf16[4,2,32,256]{3,2,1,0:T(8,128)(2,1)S(1)}, u32[]{:S(2)}) copy-start(bf16[4,2,32,256]{3,2,1,0:T(8,128)(2,1)S(1)} %collective-permute-done.6.rest_6_) | copy-start | bytes 393220
  43.1 12.4 %collective-permute-start.11 = (bf16[4,2,32,256]{3,2,1,0:T(8,128)(2,1)}, bf16[4,2,32,256]{3,2,1,0:T(8,128)(2,1)S(1)}, u32[]{:S(2)}, u32[]{:S(2)}) collective-permute-start(bf16[4,2,32,256]{3,2,1,0:T(8,128)(2,1)} %get-tuple-element.28), channel_id=1, source_target_pairs={{0,15},{1,12},{2,13},{3,14},{4,3},{5,0},{6,1},{7,2},{8,7},{9,4},{1... | collective-permute-start | bytes 393224 | tf_op jit(solution)/shard_map/ppermute | solution.py:94
  54.1 1.5 %copy-start.7 = (bf16[4,2,32,256]{3,2,1,0:T(8,128)(2,1)}, bf16[4,2,32,256]{3,2,1,0:T(8,128)(2,1)S(1)}, u32[]{:S(2)}) copy-start(bf16[4,2,32,256]{3,2,1,0:T(8,128)(2,1)S(1)} %collective-permute-done.7.rest_7_) | copy-start | bytes 393220
  54.1 1.5 %copy-start.8 = (bf16[4,2,32,256]{3,2,1,0:T(8,128)(2,1)}, bf16[4,2,32,256]{3,2,1,0:T(8,128)(2,1)S(1)}, u32[]{:S(2)}) copy-start(bf16[4,2,32,256]{3,2,1,0:T(8,128)(2,1)S(1)} %collective-permute-done.8.rest_8_) | copy-start | bytes 393220
  54.1 1.5 %copy-start.9 = (bf16[4,2,32,256]{3,2,1,0:T(8,128)(2,1)}, bf16[4,2,32,256]{3,2,1,0:T(8,128)(2,1)S(1)}, u32[]{:S(2)}) copy-start(bf16[4,2,32,256]{3,2,1,0:T(8,128)(2,1)S(1)} %collective-permute-done.9.rest_9_) | copy-start | bytes 393220
  54.1 1.5 %copy-start.10 = (bf16[4,2,32,256]{3,2,1,0:T(8,128)(2,1)}, bf16[4,2,32,256]{3,2,1,0:T(8,128)(2,1)S(1)}, u32[]{:S(2)}) copy-start(bf16[4,2,32,256]{3,2,1,0:T(8,128)(2,1)S(1)} %collective-permute-done.10.rest_10_) | copy-start | bytes 393220
  55.5 0.7 %copy-start.11 = (bf16[4,2,32,256]{3,2,1,0:T(8,128)(2,1)}, bf16[4,2,32,256]{3,2,1,0:T(8,128)(2,1)S(1)}, u32[]{:S(2)}) copy-start(bf16[4,2,32,256]{3,2,1,0:T(8,128)(2,1)S(1)} %collective-permute-done.11.rest_11_) | copy-start | bytes 393220

commit v12 on v11

--- a/solution.py
+++ b/solution.py
@@ -25,7 +25,7 @@
     return matched[:, None, :] * (ranking[:, None, :] == places[None, :, None]).astype(jnp.int32)
 
 
-def gather_kernel(span_count, slot_cap, tensor_count, off_ref, slot_ref, pool_ref, *out_refs):
+def gather_kernel(first, last, slot_cap, tensor_count, off_ref, slot_ref, pool_ref, *out_refs):
     replicas, page_count = off_ref.shape
     holder = lax.axis_index("replica")
     me = lax.axis_index("tensor")
@@ -33,7 +33,7 @@
     starts = [
         pl.multiple_of(((me + shift) % tensor_count) * lanes, lanes) for shift in range(tensor_count)
     ]
-    for distance in range(1, span_count + 1):
+    for distance in range(first, last + 1):
         reader = (holder + distance) % replicas
         chosen = [jnp.int32(0)] * slot_cap
         count = jnp.int32(0)
@@ -46,15 +46,16 @@
             count = count + matched.astype(jnp.int32)
         for slot in range(slot_cap):
             for shift in range(tensor_count):
-                out_refs[(distance - 1) * tensor_count + shift][slot] = pool_ref[
+                out_refs[(distance - first) * tensor_count + shift][slot] = pool_ref[
                     chosen[slot], :, :, pl.ds(starts[shift], lanes)
                 ]
 
 
-def pack_pages(pool_part, offsets, slots, span_count, slot_cap, tensor_count):
+def pack_pages(pool_part, offsets, slots, first, last, slot_cap, tensor_count):
     pages, kv, rows, width = pool_part.shape
     lanes = width // tensor_count
     piece = (slot_cap, kv, rows, lanes)
+    span_count = last - first + 1
     count = span_count * tensor_count
     grid_spec = pltpu.PrefetchScalarGridSpec(
         num_scalar_prefetch=2,
@@ -64,7 +65,7 @@
     )
     nbytes = 2 * (pool_part.size + span_count * slot_cap * kv * rows * width)
     return pl.pallas_call(
-        functools.partial(gather_kernel, span_count, slot_cap, tensor_count),
+        functools.partial(gather_kernel, first, last, slot_cap, tensor_count),
         grid_spec=grid_spec,
         out_shape=[jax.ShapeDtypeStruct(piece, pool_part.dtype) for _ in range(count)],
         cost_estimate=pl.CostEstimate(flops=0, transcendentals=0, bytes_accessed=nbytes),
@@ -81,7 +82,9 @@
     slot_cap = (page_count + span_count - 1) // span_count + 1
     distances = jnp.arange(1, span_count + 1, dtype=jnp.int32)
 
-    payload = pack_pages(page_pool, offsets, slots, span_count, slot_cap, tensor_count)
+    payload = pack_pages(page_pool, offsets, slots, 1, 1, slot_cap, tensor_count)
+    if span_count > 1:
+        payload = payload + pack_pages(page_pool, offsets, slots, 2, span_count, slot_cap, tensor_count)
 
     arrivals = []
     for distance in range(1, span_count + 1):

time: 64.2 us -> 62.4 us (0.972)
  Pallas kernels: 11.5 us -> 14.2 us
  waiting for transfers between devices: 13.7 us -> 11.3 us
  starting transfers between devices: 34.4 us -> 32.1 us
    pallas_call x1 -> x2, Pallas kernels: 3.63 us -> 6.39 us  [pack_pages(): pl.pallas_call(functools.partial(gather_kernel, first, last, slot_cap, te...]
    ppermute x12, waiting for transfers between devices: 13.7 us -> 11.3 us  [on_device(): lax.ppermute(payload[(distance - 1) * tensor_count + shift], ('replica',...]
    ppermute x12, starting transfers between devices: 34.4 us -> 32.1 us  [on_device(): lax.ppermute(payload[(distance - 1) * tensor_count + shift], ('replica',...]
  transfers between devices with their start and end apart: 12 -> 12, of which waited for: 3 -> 2; matrix products, arithmetic and copies ran while one was open for 6% -> 6% of each run, Pallas kernels for 0% -> 5%
where the time goes in v12:
time: 62.4 us; the launch traced here: 62.1 us
  starting transfers between devices  32.1 us (51%)
  Pallas kernels  14.2 us (23%)
  waiting for transfers between devices  11.3 us (18%)
  local copies, waits for them, and re-layouts  2.17 us (3%)
  other arithmetic  2.09 us (3%)
    ppermute x12, starting transfers between devices, on_device(): lax.ppermute(payload[(distance - 1) * tensor_count + shift], ('replica',...  32.1 us
    ppermute x12, waiting for transfers between devices, on_device(): lax.ppermute(payload[(distance - 1) * tensor_count + shift], ('replica',...  11.3 us
    pallas_call x1, Pallas kernels, attend(): pl.pallas_call(functools.partial(attention_kernel, span_count, tensor_cou...  7.83 us
    pallas_call x2, Pallas kernels, pack_pages(): pl.pallas_call(functools.partial(gather_kernel, first, last, slot_cap, te...  6.39 us
  transfers between devices with their start and end apart: 12, of which 2 were waited for; matrix products, arithmetic and copies ran while one was open for 6% of the time, Pallas kernels for 5%

profile of v12, /device:TPU:1, one launch (start us, length us, event | category | flops | bytes accessed | tf_op | source)
XLA Modules:
  0.0 62.1 jit_solution(11690222628520896978)
XLA Ops:
  0.0 3.1 %shard_map.64 = (bf16[4,2,32,256]{3,2,1,0:T(8,128)(2,1)}, bf16[4,2,32,256]{3,2,1,0:T(8,128)(2,1)}, bf16[4,2,32,256]{3,2,1,0:T(8,128)(2,1)}, bf16[4,2,32,256]{3,2,1,0:T(8,128)(2,1)}) custom-call(s32[4,8]{1,0:T(4,128)} %off_ref.3, s32[4,8]{1,0:T(4,128)} %slot_ref.3, bf16[12,2,32,1024]{3,2,1,0:T(8,128)(2,1)} %pool_ref.3), custom_call_target="tpu_custom_call" | custom-call | bytes 2097152 | tf_op jit(solution)/shard_map/pallas_call | solution.py:67
  3.1 2.1 %collective-permute-start = (bf16[4,2,32,256]{3,2,1,0:T(8,128)(2,1)}, bf16[4,2,32,256]{3,2,1,0:T(8,128)(2,1)S(1)}, u32[]{:S(2)}, u32[]{:S(2)}) collective-permute-start(bf16[4,2,32,256]{3,2,1,0:T(8,128)(2,1)} %get-tuple-element.17), channel_id=1, source_target_pairs={{0,4},{1,5},{2,6},{3,7},{4,8},{5,9},{6,10},{7,11},{8,12},{9,13},{1... | collective-permute-start | bytes 393224 | tf_op jit(solution)/shard_map/ppermute | solution.py:97
  5.2 3.1 %collective-permute-start.1 = (bf16[4,2,32,256]{3,2,1,0:T(8,128)(2,1)}, bf16[4,2,32,256]{3,2,1,0:T(8,128)(2,1)S(1)}, u32[]{:S(2)}, u32[]{:S(2)}) collective-permute-start(bf16[4,2,32,256]{3,2,1,0:T(8,128)(2,1)} %get-tuple-element.18), channel_id=1, source_target_pairs={{0,5},{1,6},{2,7},{3,4},{4,9},{5,10},{6,11},{7,8},{8,13},{9,14},{1... | collective-permute-start | bytes 393224 | tf_op jit(solution)/shard_map/ppermute | solution.py:97
  8.3 1.3 %collective-permute-start.2 = (bf16[4,2,32,256]{3,2,1,0:T(8,128)(2,1)}, bf16[4,2,32,256]{3,2,1,0:T(8,128)(2,1)S(1)}, u32[]{:S(2)}, u32[]{:S(2)}) collective-permute-start(bf16[4,2,32,256]{3,2,1,0:T(8,128)(2,1)} %get-tuple-element.19), channel_id=1, source_target_pairs={{0,6},{1,7},{2,4},{3,5},{4,10},{5,11},{6,8},{7,9},{8,14},{9,15},{1... | collective-permute-start | bytes 393224 | tf_op jit(solution)/shard_map/ppermute | solution.py:97
  9.6 0.3 collective-permute-start.3
  9.9 3.3 %shard_map.65 = (bf16[4,2,32,256]{3,2,1,0:T(8,128)(2,1)}, bf16[4,2,32,256]{3,2,1,0:T(8,128)(2,1)}, bf16[4,2,32,256]{3,2,1,0:T(8,128)(2,1)}, bf16[4,2,32,256]{3,2...) custom-call(s32[4,8]{1,0:T(4,128)} %off_ref.3, ...), custom_call_target="tpu_custom_call" | custom-call | bytes 2621440 | tf_op jit(solution)/shard_map/pallas_call | solution.py:67
  13.2 1.7 %collective-permute-start.4 = (bf16[4,2,32,256]{3,2,1,0:T(8,128)(2,1)}, bf16[4,2,32,256]{3,2,1,0:T(8,128)(2,1)S(1)}, u32[]{:S(2)}, u32[]{:S(2)}) collective-permute-start(bf16[4,2,32,256]{3,2,1,0:T(8,128)(2,1)} %get-tuple-element.21), channel_id=1, source_target_pairs={{0,8},{1,9},{2,10},{3,11},{4,12},{5,13},{6,14},{7,15},{8,0},{9,1},... | collective-permute-start | bytes 393224 | tf_op jit(solution)/shard_map/ppermute | solution.py:97
  14.9 0.1 add.76
  15.0 0.1 broadcast_add_fusion
  15.0 0.1 add.73
  15.1 0.1 add.74
  15.2 0.6 %dynamic_slice.9 = s32[1]{0:T(128)} dynamic-slice(s32[4]{0:T(128)S(1)} %copy-done.12, s32[]{:T(128)S(6)} %select_n.17), dynamic_slice_sizes={1} | dynamic-slice | bytes 12 | tf_op jit(solution)/shard_map/jit(dynamic_index_in_dim)/dynamic_slice | solution.py:103
  15.8 0.0 collective-permute-done.rest_0_
  15.8 1.9 %collective-permute-start.5 = (bf16[4,2,32,256]{3,2,1,0:T(8,128)(2,1)}, bf16[4,2,32,256]{3,2,1,0:T(8,128)(2,1)S(1)}, u32[]{:S(2)}, u32[]{:S(2)}) collective-permute-start(bf16[4,2,32,256]{3,2,1,0:T(8,128)(2,1)} %get-tuple-element.22), channel_id=1, source_target_pairs={{0,9},{1,10},{2,11},{3,8},{4,13},{5,14},{6,15},{7,12},{8,1},{9,2},... | collective-permute-start | bytes 393224 | tf_op jit(solution)/shard_map/ppermute | solution.py:97
  17.7 3.1 %collective-permute-start.6 = (bf16[4,2,32,256]{3,2,1,0:T(8,128)(2,1)}, bf16[4,2,32,256]{3,2,1,0:T(8,128)(2,1)S(1)}, u32[]{:S(2)}, u32[]{:S(2)}) collective-permute-start(bf16[4,2,32,256]{3,2,1,0:T(8,128)(2,1)} %get-tuple-element.23), channel_id=1, source_target_pairs={{0,10},{1,11},{2,8},{3,9},{4,14},{5,15},{6,12},{7,13},{8,2},{9,3},... | collective-permute-start | bytes 393224 | tf_op jit(solution)/shard_map/ppermute | solution.py:97
  20.8 1.2 %compare_convert_fusion.vis_ref = s32[8,1,128]{2,1,0:T(1,128)} fusion(s32[8,1,128]{2,1,0:T(1,128)S(1)} %add.74, s32[]{:T(128)} %bitcast.3, s32[128]{0:T(128)S(1)} %add.76), kind=kLoop, calls=%fused_computation | loop fusion | flops 3072 | bytes 8708 | tf_op jit(solution)/shard_map/convert_element_type | solution.py:116
  22.0 0.7 %dynamic-slice_bitcast_fusion = s32[8]{0:T(128)S(1)} fusion(s32[4,8]{1,0:T(4,128)} %off_ref.3, s32[]{:T(128)S(6)} %select_n.17), kind=kLoop, calls=%fused_computation.11 | loop fusion | bytes 68 | tf_op jit(solution)/shard_map/jit(dynamic_index_in_dim)/squeeze | solution.py:102
  22.7 0.1 collective-permute-start.7
  22.8 1.2 %collective-permute-start.8 = (bf16[4,2,32,256]{3,2,1,0:T(8,128)(2,1)}, bf16[4,2,32,256]{3,2,1,0:T(8,128)(2,1)S(1)}, u32[]{:S(2)}, u32[]{:S(2)}) collective-permute-start(bf16[4,2,32,256]{3,2,1,0:T(8,128)(2,1)} %get-tuple-element.25), channel_id=1, source_target_pairs={{0,12},{1,13},{2,14},{3,15},{4,0},{5,1},{6,2},{7,3},{8,4},{9,5},{1... | collective-permute-start | bytes 393224 | tf_op jit(solution)/shard_map/ppermute | solution.py:97
  24.1 9.8 %collective-permute-done.4.rest_4_ = bf16[4,2,32,256]{3,2,1,0:T(8,128)(2,1)S(1)} collective-permute-done((bf16[4,2,32,256]{3,2,1,0:T(8,128)(2,1)}, bf16[4,2,32,256]{3,2,1,0:T(8,128)(2,1)S(1)}, u32[]{:S(2)}, u32[]{:S(2)}) %collective-permute-start.4) | collective-permute-done | bytes 131104 | tf_op jit(solution)/shard_map/ppermute | solution.py:97
  33.9 6.2 %collective-permute-start.9 = (bf16[4,2,32,256]{3,2,1,0:T(8,128)(2,1)}, bf16[4,2,32,256]{3,2,1,0:T(8,128)(2,1)S(1)}, u32[]{:S(2)}, u32[]{:S(2)}) collective-permute-start(bf16[4,2,32,256]{3,2,1,0:T(8,128)(2,1)} %get-tuple-element.26), channel_id=1, source_target_pairs={{0,13},{1,14},{2,15},{3,12},{4,1},{5,2},{6,3},{7,0},{8,5},{9,6},{1... | collective-permute-start | bytes 393224 | tf_op jit(solution)/shard_map/ppermute | solution.py:97
  40.1 0.0 collective-permute-done.5.rest_5_
  40.1 2.5 %collective-permute-start.10 = (bf16[4,2,32,256]{3,2,1,0:T(8,128)(2,1)}, bf16[4,2,32,256]{3,2,1,0:T(8,128)(2,1)S(1)}, u32[]{:S(2)}, u32[]{:S(2)}) collective-permute-start(bf16[4,2,32,256]{3,2,1,0:T(8,128)(2,1)} %get-tuple-element.27), channel_id=1, source_target_pairs={{0,14},{1,15},{2,12},{3,13},{4,2},{5,3},{6,0},{7,1},{8,6},{9,7},{1... | collective-permute-start | bytes 393224 | tf_op jit(solution)/shard_map/ppermute | solution.py:97
  42.6 8.7 %collective-permute-start.11 = (bf16[4,2,32,256]{3,2,1,0:T(8,128)(2,1)}, bf16[4,2,32,256]{3,2,1,0:T(8,128)(2,1)S(1)}, u32[]{:S(2)}, u32[]{:S(2)}) collective-permute-start(bf16[4,2,32,256]{3,2,1,0:T(8,128)(2,1)} %get-tuple-element.28), channel_id=1, source_target_pairs={{0,15},{1,12},{2,13},{3,14},{4,3},{5,0},{6,1},{7,2},{8,7},{9,4},{1... | collective-permute-start | bytes 393224 | tf_op jit(solution)/shard_map/ppermute | solution.py:97
  51.3 0.2 select_reduce_fusion
  51.5 0.6 %pad_add_fusion.tab_ref = s32[16]{0:T(128)} fusion(s32[8]{0:T(128)S(1)} %select_reduce_fusion, s32[8]{0:T(128)S(1)} %dynamic-slice_bitcast_fusion), kind=kLoop, calls=%fused_computation.9 | loop fusion | flops 16 | bytes 128 | tf_op jit(solution)/shard_map/concatenate | solution.py:108
  52.1 0.0 collective-permute-done.7.rest_7_
  52.1 0.0 collective-permute-done.8.rest_8_
  52.1 0.0 collective-permute-done.9.rest_9_
  52.2 1.4 %collective-permute-done.11.rest_11_ = bf16[4,2,32,256]{3,2,1,0:T(8,128)(2,1)S(1)} collective-permute-done((bf16[4,2,32,256]{3,2,1,0:T(8,128)(2,1)}, bf16[4,2,32,256]{3,2,1,0:T(8,128)(2,1)S(1)}, u32[]{:S(2)}, u32[]{:S(2)}) %collective-permute-start.11) | collective-permute-done | bytes 131104 | tf_op jit(solution)/shard_map/ppermute | solution.py:97
  53.7 0.6 copy-done.11
  54.2 7.8 %shard_map.66 = bf16[128,2048]{1,0:T(8,128)(2,1)} custom-call(s32[16]{0:T(128)} %pad_add_fusion.tab_ref, bf16[128,2048]{1,0:T(8,128)(2,1)} %bitcast.6, bf16[2,128,256]{2,1,0:T(8,128)(2,1)} %bitcast.7, s32[8,1,128]{2,1,0:T(1,128)} %compare_convert_fusion.vis_ref, bf16[4,2,32,256]{3,2,1,0:T(8,128)(2,1)} %copy-done, bf16[4,2,32,256]{3,2,1,0:T(8,128)(2,1)} %copy-done.1, ...), custom_call_target="tpu_custom_call" | custom-call | flops 1207959552 | bytes 2752512 | tf_op jit(solution)/shard_map/pallas_call | solution.py:203
  (33 shorter events, 0.1 us)
Async XLA Ops:
  0.0 15.2 %copy-start.12 = (s32[4]{0:T(128)S(1)}, s32[4]{0:T(128)}, u32[]{:S(2)}) copy-start(s32[4]{0:T(128)} %param.11) | copy-start | bytes 52
  3.1 12.7 %collective-permute-start = (bf16[4,2,32,256]{3,2,1,0:T(8,128)(2,1)}, bf16[4,2,32,256]{3,2,1,0:T(8,128)(2,1)S(1)}, u32[]{:S(2)}, u32[]{:S(2)}) collective-permute-start(bf16[4,2,32,256]{3,2,1,0:T(8,128)(2,1)} %get-tuple-element.17), channel_id=1, source_target_pairs={{0,4},{1,5},{2,6},{3,7},{4,8},{5,9},{6,10},{7,11},{8,12},{9,13},{1... | collective-permute-start | bytes 393224 | tf_op jit(solution)/shard_map/ppermute | solution.py:97
  5.2 12.5 %collective-permute-start.1 = (bf16[4,2,32,256]{3,2,1,0:T(8,128)(2,1)}, bf16[4,2,32,256]{3,2,1,0:T(8,128)(2,1)S(1)}, u32[]{:S(2)}, u32[]{:S(2)}) collective-permute-start(bf16[4,2,32,256]{3,2,1,0:T(8,128)(2,1)} %get-tuple-element.18), channel_id=1, source_target_pairs={{0,5},{1,6},{2,7},{3,4},{4,9},{5,10},{6,11},{7,8},{8,13},{9,14},{1... | collective-permute-start | bytes 393224 | tf_op jit(solution)/shard_map/ppermute | solution.py:97
  8.3 14.4 %collective-permute-start.2 = (bf16[4,2,32,256]{3,2,1,0:T(8,128)(2,1)}, bf16[4,2,32,256]{3,2,1,0:T(8,128)(2,1)S(1)}, u32[]{:S(2)}, u32[]{:S(2)}) collective-permute-start(bf16[4,2,32,256]{3,2,1,0:T(8,128)(2,1)} %get-tuple-element.19), channel_id=1, source_target_pairs={{0,6},{1,7},{2,4},{3,5},{4,10},{5,11},{6,8},{7,9},{8,14},{9,15},{1... | collective-permute-start | bytes 393224 | tf_op jit(solution)/shard_map/ppermute | solution.py:97
  9.6 13.2 %collective-permute-start.3 = (bf16[4,2,32,256]{3,2,1,0:T(8,128)(2,1)}, bf16[4,2,32,256]{3,2,1,0:T(8,128)(2,1)S(1)}, u32[]{:S(2)}, u32[]{:S(2)}) collective-permute-start(bf16[4,2,32,256]{3,2,1,0:T(8,128)(2,1)} %get-tuple-element.20), channel_id=1, source_target_pairs={{0,7},{1,4},{2,5},{3,6},{4,11},{5,8},{6,9},{7,10},{8,15},{9,12},{1... | collective-permute-start | bytes 393224 | tf_op jit(solution)/shard_map/ppermute | solution.py:97
  13.2 20.7 %collective-permute-start.4 = (bf16[4,2,32,256]{3,2,1,0:T(8,128)(2,1)}, bf16[4,2,32,256]{3,2,1,0:T(8,128)(2,1)S(1)}, u32[]{:S(2)}, u32[]{:S(2)}) collective-permute-start(bf16[4,2,32,256]{3,2,1,0:T(8,128)(2,1)} %get-tuple-element.21), channel_id=1, source_target_pairs={{0,8},{1,9},{2,10},{3,11},{4,12},{5,13},{6,14},{7,15},{8,0},{9,1},... | collective-permute-start | bytes 393224 | tf_op jit(solution)/shard_map/ppermute | solution.py:97
  15.8 37.7 %copy-start = (bf16[4,2,32,256]{3,2,1,0:T(8,128)(2,1)}, bf16[4,2,32,256]{3,2,1,0:T(8,128)(2,1)S(1)}, u32[]{:S(2)}) copy-start(bf16[4,2,32,256]{3,2,1,0:T(8,128)(2,1)S(1)} %collective-permute-done.rest_0_) | copy-start | bytes 393220
  15.8 24.2 %collective-permute-start.5 = (bf16[4,2,32,256]{3,2,1,0:T(8,128)(2,1)}, bf16[4,2,32,256]{3,2,1,0:T(8,128)(2,1)S(1)}, u32[]{:S(2)}, u32[]{:S(2)}) collective-permute-start(bf16[4,2,32,256]{3,2,1,0:T(8,128)(2,1)} %get-tuple-element.22), channel_id=1, source_target_pairs={{0,9},{1,10},{2,11},{3,8},{4,13},{5,14},{6,15},{7,12},{8,1},{9,2},... | collective-permute-start | bytes 393224 | tf_op jit(solution)/shard_map/ppermute | solution.py:97
  17.7 35.9 %copy-start.1 = (bf16[4,2,32,256]{3,2,1,0:T(8,128)(2,1)}, bf16[4,2,32,256]{3,2,1,0:T(8,128)(2,1)S(1)}, u32[]{:S(2)}) copy-start(bf16[4,2,32,256]{3,2,1,0:T(8,128)(2,1)S(1)} %collective-permute-done.1.rest_1_) | copy-start | bytes 393220
  17.7 24.9 %collective-permute-start.6 = (bf16[4,2,32,256]{3,2,1,0:T(8,128)(2,1)}, bf16[4,2,32,256]{3,2,1,0:T(8,128)(2,1)S(1)}, u32[]{:S(2)}, u32[]{:S(2)}) collective-permute-start(bf16[4,2,32,256]{3,2,1,0:T(8,128)(2,1)} %get-tuple-element.23), channel_id=1, source_target_pairs={{0,10},{1,11},{2,8},{3,9},{4,14},{5,15},{6,12},{7,13},{8,2},{9,3},... | collective-permute-start | bytes 393224 | tf_op jit(solution)/shard_map/ppermute | solution.py:97
  22.7 30.9 %copy-start.2 = (bf16[4,2,32,256]{3,2,1,0:T(8,128)(2,1)}, bf16[4,2,32,256]{3,2,1,0:T(8,128)(2,1)S(1)}, u32[]{:S(2)}) copy-start(bf16[4,2,32,256]{3,2,1,0:T(8,128)(2,1)S(1)} %collective-permute-done.2.rest_2_) | copy-start | bytes 393220
  22.7 29.4 %collective-permute-start.7 = (bf16[4,2,32,256]{3,2,1,0:T(8,128)(2,1)}, bf16[4,2,32,256]{3,2,1,0:T(8,128)(2,1)S(1)}, u32[]{:S(2)}, u32[]{:S(2)}) collective-permute-start(bf16[4,2,32,256]{3,2,1,0:T(8,128)(2,1)} %get-tuple-element.24), channel_id=1, source_target_pairs={{0,11},{1,8},{2,9},{3,10},{4,15},{5,12},{6,13},{7,14},{8,3},{9,0},... | collective-permute-start | bytes 393224 | tf_op jit(solution)/shard_map/ppermute | solution.py:97
  22.8 30.8 %copy-start.3 = (bf16[4,2,32,256]{3,2,1,0:T(8,128)(2,1)}, bf16[4,2,32,256]{3,2,1,0:T(8,128)(2,1)S(1)}, u32[]{:S(2)}) copy-start(bf16[4,2,32,256]{3,2,1,0:T(8,128)(2,1)S(1)} %collective-permute-done.3.rest_3_) | copy-start | bytes 393220
  22.8 29.3 %collective-permute-start.8 = (bf16[4,2,32,256]{3,2,1,0:T(8,128)(2,1)}, bf16[4,2,32,256]{3,2,1,0:T(8,128)(2,1)S(1)}, u32[]{:S(2)}, u32[]{:S(2)}) collective-permute-start(bf16[4,2,32,256]{3,2,1,0:T(8,128)(2,1)} %get-tuple-element.25), channel_id=1, source_target_pairs={{0,12},{1,13},{2,14},{3,15},{4,0},{5,1},{6,2},{7,3},{8,4},{9,5},{1... | collective-permute-start | bytes 393224 | tf_op jit(solution)/shard_map/ppermute | solution.py:97
  33.9 19.7 %copy-start.4 = (bf16[4,2,32,256]{3,2,1,0:T(8,128)(2,1)}, bf16[4,2,32,256]{3,2,1,0:T(8,128)(2,1)S(1)}, u32[]{:S(2)}) copy-start(bf16[4,2,32,256]{3,2,1,0:T(8,128)(2,1)S(1)} %collective-permute-done.4.rest_4_) | copy-start | bytes 393220
  33.9 18.2 %collective-permute-start.9 = (bf16[4,2,32,256]{3,2,1,0:T(8,128)(2,1)}, bf16[4,2,32,256]{3,2,1,0:T(8,128)(2,1)S(1)}, u32[]{:S(2)}, u32[]{:S(2)}) collective-permute-start(bf16[4,2,32,256]{3,2,1,0:T(8,128)(2,1)} %get-tuple-element.26), channel_id=1, source_target_pairs={{0,13},{1,14},{2,15},{3,12},{4,1},{5,2},{6,3},{7,0},{8,5},{9,6},{1... | collective-permute-start | bytes 393224 | tf_op jit(solution)/shard_map/ppermute | solution.py:97
  40.1 13.5 %copy-start.5 = (bf16[4,2,32,256]{3,2,1,0:T(8,128)(2,1)}, bf16[4,2,32,256]{3,2,1,0:T(8,128)(2,1)S(1)}, u32[]{:S(2)}) copy-start(bf16[4,2,32,256]{3,2,1,0:T(8,128)(2,1)S(1)} %collective-permute-done.5.rest_5_) | copy-start | bytes 393220
  40.1 12.1 %collective-permute-start.10 = (bf16[4,2,32,256]{3,2,1,0:T(8,128)(2,1)}, bf16[4,2,32,256]{3,2,1,0:T(8,128)(2,1)S(1)}, u32[]{:S(2)}, u32[]{:S(2)}) collective-permute-start(bf16[4,2,32,256]{3,2,1,0:T(8,128)(2,1)} %get-tuple-element.27), channel_id=1, source_target_pairs={{0,14},{1,15},{2,12},{3,13},{4,2},{5,3},{6,0},{7,1},{8,6},{9,7},{1... | collective-permute-start | bytes 393224 | tf_op jit(solution)/shard_map/ppermute | solution.py:97
  42.6 11.0 %copy-start.6 = (bf16[4,2,32,256]{3,2,1,0:T(8,128)(2,1)}, bf16[4,2,32,256]{3,2,1,0:T(8,128)(2,1)S(1)}, u32[]{:S(2)}) copy-start(bf16[4,2,32,256]{3,2,1,0:T(8,128)(2,1)S(1)} %collective-permute-done.6.rest_6_) | copy-start | bytes 393220
  42.6 11.0 %collective-permute-start.11 = (bf16[4,2,32,256]{3,2,1,0:T(8,128)(2,1)}, bf16[4,2,32,256]{3,2,1,0:T(8,128)(2,1)S(1)}, u32[]{:S(2)}, u32[]{:S(2)}) collective-permute-start(bf16[4,2,32,256]{3,2,1,0:T(8,128)(2,1)} %get-tuple-element.28), channel_id=1, source_target_pairs={{0,15},{1,12},{2,13},{3,14},{4,3},{5,0},{6,1},{7,2},{8,7},{9,4},{1... | collective-permute-start | bytes 393224 | tf_op jit(solution)/shard_map/ppermute | solution.py:97
  52.1 1.5 %copy-start.7 = (bf16[4,2,32,256]{3,2,1,0:T(8,128)(2,1)}, bf16[4,2,32,256]{3,2,1,0:T(8,128)(2,1)S(1)}, u32[]{:S(2)}) copy-start(bf16[4,2,32,256]{3,2,1,0:T(8,128)(2,1)S(1)} %collective-permute-done.7.rest_7_) | copy-start | bytes 393220
  52.1 1.5 %copy-start.8 = (bf16[4,2,32,256]{3,2,1,0:T(8,128)(2,1)}, bf16[4,2,32,256]{3,2,1,0:T(8,128)(2,1)S(1)}, u32[]{:S(2)}) copy-start(bf16[4,2,32,256]{3,2,1,0:T(8,128)(2,1)S(1)} %collective-permute-done.8.rest_8_) | copy-start | bytes 393220
  52.1 1.5 %copy-start.9 = (bf16[4,2,32,256]{3,2,1,0:T(8,128)(2,1)}, bf16[4,2,32,256]{3,2,1,0:T(8,128)(2,1)S(1)}, u32[]{:S(2)}) copy-start(bf16[4,2,32,256]{3,2,1,0:T(8,128)(2,1)S(1)} %collective-permute-done.9.rest_9_) | copy-start | bytes 393220
  52.2 1.5 %copy-start.10 = (bf16[4,2,32,256]{3,2,1,0:T(8,128)(2,1)}, bf16[4,2,32,256]{3,2,1,0:T(8,128)(2,1)S(1)}, u32[]{:S(2)}) copy-start(bf16[4,2,32,256]{3,2,1,0:T(8,128)(2,1)S(1)} %collective-permute-done.10.rest_10_) | copy-start | bytes 393220
  53.6 0.7 %copy-start.11 = (bf16[4,2,32,256]{3,2,1,0:T(8,128)(2,1)}, bf16[4,2,32,256]{3,2,1,0:T(8,128)(2,1)S(1)}, u32[]{:S(2)}) copy-start(bf16[4,2,32,256]{3,2,1,0:T(8,128)(2,1)S(1)} %collective-permute-done.11.rest_11_) | copy-start | bytes 393220

commit v13 on v12

--- a/solution.py
+++ b/solution.py
@@ -25,7 +25,8 @@
     return matched[:, None, :] * (ranking[:, None, :] == places[None, :, None]).astype(jnp.int32)
 
 
-def gather_kernel(first, last, slot_cap, tensor_count, off_ref, slot_ref, pool_ref, *out_refs):
+def gather_kernel(first, last, slot_cap, tensor_count, off_ref, slot_ref, pool_hbm, *rest):
+    out_refs, buf, sems = rest[:-2], rest[-2], rest[-1]
     replicas, page_count = off_ref.shape
     holder = lax.axis_index("replica")
     me = lax.axis_index("tensor")
@@ -33,6 +34,7 @@
     starts = [
         pl.multiple_of(((me + shift) % tensor_count) * lanes, lanes) for shift in range(tensor_count)
     ]
+    copies = []
     for distance in range(first, last + 1):
         reader = (holder + distance) % replicas
         chosen = [jnp.int32(0)] * slot_cap
@@ -45,9 +47,18 @@
             ]
             count = count + matched.astype(jnp.int32)
         for slot in range(slot_cap):
+            index = (distance - first) * slot_cap + slot
+            copy = pltpu.make_async_copy(pool_hbm.at[chosen[slot]], buf.at[index], sems.at[index])
+            copy.start()
+            copies.append(copy)
+    for copy in copies:
+        copy.wait()
+    for distance in range(first, last + 1):
+        for slot in range(slot_cap):
+            index = (distance - first) * slot_cap + slot
             for shift in range(tensor_count):
-                out_refs[(distance - first) * tensor_count + shift][slot] = pool_ref[
-                    chosen[slot], :, :, pl.ds(starts[shift], lanes)
+                out_refs[(distance - first) * tensor_count + shift][slot] = buf[
+                    index, :, :, pl.ds(starts[shift], lanes)
                 ]
 
 
@@ -60,10 +71,14 @@
     grid_spec = pltpu.PrefetchScalarGridSpec(
         num_scalar_prefetch=2,
         grid=(1,),
-        in_specs=[pl.BlockSpec((pages, kv, rows, width), lambda i, o, s: (0, 0, 0, 0))],
+        in_specs=[pl.BlockSpec(memory_space=pl.ANY)],
         out_specs=[pl.BlockSpec(piece, lambda i, o, s: (0, 0, 0, 0)) for _ in range(count)],
-    )
-    nbytes = 2 * (pool_part.size + span_count * slot_cap * kv * rows * width)
+        scratch_shapes=[
+            pltpu.VMEM((span_count * slot_cap, kv, rows, width), pool_part.dtype),
+            pltpu.SemaphoreType.DMA((span_count * slot_cap,)),
+        ],
+    )
+    nbytes = 2 * 2 * span_count * slot_cap * kv * rows * width
     return pl.pallas_call(
         functools.partial(gather_kernel, first, last, slot_cap, tensor_count),
         grid_spec=grid_spec,

time: 62.4 us -> 62.2 us (level)
  transfers between devices with their start and end apart: 12 -> 12, of which waited for: 2 -> 2; matrix products, arithmetic and copies ran while one was open for 6% -> 6% of each run, Pallas kernels for 5% -> 6%
where the time goes in v13:
time: 62.2 us; the launch traced here: 61.9 us
  starting transfers between devices  32 us (51%)
  Pallas kernels  14.2 us (23%)
  waiting for transfers between devices  11.2 us (18%)
  local copies, waits for them, and re-layouts  2.17 us (3%)
  other arithmetic  2.09 us (3%)
    ppermute x12, starting transfers between devices, on_device(): lax.ppermute(payload[(distance - 1) * tensor_count + shift], ('replica',...  32 us
    ppermute x12, waiting for transfers between devices, on_device(): lax.ppermute(payload[(distance - 1) * tensor_count + shift], ('replica',...  11.2 us
    pallas_call x1, Pallas kernels, attend(): pl.pallas_call(functools.partial(attention_kernel, span_count, tensor_cou...  7.83 us
    pallas_call x2, Pallas kernels, pack_pages(): pl.pallas_call(functools.partial(gather_kernel, first, last, slot_cap, te...  6.37 us
  transfers between devices with their start and end apart: 12, of which 2 were waited for; matrix products, arithmetic and copies ran while one was open for 6% of the time, Pallas kernels for 6%

profile of v13, /device:TPU:1, one launch (start us, length us, event | category | flops | bytes accessed | tf_op | source)
XLA Modules:
  0.0 61.9 jit_solution(1421712812383782298)
XLA Ops:
  0.0 2.9 %shard_map.64 = (bf16[4,2,32,256]{3,2,1,0:T(8,128)(2,1)}, bf16[4,2,32,256]{3,2,1,0:T(8,128)(2,1)}, bf16[4,2,32,256]{3,2,1,0:T(8,128)(2,1)}, bf16[4,2,32,256]{3,2,1,0:T(8,128)(2,1)}) custom-call(s32[4,8]{1,0:T(4,128)} %off_ref.3, s32[4,8]{1,0:T(4,128)} %slot_ref.3, bf16[12,2,32,1024]{3,2,1,0:T(8,128)(2,1)} %pool_hbm.3), custom_call_target="tpu_custom_call" | custom-call | bytes 1048576 | tf_op jit(solution)/shard_map/pallas_call | solution.py:82
  2.9 2.2 %collective-permute-start = (bf16[4,2,32,256]{3,2,1,0:T(8,128)(2,1)}, bf16[4,2,32,256]{3,2,1,0:T(8,128)(2,1)S(1)}, u32[]{:S(2)}, u32[]{:S(2)}) collective-permute-start(bf16[4,2,32,256]{3,2,1,0:T(8,128)(2,1)} %get-tuple-element.17), channel_id=1, source_target_pairs={{0,4},{1,5},{2,6},{3,7},{4,8},{5,9},{6,10},{7,11},{8,12},{9,13},{1... | collective-permute-start | bytes 393224 | tf_op jit(solution)/shard_map/ppermute | solution.py:112
  5.1 3.1 %collective-permute-start.1 = (bf16[4,2,32,256]{3,2,1,0:T(8,128)(2,1)}, bf16[4,2,32,256]{3,2,1,0:T(8,128)(2,1)S(1)}, u32[]{:S(2)}, u32[]{:S(2)}) collective-permute-start(bf16[4,2,32,256]{3,2,1,0:T(8,128)(2,1)} %get-tuple-element.18), channel_id=1, source_target_pairs={{0,5},{1,6},{2,7},{3,4},{4,9},{5,10},{6,11},{7,8},{8,13},{9,14},{1... | collective-permute-start | bytes 393224 | tf_op jit(solution)/shard_map/ppermute | solution.py:112
  8.1 1.3 %collective-permute-start.2 = (bf16[4,2,32,256]{3,2,1,0:T(8,128)(2,1)}, bf16[4,2,32,256]{3,2,1,0:T(8,128)(2,1)S(1)}, u32[]{:S(2)}, u32[]{:S(2)}) collective-permute-start(bf16[4,2,32,256]{3,2,1,0:T(8,128)(2,1)} %get-tuple-element.19), channel_id=1, source_target_pairs={{0,6},{1,7},{2,4},{3,5},{4,10},{5,11},{6,8},{7,9},{8,14},{9,15},{1... | collective-permute-start | bytes 393224 | tf_op jit(solution)/shard_map/ppermute | solution.py:112
  9.4 0.3 collective-permute-start.3
  9.8 3.5 %shard_map.65 = (bf16[4,2,32,256]{3,2,1,0:T(8,128)(2,1)}, bf16[4,2,32,256]{3,2,1,0:T(8,128)(2,1)}, bf16[4,2,32,256]{3,2,1,0:T(8,128)(2,1)}, bf16[4,2,32,256]{3,2...) custom-call(s32[4,8]{1,0:T(4,128)} %off_ref.3, ...), custom_call_target="tpu_custom_call" | custom-call | bytes 2097152 | tf_op jit(solution)/shard_map/pallas_call | solution.py:82
  13.2 1.5 %collective-permute-start.4 = (bf16[4,2,32,256]{3,2,1,0:T(8,128)(2,1)}, bf16[4,2,32,256]{3,2,1,0:T(8,128)(2,1)S(1)}, u32[]{:S(2)}, u32[]{:S(2)}) collective-permute-start(bf16[4,2,32,256]{3,2,1,0:T(8,128)(2,1)} %get-tuple-element.21), channel_id=1, source_target_pairs={{0,8},{1,9},{2,10},{3,11},{4,12},{5,13},{6,14},{7,15},{8,0},{9,1},... | collective-permute-start | bytes 393224 | tf_op jit(solution)/shard_map/ppermute | solution.py:112
  14.8 0.1 add.76
  14.9 0.1 broadcast_add_fusion
  14.9 0.1 add.73
  15.0 0.1 add.74
  15.1 0.6 %dynamic_slice.9 = s32[1]{0:T(128)} dynamic-slice(s32[4]{0:T(128)S(1)} %copy-done.12, s32[]{:T(128)S(6)} %select_n.17), dynamic_slice_sizes={1} | dynamic-slice | bytes 12 | tf_op jit(solution)/shard_map/jit(dynamic_index_in_dim)/dynamic_slice | solution.py:118
  15.7 2.1 %collective-permute-start.5 = (bf16[4,2,32,256]{3,2,1,0:T(8,128)(2,1)}, bf16[4,2,32,256]{3,2,1,0:T(8,128)(2,1)S(1)}, u32[]{:S(2)}, u32[]{:S(2)}) collective-permute-start(bf16[4,2,32,256]{3,2,1,0:T(8,128)(2,1)} %get-tuple-element.22), channel_id=1, source_target_pairs={{0,9},{1,10},{2,11},{3,8},{4,13},{5,14},{6,15},{7,12},{8,1},{9,2},... | collective-permute-start | bytes 393224 | tf_op jit(solution)/shard_map/ppermute | solution.py:112
  17.8 2.9 %collective-permute-start.6 = (bf16[4,2,32,256]{3,2,1,0:T(8,128)(2,1)}, bf16[4,2,32,256]{3,2,1,0:T(8,128)(2,1)S(1)}, u32[]{:S(2)}, u32[]{:S(2)}) collective-permute-start(bf16[4,2,32,256]{3,2,1,0:T(8,128)(2,1)} %get-tuple-element.23), channel_id=1, source_target_pairs={{0,10},{1,11},{2,8},{3,9},{4,14},{5,15},{6,12},{7,13},{8,2},{9,3},... | collective-permute-start | bytes 393224 | tf_op jit(solution)/shard_map/ppermute | solution.py:112
  20.7 1.2 %compare_convert_fusion.vis_ref = s32[8,1,128]{2,1,0:T(1,128)} fusion(s32[8,1,128]{2,1,0:T(1,128)S(1)} %add.74, s32[]{:T(128)} %bitcast.3, s32[128]{0:T(128)S(1)} %add.76), kind=kLoop, calls=%fused_computation | loop fusion | flops 3072 | bytes 8708 | tf_op jit(solution)/shard_map/convert_element_type | solution.py:131
  21.9 0.7 %dynamic-slice_bitcast_fusion = s32[8]{0:T(128)S(1)} fusion(s32[4,8]{1,0:T(4,128)} %off_ref.3, s32[]{:T(128)S(6)} %select_n.17), kind=kLoop, calls=%fused_computation.11 | loop fusion | bytes 68 | tf_op jit(solution)/shard_map/jit(dynamic_index_in_dim)/squeeze | solution.py:117
  22.6 0.0 collective-permute-done.2.rest_2_
  22.6 0.1 collective-permute-start.7
  22.7 0.0 collective-permute-done.3.rest_3_
  22.7 1.2 %collective-permute-start.8 = (bf16[4,2,32,256]{3,2,1,0:T(8,128)(2,1)}, bf16[4,2,32,256]{3,2,1,0:T(8,128)(2,1)S(1)}, u32[]{:S(2)}, u32[]{:S(2)}) collective-permute-start(bf16[4,2,32,256]{3,2,1,0:T(8,128)(2,1)} %get-tuple-element.25), channel_id=1, source_target_pairs={{0,12},{1,13},{2,14},{3,15},{4,0},{5,1},{6,2},{7,3},{8,4},{9,5},{1... | collective-permute-start | bytes 393224 | tf_op jit(solution)/shard_map/ppermute | solution.py:112
  23.9 9.8 %collective-permute-done.4.rest_4_ = bf16[4,2,32,256]{3,2,1,0:T(8,128)(2,1)S(1)} collective-permute-done((bf16[4,2,32,256]{3,2,1,0:T(8,128)(2,1)}, bf16[4,2,32,256]{3,2,1,0:T(8,128)(2,1)S(1)}, u32[]{:S(2)}, u32[]{:S(2)}) %collective-permute-start.4) | collective-permute-done | bytes 131104 | tf_op jit(solution)/shard_map/ppermute | solution.py:112
  33.7 6.2 %collective-permute-start.9 = (bf16[4,2,32,256]{3,2,1,0:T(8,128)(2,1)}, bf16[4,2,32,256]{3,2,1,0:T(8,128)(2,1)S(1)}, u32[]{:S(2)}, u32[]{:S(2)}) collective-permute-start(bf16[4,2,32,256]{3,2,1,0:T(8,128)(2,1)} %get-tuple-element.26), channel_id=1, source_target_pairs={{0,13},{1,14},{2,15},{3,12},{4,1},{5,2},{6,3},{7,0},{8,5},{9,6},{1... | collective-permute-start | bytes 393224 | tf_op jit(solution)/shard_map/ppermute | solution.py:112
  39.9 0.0 collective-permute-done.5.rest_5_
  39.9 2.5 %collective-permute-start.10 = (bf16[4,2,32,256]{3,2,1,0:T(8,128)(2,1)}, bf16[4,2,32,256]{3,2,1,0:T(8,128)(2,1)S(1)}, u32[]{:S(2)}, u32[]{:S(2)}) collective-permute-start(bf16[4,2,32,256]{3,2,1,0:T(8,128)(2,1)} %get-tuple-element.27), channel_id=1, source_target_pairs={{0,14},{1,15},{2,12},{3,13},{4,2},{5,3},{6,0},{7,1},{8,6},{9,7},{1... | collective-permute-start | bytes 393224 | tf_op jit(solution)/shard_map/ppermute | solution.py:112
  42.4 8.7 %collective-permute-start.11 = (bf16[4,2,32,256]{3,2,1,0:T(8,128)(2,1)}, bf16[4,2,32,256]{3,2,1,0:T(8,128)(2,1)S(1)}, u32[]{:S(2)}, u32[]{:S(2)}) collective-permute-start(bf16[4,2,32,256]{3,2,1,0:T(8,128)(2,1)} %get-tuple-element.28), channel_id=1, source_target_pairs={{0,15},{1,12},{2,13},{3,14},{4,3},{5,0},{6,1},{7,2},{8,7},{9,4},{1... | collective-permute-start | bytes 393224 | tf_op jit(solution)/shard_map/ppermute | solution.py:112
  51.1 0.2 select_reduce_fusion
  51.3 0.6 %pad_add_fusion.tab_ref = s32[16]{0:T(128)} fusion(s32[8]{0:T(128)S(1)} %select_reduce_fusion, s32[8]{0:T(128)S(1)} %dynamic-slice_bitcast_fusion), kind=kLoop, calls=%fused_computation.9 | loop fusion | flops 16 | bytes 128 | tf_op jit(solution)/shard_map/concatenate | solution.py:123
  51.9 0.0 collective-permute-done.7.rest_7_
  52.0 0.0 collective-permute-done.9.rest_9_
  52.0 1.4 %collective-permute-done.11.rest_11_ = bf16[4,2,32,256]{3,2,1,0:T(8,128)(2,1)S(1)} collective-permute-done((bf16[4,2,32,256]{3,2,1,0:T(8,128)(2,1)}, bf16[4,2,32,256]{3,2,1,0:T(8,128)(2,1)S(1)}, u32[]{:S(2)}, u32[]{:S(2)}) %collective-permute-start.11) | collective-permute-done | bytes 131104 | tf_op jit(solution)/shard_map/ppermute | solution.py:112
  53.5 0.6 copy-done.11
  54.1 7.8 %shard_map.66 = bf16[128,2048]{1,0:T(8,128)(2,1)} custom-call(s32[16]{0:T(128)} %pad_add_fusion.tab_ref, bf16[128,2048]{1,0:T(8,128)(2,1)} %bitcast.6, bf16[2,128,256]{2,1,0:T(8,128)(2,1)} %bitcast.7, s32[8,1,128]{2,1,0:T(1,128)} %compare_convert_fusion.vis_ref, bf16[4,2,32,256]{3,2,1,0:T(8,128)(2,1)} %copy-done, bf16[4,2,32,256]{3,2,1,0:T(8,128)(2,1)} %copy-done.1, ...), custom_call_target="tpu_custom_call" | custom-call | flops 1207959552 | bytes 2752512 | tf_op jit(solution)/shard_map/pallas_call | solution.py:218
  (33 shorter events, 0.1 us)
Async XLA Ops:
  0.0 15.1 %copy-start.12 = (s32[4]{0:T(128)S(1)}, s32[4]{0:T(128)}, u32[]{:S(2)}) copy-start(s32[4]{0:T(128)} %param.11) | copy-start | bytes 52
  2.9 12.8 %collective-permute-start = (bf16[4,2,32,256]{3,2,1,0:T(8,128)(2,1)}, bf16[4,2,32,256]{3,2,1,0:T(8,128)(2,1)S(1)}, u32[]{:S(2)}, u32[]{:S(2)}) collective-permute-start(bf16[4,2,32,256]{3,2,1,0:T(8,128)(2,1)} %get-tuple-element.17), channel_id=1, source_target_pairs={{0,4},{1,5},{2,6},{3,7},{4,8},{5,9},{6,10},{7,11},{8,12},{9,13},{1... | collective-permute-start | bytes 393224 | tf_op jit(solution)/shard_map/ppermute | solution.py:112
  5.1 12.8 %collective-permute-start.1 = (bf16[4,2,32,256]{3,2,1,0:T(8,128)(2,1)}, bf16[4,2,32,256]{3,2,1,0:T(8,128)(2,1)S(1)}, u32[]{:S(2)}, u32[]{:S(2)}) collective-permute-start(bf16[4,2,32,256]{3,2,1,0:T(8,128)(2,1)} %get-tuple-element.18), channel_id=1, source_target_pairs={{0,5},{1,6},{2,7},{3,4},{4,9},{5,10},{6,11},{7,8},{8,13},{9,14},{1... | collective-permute-start | bytes 393224 | tf_op jit(solution)/shard_map/ppermute | solution.py:112
  8.1 14.5 %collective-permute-start.2 = (bf16[4,2,32,256]{3,2,1,0:T(8,128)(2,1)}, bf16[4,2,32,256]{3,2,1,0:T(8,128)(2,1)S(1)}, u32[]{:S(2)}, u32[]{:S(2)}) collective-permute-start(bf16[4,2,32,256]{3,2,1,0:T(8,128)(2,1)} %get-tuple-element.19), channel_id=1, source_target_pairs={{0,6},{1,7},{2,4},{3,5},{4,10},{5,11},{6,8},{7,9},{8,14},{9,15},{1... | collective-permute-start | bytes 393224 | tf_op jit(solution)/shard_map/ppermute | solution.py:112
  9.4 13.3 %collective-permute-start.3 = (bf16[4,2,32,256]{3,2,1,0:T(8,128)(2,1)}, bf16[4,2,32,256]{3,2,1,0:T(8,128)(2,1)S(1)}, u32[]{:S(2)}, u32[]{:S(2)}) collective-permute-start(bf16[4,2,32,256]{3,2,1,0:T(8,128)(2,1)} %get-tuple-element.20), channel_id=1, source_target_pairs={{0,7},{1,4},{2,5},{3,6},{4,11},{5,8},{6,9},{7,10},{8,15},{9,12},{1... | collective-permute-start | bytes 393224 | tf_op jit(solution)/shard_map/ppermute | solution.py:112
  13.2 20.5 %collective-permute-start.4 = (bf16[4,2,32,256]{3,2,1,0:T(8,128)(2,1)}, bf16[4,2,32,256]{3,2,1,0:T(8,128)(2,1)S(1)}, u32[]{:S(2)}, u32[]{:S(2)}) collective-permute-start(bf16[4,2,32,256]{3,2,1,0:T(8,128)(2,1)} %get-tuple-element.21), channel_id=1, source_target_pairs={{0,8},{1,9},{2,10},{3,11},{4,12},{5,13},{6,14},{7,15},{8,0},{9,1},... | collective-permute-start | bytes 393224 | tf_op jit(solution)/shard_map/ppermute | solution.py:112
  15.7 37.7 %copy-start = (bf16[4,2,32,256]{3,2,1,0:T(8,128)(2,1)}, bf16[4,2,32,256]{3,2,1,0:T(8,128)(2,1)S(1)}, u32[]{:S(2)}) copy-start(bf16[4,2,32,256]{3,2,1,0:T(8,128)(2,1)S(1)} %collective-permute-done.rest_0_) | copy-start | bytes 393220
  15.7 24.2 %collective-permute-start.5 = (bf16[4,2,32,256]{3,2,1,0:T(8,128)(2,1)}, bf16[4,2,32,256]{3,2,1,0:T(8,128)(2,1)S(1)}, u32[]{:S(2)}, u32[]{:S(2)}) collective-permute-start(bf16[4,2,32,256]{3,2,1,0:T(8,128)(2,1)} %get-tuple-element.22), channel_id=1, source_target_pairs={{0,9},{1,10},{2,11},{3,8},{4,13},{5,14},{6,15},{7,12},{8,1},{9,2},... | collective-permute-start | bytes 393224 | tf_op jit(solution)/shard_map/ppermute | solution.py:112
  17.8 35.6 %copy-start.1 = (bf16[4,2,32,256]{3,2,1,0:T(8,128)(2,1)}, bf16[4,2,32,256]{3,2,1,0:T(8,128)(2,1)S(1)}, u32[]{:S(2)}) copy-start(bf16[4,2,32,256]{3,2,1,0:T(8,128)(2,1)S(1)} %collective-permute-done.1.rest_1_) | copy-start | bytes 393220
  17.8 24.6 %collective-permute-start.6 = (bf16[4,2,32,256]{3,2,1,0:T(8,128)(2,1)}, bf16[4,2,32,256]{3,2,1,0:T(8,128)(2,1)S(1)}, u32[]{:S(2)}, u32[]{:S(2)}) collective-permute-start(bf16[4,2,32,256]{3,2,1,0:T(8,128)(2,1)} %get-tuple-element.23), channel_id=1, source_target_pairs={{0,10},{1,11},{2,8},{3,9},{4,14},{5,15},{6,12},{7,13},{8,2},{9,3},... | collective-permute-start | bytes 393224 | tf_op jit(solution)/shard_map/ppermute | solution.py:112
  22.6 30.8 %copy-start.2 = (bf16[4,2,32,256]{3,2,1,0:T(8,128)(2,1)}, bf16[4,2,32,256]{3,2,1,0:T(8,128)(2,1)S(1)}, u32[]{:S(2)}) copy-start(bf16[4,2,32,256]{3,2,1,0:T(8,128)(2,1)S(1)} %collective-permute-done.2.rest_2_) | copy-start | bytes 393220
  22.6 29.3 %collective-permute-start.7 = (bf16[4,2,32,256]{3,2,1,0:T(8,128)(2,1)}, bf16[4,2,32,256]{3,2,1,0:T(8,128)(2,1)S(1)}, u32[]{:S(2)}, u32[]{:S(2)}) collective-permute-start(bf16[4,2,32,256]{3,2,1,0:T(8,128)(2,1)} %get-tuple-element.24), channel_id=1, source_target_pairs={{0,11},{1,8},{2,9},{3,10},{4,15},{5,12},{6,13},{7,14},{8,3},{9,0},... | collective-permute-start | bytes 393224 | tf_op jit(solution)/shard_map/ppermute | solution.py:112
  22.7 30.7 %copy-start.3 = (bf16[4,2,32,256]{3,2,1,0:T(8,128)(2,1)}, bf16[4,2,32,256]{3,2,1,0:T(8,128)(2,1)S(1)}, u32[]{:S(2)}) copy-start(bf16[4,2,32,256]{3,2,1,0:T(8,128)(2,1)S(1)} %collective-permute-done.3.rest_3_) | copy-start | bytes 393220
  22.7 29.2 %collective-permute-start.8 = (bf16[4,2,32,256]{3,2,1,0:T(8,128)(2,1)}, bf16[4,2,32,256]{3,2,1,0:T(8,128)(2,1)S(1)}, u32[]{:S(2)}, u32[]{:S(2)}) collective-permute-start(bf16[4,2,32,256]{3,2,1,0:T(8,128)(2,1)} %get-tuple-element.25), channel_id=1, source_target_pairs={{0,12},{1,13},{2,14},{3,15},{4,0},{5,1},{6,2},{7,3},{8,4},{9,5},{1... | collective-permute-start | bytes 393224 | tf_op jit(solution)/shard_map/ppermute | solution.py:112
  33.7 19.7 %copy-start.4 = (bf16[4,2,32,256]{3,2,1,0:T(8,128)(2,1)}, bf16[4,2,32,256]{3,2,1,0:T(8,128)(2,1)S(1)}, u32[]{:S(2)}) copy-start(bf16[4,2,32,256]{3,2,1,0:T(8,128)(2,1)S(1)} %collective-permute-done.4.rest_4_) | copy-start | bytes 393220
  33.7 18.2 %collective-permute-start.9 = (bf16[4,2,32,256]{3,2,1,0:T(8,128)(2,1)}, bf16[4,2,32,256]{3,2,1,0:T(8,128)(2,1)S(1)}, u32[]{:S(2)}, u32[]{:S(2)}) collective-permute-start(bf16[4,2,32,256]{3,2,1,0:T(8,128)(2,1)} %get-tuple-element.26), channel_id=1, source_target_pairs={{0,13},{1,14},{2,15},{3,12},{4,1},{5,2},{6,3},{7,0},{8,5},{9,6},{1... | collective-permute-start | bytes 393224 | tf_op jit(solution)/shard_map/ppermute | solution.py:112
  39.9 13.5 %copy-start.5 = (bf16[4,2,32,256]{3,2,1,0:T(8,128)(2,1)}, bf16[4,2,32,256]{3,2,1,0:T(8,128)(2,1)S(1)}, u32[]{:S(2)}) copy-start(bf16[4,2,32,256]{3,2,1,0:T(8,128)(2,1)S(1)} %collective-permute-done.5.rest_5_) | copy-start | bytes 393220
  39.9 12.1 %collective-permute-start.10 = (bf16[4,2,32,256]{3,2,1,0:T(8,128)(2,1)}, bf16[4,2,32,256]{3,2,1,0:T(8,128)(2,1)S(1)}, u32[]{:S(2)}, u32[]{:S(2)}) collective-permute-start(bf16[4,2,32,256]{3,2,1,0:T(8,128)(2,1)} %get-tuple-element.27), channel_id=1, source_target_pairs={{0,14},{1,15},{2,12},{3,13},{4,2},{5,3},{6,0},{7,1},{8,6},{9,7},{1... | collective-permute-start | bytes 393224 | tf_op jit(solution)/shard_map/ppermute | solution.py:112
  42.4 11.0 %copy-start.6 = (bf16[4,2,32,256]{3,2,1,0:T(8,128)(2,1)}, bf16[4,2,32,256]{3,2,1,0:T(8,128)(2,1)S(1)}, u32[]{:S(2)}) copy-start(bf16[4,2,32,256]{3,2,1,0:T(8,128)(2,1)S(1)} %collective-permute-done.6.rest_6_) | copy-start | bytes 393220
  42.4 11.0 %collective-permute-start.11 = (bf16[4,2,32,256]{3,2,1,0:T(8,128)(2,1)}, bf16[4,2,32,256]{3,2,1,0:T(8,128)(2,1)S(1)}, u32[]{:S(2)}, u32[]{:S(2)}) collective-permute-start(bf16[4,2,32,256]{3,2,1,0:T(8,128)(2,1)} %get-tuple-element.28), channel_id=1, source_target_pairs={{0,15},{1,12},{2,13},{3,14},{4,3},{5,0},{6,1},{7,2},{8,7},{9,4},{1... | collective-permute-start | bytes 393224 | tf_op jit(solution)/shard_map/ppermute | solution.py:112
  51.9 1.5 %copy-start.7 = (bf16[4,2,32,256]{3,2,1,0:T(8,128)(2,1)}, bf16[4,2,32,256]{3,2,1,0:T(8,128)(2,1)S(1)}, u32[]{:S(2)}) copy-start(bf16[4,2,32,256]{3,2,1,0:T(8,128)(2,1)S(1)} %collective-permute-done.7.rest_7_) | copy-start | bytes 393220
  52.0 1.5 %copy-start.8 = (bf16[4,2,32,256]{3,2,1,0:T(8,128)(2,1)}, bf16[4,2,32,256]{3,2,1,0:T(8,128)(2,1)S(1)}, u32[]{:S(2)}) copy-start(bf16[4,2,32,256]{3,2,1,0:T(8,128)(2,1)S(1)} %collective-permute-done.8.rest_8_) | copy-start | bytes 393220
  52.0 1.5 %copy-start.9 = (bf16[4,2,32,256]{3,2,1,0:T(8,128)(2,1)}, bf16[4,2,32,256]{3,2,1,0:T(8,128)(2,1)S(1)}, u32[]{:S(2)}) copy-start(bf16[4,2,32,256]{3,2,1,0:T(8,128)(2,1)S(1)} %collective-permute-done.9.rest_9_) | copy-start | bytes 393220
  52.0 1.5 %copy-start.10 = (bf16[4,2,32,256]{3,2,1,0:T(8,128)(2,1)}, bf16[4,2,32,256]{3,2,1,0:T(8,128)(2,1)S(1)}, u32[]{:S(2)}) copy-start(bf16[4,2,32,256]{3,2,1,0:T(8,128)(2,1)S(1)} %collective-permute-done.10.rest_10_) | copy-start | bytes 393220
  53.4 0.7 %copy-start.11 = (bf16[4,2,32,256]{3,2,1,0:T(8,128)(2,1)}, bf16[4,2,32,256]{3,2,1,0:T(8,128)(2,1)S(1)}, u32[]{:S(2)}) copy-start(bf16[4,2,32,256]{3,2,1,0:T(8,128)(2,1)S(1)} %collective-permute-done.11.rest_11_) | copy-start | bytes 393220

commit v14 on v12

--- a/solution.py
+++ b/solution.py
@@ -25,7 +25,8 @@
     return matched[:, None, :] * (ranking[:, None, :] == places[None, :, None]).astype(jnp.int32)
 
 
-def gather_kernel(first, last, slot_cap, tensor_count, off_ref, slot_ref, pool_ref, *out_refs):
+def gather_kernel(first, last, slot_cap, tensor_count, off_ref, slot_ref, pool_hbm, *rest):
+    out_refs, sems = rest[:-1], rest[-1]
     replicas, page_count = off_ref.shape
     holder = lax.axis_index("replica")
     me = lax.axis_index("tensor")
@@ -33,6 +34,7 @@
     starts = [
         pl.multiple_of(((me + shift) % tensor_count) * lanes, lanes) for shift in range(tensor_count)
     ]
+    copies = []
     for distance in range(first, last + 1):
         reader = (holder + distance) % replicas
         chosen = [jnp.int32(0)] * slot_cap
@@ -46,9 +48,16 @@
             count = count + matched.astype(jnp.int32)
         for slot in range(slot_cap):
             for shift in range(tensor_count):
-                out_refs[(distance - first) * tensor_count + shift][slot] = pool_ref[
-                    chosen[slot], :, :, pl.ds(starts[shift], lanes)
-                ]
+                index = ((distance - first) * slot_cap + slot) * tensor_count + shift
+                copy = pltpu.make_async_copy(
+                    pool_hbm.at[chosen[slot], :, :, pl.ds(starts[shift], lanes)],
+                    out_refs[(distance - first) * tensor_count + shift].at[slot],
+                    sems.at[index],
+                )
+                copy.start()
+                copies.append(copy)
+    for copy in copies:
+        copy.wait()
 
 
 def pack_pages(pool_part, offsets, slots, first, last, slot_cap, tensor_count):
@@ -60,10 +69,11 @@
     grid_spec = pltpu.PrefetchScalarGridSpec(
         num_scalar_prefetch=2,
         grid=(1,),
-        in_specs=[pl.BlockSpec((pages, kv, rows, width), lambda i, o, s: (0, 0, 0, 0))],
+        in_specs=[pl.BlockSpec(memory_space=pl.ANY)],
         out_specs=[pl.BlockSpec(piece, lambda i, o, s: (0, 0, 0, 0)) for _ in range(count)],
-    )
-    nbytes = 2 * (pool_part.size + span_count * slot_cap * kv * rows * width)
+        scratch_shapes=[pltpu.SemaphoreType.DMA((span_count * slot_cap * tensor_count,))],
+    )
+    nbytes = 2 * 2 * span_count * slot_cap * kv * rows * width
     return pl.pallas_call(
         functools.partial(gather_kernel, first, last, slot_cap, tensor_count),
         grid_spec=grid_spec,

time: 62.4 us -> 62.3 us (level)
  no operation moved by 1% of the time
where the time goes in v14:
time: 62.3 us; the launch traced here: 61.8 us
  starting transfers between devices  32.3 us (52%)
  Pallas kernels  13.9 us (22%)
  waiting for transfers between devices  11.2 us (18%)
  local copies, waits for them, and re-layouts  2.17 us (3%)
  other arithmetic  2.09 us (3%)
    ppermute x12, starting transfers between devices, on_device(): lax.ppermute(payload[(distance - 1) * tensor_count + shift], ('replica',...  32.3 us
    ppermute x12, waiting for transfers between devices, on_device(): lax.ppermute(payload[(distance - 1) * tensor_count + shift], ('replica',...  11.2 us
    pallas_call x1, Pallas kernels, attend(): pl.pallas_call(functools.partial(attention_kernel, span_count, tensor_cou...  7.83 us
    pallas_call x2, Pallas kernels, pack_pages(): pl.pallas_call(functools.partial(gather_kernel, first, last, slot_cap, te...  6.11 us
  transfers between devices with their start and end apart: 12, of which 2 were waited for; matrix products, arithmetic and copies ran while one was open for 6% of the time, Pallas kernels for 5%

profile of v14, /device:TPU:1, one launch (start us, length us, event | category | flops | bytes accessed | tf_op | source)
XLA Modules:
  0.0 61.8 jit_solution(2818415802043293256)
XLA Ops:
  0.0 2.8 %shard_map.64 = (bf16[4,2,32,256]{3,2,1,0:T(8,128)(2,1)}, bf16[4,2,32,256]{3,2,1,0:T(8,128)(2,1)}, bf16[4,2,32,256]{3,2,1,0:T(8,128)(2,1)}, bf16[4,2,32,256]{3,2,1,0:T(8,128)(2,1)}) custom-call(s32[4,8]{1,0:T(4,128)} %off_ref.3, s32[4,8]{1,0:T(4,128)} %slot_ref.3, bf16[12,2,32,1024]{3,2,1,0:T(8,128)(2,1)} %pool_hbm.3), custom_call_target="tpu_custom_call" | custom-call | bytes 1048576 | tf_op jit(solution)/shard_map/pallas_call | solution.py:77
  2.8 2.2 %collective-permute-start = (bf16[4,2,32,256]{3,2,1,0:T(8,128)(2,1)}, bf16[4,2,32,256]{3,2,1,0:T(8,128)(2,1)S(1)}, u32[]{:S(2)}, u32[]{:S(2)}) collective-permute-start(bf16[4,2,32,256]{3,2,1,0:T(8,128)(2,1)} %get-tuple-element.17), channel_id=1, source_target_pairs={{0,4},{1,5},{2,6},{3,7},{4,8},{5,9},{6,10},{7,11},{8,12},{9,13},{1... | collective-permute-start | bytes 393224 | tf_op jit(solution)/shard_map/ppermute | solution.py:107
  5.0 3.1 %collective-permute-start.1 = (bf16[4,2,32,256]{3,2,1,0:T(8,128)(2,1)}, bf16[4,2,32,256]{3,2,1,0:T(8,128)(2,1)S(1)}, u32[]{:S(2)}, u32[]{:S(2)}) collective-permute-start(bf16[4,2,32,256]{3,2,1,0:T(8,128)(2,1)} %get-tuple-element.18), channel_id=1, source_target_pairs={{0,5},{1,6},{2,7},{3,4},{4,9},{5,10},{6,11},{7,8},{8,13},{9,14},{1... | collective-permute-start | bytes 393224 | tf_op jit(solution)/shard_map/ppermute | solution.py:107
  8.1 1.3 %collective-permute-start.2 = (bf16[4,2,32,256]{3,2,1,0:T(8,128)(2,1)}, bf16[4,2,32,256]{3,2,1,0:T(8,128)(2,1)S(1)}, u32[]{:S(2)}, u32[]{:S(2)}) collective-permute-start(bf16[4,2,32,256]{3,2,1,0:T(8,128)(2,1)} %get-tuple-element.19), channel_id=1, source_target_pairs={{0,6},{1,7},{2,4},{3,5},{4,10},{5,11},{6,8},{7,9},{8,14},{9,15},{1... | collective-permute-start | bytes 393224 | tf_op jit(solution)/shard_map/ppermute | solution.py:107
  9.4 0.3 collective-permute-start.3
  9.7 3.3 %shard_map.65 = (bf16[4,2,32,256]{3,2,1,0:T(8,128)(2,1)}, bf16[4,2,32,256]{3,2,1,0:T(8,128)(2,1)}, bf16[4,2,32,256]{3,2,1,0:T(8,128)(2,1)}, bf16[4,2,32,256]{3,2...) custom-call(s32[4,8]{1,0:T(4,128)} %off_ref.3, ...), custom_call_target="tpu_custom_call" | custom-call | bytes 2097152 | tf_op jit(solution)/shard_map/pallas_call | solution.py:77
  13.0 1.9 %collective-permute-start.4 = (bf16[4,2,32,256]{3,2,1,0:T(8,128)(2,1)}, bf16[4,2,32,256]{3,2,1,0:T(8,128)(2,1)S(1)}, u32[]{:S(2)}, u32[]{:S(2)}) collective-permute-start(bf16[4,2,32,256]{3,2,1,0:T(8,128)(2,1)} %get-tuple-element.21), channel_id=1, source_target_pairs={{0,8},{1,9},{2,10},{3,11},{4,12},{5,13},{6,14},{7,15},{8,0},{9,1},... | collective-permute-start | bytes 393224 | tf_op jit(solution)/shard_map/ppermute | solution.py:107
  14.9 0.1 add.76
  15.0 0.1 broadcast_add_fusion
  15.1 0.1 add.73
  15.2 0.1 add.74
  15.3 0.6 %dynamic_slice.9 = s32[1]{0:T(128)} dynamic-slice(s32[4]{0:T(128)S(1)} %copy-done.12, s32[]{:T(128)S(6)} %select_n.17), dynamic_slice_sizes={1} | dynamic-slice | bytes 12 | tf_op jit(solution)/shard_map/jit(dynamic_index_in_dim)/dynamic_slice | solution.py:113
  15.9 0.0 collective-permute-done.rest_0_
  15.9 1.7 %collective-permute-start.5 = (bf16[4,2,32,256]{3,2,1,0:T(8,128)(2,1)}, bf16[4,2,32,256]{3,2,1,0:T(8,128)(2,1)S(1)}, u32[]{:S(2)}, u32[]{:S(2)}) collective-permute-start(bf16[4,2,32,256]{3,2,1,0:T(8,128)(2,1)} %get-tuple-element.22), channel_id=1, source_target_pairs={{0,9},{1,10},{2,11},{3,8},{4,13},{5,14},{6,15},{7,12},{8,1},{9,2},... | collective-permute-start | bytes 393224 | tf_op jit(solution)/shard_map/ppermute | solution.py:107
  17.6 0.0 collective-permute-done.1.rest_1_
  17.6 3.3 %collective-permute-start.6 = (bf16[4,2,32,256]{3,2,1,0:T(8,128)(2,1)}, bf16[4,2,32,256]{3,2,1,0:T(8,128)(2,1)S(1)}, u32[]{:S(2)}, u32[]{:S(2)}) collective-permute-start(bf16[4,2,32,256]{3,2,1,0:T(8,128)(2,1)} %get-tuple-element.23), channel_id=1, source_target_pairs={{0,10},{1,11},{2,8},{3,9},{4,14},{5,15},{6,12},{7,13},{8,2},{9,3},... | collective-permute-start | bytes 393224 | tf_op jit(solution)/shard_map/ppermute | solution.py:107
  20.9 1.2 %compare_convert_fusion.vis_ref = s32[8,1,128]{2,1,0:T(1,128)} fusion(s32[8,1,128]{2,1,0:T(1,128)S(1)} %add.74, s32[]{:T(128)} %bitcast.3, s32[128]{0:T(128)S(1)} %add.76), kind=kLoop, calls=%fused_computation | loop fusion | flops 3072 | bytes 8708 | tf_op jit(solution)/shard_map/convert_element_type | solution.py:126
  22.1 0.7 %dynamic-slice_bitcast_fusion = s32[8]{0:T(128)S(1)} fusion(s32[4,8]{1,0:T(4,128)} %off_ref.3, s32[]{:T(128)S(6)} %select_n.17), kind=kLoop, calls=%fused_computation.11 | loop fusion | bytes 68 | tf_op jit(solution)/shard_map/jit(dynamic_index_in_dim)/squeeze | solution.py:112
  22.8 0.0 collective-permute-done.2.rest_2_
  22.8 0.1 collective-permute-start.7
  22.9 1.0 %collective-permute-start.8 = (bf16[4,2,32,256]{3,2,1,0:T(8,128)(2,1)}, bf16[4,2,32,256]{3,2,1,0:T(8,128)(2,1)S(1)}, u32[]{:S(2)}, u32[]{:S(2)}) collective-permute-start(bf16[4,2,32,256]{3,2,1,0:T(8,128)(2,1)} %get-tuple-element.25), channel_id=1, source_target_pairs={{0,12},{1,13},{2,14},{3,15},{4,0},{5,1},{6,2},{7,3},{8,4},{9,5},{1... | collective-permute-start | bytes 393224 | tf_op jit(solution)/shard_map/ppermute | solution.py:107
  23.9 9.8 %collective-permute-done.4.rest_4_ = bf16[4,2,32,256]{3,2,1,0:T(8,128)(2,1)S(1)} collective-permute-done((bf16[4,2,32,256]{3,2,1,0:T(8,128)(2,1)}, bf16[4,2,32,256]{3,2,1,0:T(8,128)(2,1)S(1)}, u32[]{:S(2)}, u32[]{:S(2)}) %collective-permute-start.4) | collective-permute-done | bytes 131104 | tf_op jit(solution)/shard_map/ppermute | solution.py:107
  33.7 6.2 %collective-permute-start.9 = (bf16[4,2,32,256]{3,2,1,0:T(8,128)(2,1)}, bf16[4,2,32,256]{3,2,1,0:T(8,128)(2,1)S(1)}, u32[]{:S(2)}, u32[]{:S(2)}) collective-permute-start(bf16[4,2,32,256]{3,2,1,0:T(8,128)(2,1)} %get-tuple-element.26), channel_id=1, source_target_pairs={{0,13},{1,14},{2,15},{3,12},{4,1},{5,2},{6,3},{7,0},{8,5},{9,6},{1... | collective-permute-start | bytes 393224 | tf_op jit(solution)/shard_map/ppermute | solution.py:107
  39.9 2.5 %collective-permute-start.10 = (bf16[4,2,32,256]{3,2,1,0:T(8,128)(2,1)}, bf16[4,2,32,256]{3,2,1,0:T(8,128)(2,1)S(1)}, u32[]{:S(2)}, u32[]{:S(2)}) collective-permute-start(bf16[4,2,32,256]{3,2,1,0:T(8,128)(2,1)} %get-tuple-element.27), channel_id=1, source_target_pairs={{0,14},{1,15},{2,12},{3,13},{4,2},{5,3},{6,0},{7,1},{8,6},{9,7},{1... | collective-permute-start | bytes 393224 | tf_op jit(solution)/shard_map/ppermute | solution.py:107
  42.4 0.0 collective-permute-done.6.rest_6_
  42.4 8.7 %collective-permute-start.11 = (bf16[4,2,32,256]{3,2,1,0:T(8,128)(2,1)}, bf16[4,2,32,256]{3,2,1,0:T(8,128)(2,1)S(1)}, u32[]{:S(2)}, u32[]{:S(2)}) collective-permute-start(bf16[4,2,32,256]{3,2,1,0:T(8,128)(2,1)} %get-tuple-element.28), channel_id=1, source_target_pairs={{0,15},{1,12},{2,13},{3,14},{4,3},{5,0},{6,1},{7,2},{8,7},{9,4},{1... | collective-permute-start | bytes 393224 | tf_op jit(solution)/shard_map/ppermute | solution.py:107
  51.1 0.2 select_reduce_fusion
  51.3 0.6 %pad_add_fusion.tab_ref = s32[16]{0:T(128)} fusion(s32[8]{0:T(128)S(1)} %select_reduce_fusion, s32[8]{0:T(128)S(1)} %dynamic-slice_bitcast_fusion), kind=kLoop, calls=%fused_computation.9 | loop fusion | flops 16 | bytes 128 | tf_op jit(solution)/shard_map/concatenate | solution.py:118
  51.9 0.0 collective-permute-done.9.rest_9_
  52.0 1.4 %collective-permute-done.11.rest_11_ = bf16[4,2,32,256]{3,2,1,0:T(8,128)(2,1)S(1)} collective-permute-done((bf16[4,2,32,256]{3,2,1,0:T(8,128)(2,1)}, bf16[4,2,32,256]{3,2,1,0:T(8,128)(2,1)S(1)}, u32[]{:S(2)}, u32[]{:S(2)}) %collective-permute-start.11) | collective-permute-done | bytes 131104 | tf_op jit(solution)/shard_map/ppermute | solution.py:107
  53.5 0.6 copy-done.11
  54.0 7.8 %shard_map.66 = bf16[128,2048]{1,0:T(8,128)(2,1)} custom-call(s32[16]{0:T(128)} %pad_add_fusion.tab_ref, bf16[128,2048]{1,0:T(8,128)(2,1)} %bitcast.6, bf16[2,128,256]{2,1,0:T(8,128)(2,1)} %bitcast.7, s32[8,1,128]{2,1,0:T(1,128)} %compare_convert_fusion.vis_ref, bf16[4,2,32,256]{3,2,1,0:T(8,128)(2,1)} %copy-done, bf16[4,2,32,256]{3,2,1,0:T(8,128)(2,1)} %copy-done.1, ...), custom_call_target="tpu_custom_call" | custom-call | flops 1207959552 | bytes 2752512 | tf_op jit(solution)/shard_map/pallas_call | solution.py:213
  (33 shorter events, 0.1 us)
Async XLA Ops:
  0.0 15.3 %copy-start.12 = (s32[4]{0:T(128)S(1)}, s32[4]{0:T(128)}, u32[]{:S(2)}) copy-start(s32[4]{0:T(128)} %param.11) | copy-start | bytes 52
  2.8 13.0 %collective-permute-start = (bf16[4,2,32,256]{3,2,1,0:T(8,128)(2,1)}, bf16[4,2,32,256]{3,2,1,0:T(8,128)(2,1)S(1)}, u32[]{:S(2)}, u32[]{:S(2)}) collective-permute-start(bf16[4,2,32,256]{3,2,1,0:T(8,128)(2,1)} %get-tuple-element.17), channel_id=1, source_target_pairs={{0,4},{1,5},{2,6},{3,7},{4,8},{5,9},{6,10},{7,11},{8,12},{9,13},{1... | collective-permute-start | bytes 393224 | tf_op jit(solution)/shard_map/ppermute | solution.py:107
  5.0 12.5 %collective-permute-start.1 = (bf16[4,2,32,256]{3,2,1,0:T(8,128)(2,1)}, bf16[4,2,32,256]{3,2,1,0:T(8,128)(2,1)S(1)}, u32[]{:S(2)}, u32[]{:S(2)}) collective-permute-start(bf16[4,2,32,256]{3,2,1,0:T(8,128)(2,1)} %get-tuple-element.18), channel_id=1, source_target_pairs={{0,5},{1,6},{2,7},{3,4},{4,9},{5,10},{6,11},{7,8},{8,13},{9,14},{1... | collective-permute-start | bytes 393224 | tf_op jit(solution)/shard_map/ppermute | solution.py:107
  8.1 14.7 %collective-permute-start.2 = (bf16[4,2,32,256]{3,2,1,0:T(8,128)(2,1)}, bf16[4,2,32,256]{3,2,1,0:T(8,128)(2,1)S(1)}, u32[]{:S(2)}, u32[]{:S(2)}) collective-permute-start(bf16[4,2,32,256]{3,2,1,0:T(8,128)(2,1)} %get-tuple-element.19), channel_id=1, source_target_pairs={{0,6},{1,7},{2,4},{3,5},{4,10},{5,11},{6,8},{7,9},{8,14},{9,15},{1... | collective-permute-start | bytes 393224 | tf_op jit(solution)/shard_map/ppermute | solution.py:107
  9.4 13.5 %collective-permute-start.3 = (bf16[4,2,32,256]{3,2,1,0:T(8,128)(2,1)}, bf16[4,2,32,256]{3,2,1,0:T(8,128)(2,1)S(1)}, u32[]{:S(2)}, u32[]{:S(2)}) collective-permute-start(bf16[4,2,32,256]{3,2,1,0:T(8,128)(2,1)} %get-tuple-element.20), channel_id=1, source_target_pairs={{0,7},{1,4},{2,5},{3,6},{4,11},{5,8},{6,9},{7,10},{8,15},{9,12},{1... | collective-permute-start | bytes 393224 | tf_op jit(solution)/shard_map/ppermute | solution.py:107
  13.0 20.7 %collective-permute-start.4 = (bf16[4,2,32,256]{3,2,1,0:T(8,128)(2,1)}, bf16[4,2,32,256]{3,2,1,0:T(8,128)(2,1)S(1)}, u32[]{:S(2)}, u32[]{:S(2)}) collective-permute-start(bf16[4,2,32,256]{3,2,1,0:T(8,128)(2,1)} %get-tuple-element.21), channel_id=1, source_target_pairs={{0,8},{1,9},{2,10},{3,11},{4,12},{5,13},{6,14},{7,15},{8,0},{9,1},... | collective-permute-start | bytes 393224 | tf_op jit(solution)/shard_map/ppermute | solution.py:107
  15.9 37.5 %copy-start = (bf16[4,2,32,256]{3,2,1,0:T(8,128)(2,1)}, bf16[4,2,32,256]{3,2,1,0:T(8,128)(2,1)S(1)}, u32[]{:S(2)}) copy-start(bf16[4,2,32,256]{3,2,1,0:T(8,128)(2,1)S(1)} %collective-permute-done.rest_0_) | copy-start | bytes 393220
  15.9 24.0 %collective-permute-start.5 = (bf16[4,2,32,256]{3,2,1,0:T(8,128)(2,1)}, bf16[4,2,32,256]{3,2,1,0:T(8,128)(2,1)S(1)}, u32[]{:S(2)}, u32[]{:S(2)}) collective-permute-start(bf16[4,2,32,256]{3,2,1,0:T(8,128)(2,1)} %get-tuple-element.22), channel_id=1, source_target_pairs={{0,9},{1,10},{2,11},{3,8},{4,13},{5,14},{6,15},{7,12},{8,1},{9,2},... | collective-permute-start | bytes 393224 | tf_op jit(solution)/shard_map/ppermute | solution.py:107
  17.6 35.8 %copy-start.1 = (bf16[4,2,32,256]{3,2,1,0:T(8,128)(2,1)}, bf16[4,2,32,256]{3,2,1,0:T(8,128)(2,1)S(1)}, u32[]{:S(2)}) copy-start(bf16[4,2,32,256]{3,2,1,0:T(8,128)(2,1)S(1)} %collective-permute-done.1.rest_1_) | copy-start | bytes 393220
  17.6 24.8 %collective-permute-start.6 = (bf16[4,2,32,256]{3,2,1,0:T(8,128)(2,1)}, bf16[4,2,32,256]{3,2,1,0:T(8,128)(2,1)S(1)}, u32[]{:S(2)}, u32[]{:S(2)}) collective-permute-start(bf16[4,2,32,256]{3,2,1,0:T(8,128)(2,1)} %get-tuple-element.23), channel_id=1, source_target_pairs={{0,10},{1,11},{2,8},{3,9},{4,14},{5,15},{6,12},{7,13},{8,2},{9,3},... | collective-permute-start | bytes 393224 | tf_op jit(solution)/shard_map/ppermute | solution.py:107
  22.8 30.6 %copy-start.2 = (bf16[4,2,32,256]{3,2,1,0:T(8,128)(2,1)}, bf16[4,2,32,256]{3,2,1,0:T(8,128)(2,1)S(1)}, u32[]{:S(2)}) copy-start(bf16[4,2,32,256]{3,2,1,0:T(8,128)(2,1)S(1)} %collective-permute-done.2.rest_2_) | copy-start | bytes 393220
  22.8 29.1 %collective-permute-start.7 = (bf16[4,2,32,256]{3,2,1,0:T(8,128)(2,1)}, bf16[4,2,32,256]{3,2,1,0:T(8,128)(2,1)S(1)}, u32[]{:S(2)}, u32[]{:S(2)}) collective-permute-start(bf16[4,2,32,256]{3,2,1,0:T(8,128)(2,1)} %get-tuple-element.24), channel_id=1, source_target_pairs={{0,11},{1,8},{2,9},{3,10},{4,15},{5,12},{6,13},{7,14},{8,3},{9,0},... | collective-permute-start | bytes 393224 | tf_op jit(solution)/shard_map/ppermute | solution.py:107
  22.9 30.5 %copy-start.3 = (bf16[4,2,32,256]{3,2,1,0:T(8,128)(2,1)}, bf16[4,2,32,256]{3,2,1,0:T(8,128)(2,1)S(1)}, u32[]{:S(2)}) copy-start(bf16[4,2,32,256]{3,2,1,0:T(8,128)(2,1)S(1)} %collective-permute-done.3.rest_3_) | copy-start | bytes 393220
  22.9 29.0 %collective-permute-start.8 = (bf16[4,2,32,256]{3,2,1,0:T(8,128)(2,1)}, bf16[4,2,32,256]{3,2,1,0:T(8,128)(2,1)S(1)}, u32[]{:S(2)}, u32[]{:S(2)}) collective-permute-start(bf16[4,2,32,256]{3,2,1,0:T(8,128)(2,1)} %get-tuple-element.25), channel_id=1, source_target_pairs={{0,12},{1,13},{2,14},{3,15},{4,0},{5,1},{6,2},{7,3},{8,4},{9,5},{1... | collective-permute-start | bytes 393224 | tf_op jit(solution)/shard_map/ppermute | solution.py:107
  33.7 19.7 %copy-start.4 = (bf16[4,2,32,256]{3,2,1,0:T(8,128)(2,1)}, bf16[4,2,32,256]{3,2,1,0:T(8,128)(2,1)S(1)}, u32[]{:S(2)}) copy-start(bf16[4,2,32,256]{3,2,1,0:T(8,128)(2,1)S(1)} %collective-permute-done.4.rest_4_) | copy-start | bytes 393220
  33.7 18.2 %collective-permute-start.9 = (bf16[4,2,32,256]{3,2,1,0:T(8,128)(2,1)}, bf16[4,2,32,256]{3,2,1,0:T(8,128)(2,1)S(1)}, u32[]{:S(2)}, u32[]{:S(2)}) collective-permute-start(bf16[4,2,32,256]{3,2,1,0:T(8,128)(2,1)} %get-tuple-element.26), channel_id=1, source_target_pairs={{0,13},{1,14},{2,15},{3,12},{4,1},{5,2},{6,3},{7,0},{8,5},{9,6},{1... | collective-permute-start | bytes 393224 | tf_op jit(solution)/shard_map/ppermute | solution.py:107
  39.9 13.5 %copy-start.5 = (bf16[4,2,32,256]{3,2,1,0:T(8,128)(2,1)}, bf16[4,2,32,256]{3,2,1,0:T(8,128)(2,1)S(1)}, u32[]{:S(2)}) copy-start(bf16[4,2,32,256]{3,2,1,0:T(8,128)(2,1)S(1)} %collective-permute-done.5.rest_5_) | copy-start | bytes 393220
  39.9 12.1 %collective-permute-start.10 = (bf16[4,2,32,256]{3,2,1,0:T(8,128)(2,1)}, bf16[4,2,32,256]{3,2,1,0:T(8,128)(2,1)S(1)}, u32[]{:S(2)}, u32[]{:S(2)}) collective-permute-start(bf16[4,2,32,256]{3,2,1,0:T(8,128)(2,1)} %get-tuple-element.27), channel_id=1, source_target_pairs={{0,14},{1,15},{2,12},{3,13},{4,2},{5,3},{6,0},{7,1},{8,6},{9,7},{1... | collective-permute-start | bytes 393224 | tf_op jit(solution)/shard_map/ppermute | solution.py:107
  42.4 11.0 %copy-start.6 = (bf16[4,2,32,256]{3,2,1,0:T(8,128)(2,1)}, bf16[4,2,32,256]{3,2,1,0:T(8,128)(2,1)S(1)}, u32[]{:S(2)}) copy-start(bf16[4,2,32,256]{3,2,1,0:T(8,128)(2,1)S(1)} %collective-permute-done.6.rest_6_) | copy-start | bytes 393220
  42.4 11.0 %collective-permute-start.11 = (bf16[4,2,32,256]{3,2,1,0:T(8,128)(2,1)}, bf16[4,2,32,256]{3,2,1,0:T(8,128)(2,1)S(1)}, u32[]{:S(2)}, u32[]{:S(2)}) collective-permute-start(bf16[4,2,32,256]{3,2,1,0:T(8,128)(2,1)} %get-tuple-element.28), channel_id=1, source_target_pairs={{0,15},{1,12},{2,13},{3,14},{4,3},{5,0},{6,1},{7,2},{8,7},{9,4},{1... | collective-permute-start | bytes 393224 | tf_op jit(solution)/shard_map/ppermute | solution.py:107
  51.9 1.5 %copy-start.7 = (bf16[4,2,32,256]{3,2,1,0:T(8,128)(2,1)}, bf16[4,2,32,256]{3,2,1,0:T(8,128)(2,1)S(1)}, u32[]{:S(2)}) copy-start(bf16[4,2,32,256]{3,2,1,0:T(8,128)(2,1)S(1)} %collective-permute-done.7.rest_7_) | copy-start | bytes 393220
  51.9 1.5 %copy-start.8 = (bf16[4,2,32,256]{3,2,1,0:T(8,128)(2,1)}, bf16[4,2,32,256]{3,2,1,0:T(8,128)(2,1)S(1)}, u32[]{:S(2)}) copy-start(bf16[4,2,32,256]{3,2,1,0:T(8,128)(2,1)S(1)} %collective-permute-done.8.rest_8_) | copy-start | bytes 393220
  51.9 1.5 %copy-start.9 = (bf16[4,2,32,256]{3,2,1,0:T(8,128)(2,1)}, bf16[4,2,32,256]{3,2,1,0:T(8,128)(2,1)S(1)}, u32[]{:S(2)}) copy-start(bf16[4,2,32,256]{3,2,1,0:T(8,128)(2,1)S(1)} %collective-permute-done.9.rest_9_) | copy-start | bytes 393220
  52.0 1.5 %copy-start.10 = (bf16[4,2,32,256]{3,2,1,0:T(8,128)(2,1)}, bf16[4,2,32,256]{3,2,1,0:T(8,128)(2,1)S(1)}, u32[]{:S(2)}) copy-start(bf16[4,2,32,256]{3,2,1,0:T(8,128)(2,1)S(1)} %collective-permute-done.10.rest_10_) | copy-start | bytes 393220
  53.4 0.7 %copy-start.11 = (bf16[4,2,32,256]{3,2,1,0:T(8,128)(2,1)}, bf16[4,2,32,256]{3,2,1,0:T(8,128)(2,1)S(1)}, u32[]{:S(2)}) copy-start(bf16[4,2,32,256]{3,2,1,0:T(8,128)(2,1)S(1)} %collective-permute-done.11.rest_11_) | copy-start | bytes 393220

commit v15 on v14

--- a/solution.py
+++ b/solution.py
@@ -129,8 +129,26 @@
 
 
 def attention_kernel(span_count, tensor_count, tab_ref, q_ref, suf_ref, vis_ref, *rest):
-    chunk_refs, o_ref = rest[:-1], rest[-1]
+    chunk_refs, o_ref, page_buf, sems = rest[:-3], rest[-3], rest[-2], rest[-1]
     page_count = vis_ref.shape[0]
+    for page in range(page_count):
+        distance, slot = tab_ref[page], tab_ref[page_count + page]
+        for shift in range(tensor_count):
+            for d in range(1, span_count + 1):
+
+                @pl.when(distance == d)
+                def _():
+                    pltpu.make_async_copy(
+                        chunk_refs[(d - 1) * tensor_count + shift].at[slot],
+                        page_buf.at[page, shift],
+                        sems.at[page * tensor_count + shift],
+                    ).start()
+
+    for page in range(page_count):
+        for shift in range(tensor_count):
+            pltpu.make_async_copy(
+                chunk_refs[shift].at[0], page_buf.at[page, shift], sems.at[page * tensor_count + shift]
+            ).wait()
     rows, width = q_ref.shape
     group = HEADS // KV_HEADS
     kv_local = width // (group * HEAD_DIM)
@@ -146,15 +164,9 @@
         )
 
         def page_part(page, part):
-            distance, slot = tab_ref[page], tab_ref[page_count + page]
-            pieces = []
-            for shift in range(tensor_count):
-                piece = chunk_refs[shift][slot, part, :, lanes]
-                for d in range(2, span_count + 1):
-                    other = chunk_refs[(d - 1) * tensor_count + shift][slot, part, :, lanes]
-                    piece = jnp.where(distance == d, other, piece)
-                pieces.append(piece)
-            return jnp.concatenate(pieces, axis=0)
+            return jnp.concatenate(
+                [page_buf[page, shift, part, :, lanes] for shift in range(tensor_count)], axis=0
+            )
 
         keys = [suf_ref[0, :, lanes]]
         vals = [suf_ref[1, :, lanes]]
@@ -204,11 +216,18 @@
     def whole(a):
         return pl.BlockSpec(a.shape, lambda i, t: (0,) * a.ndim)
 
+    page_count = visible.shape[0]
+    slot_cap, kv, quarter, lanes = chunks[0].shape
     grid_spec = pltpu.PrefetchScalarGridSpec(
         num_scalar_prefetch=1,
         grid=(1,),
-        in_specs=[whole(q), whole(suf), whole(visible)] + [whole(c) for c in chunks],
+        in_specs=[whole(q), whole(suf), whole(visible)]
+        + [pl.BlockSpec(memory_space=pl.ANY) for _ in chunks],
         out_specs=pl.BlockSpec((rows, width), lambda i, t: (0, 0)),
+        scratch_shapes=[
+            pltpu.VMEM((page_count, tensor_count, kv, quarter, lanes), chunks[0].dtype),
+            pltpu.SemaphoreType.DMA((page_count * tensor_count,)),
+        ],
     )
     return pl.pallas_call(
         functools.partial(attention_kernel, span_count, tensor_count),

time: 62.3 us -> 63.6 us (1.021); the launches traced: 61.8 us -> 62.5 us
  Pallas kernels: 13.9 us -> 14.6 us
where the time goes in v15:
time: 63.6 us; the launch traced here: 62.5 us
  starting transfers between devices  32.2 us (51%)
  Pallas kernels  14.6 us (23%)
  waiting for transfers between devices  11.2 us (18%)
  local copies, waits for them, and re-layouts  2.17 us (3%)
  other arithmetic  2.09 us (3%)
    ppermute x12, starting transfers between devices, on_device(): lax.ppermute(payload[(distance - 1) * tensor_count + shift], ('replica',...  32.2 us
    ppermute x12, waiting for transfers between devices, on_device(): lax.ppermute(payload[(distance - 1) * tensor_count + shift], ('replica',...  11.2 us
    pallas_call x1, Pallas kernels, attend(): pl.pallas_call(functools.partial(attention_kernel, span_count, tensor_cou...  8.46 us
    pallas_call x2, Pallas kernels, pack_pages(): pl.pallas_call(functools.partial(gather_kernel, first, last, slot_cap, te...  6.13 us
  transfers between devices with their start and end apart: 12, of which 2 were waited for; matrix products, arithmetic and copies ran while one was open for 6% of the time, Pallas kernels for 5%

profile of v15, /device:TPU:1, one launch (start us, length us, event | category | flops | bytes accessed | tf_op | source)
XLA Modules:
  0.0 62.5 jit_solution(9229301697446391173)
XLA Ops:
  0.0 2.9 %shard_map.64 = (bf16[4,2,32,256]{3,2,1,0:T(8,128)(2,1)}, bf16[4,2,32,256]{3,2,1,0:T(8,128)(2,1)}, bf16[4,2,32,256]{3,2,1,0:T(8,128)(2,1)}, bf16[4,2,32,256]{3,2,1,0:T(8,128)(2,1)}) custom-call(s32[4,8]{1,0:T(4,128)} %off_ref.3, s32[4,8]{1,0:T(4,128)} %slot_ref.3, bf16[12,2,32,1024]{3,2,1,0:T(8,128)(2,1)} %pool_hbm.3), custom_call_target="tpu_custom_call" | custom-call | bytes 1048576 | tf_op jit(solution)/shard_map/pallas_call | solution.py:77
  2.9 2.1 %collective-permute-start = (bf16[4,2,32,256]{3,2,1,0:T(8,128)(2,1)}, bf16[4,2,32,256]{3,2,1,0:T(8,128)(2,1)S(1)}, u32[]{:S(2)}, u32[]{:S(2)}) collective-permute-start(bf16[4,2,32,256]{3,2,1,0:T(8,128)(2,1)} %get-tuple-element.17), channel_id=1, source_target_pairs={{0,4},{1,5},{2,6},{3,7},{4,8},{5,9},{6,10},{7,11},{8,12},{9,13},{1... | collective-permute-start | bytes 393224 | tf_op jit(solution)/shard_map/ppermute | solution.py:107
  5.0 3.1 %collective-permute-start.1 = (bf16[4,2,32,256]{3,2,1,0:T(8,128)(2,1)}, bf16[4,2,32,256]{3,2,1,0:T(8,128)(2,1)S(1)}, u32[]{:S(2)}, u32[]{:S(2)}) collective-permute-start(bf16[4,2,32,256]{3,2,1,0:T(8,128)(2,1)} %get-tuple-element.18), channel_id=1, source_target_pairs={{0,5},{1,6},{2,7},{3,4},{4,9},{5,10},{6,11},{7,8},{8,13},{9,14},{1... | collective-permute-start | bytes 393224 | tf_op jit(solution)/shard_map/ppermute | solution.py:107
  8.1 1.3 %collective-permute-start.2 = (bf16[4,2,32,256]{3,2,1,0:T(8,128)(2,1)}, bf16[4,2,32,256]{3,2,1,0:T(8,128)(2,1)S(1)}, u32[]{:S(2)}, u32[]{:S(2)}) collective-permute-start(bf16[4,2,32,256]{3,2,1,0:T(8,128)(2,1)} %get-tuple-element.19), channel_id=1, source_target_pairs={{0,6},{1,7},{2,4},{3,5},{4,10},{5,11},{6,8},{7,9},{8,14},{9,15},{1... | collective-permute-start | bytes 393224 | tf_op jit(solution)/shard_map/ppermute | solution.py:107
  9.4 0.3 collective-permute-start.3
  9.7 3.2 %shard_map.65 = (bf16[4,2,32,256]{3,2,1,0:T(8,128)(2,1)}, bf16[4,2,32,256]{3,2,1,0:T(8,128)(2,1)}, bf16[4,2,32,256]{3,2,1,0:T(8,128)(2,1)}, bf16[4,2,32,256]{3,2...) custom-call(s32[4,8]{1,0:T(4,128)} %off_ref.3, ...), custom_call_target="tpu_custom_call" | custom-call | bytes 2097152 | tf_op jit(solution)/shard_map/pallas_call | solution.py:77
  12.9 1.9 %collective-permute-start.4 = (bf16[4,2,32,256]{3,2,1,0:T(8,128)(2,1)}, bf16[4,2,32,256]{3,2,1,0:T(8,128)(2,1)S(1)}, u32[]{:S(2)}, u32[]{:S(2)}) collective-permute-start(bf16[4,2,32,256]{3,2,1,0:T(8,128)(2,1)} %get-tuple-element.21), channel_id=1, source_target_pairs={{0,8},{1,9},{2,10},{3,11},{4,12},{5,13},{6,14},{7,15},{8,0},{9,1},... | collective-permute-start | bytes 393224 | tf_op jit(solution)/shard_map/ppermute | solution.py:107
  14.9 0.1 add.76
  14.9 0.1 broadcast_add_fusion
  15.0 0.1 add.73
  15.1 0.1 add.74
  15.2 0.6 dynamic_slice.9
  15.8 0.0 collective-permute-done.rest_0_
  15.8 1.7 %collective-permute-start.5 = (bf16[4,2,32,256]{3,2,1,0:T(8,128)(2,1)}, bf16[4,2,32,256]{3,2,1,0:T(8,128)(2,1)S(1)}, u32[]{:S(2)}, u32[]{:S(2)}) collective-permute-start(bf16[4,2,32,256]{3,2,1,0:T(8,128)(2,1)} %get-tuple-element.22), channel_id=1, source_target_pairs={{0,9},{1,10},{2,11},{3,8},{4,13},{5,14},{6,15},{7,12},{8,1},{9,2},... | collective-permute-start | bytes 393224 | tf_op jit(solution)/shard_map/ppermute | solution.py:107
  17.5 0.0 collective-permute-done.1.rest_1_
  17.5 3.3 %collective-permute-start.6 = (bf16[4,2,32,256]{3,2,1,0:T(8,128)(2,1)}, bf16[4,2,32,256]{3,2,1,0:T(8,128)(2,1)S(1)}, u32[]{:S(2)}, u32[]{:S(2)}) collective-permute-start(bf16[4,2,32,256]{3,2,1,0:T(8,128)(2,1)} %get-tuple-element.23), channel_id=1, source_target_pairs={{0,10},{1,11},{2,8},{3,9},{4,14},{5,15},{6,12},{7,13},{8,2},{9,3},... | collective-permute-start | bytes 393224 | tf_op jit(solution)/shard_map/ppermute | solution.py:107
  20.8 1.2 %compare_convert_fusion.vis_ref = s32[8,1,128]{2,1,0:T(1,128)} fusion(s32[8,1,128]{2,1,0:T(1,128)S(1)} %add.74, s32[]{:T(128)} %bitcast.3, s32[128]{0:T(128)S(1)} %add.76), kind=kLoop, calls=%fused_computation | loop fusion | flops 3072 | bytes 8708 | tf_op jit(solution)/shard_map/convert_element_type | solution.py:126
  22.0 0.7 %dynamic-slice_bitcast_fusion = s32[8]{0:T(128)S(1)} fusion(s32[4,8]{1,0:T(4,128)} %off_ref.3, s32[]{:T(128)S(6)} %select_n.17), kind=kLoop, calls=%fused_computation.11 | loop fusion | bytes 68 | tf_op jit(solution)/shard_map/jit(dynamic_index_in_dim)/squeeze | solution.py:112
  22.7 0.1 collective-permute-start.7
  22.8 0.0 collective-permute-done.3.rest_3_
  22.8 1.1 %collective-permute-start.8 = (bf16[4,2,32,256]{3,2,1,0:T(8,128)(2,1)}, bf16[4,2,32,256]{3,2,1,0:T(8,128)(2,1)S(1)}, u32[]{:S(2)}, u32[]{:S(2)}) collective-permute-start(bf16[4,2,32,256]{3,2,1,0:T(8,128)(2,1)} %get-tuple-element.25), channel_id=1, source_target_pairs={{0,12},{1,13},{2,14},{3,15},{4,0},{5,1},{6,2},{7,3},{8,4},{9,5},{1... | collective-permute-start | bytes 393224 | tf_op jit(solution)/shard_map/ppermute | solution.py:107
  23.9 9.8 %collective-permute-done.4.rest_4_ = bf16[4,2,32,256]{3,2,1,0:T(8,128)(2,1)S(1)} collective-permute-done((bf16[4,2,32,256]{3,2,1,0:T(8,128)(2,1)}, bf16[4,2,32,256]{3,2,1,0:T(8,128)(2,1)S(1)}, u32[]{:S(2)}, u32[]{:S(2)}) %collective-permute-start.4) | collective-permute-done | bytes 131104 | tf_op jit(solution)/shard_map/ppermute | solution.py:107
  33.7 6.2 %collective-permute-start.9 = (bf16[4,2,32,256]{3,2,1,0:T(8,128)(2,1)}, bf16[4,2,32,256]{3,2,1,0:T(8,128)(2,1)S(1)}, u32[]{:S(2)}, u32[]{:S(2)}) collective-permute-start(bf16[4,2,32,256]{3,2,1,0:T(8,128)(2,1)} %get-tuple-element.26), channel_id=1, source_target_pairs={{0,13},{1,14},{2,15},{3,12},{4,1},{5,2},{6,3},{7,0},{8,5},{9,6},{1... | collective-permute-start | bytes 393224 | tf_op jit(solution)/shard_map/ppermute | solution.py:107
  39.9 2.5 %collective-permute-start.10 = (bf16[4,2,32,256]{3,2,1,0:T(8,128)(2,1)}, bf16[4,2,32,256]{3,2,1,0:T(8,128)(2,1)S(1)}, u32[]{:S(2)}, u32[]{:S(2)}) collective-permute-start(bf16[4,2,32,256]{3,2,1,0:T(8,128)(2,1)} %get-tuple-element.27), channel_id=1, source_target_pairs={{0,14},{1,15},{2,12},{3,13},{4,2},{5,3},{6,0},{7,1},{8,6},{9,7},{1... | collective-permute-start | bytes 393224 | tf_op jit(solution)/shard_map/ppermute | solution.py:107
  42.4 0.0 collective-permute-done.6.rest_6_
  42.4 8.7 %collective-permute-start.11 = (bf16[4,2,32,256]{3,2,1,0:T(8,128)(2,1)}, bf16[4,2,32,256]{3,2,1,0:T(8,128)(2,1)S(1)}, u32[]{:S(2)}, u32[]{:S(2)}) collective-permute-start(bf16[4,2,32,256]{3,2,1,0:T(8,128)(2,1)} %get-tuple-element.28), channel_id=1, source_target_pairs={{0,15},{1,12},{2,13},{3,14},{4,3},{5,0},{6,1},{7,2},{8,7},{9,4},{1... | collective-permute-start | bytes 393224 | tf_op jit(solution)/shard_map/ppermute | solution.py:107
  51.1 0.2 select_reduce_fusion
  51.3 0.6 pad_add_fusion.tab_ref
  51.9 0.0 collective-permute-done.9.rest_9_
  52.0 1.4 %collective-permute-done.11.rest_11_ = bf16[4,2,32,256]{3,2,1,0:T(8,128)(2,1)S(1)} collective-permute-done((bf16[4,2,32,256]{3,2,1,0:T(8,128)(2,1)}, bf16[4,2,32,256]{3,2,1,0:T(8,128)(2,1)S(1)}, u32[]{:S(2)}, u32[]{:S(2)}) %collective-permute-start.11) | collective-permute-done | bytes 131104 | tf_op jit(solution)/shard_map/ppermute | solution.py:107
  53.5 0.6 copy-done.11
  54.0 8.5 %shard_map.66 = bf16[128,2048]{1,0:T(8,128)(2,1)} custom-call(s32[16]{0:T(128)} %pad_add_fusion.tab_ref, bf16[128,2048]{1,0:T(8,128)(2,1)} %bitcast.6, bf16[2,128,256]{2,1,0:T(8,128)(2,1)} %bitcast.7, s32[8,1,128]{2,1,0:T(1,128)} %compare_convert_fusion.vis_ref, bf16[4,2,32,256]{3,2,1,0:T(8,128)(2,1)} %copy-done, bf16[4,2,32,256]{3,2,1,0:T(8,128)(2,1)} %copy-done.1, ...), custom_call_target="tpu_custom_call" | custom-call | flops 1207959552 | bytes 2752512 | tf_op jit(solution)/shard_map/pallas_call | solution.py:232
  (33 shorter events, 0.1 us)
Async XLA Ops:
  0.0 15.2 %copy-start.12 = (s32[4]{0:T(128)S(1)}, s32[4]{0:T(128)}, u32[]{:S(2)}) copy-start(s32[4]{0:T(128)} %param.11) | copy-start | bytes 52
  2.9 12.9 %collective-permute-start = (bf16[4,2,32,256]{3,2,1,0:T(8,128)(2,1)}, bf16[4,2,32,256]{3,2,1,0:T(8,128)(2,1)S(1)}, u32[]{:S(2)}, u32[]{:S(2)}) collective-permute-start(bf16[4,2,32,256]{3,2,1,0:T(8,128)(2,1)} %get-tuple-element.17), channel_id=1, source_target_pairs={{0,4},{1,5},{2,6},{3,7},{4,8},{5,9},{6,10},{7,11},{8,12},{9,13},{1... | collective-permute-start | bytes 393224 | tf_op jit(solution)/shard_map/ppermute | solution.py:107
  5.0 12.5 %collective-permute-start.1 = (bf16[4,2,32,256]{3,2,1,0:T(8,128)(2,1)}, bf16[4,2,32,256]{3,2,1,0:T(8,128)(2,1)S(1)}, u32[]{:S(2)}, u32[]{:S(2)}) collective-permute-start(bf16[4,2,32,256]{3,2,1,0:T(8,128)(2,1)} %get-tuple-element.18), channel_id=1, source_target_pairs={{0,5},{1,6},{2,7},{3,4},{4,9},{5,10},{6,11},{7,8},{8,13},{9,14},{1... | collective-permute-start | bytes 393224 | tf_op jit(solution)/shard_map/ppermute | solution.py:107
  8.1 14.6 %collective-permute-start.2 = (bf16[4,2,32,256]{3,2,1,0:T(8,128)(2,1)}, bf16[4,2,32,256]{3,2,1,0:T(8,128)(2,1)S(1)}, u32[]{:S(2)}, u32[]{:S(2)}) collective-permute-start(bf16[4,2,32,256]{3,2,1,0:T(8,128)(2,1)} %get-tuple-element.19), channel_id=1, source_target_pairs={{0,6},{1,7},{2,4},{3,5},{4,10},{5,11},{6,8},{7,9},{8,14},{9,15},{1... | collective-permute-start | bytes 393224 | tf_op jit(solution)/shard_map/ppermute | solution.py:107
  9.4 13.4 %collective-permute-start.3 = (bf16[4,2,32,256]{3,2,1,0:T(8,128)(2,1)}, bf16[4,2,32,256]{3,2,1,0:T(8,128)(2,1)S(1)}, u32[]{:S(2)}, u32[]{:S(2)}) collective-permute-start(bf16[4,2,32,256]{3,2,1,0:T(8,128)(2,1)} %get-tuple-element.20), channel_id=1, source_target_pairs={{0,7},{1,4},{2,5},{3,6},{4,11},{5,8},{6,9},{7,10},{8,15},{9,12},{1... | collective-permute-start | bytes 393224 | tf_op jit(solution)/shard_map/ppermute | solution.py:107
  12.9 20.7 %collective-permute-start.4 = (bf16[4,2,32,256]{3,2,1,0:T(8,128)(2,1)}, bf16[4,2,32,256]{3,2,1,0:T(8,128)(2,1)S(1)}, u32[]{:S(2)}, u32[]{:S(2)}) collective-permute-start(bf16[4,2,32,256]{3,2,1,0:T(8,128)(2,1)} %get-tuple-element.21), channel_id=1, source_target_pairs={{0,8},{1,9},{2,10},{3,11},{4,12},{5,13},{6,14},{7,15},{8,0},{9,1},... | collective-permute-start | bytes 393224 | tf_op jit(solution)/shard_map/ppermute | solution.py:107
  15.8 37.6 %copy-start = (bf16[4,2,32,256]{3,2,1,0:T(8,128)(2,1)}, bf16[4,2,32,256]{3,2,1,0:T(8,128)(2,1)S(1)}, u32[]{:S(2)}) copy-start(bf16[4,2,32,256]{3,2,1,0:T(8,128)(2,1)S(1)} %collective-permute-done.rest_0_) | copy-start | bytes 393220
  15.8 24.1 %collective-permute-start.5 = (bf16[4,2,32,256]{3,2,1,0:T(8,128)(2,1)}, bf16[4,2,32,256]{3,2,1,0:T(8,128)(2,1)S(1)}, u32[]{:S(2)}, u32[]{:S(2)}) collective-permute-start(bf16[4,2,32,256]{3,2,1,0:T(8,128)(2,1)} %get-tuple-element.22), channel_id=1, source_target_pairs={{0,9},{1,10},{2,11},{3,8},{4,13},{5,14},{6,15},{7,12},{8,1},{9,2},... | collective-permute-start | bytes 393224 | tf_op jit(solution)/shard_map/ppermute | solution.py:107
  17.5 35.8 %copy-start.1 = (bf16[4,2,32,256]{3,2,1,0:T(8,128)(2,1)}, bf16[4,2,32,256]{3,2,1,0:T(8,128)(2,1)S(1)}, u32[]{:S(2)}) copy-start(bf16[4,2,32,256]{3,2,1,0:T(8,128)(2,1)S(1)} %collective-permute-done.1.rest_1_) | copy-start | bytes 393220
  17.5 24.9 %collective-permute-start.6 = (bf16[4,2,32,256]{3,2,1,0:T(8,128)(2,1)}, bf16[4,2,32,256]{3,2,1,0:T(8,128)(2,1)S(1)}, u32[]{:S(2)}, u32[]{:S(2)}) collective-permute-start(bf16[4,2,32,256]{3,2,1,0:T(8,128)(2,1)} %get-tuple-element.23), channel_id=1, source_target_pairs={{0,10},{1,11},{2,8},{3,9},{4,14},{5,15},{6,12},{7,13},{8,2},{9,3},... | collective-permute-start | bytes 393224 | tf_op jit(solution)/shard_map/ppermute | solution.py:107
  22.7 30.6 %copy-start.2 = (bf16[4,2,32,256]{3,2,1,0:T(8,128)(2,1)}, bf16[4,2,32,256]{3,2,1,0:T(8,128)(2,1)S(1)}, u32[]{:S(2)}) copy-start(bf16[4,2,32,256]{3,2,1,0:T(8,128)(2,1)S(1)} %collective-permute-done.2.rest_2_) | copy-start | bytes 393220
  22.7 29.2 %collective-permute-start.7 = (bf16[4,2,32,256]{3,2,1,0:T(8,128)(2,1)}, bf16[4,2,32,256]{3,2,1,0:T(8,128)(2,1)S(1)}, u32[]{:S(2)}, u32[]{:S(2)}) collective-permute-start(bf16[4,2,32,256]{3,2,1,0:T(8,128)(2,1)} %get-tuple-element.24), channel_id=1, source_target_pairs={{0,11},{1,8},{2,9},{3,10},{4,15},{5,12},{6,13},{7,14},{8,3},{9,0},... | collective-permute-start | bytes 393224 | tf_op jit(solution)/shard_map/ppermute | solution.py:107
  22.8 30.6 %copy-start.3 = (bf16[4,2,32,256]{3,2,1,0:T(8,128)(2,1)}, bf16[4,2,32,256]{3,2,1,0:T(8,128)(2,1)S(1)}, u32[]{:S(2)}) copy-start(bf16[4,2,32,256]{3,2,1,0:T(8,128)(2,1)S(1)} %collective-permute-done.3.rest_3_) | copy-start | bytes 393220
  22.8 29.1 %collective-permute-start.8 = (bf16[4,2,32,256]{3,2,1,0:T(8,128)(2,1)}, bf16[4,2,32,256]{3,2,1,0:T(8,128)(2,1)S(1)}, u32[]{:S(2)}, u32[]{:S(2)}) collective-permute-start(bf16[4,2,32,256]{3,2,1,0:T(8,128)(2,1)} %get-tuple-element.25), channel_id=1, source_target_pairs={{0,12},{1,13},{2,14},{3,15},{4,0},{5,1},{6,2},{7,3},{8,4},{9,5},{1... | collective-permute-start | bytes 393224 | tf_op jit(solution)/shard_map/ppermute | solution.py:107
  33.7 19.7 %copy-start.4 = (bf16[4,2,32,256]{3,2,1,0:T(8,128)(2,1)}, bf16[4,2,32,256]{3,2,1,0:T(8,128)(2,1)S(1)}, u32[]{:S(2)}) copy-start(bf16[4,2,32,256]{3,2,1,0:T(8,128)(2,1)S(1)} %collective-permute-done.4.rest_4_) | copy-start | bytes 393220
  33.7 18.2 %collective-permute-start.9 = (bf16[4,2,32,256]{3,2,1,0:T(8,128)(2,1)}, bf16[4,2,32,256]{3,2,1,0:T(8,128)(2,1)S(1)}, u32[]{:S(2)}, u32[]{:S(2)}) collective-permute-start(bf16[4,2,32,256]{3,2,1,0:T(8,128)(2,1)} %get-tuple-element.26), channel_id=1, source_target_pairs={{0,13},{1,14},{2,15},{3,12},{4,1},{5,2},{6,3},{7,0},{8,5},{9,6},{1... | collective-permute-start | bytes 393224 | tf_op jit(solution)/shard_map/ppermute | solution.py:107
  39.9 13.5 %copy-start.5 = (bf16[4,2,32,256]{3,2,1,0:T(8,128)(2,1)}, bf16[4,2,32,256]{3,2,1,0:T(8,128)(2,1)S(1)}, u32[]{:S(2)}) copy-start(bf16[4,2,32,256]{3,2,1,0:T(8,128)(2,1)S(1)} %collective-permute-done.5.rest_5_) | copy-start | bytes 393220
  39.9 12.1 %collective-permute-start.10 = (bf16[4,2,32,256]{3,2,1,0:T(8,128)(2,1)}, bf16[4,2,32,256]{3,2,1,0:T(8,128)(2,1)S(1)}, u32[]{:S(2)}, u32[]{:S(2)}) collective-permute-start(bf16[4,2,32,256]{3,2,1,0:T(8,128)(2,1)} %get-tuple-element.27), channel_id=1, source_target_pairs={{0,14},{1,15},{2,12},{3,13},{4,2},{5,3},{6,0},{7,1},{8,6},{9,7},{1... | collective-permute-start | bytes 393224 | tf_op jit(solution)/shard_map/ppermute | solution.py:107
  42.4 11.0 %copy-start.6 = (bf16[4,2,32,256]{3,2,1,0:T(8,128)(2,1)}, bf16[4,2,32,256]{3,2,1,0:T(8,128)(2,1)S(1)}, u32[]{:S(2)}) copy-start(bf16[4,2,32,256]{3,2,1,0:T(8,128)(2,1)S(1)} %collective-permute-done.6.rest_6_) | copy-start | bytes 393220
  42.4 11.0 %collective-permute-start.11 = (bf16[4,2,32,256]{3,2,1,0:T(8,128)(2,1)}, bf16[4,2,32,256]{3,2,1,0:T(8,128)(2,1)S(1)}, u32[]{:S(2)}, u32[]{:S(2)}) collective-permute-start(bf16[4,2,32,256]{3,2,1,0:T(8,128)(2,1)} %get-tuple-element.28), channel_id=1, source_target_pairs={{0,15},{1,12},{2,13},{3,14},{4,3},{5,0},{6,1},{7,2},{8,7},{9,4},{1... | collective-permute-start | bytes 393224 | tf_op jit(solution)/shard_map/ppermute | solution.py:107
  51.9 1.5 %copy-start.7 = (bf16[4,2,32,256]{3,2,1,0:T(8,128)(2,1)}, bf16[4,2,32,256]{3,2,1,0:T(8,128)(2,1)S(1)}, u32[]{:S(2)}) copy-start(bf16[4,2,32,256]{3,2,1,0:T(8,128)(2,1)S(1)} %collective-permute-done.7.rest_7_) | copy-start | bytes 393220
  51.9 1.5 %copy-start.8 = (bf16[4,2,32,256]{3,2,1,0:T(8,128)(2,1)}, bf16[4,2,32,256]{3,2,1,0:T(8,128)(2,1)S(1)}, u32[]{:S(2)}) copy-start(bf16[4,2,32,256]{3,2,1,0:T(8,128)(2,1)S(1)} %collective-permute-done.8.rest_8_) | copy-start | bytes 393220
  51.9 1.5 %copy-start.9 = (bf16[4,2,32,256]{3,2,1,0:T(8,128)(2,1)}, bf16[4,2,32,256]{3,2,1,0:T(8,128)(2,1)S(1)}, u32[]{:S(2)}) copy-start(bf16[4,2,32,256]{3,2,1,0:T(8,128)(2,1)S(1)} %collective-permute-done.9.rest_9_) | copy-start | bytes 393220
  52.0 1.5 %copy-start.10 = (bf16[4,2,32,256]{3,2,1,0:T(8,128)(2,1)}, bf16[4,2,32,256]{3,2,1,0:T(8,128)(2,1)S(1)}, u32[]{:S(2)}) copy-start(bf16[4,2,32,256]{3,2,1,0:T(8,128)(2,1)S(1)} %collective-permute-done.10.rest_10_) | copy-start | bytes 393220
  53.4 0.7 %copy-start.11 = (bf16[4,2,32,256]{3,2,1,0:T(8,128)(2,1)}, bf16[4,2,32,256]{3,2,1,0:T(8,128)(2,1)S(1)}, u32[]{:S(2)}) copy-start(bf16[4,2,32,256]{3,2,1,0:T(8,128)(2,1)S(1)} %collective-permute-done.11.rest_11_) | copy-start | bytes 393220

commit v16 on v14

--- a/solution.py
+++ b/solution.py
@@ -115,7 +115,8 @@
     earlier = (page_ids[None, :] < page_ids[:, None]).astype(jnp.int32)
     same = (own_offsets[:, None] == own_offsets[None, :]).astype(jnp.int32)
     rank = jnp.sum(same * earlier, axis=1)
-    table = jnp.concatenate([own_offsets, rank]).astype(jnp.int32)
+    whole_page = ((page_ids + 1) * page_rows <= own_length).astype(jnp.int32)
+    table = jnp.concatenate([own_offsets, rank, whole_page]).astype(jnp.int32)
     shifts = jnp.arange(tensor_count, dtype=jnp.int32)
     row_ids = jnp.arange(quarter, dtype=jnp.int32)
     position = (
@@ -167,9 +168,16 @@
                 jnp.concatenate([vis_ref[p] for p in range(page, page + join)], axis=-1) > 0
             )
         scores = []
-        for key, mask in zip(keys, masks):
+        for number, (key, mask) in enumerate(zip(keys, masks)):
             s = lax.dot_general(q_all, key, dims, preferred_element_type=jnp.float32)
-            scores.append(jnp.where(mask, s, NEG_FILL))
+            if number == 0:
+                scores.append(jnp.where(mask, s, NEG_FILL))
+            else:
+                first_page = (number - 1) * join
+                whole_tile = tab_ref[2 * page_count + first_page + join - 1] > 0
+                scores.append(
+                    lax.cond(whole_tile, lambda x: x, lambda x: jnp.where(mask, x, NEG_FILL), s)
+                )
         widths = sorted(set(s.shape[-1] for s in scores))
         top = None
         for width_now in widths:

time: 62.3 us -> 65.9 us (1.058)
  Pallas kernels: 13.9 us -> 17.4 us
  waiting for transfers between devices: 11.2 us -> 10.4 us
    pallas_call x1, Pallas kernels: 7.83 us -> 11.4 us  [attend(): pl.pallas_call(functools.partial(attention_kernel, span_count, tensor_cou...]
    ppermute x12, waiting for transfers between devices: 11.2 us -> 10.4 us  [on_device(): lax.ppermute(payload[(distance - 1) * tensor_count + shift], ('replica',...]
  transfers between devices with their start and end apart: 12 -> 12, of which waited for: 2 -> 2; matrix products, arithmetic and copies ran while one was open for 6% -> 7% of each run, Pallas kernels for 5% -> 5%
where the time goes in v16:
time: 65.9 us; the launch traced here: 65.5 us
  starting transfers between devices  32.6 us (49%)
  Pallas kernels  17.4 us (26%)
  waiting for transfers between devices  10.4 us (16%)
  other arithmetic  2.7 us (4%)
  local copies, waits for them, and re-layouts  2.17 us (3%)
    ppermute x12, starting transfers between devices, on_device(): lax.ppermute(payload[(distance - 1) * tensor_count + shift], ('replica',...  32.6 us
    pallas_call x1, Pallas kernels, attend(): pl.pallas_call(functools.partial(attention_kernel, span_count, tensor_cou...  11.4 us
    ppermute x12, waiting for transfers between devices, on_device(): lax.ppermute(payload[(distance - 1) * tensor_count + shift], ('replica',...  10.4 us
    pallas_call x2, Pallas kernels, pack_pages(): pl.pallas_call(functools.partial(gather_kernel, first, last, slot_cap, te...  6.05 us
  transfers between devices with their start and end apart: 12, of which 2 were waited for; matrix products, arithmetic and copies ran while one was open for 7% of the time, Pallas kernels for 5%

profile of v16, /device:TPU:1, one launch (start us, length us, event | category | flops | bytes accessed | tf_op | source)
XLA Modules:
  0.0 65.5 jit_solution(17508294162544399666)
XLA Ops:
  0.0 2.8 %shard_map.64 = (bf16[4,2,32,256]{3,2,1,0:T(8,128)(2,1)}, bf16[4,2,32,256]{3,2,1,0:T(8,128)(2,1)}, bf16[4,2,32,256]{3,2,1,0:T(8,128)(2,1)}, bf16[4,2,32,256]{3,2,1,0:T(8,128)(2,1)}) custom-call(s32[4,8]{1,0:T(4,128)} %off_ref.3, s32[4,8]{1,0:T(4,128)} %slot_ref.3, bf16[12,2,32,1024]{3,2,1,0:T(8,128)(2,1)} %pool_hbm.3), custom_call_target="tpu_custom_call" | custom-call | bytes 1048576 | tf_op jit(solution)/shard_map/pallas_call | solution.py:77
  2.9 2.2 %collective-permute-start = (bf16[4,2,32,256]{3,2,1,0:T(8,128)(2,1)}, bf16[4,2,32,256]{3,2,1,0:T(8,128)(2,1)S(1)}, u32[]{:S(2)}, u32[]{:S(2)}) collective-permute-start(bf16[4,2,32,256]{3,2,1,0:T(8,128)(2,1)} %get-tuple-element.17), channel_id=1, source_target_pairs={{0,4},{1,5},{2,6},{3,7},{4,8},{5,9},{6,10},{7,11},{8,12},{9,13},{1... | collective-permute-start | bytes 393224 | tf_op jit(solution)/shard_map/ppermute | solution.py:107
  5.0 3.1 %collective-permute-start.1 = (bf16[4,2,32,256]{3,2,1,0:T(8,128)(2,1)}, bf16[4,2,32,256]{3,2,1,0:T(8,128)(2,1)S(1)}, u32[]{:S(2)}, u32[]{:S(2)}) collective-permute-start(bf16[4,2,32,256]{3,2,1,0:T(8,128)(2,1)} %get-tuple-element.18), channel_id=1, source_target_pairs={{0,5},{1,6},{2,7},{3,4},{4,9},{5,10},{6,11},{7,8},{8,13},{9,14},{1... | collective-permute-start | bytes 393224 | tf_op jit(solution)/shard_map/ppermute | solution.py:107
  8.1 1.2 %collective-permute-start.2 = (bf16[4,2,32,256]{3,2,1,0:T(8,128)(2,1)}, bf16[4,2,32,256]{3,2,1,0:T(8,128)(2,1)S(1)}, u32[]{:S(2)}, u32[]{:S(2)}) collective-permute-start(bf16[4,2,32,256]{3,2,1,0:T(8,128)(2,1)} %get-tuple-element.19), channel_id=1, source_target_pairs={{0,6},{1,7},{2,4},{3,5},{4,10},{5,11},{6,8},{7,9},{8,14},{9,15},{1... | collective-permute-start | bytes 393224 | tf_op jit(solution)/shard_map/ppermute | solution.py:107
  9.4 0.3 collective-permute-start.3
  9.7 3.2 %shard_map.65 = (bf16[4,2,32,256]{3,2,1,0:T(8,128)(2,1)}, bf16[4,2,32,256]{3,2,1,0:T(8,128)(2,1)}, bf16[4,2,32,256]{3,2,1,0:T(8,128)(2,1)}, bf16[4,2,32,256]{3,2...) custom-call(s32[4,8]{1,0:T(4,128)} %off_ref.3, ...), custom_call_target="tpu_custom_call" | custom-call | bytes 2097152 | tf_op jit(solution)/shard_map/pallas_call | solution.py:77
  12.9 1.9 %collective-permute-start.4 = (bf16[4,2,32,256]{3,2,1,0:T(8,128)(2,1)}, bf16[4,2,32,256]{3,2,1,0:T(8,128)(2,1)S(1)}, u32[]{:S(2)}, u32[]{:S(2)}) collective-permute-start(bf16[4,2,32,256]{3,2,1,0:T(8,128)(2,1)} %get-tuple-element.21), channel_id=1, source_target_pairs={{0,8},{1,9},{2,10},{3,11},{4,12},{5,13},{6,14},{7,15},{8,0},{9,1},... | collective-permute-start | bytes 393224 | tf_op jit(solution)/shard_map/ppermute | solution.py:107
  14.8 0.1 add.80
  14.9 0.1 broadcast_add_fusion
  15.0 0.1 add.77
  15.1 0.1 add.78
  15.2 0.6 dynamic_slice.9
  15.8 1.2 %compare_convert_fusion.vis_ref = s32[8,1,128]{2,1,0:T(1,128)} fusion(s32[8,1,128]{2,1,0:T(1,128)S(1)} %add.78, s32[]{:T(128)} %bitcast.1, s32[128]{0:T(128)S(1)} %add.80), kind=kLoop, calls=%fused_computation | loop fusion | flops 3072 | bytes 8708 | tf_op jit(solution)/shard_map/convert_element_type | solution.py:127
  17.0 0.0 collective-permute-done.rest_0_
  17.0 1.7 %collective-permute-start.5 = (bf16[4,2,32,256]{3,2,1,0:T(8,128)(2,1)}, bf16[4,2,32,256]{3,2,1,0:T(8,128)(2,1)S(1)}, u32[]{:S(2)}, u32[]{:S(2)}) collective-permute-start(bf16[4,2,32,256]{3,2,1,0:T(8,128)(2,1)} %get-tuple-element.22), channel_id=1, source_target_pairs={{0,9},{1,10},{2,11},{3,8},{4,13},{5,14},{6,15},{7,12},{8,1},{9,2},... | collective-permute-start | bytes 393224 | tf_op jit(solution)/shard_map/ppermute | solution.py:107
  18.7 3.3 %collective-permute-start.6 = (bf16[4,2,32,256]{3,2,1,0:T(8,128)(2,1)}, bf16[4,2,32,256]{3,2,1,0:T(8,128)(2,1)S(1)}, u32[]{:S(2)}, u32[]{:S(2)}) collective-permute-start(bf16[4,2,32,256]{3,2,1,0:T(8,128)(2,1)} %get-tuple-element.23), channel_id=1, source_target_pairs={{0,10},{1,11},{2,8},{3,9},{4,14},{5,15},{6,12},{7,13},{8,2},{9,3},... | collective-permute-start | bytes 393224 | tf_op jit(solution)/shard_map/ppermute | solution.py:107
  22.0 0.7 %dynamic-slice_bitcast_fusion = s32[8]{0:T(128)S(1)} fusion(s32[4,8]{1,0:T(4,128)} %off_ref.3, s32[]{:T(128)S(6)} %select_n.17), kind=kLoop, calls=%fused_computation.12 | loop fusion | bytes 68 | tf_op jit(solution)/shard_map/jit(dynamic_index_in_dim)/squeeze | solution.py:112
  22.7 0.2 select_reduce_fusion
  22.9 0.0 collective-permute-done.2.rest_2_
  22.9 0.1 collective-permute-start.7
  23.0 0.0 collective-permute-done.3.rest_3_
  23.0 1.3 %collective-permute-start.8 = (bf16[4,2,32,256]{3,2,1,0:T(8,128)(2,1)}, bf16[4,2,32,256]{3,2,1,0:T(8,128)(2,1)S(1)}, u32[]{:S(2)}, u32[]{:S(2)}) collective-permute-start(bf16[4,2,32,256]{3,2,1,0:T(8,128)(2,1)} %get-tuple-element.25), channel_id=1, source_target_pairs={{0,12},{1,13},{2,14},{3,15},{4,0},{5,1},{6,2},{7,3},{8,4},{9,5},{1... | collective-permute-start | bytes 393224 | tf_op jit(solution)/shard_map/ppermute | solution.py:107
  24.3 9.4 %collective-permute-done.4.rest_4_ = bf16[4,2,32,256]{3,2,1,0:T(8,128)(2,1)S(1)} collective-permute-done((bf16[4,2,32,256]{3,2,1,0:T(8,128)(2,1)}, bf16[4,2,32,256]{3,2,1,0:T(8,128)(2,1)S(1)}, u32[]{:S(2)}, u32[]{:S(2)}) %collective-permute-start.4) | collective-permute-done | bytes 131104 | tf_op jit(solution)/shard_map/ppermute | solution.py:107
  33.7 6.2 %collective-permute-start.9 = (bf16[4,2,32,256]{3,2,1,0:T(8,128)(2,1)}, bf16[4,2,32,256]{3,2,1,0:T(8,128)(2,1)S(1)}, u32[]{:S(2)}, u32[]{:S(2)}) collective-permute-start(bf16[4,2,32,256]{3,2,1,0:T(8,128)(2,1)} %get-tuple-element.26), channel_id=1, source_target_pairs={{0,13},{1,14},{2,15},{3,12},{4,1},{5,2},{6,3},{7,0},{8,5},{9,6},{1... | collective-permute-start | bytes 393224 | tf_op jit(solution)/shard_map/ppermute | solution.py:107
  40.0 2.5 %collective-permute-start.10 = (bf16[4,2,32,256]{3,2,1,0:T(8,128)(2,1)}, bf16[4,2,32,256]{3,2,1,0:T(8,128)(2,1)S(1)}, u32[]{:S(2)}, u32[]{:S(2)}) collective-permute-start(bf16[4,2,32,256]{3,2,1,0:T(8,128)(2,1)} %get-tuple-element.27), channel_id=1, source_target_pairs={{0,14},{1,15},{2,12},{3,13},{4,2},{5,3},{6,0},{7,1},{8,6},{9,7},{1... | collective-permute-start | bytes 393224 | tf_op jit(solution)/shard_map/ppermute | solution.py:107
  42.5 8.7 %collective-permute-start.11 = (bf16[4,2,32,256]{3,2,1,0:T(8,128)(2,1)}, bf16[4,2,32,256]{3,2,1,0:T(8,128)(2,1)S(1)}, u32[]{:S(2)}, u32[]{:S(2)}) collective-permute-start(bf16[4,2,32,256]{3,2,1,0:T(8,128)(2,1)} %get-tuple-element.28), channel_id=1, source_target_pairs={{0,15},{1,12},{2,13},{3,14},{4,3},{5,0},{6,1},{7,2},{8,7},{9,4},{1... | collective-permute-start | bytes 393224 | tf_op jit(solution)/shard_map/ppermute | solution.py:107
  51.2 0.6 compare_convert_fusion.1
  51.8 0.6 pad_add_fusion.tab_ref
  52.4 0.0 collective-permute-done.7.rest_7_
  52.5 1.0 %collective-permute-done.11.rest_11_ = bf16[4,2,32,256]{3,2,1,0:T(8,128)(2,1)S(1)} collective-permute-done((bf16[4,2,32,256]{3,2,1,0:T(8,128)(2,1)}, bf16[4,2,32,256]{3,2,1,0:T(8,128)(2,1)S(1)}, u32[]{:S(2)}, u32[]{:S(2)}) %collective-permute-start.11) | collective-permute-done | bytes 131104 | tf_op jit(solution)/shard_map/ppermute | solution.py:107
  53.5 0.6 copy-done.11
  54.1 11.4 %shard_map.66 = bf16[128,2048]{1,0:T(8,128)(2,1)} custom-call(s32[24]{0:T(128)} %pad_add_fusion.tab_ref, bf16[128,2048]{1,0:T(8,128)(2,1)} %bitcast.6, bf16[2,128,256]{2,1,0:T(8,128)(2,1)} %bitcast.7, s32[8,1,128]{2,1,0:T(1,128)} %compare_convert_fusion.vis_ref, bf16[4,2,32,256]{3,2,1,0:T(8,128)(2,1)} %copy-done, bf16[4,2,32,256]{3,2,1,0:T(8,128)(2,1)} %copy-done.1, ...), custom_call_target="tpu_custom_call" | custom-call | flops 1207959552 | bytes 2752512 | tf_op jit(solution)/shard_map/pallas_call | solution.py:221
  (34 shorter events, 0.1 us)
Async XLA Ops:
  0.0 15.2 %copy-start.12 = (s32[4]{0:T(128)S(1)}, s32[4]{0:T(128)}, u32[]{:S(2)}) copy-start(s32[4]{0:T(128)} %param.11) | copy-start | bytes 52
  2.9 14.1 %collective-permute-start = (bf16[4,2,32,256]{3,2,1,0:T(8,128)(2,1)}, bf16[4,2,32,256]{3,2,1,0:T(8,128)(2,1)S(1)}, u32[]{:S(2)}, u32[]{:S(2)}) collective-permute-start(bf16[4,2,32,256]{3,2,1,0:T(8,128)(2,1)} %get-tuple-element.17), channel_id=1, source_target_pairs={{0,4},{1,5},{2,6},{3,7},{4,8},{5,9},{6,10},{7,11},{8,12},{9,13},{1... | collective-permute-start | bytes 393224 | tf_op jit(solution)/shard_map/ppermute | solution.py:107
  5.0 13.7 %collective-permute-start.1 = (bf16[4,2,32,256]{3,2,1,0:T(8,128)(2,1)}, bf16[4,2,32,256]{3,2,1,0:T(8,128)(2,1)S(1)}, u32[]{:S(2)}, u32[]{:S(2)}) collective-permute-start(bf16[4,2,32,256]{3,2,1,0:T(8,128)(2,1)} %get-tuple-element.18), channel_id=1, source_target_pairs={{0,5},{1,6},{2,7},{3,4},{4,9},{5,10},{6,11},{7,8},{8,13},{9,14},{1... | collective-permute-start | bytes 393224 | tf_op jit(solution)/shard_map/ppermute | solution.py:107
  8.1 14.8 %collective-permute-start.2 = (bf16[4,2,32,256]{3,2,1,0:T(8,128)(2,1)}, bf16[4,2,32,256]{3,2,1,0:T(8,128)(2,1)S(1)}, u32[]{:S(2)}, u32[]{:S(2)}) collective-permute-start(bf16[4,2,32,256]{3,2,1,0:T(8,128)(2,1)} %get-tuple-element.19), channel_id=1, source_target_pairs={{0,6},{1,7},{2,4},{3,5},{4,10},{5,11},{6,8},{7,9},{8,14},{9,15},{1... | collective-permute-start | bytes 393224 | tf_op jit(solution)/shard_map/ppermute | solution.py:107
  9.4 13.6 %collective-permute-start.3 = (bf16[4,2,32,256]{3,2,1,0:T(8,128)(2,1)}, bf16[4,2,32,256]{3,2,1,0:T(8,128)(2,1)S(1)}, u32[]{:S(2)}, u32[]{:S(2)}) collective-permute-start(bf16[4,2,32,256]{3,2,1,0:T(8,128)(2,1)} %get-tuple-element.20), channel_id=1, source_target_pairs={{0,7},{1,4},{2,5},{3,6},{4,11},{5,8},{6,9},{7,10},{8,15},{9,12},{1... | collective-permute-start | bytes 393224 | tf_op jit(solution)/shard_map/ppermute | solution.py:107
  12.9 20.8 %collective-permute-start.4 = (bf16[4,2,32,256]{3,2,1,0:T(8,128)(2,1)}, bf16[4,2,32,256]{3,2,1,0:T(8,128)(2,1)S(1)}, u32[]{:S(2)}, u32[]{:S(2)}) collective-permute-start(bf16[4,2,32,256]{3,2,1,0:T(8,128)(2,1)} %get-tuple-element.21), channel_id=1, source_target_pairs={{0,8},{1,9},{2,10},{3,11},{4,12},{5,13},{6,14},{7,15},{8,0},{9,1},... | collective-permute-start | bytes 393224 | tf_op jit(solution)/shard_map/ppermute | solution.py:107
  17.0 36.5 %copy-start = (bf16[4,2,32,256]{3,2,1,0:T(8,128)(2,1)}, bf16[4,2,32,256]{3,2,1,0:T(8,128)(2,1)S(1)}, u32[]{:S(2)}) copy-start(bf16[4,2,32,256]{3,2,1,0:T(8,128)(2,1)S(1)} %collective-permute-done.rest_0_) | copy-start | bytes 393220
  17.0 23.0 %collective-permute-start.5 = (bf16[4,2,32,256]{3,2,1,0:T(8,128)(2,1)}, bf16[4,2,32,256]{3,2,1,0:T(8,128)(2,1)S(1)}, u32[]{:S(2)}, u32[]{:S(2)}) collective-permute-start(bf16[4,2,32,256]{3,2,1,0:T(8,128)(2,1)} %get-tuple-element.22), channel_id=1, source_target_pairs={{0,9},{1,10},{2,11},{3,8},{4,13},{5,14},{6,15},{7,12},{8,1},{9,2},... | collective-permute-start | bytes 393224 | tf_op jit(solution)/shard_map/ppermute | solution.py:107
  18.7 34.7 %copy-start.1 = (bf16[4,2,32,256]{3,2,1,0:T(8,128)(2,1)}, bf16[4,2,32,256]{3,2,1,0:T(8,128)(2,1)S(1)}, u32[]{:S(2)}) copy-start(bf16[4,2,32,256]{3,2,1,0:T(8,128)(2,1)S(1)} %collective-permute-done.1.rest_1_) | copy-start | bytes 393220
  18.7 23.8 %collective-permute-start.6 = (bf16[4,2,32,256]{3,2,1,0:T(8,128)(2,1)}, bf16[4,2,32,256]{3,2,1,0:T(8,128)(2,1)S(1)}, u32[]{:S(2)}, u32[]{:S(2)}) collective-permute-start(bf16[4,2,32,256]{3,2,1,0:T(8,128)(2,1)} %get-tuple-element.23), channel_id=1, source_target_pairs={{0,10},{1,11},{2,8},{3,9},{4,14},{5,15},{6,12},{7,13},{8,2},{9,3},... | collective-permute-start | bytes 393224 | tf_op jit(solution)/shard_map/ppermute | solution.py:107
  22.9 30.6 %copy-start.2 = (bf16[4,2,32,256]{3,2,1,0:T(8,128)(2,1)}, bf16[4,2,32,256]{3,2,1,0:T(8,128)(2,1)S(1)}, u32[]{:S(2)}) copy-start(bf16[4,2,32,256]{3,2,1,0:T(8,128)(2,1)S(1)} %collective-permute-done.2.rest_2_) | copy-start | bytes 393220
  22.9 29.5 %collective-permute-start.7 = (bf16[4,2,32,256]{3,2,1,0:T(8,128)(2,1)}, bf16[4,2,32,256]{3,2,1,0:T(8,128)(2,1)S(1)}, u32[]{:S(2)}, u32[]{:S(2)}) collective-permute-start(bf16[4,2,32,256]{3,2,1,0:T(8,128)(2,1)} %get-tuple-element.24), channel_id=1, source_target_pairs={{0,11},{1,8},{2,9},{3,10},{4,15},{5,12},{6,13},{7,14},{8,3},{9,0},... | collective-permute-start | bytes 393224 | tf_op jit(solution)/shard_map/ppermute | solution.py:107
  23.0 30.5 %copy-start.3 = (bf16[4,2,32,256]{3,2,1,0:T(8,128)(2,1)}, bf16[4,2,32,256]{3,2,1,0:T(8,128)(2,1)S(1)}, u32[]{:S(2)}) copy-start(bf16[4,2,32,256]{3,2,1,0:T(8,128)(2,1)S(1)} %collective-permute-done.3.rest_3_) | copy-start | bytes 393220
  23.0 29.4 %collective-permute-start.8 = (bf16[4,2,32,256]{3,2,1,0:T(8,128)(2,1)}, bf16[4,2,32,256]{3,2,1,0:T(8,128)(2,1)S(1)}, u32[]{:S(2)}, u32[]{:S(2)}) collective-permute-start(bf16[4,2,32,256]{3,2,1,0:T(8,128)(2,1)} %get-tuple-element.25), channel_id=1, source_target_pairs={{0,12},{1,13},{2,14},{3,15},{4,0},{5,1},{6,2},{7,3},{8,4},{9,5},{1... | collective-permute-start | bytes 393224 | tf_op jit(solution)/shard_map/ppermute | solution.py:107
  33.7 19.8 %copy-start.4 = (bf16[4,2,32,256]{3,2,1,0:T(8,128)(2,1)}, bf16[4,2,32,256]{3,2,1,0:T(8,128)(2,1)S(1)}, u32[]{:S(2)}) copy-start(bf16[4,2,32,256]{3,2,1,0:T(8,128)(2,1)S(1)} %collective-permute-done.4.rest_4_) | copy-start | bytes 393220
  33.7 18.7 %collective-permute-start.9 = (bf16[4,2,32,256]{3,2,1,0:T(8,128)(2,1)}, bf16[4,2,32,256]{3,2,1,0:T(8,128)(2,1)S(1)}, u32[]{:S(2)}, u32[]{:S(2)}) collective-permute-start(bf16[4,2,32,256]{3,2,1,0:T(8,128)(2,1)} %get-tuple-element.26), channel_id=1, source_target_pairs={{0,13},{1,14},{2,15},{3,12},{4,1},{5,2},{6,3},{7,0},{8,5},{9,6},{1... | collective-permute-start | bytes 393224 | tf_op jit(solution)/shard_map/ppermute | solution.py:107
  39.9 13.5 %copy-start.5 = (bf16[4,2,32,256]{3,2,1,0:T(8,128)(2,1)}, bf16[4,2,32,256]{3,2,1,0:T(8,128)(2,1)S(1)}, u32[]{:S(2)}) copy-start(bf16[4,2,32,256]{3,2,1,0:T(8,128)(2,1)S(1)} %collective-permute-done.5.rest_5_) | copy-start | bytes 393220
  40.0 12.5 %collective-permute-start.10 = (bf16[4,2,32,256]{3,2,1,0:T(8,128)(2,1)}, bf16[4,2,32,256]{3,2,1,0:T(8,128)(2,1)S(1)}, u32[]{:S(2)}, u32[]{:S(2)}) collective-permute-start(bf16[4,2,32,256]{3,2,1,0:T(8,128)(2,1)} %get-tuple-element.27), channel_id=1, source_target_pairs={{0,14},{1,15},{2,12},{3,13},{4,2},{5,3},{6,0},{7,1},{8,6},{9,7},{1... | collective-permute-start | bytes 393224 | tf_op jit(solution)/shard_map/ppermute | solution.py:107
  42.5 11.0 %copy-start.6 = (bf16[4,2,32,256]{3,2,1,0:T(8,128)(2,1)}, bf16[4,2,32,256]{3,2,1,0:T(8,128)(2,1)S(1)}, u32[]{:S(2)}) copy-start(bf16[4,2,32,256]{3,2,1,0:T(8,128)(2,1)S(1)} %collective-permute-done.6.rest_6_) | copy-start | bytes 393220
  42.5 11.0 %collective-permute-start.11 = (bf16[4,2,32,256]{3,2,1,0:T(8,128)(2,1)}, bf16[4,2,32,256]{3,2,1,0:T(8,128)(2,1)S(1)}, u32[]{:S(2)}, u32[]{:S(2)}) collective-permute-start(bf16[4,2,32,256]{3,2,1,0:T(8,128)(2,1)} %get-tuple-element.28), channel_id=1, source_target_pairs={{0,15},{1,12},{2,13},{3,14},{4,3},{5,0},{6,1},{7,2},{8,7},{9,4},{1... | collective-permute-start | bytes 393224 | tf_op jit(solution)/shard_map/ppermute | solution.py:107
  52.4 1.1 %copy-start.7 = (bf16[4,2,32,256]{3,2,1,0:T(8,128)(2,1)}, bf16[4,2,32,256]{3,2,1,0:T(8,128)(2,1)S(1)}, u32[]{:S(2)}) copy-start(bf16[4,2,32,256]{3,2,1,0:T(8,128)(2,1)S(1)} %collective-permute-done.7.rest_7_) | copy-start | bytes 393220
  52.4 1.1 %copy-start.8 = (bf16[4,2,32,256]{3,2,1,0:T(8,128)(2,1)}, bf16[4,2,32,256]{3,2,1,0:T(8,128)(2,1)S(1)}, u32[]{:S(2)}) copy-start(bf16[4,2,32,256]{3,2,1,0:T(8,128)(2,1)S(1)} %collective-permute-done.8.rest_8_) | copy-start | bytes 393220
  52.5 1.1 %copy-start.9 = (bf16[4,2,32,256]{3,2,1,0:T(8,128)(2,1)}, bf16[4,2,32,256]{3,2,1,0:T(8,128)(2,1)S(1)}, u32[]{:S(2)}) copy-start(bf16[4,2,32,256]{3,2,1,0:T(8,128)(2,1)S(1)} %collective-permute-done.9.rest_9_) | copy-start | bytes 393220
  52.5 1.1 %copy-start.10 = (bf16[4,2,32,256]{3,2,1,0:T(8,128)(2,1)}, bf16[4,2,32,256]{3,2,1,0:T(8,128)(2,1)S(1)}, u32[]{:S(2)}) copy-start(bf16[4,2,32,256]{3,2,1,0:T(8,128)(2,1)S(1)} %collective-permute-done.10.rest_10_) | copy-start | bytes 393220
  53.4 0.7 copy-start.11

commit v17 on v13

--- a/solution.py
+++ b/solution.py
@@ -25,7 +25,7 @@
     return matched[:, None, :] * (ranking[:, None, :] == places[None, :, None]).astype(jnp.int32)
 
 
-def gather_kernel(first, last, slot_cap, tensor_count, off_ref, slot_ref, pool_hbm, *rest):
+def gather_kernel(chosen_distances, slot_cap, tensor_count, off_ref, slot_ref, pool_hbm, *rest):
     out_refs, buf, sems = rest[:-2], rest[-2], rest[-1]
     replicas, page_count = off_ref.shape
     holder = lax.axis_index("replica")
@@ -35,7 +35,7 @@
         pl.multiple_of(((me + shift) % tensor_count) * lanes, lanes) for shift in range(tensor_count)
     ]
     copies = []
-    for distance in range(first, last + 1):
+    for number, distance in enumerate(chosen_distances):
         reader = (holder + distance) % replicas
         chosen = [jnp.int32(0)] * slot_cap
         count = jnp.int32(0)
@@ -47,26 +47,26 @@
             ]
             count = count + matched.astype(jnp.int32)
         for slot in range(slot_cap):
-            index = (distance - first) * slot_cap + slot
+            index = number * slot_cap + slot
             copy = pltpu.make_async_copy(pool_hbm.at[chosen[slot]], buf.at[index], sems.at[index])
             copy.start()
             copies.append(copy)
     for copy in copies:
         copy.wait()
-    for distance in range(first, last + 1):
+    for number in range(len(chosen_distances)):
         for slot in range(slot_cap):
-            index = (distance - first) * slot_cap + slot
+            index = number * slot_cap + slot
             for shift in range(tensor_count):
-                out_refs[(distance - first) * tensor_count + shift][slot] = buf[
+                out_refs[number * tensor_count + shift][slot] = buf[
                     index, :, :, pl.ds(starts[shift], lanes)
                 ]
 
 
-def pack_pages(pool_part, offsets, slots, first, last, slot_cap, tensor_count):
+def pack_pages(pool_part, offsets, slots, chosen_distances, slot_cap, tensor_count):
     pages, kv, rows, width = pool_part.shape
     lanes = width // tensor_count
     piece = (slot_cap, kv, rows, lanes)
-    span_count = last - first + 1
+    span_count = len(chosen_distances)
     count = span_count * tensor_count
     grid_spec = pltpu.PrefetchScalarGridSpec(
         num_scalar_prefetch=2,
@@ -80,7 +80,7 @@
     )
     nbytes = 2 * 2 * span_count * slot_cap * kv * rows * width
     return pl.pallas_call(
-        functools.partial(gather_kernel, first, last, slot_cap, tensor_count),
+        functools.partial(gather_kernel, tuple(chosen_distances), slot_cap, tensor_count),
         grid_spec=grid_spec,
         out_shape=[jax.ShapeDtypeStruct(piece, pool_part.dtype) for _ in range(count)],
         cost_estimate=pl.CostEstimate(flops=0, transcendentals=0, bytes_accessed=nbytes),
@@ -97,9 +97,16 @@
     slot_cap = (page_count + span_count - 1) // span_count + 1
     distances = jnp.arange(1, span_count + 1, dtype=jnp.int32)
 
-    payload = pack_pages(page_pool, offsets, slots, 1, 1, slot_cap, tensor_count)
-    if span_count > 1:
-        payload = payload + pack_pages(page_pool, offsets, slots, 2, span_count, slot_cap, tensor_count)
+    lead = max(range(1, span_count + 1), key=lambda d: min(d, replicas - d))
+    rest = [d for d in range(1, span_count + 1) if d != lead]
+    packed = pack_pages(page_pool, offsets, slots, [lead], slot_cap, tensor_count)
+    if rest:
+        packed = packed + pack_pages(page_pool, offsets, slots, rest, slot_cap, tensor_count)
+    order = [lead] + rest
+    payload = [None] * (span_count * tensor_count)
+    for number, distance in enumerate(order):
+        for shift in range(tensor_count):
+            payload[(distance - 1) * tensor_count + shift] = packed[number * tensor_count + shift]
 
     arrivals = []
     for distance in range(1, span_count + 1):

time: 62.2 us -> 64.5 us (1.037)
  the two profiles are of different devices: /device:TPU:1 before, /device:TPU:0 now
where the time goes in v17:
time: 64.5 us; the launch traced here: 64.2 us
  waiting for transfers between devices  31 us (48%)
  starting transfers between devices  14.9 us (23%)
  Pallas kernels  14 us (22%)
  local copies, waits for them, and re-layouts  2.19 us (3%)
  other arithmetic  2.12 us (3%)
    ppermute x12, waiting for transfers between devices, on_device(): lax.ppermute(payload[(distance - 1) * tensor_count + shift], ('replica',...  31 us
    ppermute x12, starting transfers between devices, on_device(): lax.ppermute(payload[(distance - 1) * tensor_count + shift], ('replica',...  14.9 us
    pallas_call x1, Pallas kernels, attend(): pl.pallas_call(functools.partial(attention_kernel, span_count, tensor_cou...  7.83 us
    pallas_call x2, Pallas kernels, pack_pages(): pl.pallas_call(functools.partial(gather_kernel, tuple(chosen_distances),...  6.15 us
  transfers between devices with their start and end apart: 12, of which 9 were waited for; matrix products, arithmetic and copies ran while one was open for 6% of the time, Pallas kernels for 5%

profile of v17, /device:TPU:0, one launch (start us, length us, event | category | flops | bytes accessed | tf_op | source)
XLA Modules:
  0.0 64.2 jit_solution(9768326859919783201)
XLA Ops:
  0.0 2.9 %shard_map.65 = (bf16[4,2,32,256]{3,2,1,0:T(8,128)(2,1)}, bf16[4,2,32,256]{3,2,1,0:T(8,128)(2,1)}, bf16[4,2,32,256]{3,2,1,0:T(8,128)(2,1)}, bf16[4,2,32,256]{3,2,1,0:T(8,128)(2,1)}) custom-call(s32[4,8]{1,0:T(4,128)} %off_ref.3, s32[4,8]{1,0:T(4,128)} %slot_ref.3, bf16[12,2,32,1024]{3,2,1,0:T(8,128)(2,1)} %pool_hbm.3), custom_call_target="tpu_custom_call" | custom-call | bytes 1048576 | tf_op jit(solution)/shard_map/pallas_call | solution.py:82
  2.9 4.1 %collective-permute-start.4 = (bf16[4,2,32,256]{3,2,1,0:T(8,128)(2,1)}, bf16[4,2,32,256]{3,2,1,0:T(8,128)(2,1)S(1)}, u32[]{:S(2)}, u32[]{:S(2)}) collective-permute-start(bf16[4,2,32,256]{3,2,1,0:T(8,128)(2,1)} %get-tuple-element.21), channel_id=1, source_target_pairs={{0,8},{1,9},{2,10},{3,11},{4,12},{5,13},{6,14},{7,15},{8,0},{9,1},... | collective-permute-start | bytes 393224 | tf_op jit(solution)/shard_map/ppermute | solution.py:119
  7.0 3.0 %collective-permute-start.6 = (bf16[4,2,32,256]{3,2,1,0:T(8,128)(2,1)}, bf16[4,2,32,256]{3,2,1,0:T(8,128)(2,1)S(1)}, u32[]{:S(2)}, u32[]{:S(2)}) collective-permute-start(bf16[4,2,32,256]{3,2,1,0:T(8,128)(2,1)} %get-tuple-element.23), channel_id=1, source_target_pairs={{0,10},{1,11},{2,8},{3,9},{4,14},{5,15},{6,12},{7,13},{8,2},{9,3},... | collective-permute-start | bytes 393224 | tf_op jit(solution)/shard_map/ppermute | solution.py:119
  10.1 1.5 %collective-permute-start.7 = (bf16[4,2,32,256]{3,2,1,0:T(8,128)(2,1)}, bf16[4,2,32,256]{3,2,1,0:T(8,128)(2,1)S(1)}, u32[]{:S(2)}, u32[]{:S(2)}) collective-permute-start(bf16[4,2,32,256]{3,2,1,0:T(8,128)(2,1)} %get-tuple-element.24), channel_id=1, source_target_pairs={{0,11},{1,8},{2,9},{3,10},{4,15},{5,12},{6,13},{7,14},{8,3},{9,0},... | collective-permute-start | bytes 393224 | tf_op jit(solution)/shard_map/ppermute | solution.py:119
  11.6 3.2 %shard_map.64 = (bf16[4,2,32,256]{3,2,1,0:T(8,128)(2,1)}, bf16[4,2,32,256]{3,2,1,0:T(8,128)(2,1)}, bf16[4,2,32,256]{3,2,1,0:T(8,128)(2,1)}, bf16[4,2,32,256]{3,2...) custom-call(s32[4,8]{1,0:T(4,128)} %off_ref.3, ...), custom_call_target="tpu_custom_call" | custom-call | bytes 2097152 | tf_op jit(solution)/shard_map/pallas_call | solution.py:82
  14.8 1.7 %collective-permute-start = (bf16[4,2,32,256]{3,2,1,0:T(8,128)(2,1)}, bf16[4,2,32,256]{3,2,1,0:T(8,128)(2,1)S(1)}, u32[]{:S(2)}, u32[]{:S(2)}) collective-permute-start(bf16[4,2,32,256]{3,2,1,0:T(8,128)(2,1)} %get-tuple-element.17), channel_id=1, source_target_pairs={{0,4},{1,5},{2,6},{3,7},{4,8},{5,9},{6,10},{7,11},{8,12},{9,13},{1... | collective-permute-start | bytes 393224 | tf_op jit(solution)/shard_map/ppermute | solution.py:119
  16.5 0.1 add.76
  16.6 0.1 broadcast_add_fusion
  16.6 0.1 add.73
  16.7 0.1 add.74
  16.8 0.7 %dynamic_slice.9 = s32[1]{0:T(128)} dynamic-slice(s32[4]{0:T(128)S(1)} %copy-done.12, s32[]{:T(128)S(6)} %select_n.17), dynamic_slice_sizes={1} | dynamic-slice | bytes 12 | tf_op jit(solution)/shard_map/jit(dynamic_index_in_dim)/dynamic_slice | solution.py:125
  17.5 8.2 %collective-permute-done.4.rest_4_ = bf16[4,2,32,256]{3,2,1,0:T(8,128)(2,1)S(1)} collective-permute-done((bf16[4,2,32,256]{3,2,1,0:T(8,128)(2,1)}, bf16[4,2,32,256]{3,2,1,0:T(8,128)(2,1)S(1)}, u32[]{:S(2)}, u32[]{:S(2)}) %collective-permute-start.4) | collective-permute-done | bytes 131104 | tf_op jit(solution)/shard_map/ppermute | solution.py:119
  25.6 1.8 %collective-permute-done.5.rest_5_ = bf16[4,2,32,256]{3,2,1,0:T(8,128)(2,1)S(1)} collective-permute-done((bf16[4,2,32,256]{3,2,1,0:T(8,128)(2,1)}, bf16[4,2,32,256]{3,2,1,0:T(8,128)(2,1)S(1)}, u32[]{:S(2)}, u32[]{:S(2)}) %collective-permute-start.5) | collective-permute-done | bytes 131104 | tf_op jit(solution)/shard_map/ppermute | solution.py:119
  27.5 1.2 %compare_convert_fusion.vis_ref = s32[8,1,128]{2,1,0:T(1,128)} fusion(s32[8,1,128]{2,1,0:T(1,128)S(1)} %add.74, s32[]{:T(128)} %bitcast.3, s32[128]{0:T(128)S(1)} %add.76), kind=kLoop, calls=%fused_computation | loop fusion | flops 3072 | bytes 8708 | tf_op jit(solution)/shard_map/convert_element_type | solution.py:138
  28.7 0.7 %dynamic-slice_bitcast_fusion = s32[8]{0:T(128)S(1)} fusion(s32[4,8]{1,0:T(4,128)} %off_ref.3, s32[]{:T(128)S(6)} %select_n.17), kind=kLoop, calls=%fused_computation.11 | loop fusion | bytes 68 | tf_op jit(solution)/shard_map/jit(dynamic_index_in_dim)/squeeze | solution.py:124
  29.4 8.8 %collective-permute-done.6.rest_6_ = bf16[4,2,32,256]{3,2,1,0:T(8,128)(2,1)S(1)} collective-permute-done((bf16[4,2,32,256]{3,2,1,0:T(8,128)(2,1)}, bf16[4,2,32,256]{3,2,1,0:T(8,128)(2,1)S(1)}, u32[]{:S(2)}, u32[]{:S(2)}) %collective-permute-start.6) | collective-permute-done | bytes 131104 | tf_op jit(solution)/shard_map/ppermute | solution.py:119
  38.1 0.0 collective-permute-start.3
  38.1 1.3 %collective-permute-done.7.rest_7_ = bf16[4,2,32,256]{3,2,1,0:T(8,128)(2,1)S(1)} collective-permute-done((bf16[4,2,32,256]{3,2,1,0:T(8,128)(2,1)}, bf16[4,2,32,256]{3,2,1,0:T(8,128)(2,1)S(1)}, u32[]{:S(2)}, u32[]{:S(2)}) %collective-permute-start.7) | collective-permute-done | bytes 131104 | tf_op jit(solution)/shard_map/ppermute | solution.py:119
  39.4 0.0 collective-permute-done.rest_0_
  39.4 2.3 %collective-permute-start.9 = (bf16[4,2,32,256]{3,2,1,0:T(8,128)(2,1)}, bf16[4,2,32,256]{3,2,1,0:T(8,128)(2,1)S(1)}, u32[]{:S(2)}, u32[]{:S(2)}) collective-permute-start(bf16[4,2,32,256]{3,2,1,0:T(8,128)(2,1)} %get-tuple-element.26), channel_id=1, source_target_pairs={{0,13},{1,14},{2,15},{3,12},{4,1},{5,2},{6,3},{7,0},{8,5},{9,6},{1... | collective-permute-start | bytes 393224 | tf_op jit(solution)/shard_map/ppermute | solution.py:119
  41.8 0.0 collective-permute-done.1.rest_1_
  41.8 1.0 %collective-permute-start.10 = (bf16[4,2,32,256]{3,2,1,0:T(8,128)(2,1)}, bf16[4,2,32,256]{3,2,1,0:T(8,128)(2,1)S(1)}, u32[]{:S(2)}, u32[]{:S(2)}) collective-permute-start(bf16[4,2,32,256]{3,2,1,0:T(8,128)(2,1)} %get-tuple-element.27), channel_id=1, source_target_pairs={{0,14},{1,15},{2,12},{3,13},{4,2},{5,3},{6,0},{7,1},{8,6},{9,7},{1... | collective-permute-start | bytes 393224 | tf_op jit(solution)/shard_map/ppermute | solution.py:119
  42.8 1.2 %collective-permute-start.11 = (bf16[4,2,32,256]{3,2,1,0:T(8,128)(2,1)}, bf16[4,2,32,256]{3,2,1,0:T(8,128)(2,1)S(1)}, u32[]{:S(2)}, u32[]{:S(2)}) collective-permute-start(bf16[4,2,32,256]{3,2,1,0:T(8,128)(2,1)} %get-tuple-element.28), channel_id=1, source_target_pairs={{0,15},{1,12},{2,13},{3,14},{4,3},{5,0},{6,1},{7,2},{8,7},{9,4},{1... | collective-permute-start | bytes 393224 | tf_op jit(solution)/shard_map/ppermute | solution.py:119
  44.0 0.2 select_reduce_fusion
  44.2 0.6 pad_add_fusion.tab_ref
  44.8 1.1 %collective-permute-done.3.rest_3_ = bf16[4,2,32,256]{3,2,1,0:T(8,128)(2,1)S(1)} collective-permute-done((bf16[4,2,32,256]{3,2,1,0:T(8,128)(2,1)}, bf16[4,2,32,256]{3,2,1,0:T(8,128)(2,1)S(1)}, u32[]{:S(2)}, u32[]{:S(2)}) %collective-permute-start.3) | collective-permute-done | bytes 131104 | tf_op jit(solution)/shard_map/ppermute | solution.py:119
  45.9 0.9 %collective-permute-done.8.rest_8_ = bf16[4,2,32,256]{3,2,1,0:T(8,128)(2,1)S(1)} collective-permute-done((bf16[4,2,32,256]{3,2,1,0:T(8,128)(2,1)}, bf16[4,2,32,256]{3,2,1,0:T(8,128)(2,1)S(1)}, u32[]{:S(2)}, u32[]{:S(2)}) %collective-permute-start.8) | collective-permute-done | bytes 131104 | tf_op jit(solution)/shard_map/ppermute | solution.py:119
  46.8 3.1 %collective-permute-done.9.rest_9_ = bf16[4,2,32,256]{3,2,1,0:T(8,128)(2,1)S(1)} collective-permute-done((bf16[4,2,32,256]{3,2,1,0:T(8,128)(2,1)}, bf16[4,2,32,256]{3,2,1,0:T(8,128)(2,1)S(1)}, u32[]{:S(2)}, u32[]{:S(2)}) %collective-permute-start.9) | collective-permute-done | bytes 131104 | tf_op jit(solution)/shard_map/ppermute | solution.py:119
  50.0 1.9 %collective-permute-done.10.rest_10_ = bf16[4,2,32,256]{3,2,1,0:T(8,128)(2,1)S(1)} collective-permute-done((bf16[4,2,32,256]{3,2,1,0:T(8,128)(2,1)}, bf16[4,2,32,256]{3,2,1,0:T(8,128)(2,1)S(1)}, u32[]{:S(2)}, u32[]{:S(2)}) %collective-permute-start.10) | collective-permute-done | bytes 131104 | tf_op jit(solution)/shard_map/ppermute | solution.py:119
  51.8 3.9 %collective-permute-done.11.rest_11_ = bf16[4,2,32,256]{3,2,1,0:T(8,128)(2,1)S(1)} collective-permute-done((bf16[4,2,32,256]{3,2,1,0:T(8,128)(2,1)}, bf16[4,2,32,256]{3,2,1,0:T(8,128)(2,1)S(1)}, u32[]{:S(2)}, u32[]{:S(2)}) %collective-permute-start.11) | collective-permute-done | bytes 131104 | tf_op jit(solution)/shard_map/ppermute | solution.py:119
  55.9 0.5 copy-done.11
  56.4 7.8 %shard_map.66 = bf16[128,2048]{1,0:T(8,128)(2,1)} custom-call(s32[16]{0:T(128)} %pad_add_fusion.tab_ref, bf16[128,2048]{1,0:T(8,128)(2,1)} %bitcast.6, bf16[2,128,256]{2,1,0:T(8,128)(2,1)} %bitcast.7, s32[8,1,128]{2,1,0:T(1,128)} %compare_convert_fusion.vis_ref, bf16[4,2,32,256]{3,2,1,0:T(8,128)(2,1)} %copy-done.4, bf16[4,2,32,256]{3,2,1,0:T(8,128)(2,1)} %copy-done.5, ...), custom_call_target="tpu_custom_call" | custom-call | flops 1207959552 | bytes 2752512 | tf_op jit(solution)/shard_map/pallas_call | solution.py:225
  (33 shorter events, 0.1 us)
Async XLA Ops:
  0.0 16.8 %copy-start.12 = (s32[4]{0:T(128)S(1)}, s32[4]{0:T(128)}, u32[]{:S(2)}) copy-start(s32[4]{0:T(128)} %param.11) | copy-start | bytes 52
  2.9 22.7 %collective-permute-start.4 = (bf16[4,2,32,256]{3,2,1,0:T(8,128)(2,1)}, bf16[4,2,32,256]{3,2,1,0:T(8,128)(2,1)S(1)}, u32[]{:S(2)}, u32[]{:S(2)}) collective-permute-start(bf16[4,2,32,256]{3,2,1,0:T(8,128)(2,1)} %get-tuple-element.21), channel_id=1, source_target_pairs={{0,8},{1,9},{2,10},{3,11},{4,12},{5,13},{6,14},{7,15},{8,0},{9,1},... | collective-permute-start | bytes 393224 | tf_op jit(solution)/shard_map/ppermute | solution.py:119
  7.0 20.4 %collective-permute-start.5 = (bf16[4,2,32,256]{3,2,1,0:T(8,128)(2,1)}, bf16[4,2,32,256]{3,2,1,0:T(8,128)(2,1)S(1)}, u32[]{:S(2)}, u32[]{:S(2)}) collective-permute-start(bf16[4,2,32,256]{3,2,1,0:T(8,128)(2,1)} %get-tuple-element.22), channel_id=1, source_target_pairs={{0,9},{1,10},{2,11},{3,8},{4,13},{5,14},{6,15},{7,12},{8,1},{9,2},... | collective-permute-start | bytes 393224 | tf_op jit(solution)/shard_map/ppermute | solution.py:119
  7.0 31.1 %collective-permute-start.6 = (bf16[4,2,32,256]{3,2,1,0:T(8,128)(2,1)}, bf16[4,2,32,256]{3,2,1,0:T(8,128)(2,1)S(1)}, u32[]{:S(2)}, u32[]{:S(2)}) collective-permute-start(bf16[4,2,32,256]{3,2,1,0:T(8,128)(2,1)} %get-tuple-element.23), channel_id=1, source_target_pairs={{0,10},{1,11},{2,8},{3,9},{4,14},{5,15},{6,12},{7,13},{8,2},{9,3},... | collective-permute-start | bytes 393224 | tf_op jit(solution)/shard_map/ppermute | solution.py:119
  10.1 29.4 %collective-permute-start.7 = (bf16[4,2,32,256]{3,2,1,0:T(8,128)(2,1)}, bf16[4,2,32,256]{3,2,1,0:T(8,128)(2,1)S(1)}, u32[]{:S(2)}, u32[]{:S(2)}) collective-permute-start(bf16[4,2,32,256]{3,2,1,0:T(8,128)(2,1)} %get-tuple-element.24), channel_id=1, source_target_pairs={{0,11},{1,8},{2,9},{3,10},{4,15},{5,12},{6,13},{7,14},{8,3},{9,0},... | collective-permute-start | bytes 393224 | tf_op jit(solution)/shard_map/ppermute | solution.py:119
  14.8 24.6 %collective-permute-start = (bf16[4,2,32,256]{3,2,1,0:T(8,128)(2,1)}, bf16[4,2,32,256]{3,2,1,0:T(8,128)(2,1)S(1)}, u32[]{:S(2)}, u32[]{:S(2)}) collective-permute-start(bf16[4,2,32,256]{3,2,1,0:T(8,128)(2,1)} %get-tuple-element.17), channel_id=1, source_target_pairs={{0,4},{1,5},{2,6},{3,7},{4,8},{5,9},{6,10},{7,11},{8,12},{9,13},{1... | collective-permute-start | bytes 393224 | tf_op jit(solution)/shard_map/ppermute | solution.py:119
  25.6 30.2 %copy-start = (bf16[4,2,32,256]{3,2,1,0:T(8,128)(2,1)}, bf16[4,2,32,256]{3,2,1,0:T(8,128)(2,1)S(1)}, u32[]{:S(2)}) copy-start(bf16[4,2,32,256]{3,2,1,0:T(8,128)(2,1)S(1)} %collective-permute-done.4.rest_4_) | copy-start | bytes 393220
  25.6 16.1 %collective-permute-start.1 = (bf16[4,2,32,256]{3,2,1,0:T(8,128)(2,1)}, bf16[4,2,32,256]{3,2,1,0:T(8,128)(2,1)S(1)}, u32[]{:S(2)}, u32[]{:S(2)}) collective-permute-start(bf16[4,2,32,256]{3,2,1,0:T(8,128)(2,1)} %get-tuple-element.18), channel_id=1, source_target_pairs={{0,5},{1,6},{2,7},{3,4},{4,9},{5,10},{6,11},{7,8},{8,13},{9,14},{1... | collective-permute-start | bytes 393224 | tf_op jit(solution)/shard_map/ppermute | solution.py:119
  27.4 28.3 %copy-start.1 = (bf16[4,2,32,256]{3,2,1,0:T(8,128)(2,1)}, bf16[4,2,32,256]{3,2,1,0:T(8,128)(2,1)S(1)}, u32[]{:S(2)}) copy-start(bf16[4,2,32,256]{3,2,1,0:T(8,128)(2,1)S(1)} %collective-permute-done.5.rest_5_) | copy-start | bytes 393220
  27.5 15.4 %collective-permute-start.2 = (bf16[4,2,32,256]{3,2,1,0:T(8,128)(2,1)}, bf16[4,2,32,256]{3,2,1,0:T(8,128)(2,1)S(1)}, u32[]{:S(2)}, u32[]{:S(2)}) collective-permute-start(bf16[4,2,32,256]{3,2,1,0:T(8,128)(2,1)} %get-tuple-element.19), channel_id=1, source_target_pairs={{0,6},{1,7},{2,4},{3,5},{4,10},{5,11},{6,8},{7,9},{8,14},{9,15},{1... | collective-permute-start | bytes 393224 | tf_op jit(solution)/shard_map/ppermute | solution.py:119
  38.1 17.6 %copy-start.2 = (bf16[4,2,32,256]{3,2,1,0:T(8,128)(2,1)}, bf16[4,2,32,256]{3,2,1,0:T(8,128)(2,1)S(1)}, u32[]{:S(2)}) copy-start(bf16[4,2,32,256]{3,2,1,0:T(8,128)(2,1)S(1)} %collective-permute-done.6.rest_6_) | copy-start | bytes 393220
  38.1 7.8 %collective-permute-start.3 = (bf16[4,2,32,256]{3,2,1,0:T(8,128)(2,1)}, bf16[4,2,32,256]{3,2,1,0:T(8,128)(2,1)S(1)}, u32[]{:S(2)}, u32[]{:S(2)}) collective-permute-start(bf16[4,2,32,256]{3,2,1,0:T(8,128)(2,1)} %get-tuple-element.20), channel_id=1, source_target_pairs={{0,7},{1,4},{2,5},{3,6},{4,11},{5,8},{6,9},{7,10},{8,15},{9,12},{1... | collective-permute-start | bytes 393224 | tf_op jit(solution)/shard_map/ppermute | solution.py:119
  39.4 16.4 %copy-start.3 = (bf16[4,2,32,256]{3,2,1,0:T(8,128)(2,1)}, bf16[4,2,32,256]{3,2,1,0:T(8,128)(2,1)S(1)}, u32[]{:S(2)}) copy-start(bf16[4,2,32,256]{3,2,1,0:T(8,128)(2,1)S(1)} %collective-permute-done.7.rest_7_) | copy-start | bytes 393220
  39.4 7.4 %collective-permute-start.8 = (bf16[4,2,32,256]{3,2,1,0:T(8,128)(2,1)}, bf16[4,2,32,256]{3,2,1,0:T(8,128)(2,1)S(1)}, u32[]{:S(2)}, u32[]{:S(2)}) collective-permute-start(bf16[4,2,32,256]{3,2,1,0:T(8,128)(2,1)} %get-tuple-element.25), channel_id=1, source_target_pairs={{0,12},{1,13},{2,14},{3,15},{4,0},{5,1},{6,2},{7,3},{8,4},{9,5},{1... | collective-permute-start | bytes 393224 | tf_op jit(solution)/shard_map/ppermute | solution.py:119
  39.4 16.4 %copy-start.4 = (bf16[4,2,32,256]{3,2,1,0:T(8,128)(2,1)}, bf16[4,2,32,256]{3,2,1,0:T(8,128)(2,1)S(1)}, u32[]{:S(2)}) copy-start(bf16[4,2,32,256]{3,2,1,0:T(8,128)(2,1)S(1)} %collective-permute-done.rest_0_) | copy-start | bytes 393220
  39.4 10.5 %collective-permute-start.9 = (bf16[4,2,32,256]{3,2,1,0:T(8,128)(2,1)}, bf16[4,2,32,256]{3,2,1,0:T(8,128)(2,1)S(1)}, u32[]{:S(2)}, u32[]{:S(2)}) collective-permute-start(bf16[4,2,32,256]{3,2,1,0:T(8,128)(2,1)} %get-tuple-element.26), channel_id=1, source_target_pairs={{0,13},{1,14},{2,15},{3,12},{4,1},{5,2},{6,3},{7,0},{8,5},{9,6},{1... | collective-permute-start | bytes 393224 | tf_op jit(solution)/shard_map/ppermute | solution.py:119
  41.8 14.0 %copy-start.5 = (bf16[4,2,32,256]{3,2,1,0:T(8,128)(2,1)}, bf16[4,2,32,256]{3,2,1,0:T(8,128)(2,1)S(1)}, u32[]{:S(2)}) copy-start(bf16[4,2,32,256]{3,2,1,0:T(8,128)(2,1)S(1)} %collective-permute-done.1.rest_1_) | copy-start | bytes 393220
  41.8 10.1 %collective-permute-start.10 = (bf16[4,2,32,256]{3,2,1,0:T(8,128)(2,1)}, bf16[4,2,32,256]{3,2,1,0:T(8,128)(2,1)S(1)}, u32[]{:S(2)}, u32[]{:S(2)}) collective-permute-start(bf16[4,2,32,256]{3,2,1,0:T(8,128)(2,1)} %get-tuple-element.27), channel_id=1, source_target_pairs={{0,14},{1,15},{2,12},{3,13},{4,2},{5,3},{6,0},{7,1},{8,6},{9,7},{1... | collective-permute-start | bytes 393224 | tf_op jit(solution)/shard_map/ppermute | solution.py:119
  42.8 13.0 %copy-start.6 = (bf16[4,2,32,256]{3,2,1,0:T(8,128)(2,1)}, bf16[4,2,32,256]{3,2,1,0:T(8,128)(2,1)S(1)}, u32[]{:S(2)}) copy-start(bf16[4,2,32,256]{3,2,1,0:T(8,128)(2,1)S(1)} %collective-permute-done.2.rest_2_) | copy-start | bytes 393220
  42.8 13.0 %collective-permute-start.11 = (bf16[4,2,32,256]{3,2,1,0:T(8,128)(2,1)}, bf16[4,2,32,256]{3,2,1,0:T(8,128)(2,1)S(1)}, u32[]{:S(2)}, u32[]{:S(2)}) collective-permute-start(bf16[4,2,32,256]{3,2,1,0:T(8,128)(2,1)} %get-tuple-element.28), channel_id=1, source_target_pairs={{0,15},{1,12},{2,13},{3,14},{4,3},{5,0},{6,1},{7,2},{8,7},{9,4},{1... | collective-permute-start | bytes 393224 | tf_op jit(solution)/shard_map/ppermute | solution.py:119
  45.9 9.9 %copy-start.7 = (bf16[4,2,32,256]{3,2,1,0:T(8,128)(2,1)}, bf16[4,2,32,256]{3,2,1,0:T(8,128)(2,1)S(1)}, u32[]{:S(2)}) copy-start(bf16[4,2,32,256]{3,2,1,0:T(8,128)(2,1)S(1)} %collective-permute-done.3.rest_3_) | copy-start | bytes 393220
  46.8 9.0 %copy-start.8 = (bf16[4,2,32,256]{3,2,1,0:T(8,128)(2,1)}, bf16[4,2,32,256]{3,2,1,0:T(8,128)(2,1)S(1)}, u32[]{:S(2)}) copy-start(bf16[4,2,32,256]{3,2,1,0:T(8,128)(2,1)S(1)} %collective-permute-done.8.rest_8_) | copy-start | bytes 393220
  50.0 5.9 %copy-start.9 = (bf16[4,2,32,256]{3,2,1,0:T(8,128)(2,1)}, bf16[4,2,32,256]{3,2,1,0:T(8,128)(2,1)S(1)}, u32[]{:S(2)}) copy-start(bf16[4,2,32,256]{3,2,1,0:T(8,128)(2,1)S(1)} %collective-permute-done.9.rest_9_) | copy-start | bytes 393220
  51.8 4.0 %copy-start.10 = (bf16[4,2,32,256]{3,2,1,0:T(8,128)(2,1)}, bf16[4,2,32,256]{3,2,1,0:T(8,128)(2,1)S(1)}, u32[]{:S(2)}) copy-start(bf16[4,2,32,256]{3,2,1,0:T(8,128)(2,1)S(1)} %collective-permute-done.10.rest_10_) | copy-start | bytes 393220
  55.8 0.6 copy-start.11

commit v18 on v13

--- a/solution.py
+++ b/solution.py
@@ -114,28 +114,25 @@
     quarter = page_pool.shape[2]
     page_rows = quarter * tensor_count
     suffix_rows = queries.shape[1]
-    own_offsets = lax.dynamic_index_in_dim(offsets, reader, 0, keepdims=False)
-    own_length = lax.dynamic_index_in_dim(prefix_len, reader, 0, keepdims=False)
-    page_ids = jnp.arange(page_count, dtype=jnp.int32)
-    earlier = (page_ids[None, :] < page_ids[:, None]).astype(jnp.int32)
-    same = (own_offsets[:, None] == own_offsets[None, :]).astype(jnp.int32)
-    rank = jnp.sum(same * earlier, axis=1)
-    table = jnp.concatenate([own_offsets, rank]).astype(jnp.int32)
-    shifts = jnp.arange(tensor_count, dtype=jnp.int32)
-    row_ids = jnp.arange(quarter, dtype=jnp.int32)
-    position = (
-        page_ids[:, None, None] * page_rows
-        + ((me - shifts + tensor_count) % tensor_count)[None, :, None] * quarter
-        + row_ids[None, None, :]
-    )
-    visible = (position < own_length).astype(jnp.int32).reshape(page_count, 1, -1)
-    result = attend(queries[0], suffix_kv[0], table, visible, arrivals, span_count, tensor_count)
+    result = attend(queries[0], suffix_kv[0], offsets, prefix_len, arrivals, span_count, tensor_count)
     return result.reshape(1, suffix_rows, result.shape[1])
 
 
-def attention_kernel(span_count, tensor_count, tab_ref, q_ref, suf_ref, vis_ref, *rest):
+def attention_kernel(span_count, tensor_count, off_ref, len_ref, q_ref, suf_ref, *rest):
     chunk_refs, o_ref = rest[:-1], rest[-1]
-    page_count = vis_ref.shape[0]
+    replicas, page_count = off_ref.shape
+    reader = lax.axis_index("replica")
+    me = lax.axis_index("tensor")
+    length = len_ref[reader]
+    quarter = chunk_refs[0].shape[2]
+    page_rows = quarter * tensor_count
+    page_distance = [off_ref[reader, page] for page in range(page_count)]
+    page_slot = []
+    for page in range(page_count):
+        rank = jnp.int32(0)
+        for other in range(page):
+            rank = rank + (page_distance[other] == page_distance[page]).astype(jnp.int32)
+        page_slot.append(rank)
     rows, width = q_ref.shape
     group = HEADS // KV_HEADS
     kv_local = width // (group * HEAD_DIM)
@@ -144,6 +141,14 @@
     row_pos = lax.broadcasted_iota(jnp.int32, (group * rows, rows), 0) % rows
     col_pos = lax.broadcasted_iota(jnp.int32, (group * rows, rows), 1)
     causal = col_pos <= row_pos
+
+    def page_mask(first, count):
+        col = lax.broadcasted_iota(jnp.int32, (1, count * page_rows), 1)
+        page = first + col // page_rows
+        shift = (col % page_rows) // quarter
+        position = page * page_rows + ((me - shift + tensor_count) % tensor_count) * quarter + col % quarter
+        return position < length
+
     for head in range(kv_local):
         lanes = pl.ds(head * HEAD_DIM, HEAD_DIM)
         q_all = jnp.concatenate(
@@ -151,7 +156,7 @@
         )
 
         def page_part(page, part):
-            distance, slot = tab_ref[page], tab_ref[page_count + page]
+            distance, slot = page_distance[page], page_slot[page]
             pieces = []
             for shift in range(tensor_count):
                 piece = chunk_refs[shift][slot, part, :, lanes]
@@ -168,9 +173,7 @@
         for page in range(0, page_count, join):
             keys.append(jnp.concatenate([page_part(p, 0) for p in range(page, page + join)], axis=0))
             vals.append(jnp.concatenate([page_part(p, 1) for p in range(page, page + join)], axis=0))
-            masks.append(
-                jnp.concatenate([vis_ref[p] for p in range(page, page + join)], axis=-1) > 0
-            )
+            masks.append(page_mask(page, join))
         scores = []
         for key, mask in zip(keys, masks):
             s = lax.dot_general(q_all, key, dims, preferred_element_type=jnp.float32)
@@ -200,20 +203,22 @@
             o_ref[:, pl.ds((head * group + g) * HEAD_DIM, HEAD_DIM)] = out[g * rows:(g + 1) * rows]
 
 
-def attend(q, suf, table, visible, chunks, span_count, tensor_count):
+def attend(q, suf, offsets, prefix_len, chunks, span_count, tensor_count):
     rows, width = q.shape
-    keys_total = suf.shape[1] + visible.shape[0] * visible.shape[2]
+    page_count = offsets.shape[1]
+    chunk_keys = chunks[0].shape[0] * chunks[0].shape[2] * tensor_count // chunks[0].shape[0]
+    keys_total = suf.shape[1] + page_count * chunk_keys
     flops = 4 * rows * width * keys_total
     nbytes = 2 * (q.size * 2 + suf.size + sum(c.size for c in chunks))
 
     def whole(a):
-        return pl.BlockSpec(a.shape, lambda i, t: (0,) * a.ndim)
+        return pl.BlockSpec(a.shape, lambda i, o, n: (0,) * a.ndim)
 
     grid_spec = pltpu.PrefetchScalarGridSpec(
-        num_scalar_prefetch=1,
+        num_scalar_prefetch=2,
         grid=(1,),
-        in_specs=[whole(q), whole(suf), whole(visible)] + [whole(c) for c in chunks],
-        out_specs=pl.BlockSpec((rows, width), lambda i, t: (0, 0)),
+        in_specs=[whole(q), whole(suf)] + [whole(c) for c in chunks],
+        out_specs=pl.BlockSpec((rows, width), lambda i, o, n: (0, 0)),
     )
     return pl.pallas_call(
         functools.partial(attention_kernel, span_count, tensor_count),
@@ -222,7 +227,7 @@
         cost_estimate=pl.CostEstimate(
             flops=flops, transcendentals=rows * (width // HEAD_DIM) * keys_total, bytes_accessed=nbytes
         ),
-    )(table, q, suf, visible, *chunks)
+    )(offsets, prefix_len, q, suf, *chunks)
 
 
 def solution(mesh):

time: 62.2 us -> 61.9 us (level)
  waiting for transfers between devices: 11.2 us -> 15.4 us
  other arithmetic: 2.09 us -> 0 us
  local copies, waits for them, and re-layouts: 2.17 us -> 0.59 us
    ppermute x12, waiting for transfers between devices: 11.2 us -> 15.4 us  [on_device(): lax.ppermute(payload[(distance - 1) * tensor_count + shift], ('replica',...]
    convert_element_type x1 -> x0, other arithmetic: 1.2 us -> none  [on_device(): (position < own_length).astype(jnp.int32).reshape(page_count, 1, -1)]
    squeeze x1 -> x0, local copies, waits for them, and re-layouts: 0.69 us -> none  [on_device(): own_offsets = lax.dynamic_index_in_dim(offsets, reader, 0, keepdims=False)]
    dynamic_slice x1 -> x0, local copies, waits for them, and re-layouts: 0.62 us -> none  [on_device(): own_length = lax.dynamic_index_in_dim(prefix_len, reader, 0, keepdims=False)]
    concatenate x1 -> x0, other arithmetic: 0.62 us -> none  [on_device(): table = jnp.concatenate([own_offsets, rank]).astype(jnp.int32)]
  transfers between devices with their start and end apart: 12 -> 12, of which waited for: 2 -> 3; matrix products, arithmetic and copies ran while one was open for 6% -> 0% of each run, Pallas kernels for 6% -> 6%
where the time goes in v18:
time: 61.9 us; the launch traced here: 61.6 us
  starting transfers between devices  31.7 us (51%)
  waiting for transfers between devices  15.4 us (25%)
  Pallas kernels  13.9 us (22%)
    ppermute x12, starting transfers between devices, on_device(): lax.ppermute(payload[(distance - 1) * tensor_count + shift], ('replica',...  31.7 us
    ppermute x12, waiting for transfers between devices, on_device(): lax.ppermute(payload[(distance - 1) * tensor_count + shift], ('replica',...  15.4 us
    pallas_call x1, Pallas kernels, attend(): pl.pallas_call(functools.partial(attention_kernel, span_count, tensor_cou...  7.74 us
    pallas_call x2, Pallas kernels, pack_pages(): pl.pallas_call(functools.partial(gather_kernel, first, last, slot_cap, te...  6.15 us
  transfers between devices with their start and end apart: 12, of which 3 were waited for; matrix products, arithmetic and copies ran while one was open for 0% of the time, Pallas kernels for 6%

profile of v18, /device:TPU:1, one launch (start us, length us, event | category | flops | bytes accessed | tf_op | source)
XLA Modules:
  0.0 61.6 jit_solution(1039143805600746759)
XLA Ops:
  0.0 2.7 %shard_map.64 = (bf16[4,2,32,256]{3,2,1,0:T(8,128)(2,1)}, bf16[4,2,32,256]{3,2,1,0:T(8,128)(2,1)}, bf16[4,2,32,256]{3,2,1,0:T(8,128)(2,1)}, bf16[4,2,32,256]{3,2,1,0:T(8,128)(2,1)}) custom-call(s32[4,8]{1,0:T(4,128)} %off_ref.5, s32[4,8]{1,0:T(4,128)} %slot_ref.3, bf16[12,2,32,1024]{3,2,1,0:T(8,128)(2,1)} %pool_hbm.3), custom_call_target="tpu_custom_call" | custom-call | bytes 1048576 | tf_op jit(solution)/shard_map/pallas_call | solution.py:82
  2.8 2.2 %collective-permute-start = (bf16[4,2,32,256]{3,2,1,0:T(8,128)(2,1)}, bf16[4,2,32,256]{3,2,1,0:T(8,128)(2,1)S(1)}, u32[]{:S(2)}, u32[]{:S(2)}) collective-permute-start(bf16[4,2,32,256]{3,2,1,0:T(8,128)(2,1)} %get-tuple-element.17), channel_id=1, source_target_pairs={{0,4},{1,5},{2,6},{3,7},{4,8},{5,9},{6,10},{7,11},{8,12},{9,13},{1... | collective-permute-start | bytes 393224 | tf_op jit(solution)/shard_map/ppermute | solution.py:112
  4.9 3.1 %collective-permute-start.1 = (bf16[4,2,32,256]{3,2,1,0:T(8,128)(2,1)}, bf16[4,2,32,256]{3,2,1,0:T(8,128)(2,1)S(1)}, u32[]{:S(2)}, u32[]{:S(2)}) collective-permute-start(bf16[4,2,32,256]{3,2,1,0:T(8,128)(2,1)} %get-tuple-element.18), channel_id=1, source_target_pairs={{0,5},{1,6},{2,7},{3,4},{4,9},{5,10},{6,11},{7,8},{8,13},{9,14},{1... | collective-permute-start | bytes 393224 | tf_op jit(solution)/shard_map/ppermute | solution.py:112
  8.0 1.3 %collective-permute-start.2 = (bf16[4,2,32,256]{3,2,1,0:T(8,128)(2,1)}, bf16[4,2,32,256]{3,2,1,0:T(8,128)(2,1)S(1)}, u32[]{:S(2)}, u32[]{:S(2)}) collective-permute-start(bf16[4,2,32,256]{3,2,1,0:T(8,128)(2,1)} %get-tuple-element.19), channel_id=1, source_target_pairs={{0,6},{1,7},{2,4},{3,5},{4,10},{5,11},{6,8},{7,9},{8,14},{9,15},{1... | collective-permute-start | bytes 393224 | tf_op jit(solution)/shard_map/ppermute | solution.py:112
  9.3 0.3 collective-permute-start.3
  9.6 3.4 %shard_map.65 = (bf16[4,2,32,256]{3,2,1,0:T(8,128)(2,1)}, bf16[4,2,32,256]{3,2,1,0:T(8,128)(2,1)}, bf16[4,2,32,256]{3,2,1,0:T(8,128)(2,1)}, bf16[4,2,32,256]{3,2...) custom-call(s32[4,8]{1,0:T(4,128)} %off_ref.5, ...), custom_call_target="tpu_custom_call" | custom-call | bytes 2097152 | tf_op jit(solution)/shard_map/pallas_call | solution.py:82
  13.0 1.6 %collective-permute-start.4 = (bf16[4,2,32,256]{3,2,1,0:T(8,128)(2,1)}, bf16[4,2,32,256]{3,2,1,0:T(8,128)(2,1)S(1)}, u32[]{:S(2)}, u32[]{:S(2)}) collective-permute-start(bf16[4,2,32,256]{3,2,1,0:T(8,128)(2,1)} %get-tuple-element.21), channel_id=1, source_target_pairs={{0,8},{1,9},{2,10},{3,11},{4,12},{5,13},{6,14},{7,15},{8,0},{9,1},... | collective-permute-start | bytes 393224 | tf_op jit(solution)/shard_map/ppermute | solution.py:112
  14.6 0.0 collective-permute-done.rest_0_
  14.6 2.0 %collective-permute-start.5 = (bf16[4,2,32,256]{3,2,1,0:T(8,128)(2,1)}, bf16[4,2,32,256]{3,2,1,0:T(8,128)(2,1)S(1)}, u32[]{:S(2)}, u32[]{:S(2)}) collective-permute-start(bf16[4,2,32,256]{3,2,1,0:T(8,128)(2,1)} %get-tuple-element.22), channel_id=1, source_target_pairs={{0,9},{1,10},{2,11},{3,8},{4,13},{5,14},{6,15},{7,12},{8,1},{9,2},... | collective-permute-start | bytes 393224 | tf_op jit(solution)/shard_map/ppermute | solution.py:112
  16.6 0.0 collective-permute-done.1.rest_1_
  16.6 3.0 %collective-permute-start.6 = (bf16[4,2,32,256]{3,2,1,0:T(8,128)(2,1)}, bf16[4,2,32,256]{3,2,1,0:T(8,128)(2,1)S(1)}, u32[]{:S(2)}, u32[]{:S(2)}) collective-permute-start(bf16[4,2,32,256]{3,2,1,0:T(8,128)(2,1)} %get-tuple-element.23), channel_id=1, source_target_pairs={{0,10},{1,11},{2,8},{3,9},{4,14},{5,15},{6,12},{7,13},{8,2},{9,3},... | collective-permute-start | bytes 393224 | tf_op jit(solution)/shard_map/ppermute | solution.py:112
  19.6 0.0 collective-permute-done.2.rest_2_
  19.6 0.0 collective-permute-start.7
  19.6 1.5 %collective-permute-done.3.rest_3_ = bf16[4,2,32,256]{3,2,1,0:T(8,128)(2,1)S(1)} collective-permute-done((bf16[4,2,32,256]{3,2,1,0:T(8,128)(2,1)}, bf16[4,2,32,256]{3,2,1,0:T(8,128)(2,1)S(1)}, u32[]{:S(2)}, u32[]{:S(2)}) %collective-permute-start.3) | collective-permute-done | bytes 131104 | tf_op jit(solution)/shard_map/ppermute | solution.py:112
  21.2 0.8 %collective-permute-start.8 = (bf16[4,2,32,256]{3,2,1,0:T(8,128)(2,1)}, bf16[4,2,32,256]{3,2,1,0:T(8,128)(2,1)S(1)}, u32[]{:S(2)}, u32[]{:S(2)}) collective-permute-start(bf16[4,2,32,256]{3,2,1,0:T(8,128)(2,1)} %get-tuple-element.25), channel_id=1, source_target_pairs={{0,12},{1,13},{2,14},{3,15},{4,0},{5,1},{6,2},{7,3},{8,4},{9,5},{1... | collective-permute-start | bytes 393224 | tf_op jit(solution)/shard_map/ppermute | solution.py:112
  22.0 11.6 %collective-permute-done.4.rest_4_ = bf16[4,2,32,256]{3,2,1,0:T(8,128)(2,1)S(1)} collective-permute-done((bf16[4,2,32,256]{3,2,1,0:T(8,128)(2,1)}, bf16[4,2,32,256]{3,2,1,0:T(8,128)(2,1)S(1)}, u32[]{:S(2)}, u32[]{:S(2)}) %collective-permute-start.4) | collective-permute-done | bytes 131104 | tf_op jit(solution)/shard_map/ppermute | solution.py:112
  33.6 6.2 %collective-permute-start.9 = (bf16[4,2,32,256]{3,2,1,0:T(8,128)(2,1)}, bf16[4,2,32,256]{3,2,1,0:T(8,128)(2,1)S(1)}, u32[]{:S(2)}, u32[]{:S(2)}) collective-permute-start(bf16[4,2,32,256]{3,2,1,0:T(8,128)(2,1)} %get-tuple-element.26), channel_id=1, source_target_pairs={{0,13},{1,14},{2,15},{3,12},{4,1},{5,2},{6,3},{7,0},{8,5},{9,6},{1... | collective-permute-start | bytes 393224 | tf_op jit(solution)/shard_map/ppermute | solution.py:112
  39.8 0.0 collective-permute-done.5.rest_5_
  39.8 2.5 %collective-permute-start.10 = (bf16[4,2,32,256]{3,2,1,0:T(8,128)(2,1)}, bf16[4,2,32,256]{3,2,1,0:T(8,128)(2,1)S(1)}, u32[]{:S(2)}, u32[]{:S(2)}) collective-permute-start(bf16[4,2,32,256]{3,2,1,0:T(8,128)(2,1)} %get-tuple-element.27), channel_id=1, source_target_pairs={{0,14},{1,15},{2,12},{3,13},{4,2},{5,3},{6,0},{7,1},{8,6},{9,7},{1... | collective-permute-start | bytes 393224 | tf_op jit(solution)/shard_map/ppermute | solution.py:112
  42.3 0.0 collective-permute-done.6.rest_6_
  42.3 8.7 %collective-permute-start.11 = (bf16[4,2,32,256]{3,2,1,0:T(8,128)(2,1)}, bf16[4,2,32,256]{3,2,1,0:T(8,128)(2,1)S(1)}, u32[]{:S(2)}, u32[]{:S(2)}) collective-permute-start(bf16[4,2,32,256]{3,2,1,0:T(8,128)(2,1)} %get-tuple-element.28), channel_id=1, source_target_pairs={{0,15},{1,12},{2,13},{3,14},{4,3},{5,0},{6,1},{7,2},{8,7},{9,4},{1... | collective-permute-start | bytes 393224 | tf_op jit(solution)/shard_map/ppermute | solution.py:112
  51.0 0.0 collective-permute-done.7.rest_7_
  51.0 0.0 collective-permute-done.8.rest_8_
  51.0 0.0 collective-permute-done.9.rest_9_
  51.0 0.0 collective-permute-done.10.rest_10_
  51.1 2.2 %collective-permute-done.11.rest_11_ = bf16[4,2,32,256]{3,2,1,0:T(8,128)(2,1)S(1)} collective-permute-done((bf16[4,2,32,256]{3,2,1,0:T(8,128)(2,1)}, bf16[4,2,32,256]{3,2,1,0:T(8,128)(2,1)S(1)}, u32[]{:S(2)}, u32[]{:S(2)}) %collective-permute-start.11) | collective-permute-done | bytes 131104 | tf_op jit(solution)/shard_map/ppermute | solution.py:112
  53.3 0.0 copy-done.3
  53.3 0.0 copy-done.4
  53.3 0.0 copy-done.5
  53.3 0.0 copy-done.6
  53.4 0.6 copy-done.11
  53.9 7.7 %shard_map.66 = bf16[128,2048]{1,0:T(8,128)(2,1)} custom-call(s32[4,8]{1,0:T(4,128)} %off_ref.5, s32[4]{0:T(128)} %len_ref.1, bf16[128,2048]{1,0:T(8,128)(2,1)} %bitcast.3, bf16[2,128,256]{2,1,0:T(8,128)(2,1)} %bitcast.4, bf16[4,2,32,256]{3,2,1,0:T(8,128)(2,1)} %copy-done, bf16[4,2,32,256]{3,2,1,0:T(8,128)(2,1)} %copy-done.1, ...), custom_call_target="tpu_custom_call" | custom-call | flops 1207959552 | bytes 2752512 | tf_op jit(solution)/shard_map/pallas_call | solution.py:223
  (19 shorter events, 0.0 us)
Async XLA Ops:
  2.8 11.9 %collective-permute-start = (bf16[4,2,32,256]{3,2,1,0:T(8,128)(2,1)}, bf16[4,2,32,256]{3,2,1,0:T(8,128)(2,1)S(1)}, u32[]{:S(2)}, u32[]{:S(2)}) collective-permute-start(bf16[4,2,32,256]{3,2,1,0:T(8,128)(2,1)} %get-tuple-element.17), channel_id=1, source_target_pairs={{0,4},{1,5},{2,6},{3,7},{4,8},{5,9},{6,10},{7,11},{8,12},{9,13},{1... | collective-permute-start | bytes 393224 | tf_op jit(solution)/shard_map/ppermute | solution.py:112
  4.9 11.7 %collective-permute-start.1 = (bf16[4,2,32,256]{3,2,1,0:T(8,128)(2,1)}, bf16[4,2,32,256]{3,2,1,0:T(8,128)(2,1)S(1)}, u32[]{:S(2)}, u32[]{:S(2)}) collective-permute-start(bf16[4,2,32,256]{3,2,1,0:T(8,128)(2,1)} %get-tuple-element.18), channel_id=1, source_target_pairs={{0,5},{1,6},{2,7},{3,4},{4,9},{5,10},{6,11},{7,8},{8,13},{9,14},{1... | collective-permute-start | bytes 393224 | tf_op jit(solution)/shard_map/ppermute | solution.py:112
  8.0 11.6 %collective-permute-start.2 = (bf16[4,2,32,256]{3,2,1,0:T(8,128)(2,1)}, bf16[4,2,32,256]{3,2,1,0:T(8,128)(2,1)S(1)}, u32[]{:S(2)}, u32[]{:S(2)}) collective-permute-start(bf16[4,2,32,256]{3,2,1,0:T(8,128)(2,1)} %get-tuple-element.19), channel_id=1, source_target_pairs={{0,6},{1,7},{2,4},{3,5},{4,10},{5,11},{6,8},{7,9},{8,14},{9,15},{1... | collective-permute-start | bytes 393224 | tf_op jit(solution)/shard_map/ppermute | solution.py:112
  9.3 11.9 %collective-permute-start.3 = (bf16[4,2,32,256]{3,2,1,0:T(8,128)(2,1)}, bf16[4,2,32,256]{3,2,1,0:T(8,128)(2,1)S(1)}, u32[]{:S(2)}, u32[]{:S(2)}) collective-permute-start(bf16[4,2,32,256]{3,2,1,0:T(8,128)(2,1)} %get-tuple-element.20), channel_id=1, source_target_pairs={{0,7},{1,4},{2,5},{3,6},{4,11},{5,8},{6,9},{7,10},{8,15},{9,12},{1... | collective-permute-start | bytes 393224 | tf_op jit(solution)/shard_map/ppermute | solution.py:112
  13.0 20.6 %collective-permute-start.4 = (bf16[4,2,32,256]{3,2,1,0:T(8,128)(2,1)}, bf16[4,2,32,256]{3,2,1,0:T(8,128)(2,1)S(1)}, u32[]{:S(2)}, u32[]{:S(2)}) collective-permute-start(bf16[4,2,32,256]{3,2,1,0:T(8,128)(2,1)} %get-tuple-element.21), channel_id=1, source_target_pairs={{0,8},{1,9},{2,10},{3,11},{4,12},{5,13},{6,14},{7,15},{8,0},{9,1},... | collective-permute-start | bytes 393224 | tf_op jit(solution)/shard_map/ppermute | solution.py:112
  14.6 38.7 %copy-start = (bf16[4,2,32,256]{3,2,1,0:T(8,128)(2,1)}, bf16[4,2,32,256]{3,2,1,0:T(8,128)(2,1)S(1)}, u32[]{:S(2)}) copy-start(bf16[4,2,32,256]{3,2,1,0:T(8,128)(2,1)S(1)} %collective-permute-done.rest_0_) | copy-start | bytes 393220
  14.6 25.2 %collective-permute-start.5 = (bf16[4,2,32,256]{3,2,1,0:T(8,128)(2,1)}, bf16[4,2,32,256]{3,2,1,0:T(8,128)(2,1)S(1)}, u32[]{:S(2)}, u32[]{:S(2)}) collective-permute-start(bf16[4,2,32,256]{3,2,1,0:T(8,128)(2,1)} %get-tuple-element.22), channel_id=1, source_target_pairs={{0,9},{1,10},{2,11},{3,8},{4,13},{5,14},{6,15},{7,12},{8,1},{9,2},... | collective-permute-start | bytes 393224 | tf_op jit(solution)/shard_map/ppermute | solution.py:112
  16.6 36.6 %copy-start.1 = (bf16[4,2,32,256]{3,2,1,0:T(8,128)(2,1)}, bf16[4,2,32,256]{3,2,1,0:T(8,128)(2,1)S(1)}, u32[]{:S(2)}) copy-start(bf16[4,2,32,256]{3,2,1,0:T(8,128)(2,1)S(1)} %collective-permute-done.1.rest_1_) | copy-start | bytes 393220
  16.6 25.7 %collective-permute-start.6 = (bf16[4,2,32,256]{3,2,1,0:T(8,128)(2,1)}, bf16[4,2,32,256]{3,2,1,0:T(8,128)(2,1)S(1)}, u32[]{:S(2)}, u32[]{:S(2)}) collective-permute-start(bf16[4,2,32,256]{3,2,1,0:T(8,128)(2,1)} %get-tuple-element.23), channel_id=1, source_target_pairs={{0,10},{1,11},{2,8},{3,9},{4,14},{5,15},{6,12},{7,13},{8,2},{9,3},... | collective-permute-start | bytes 393224 | tf_op jit(solution)/shard_map/ppermute | solution.py:112
  19.6 33.6 %copy-start.2 = (bf16[4,2,32,256]{3,2,1,0:T(8,128)(2,1)}, bf16[4,2,32,256]{3,2,1,0:T(8,128)(2,1)S(1)}, u32[]{:S(2)}) copy-start(bf16[4,2,32,256]{3,2,1,0:T(8,128)(2,1)S(1)} %collective-permute-done.2.rest_2_) | copy-start | bytes 393220
  19.6 31.4 %collective-permute-start.7 = (bf16[4,2,32,256]{3,2,1,0:T(8,128)(2,1)}, bf16[4,2,32,256]{3,2,1,0:T(8,128)(2,1)S(1)}, u32[]{:S(2)}, u32[]{:S(2)}) collective-permute-start(bf16[4,2,32,256]{3,2,1,0:T(8,128)(2,1)} %get-tuple-element.24), channel_id=1, source_target_pairs={{0,11},{1,8},{2,9},{3,10},{4,15},{5,12},{6,13},{7,14},{8,3},{9,0},... | collective-permute-start | bytes 393224 | tf_op jit(solution)/shard_map/ppermute | solution.py:112
  21.1 32.1 %copy-start.3 = (bf16[4,2,32,256]{3,2,1,0:T(8,128)(2,1)}, bf16[4,2,32,256]{3,2,1,0:T(8,128)(2,1)S(1)}, u32[]{:S(2)}) copy-start(bf16[4,2,32,256]{3,2,1,0:T(8,128)(2,1)S(1)} %collective-permute-done.3.rest_3_) | copy-start | bytes 393220
  21.2 29.9 %collective-permute-start.8 = (bf16[4,2,32,256]{3,2,1,0:T(8,128)(2,1)}, bf16[4,2,32,256]{3,2,1,0:T(8,128)(2,1)S(1)}, u32[]{:S(2)}, u32[]{:S(2)}) collective-permute-start(bf16[4,2,32,256]{3,2,1,0:T(8,128)(2,1)} %get-tuple-element.25), channel_id=1, source_target_pairs={{0,12},{1,13},{2,14},{3,15},{4,0},{5,1},{6,2},{7,3},{8,4},{9,5},{1... | collective-permute-start | bytes 393224 | tf_op jit(solution)/shard_map/ppermute | solution.py:112
  33.6 19.7 %copy-start.4 = (bf16[4,2,32,256]{3,2,1,0:T(8,128)(2,1)}, bf16[4,2,32,256]{3,2,1,0:T(8,128)(2,1)S(1)}, u32[]{:S(2)}) copy-start(bf16[4,2,32,256]{3,2,1,0:T(8,128)(2,1)S(1)} %collective-permute-done.4.rest_4_) | copy-start | bytes 393220
  33.6 17.4 %collective-permute-start.9 = (bf16[4,2,32,256]{3,2,1,0:T(8,128)(2,1)}, bf16[4,2,32,256]{3,2,1,0:T(8,128)(2,1)S(1)}, u32[]{:S(2)}, u32[]{:S(2)}) collective-permute-start(bf16[4,2,32,256]{3,2,1,0:T(8,128)(2,1)} %get-tuple-element.26), channel_id=1, source_target_pairs={{0,13},{1,14},{2,15},{3,12},{4,1},{5,2},{6,3},{7,0},{8,5},{9,6},{1... | collective-permute-start | bytes 393224 | tf_op jit(solution)/shard_map/ppermute | solution.py:112
  39.8 13.5 %copy-start.5 = (bf16[4,2,32,256]{3,2,1,0:T(8,128)(2,1)}, bf16[4,2,32,256]{3,2,1,0:T(8,128)(2,1)S(1)}, u32[]{:S(2)}) copy-start(bf16[4,2,32,256]{3,2,1,0:T(8,128)(2,1)S(1)} %collective-permute-done.5.rest_5_) | copy-start | bytes 393220
  39.8 11.3 %collective-permute-start.10 = (bf16[4,2,32,256]{3,2,1,0:T(8,128)(2,1)}, bf16[4,2,32,256]{3,2,1,0:T(8,128)(2,1)S(1)}, u32[]{:S(2)}, u32[]{:S(2)}) collective-permute-start(bf16[4,2,32,256]{3,2,1,0:T(8,128)(2,1)} %get-tuple-element.27), channel_id=1, source_target_pairs={{0,14},{1,15},{2,12},{3,13},{4,2},{5,3},{6,0},{7,1},{8,6},{9,7},{1... | collective-permute-start | bytes 393224 | tf_op jit(solution)/shard_map/ppermute | solution.py:112
  42.3 11.0 %copy-start.6 = (bf16[4,2,32,256]{3,2,1,0:T(8,128)(2,1)}, bf16[4,2,32,256]{3,2,1,0:T(8,128)(2,1)S(1)}, u32[]{:S(2)}) copy-start(bf16[4,2,32,256]{3,2,1,0:T(8,128)(2,1)S(1)} %collective-permute-done.6.rest_6_) | copy-start | bytes 393220
  42.3 11.0 %collective-permute-start.11 = (bf16[4,2,32,256]{3,2,1,0:T(8,128)(2,1)}, bf16[4,2,32,256]{3,2,1,0:T(8,128)(2,1)S(1)}, u32[]{:S(2)}, u32[]{:S(2)}) collective-permute-start(bf16[4,2,32,256]{3,2,1,0:T(8,128)(2,1)} %get-tuple-element.28), channel_id=1, source_target_pairs={{0,15},{1,12},{2,13},{3,14},{4,3},{5,0},{6,1},{7,2},{8,7},{9,4},{1... | collective-permute-start | bytes 393224 | tf_op jit(solution)/shard_map/ppermute | solution.py:112
  51.0 2.3 %copy-start.7 = (bf16[4,2,32,256]{3,2,1,0:T(8,128)(2,1)}, bf16[4,2,32,256]{3,2,1,0:T(8,128)(2,1)S(1)}, u32[]{:S(2)}) copy-start(bf16[4,2,32,256]{3,2,1,0:T(8,128)(2,1)S(1)} %collective-permute-done.7.rest_7_) | copy-start | bytes 393220
  51.0 2.3 %copy-start.8 = (bf16[4,2,32,256]{3,2,1,0:T(8,128)(2,1)}, bf16[4,2,32,256]{3,2,1,0:T(8,128)(2,1)S(1)}, u32[]{:S(2)}) copy-start(bf16[4,2,32,256]{3,2,1,0:T(8,128)(2,1)S(1)} %collective-permute-done.8.rest_8_) | copy-start | bytes 393220
  51.0 2.3 %copy-start.9 = (bf16[4,2,32,256]{3,2,1,0:T(8,128)(2,1)}, bf16[4,2,32,256]{3,2,1,0:T(8,128)(2,1)S(1)}, u32[]{:S(2)}) copy-start(bf16[4,2,32,256]{3,2,1,0:T(8,128)(2,1)S(1)} %collective-permute-done.9.rest_9_) | copy-start | bytes 393220
  51.0 2.3 %copy-start.10 = (bf16[4,2,32,256]{3,2,1,0:T(8,128)(2,1)}, bf16[4,2,32,256]{3,2,1,0:T(8,128)(2,1)S(1)}, u32[]{:S(2)}) copy-start(bf16[4,2,32,256]{3,2,1,0:T(8,128)(2,1)S(1)} %collective-permute-done.10.rest_10_) | copy-start | bytes 393220
  53.3 0.6 %copy-start.11 = (bf16[4,2,32,256]{3,2,1,0:T(8,128)(2,1)}, bf16[4,2,32,256]{3,2,1,0:T(8,128)(2,1)S(1)}, u32[]{:S(2)}) copy-start(bf16[4,2,32,256]{3,2,1,0:T(8,128)(2,1)S(1)} %collective-permute-done.11.rest_11_) | copy-start | bytes 393220

commit v19 on v18

--- a/solution.py
+++ b/solution.py
@@ -31,8 +31,9 @@
     holder = lax.axis_index("replica")
     me = lax.axis_index("tensor")
     lanes = out_refs[0].shape[-1]
+    pair_count = tensor_count // 2
     starts = [
-        pl.multiple_of(((me + shift) % tensor_count) * lanes, lanes) for shift in range(tensor_count)
+        pl.multiple_of(((me // 2 + shift) % pair_count) * lanes, lanes) for shift in range(pair_count)
     ]
     copies = []
     for distance in range(first, last + 1):
@@ -56,18 +57,18 @@
     for distance in range(first, last + 1):
         for slot in range(slot_cap):
             index = (distance - first) * slot_cap + slot
-            for shift in range(tensor_count):
-                out_refs[(distance - first) * tensor_count + shift][slot] = buf[
+            for shift in range(pair_count):
+                out_refs[(distance - first) * pair_count + shift][slot] = buf[
                     index, :, :, pl.ds(starts[shift], lanes)
                 ]
 
 
 def pack_pages(pool_part, offsets, slots, first, last, slot_cap, tensor_count):
     pages, kv, rows, width = pool_part.shape
-    lanes = width // tensor_count
+    lanes = 2 * width // tensor_count
     piece = (slot_cap, kv, rows, lanes)
     span_count = last - first + 1
-    count = span_count * tensor_count
+    count = span_count * (tensor_count // 2)
     grid_spec = pltpu.PrefetchScalarGridSpec(
         num_scalar_prefetch=2,
         grid=(1,),
@@ -101,18 +102,20 @@
     if span_count > 1:
         payload = payload + pack_pages(page_pool, offsets, slots, 2, span_count, slot_cap, tensor_count)
 
+    pair_count = tensor_count // 2
     arrivals = []
     for distance in range(1, span_count + 1):
-        for shift in range(tensor_count):
+        for shift in range(pair_count):
             pairs = []
             for source in range(replicas):
                 for peer in range(tensor_count):
-                    target = ((source + distance) % replicas) * tensor_count + (peer + shift) % tensor_count
+                    lead = ((peer // 2 + shift) % pair_count) * 2 + peer % 2
+                    target = ((source + distance) % replicas) * tensor_count + lead
                     pairs.append((source * tensor_count + peer, target))
-            arrivals.append(lax.ppermute(payload[(distance - 1) * tensor_count + shift], ("replica", "tensor"), pairs))
-
-    quarter = page_pool.shape[2]
-    page_rows = quarter * tensor_count
+            arrivals.append(lax.ppermute(payload[(distance - 1) * pair_count + shift], ("replica", "tensor"), pairs))
+    swap = [(peer, peer ^ 1) for peer in range(tensor_count)]
+    arrivals = arrivals + [lax.ppermute(a, "tensor", swap) for a in arrivals]
+
     suffix_rows = queries.shape[1]
     result = attend(queries[0], suffix_kv[0], offsets, prefix_len, arrivals, span_count, tensor_count)
     return result.reshape(1, suffix_rows, result.shape[1])
@@ -142,15 +145,26 @@
     col_pos = lax.broadcasted_iota(jnp.int32, (group * rows, rows), 1)
     causal = col_pos <= row_pos
 
+    pair_count = tensor_count // 2
+    pair, side = me // 2, me % 2
+    piece_quarter = []
+    for shift in range(pair_count):
+        source_pair = (pair - shift + pair_count) % pair_count
+        piece_quarter += [source_pair * 2 + side, source_pair * 2 + 1 - side]
+
     def page_mask(first, count):
         col = lax.broadcasted_iota(jnp.int32, (1, count * page_rows), 1)
         page = first + col // page_rows
-        shift = (col % page_rows) // quarter
-        position = page * page_rows + ((me - shift + tensor_count) % tensor_count) * quarter + col % quarter
+        piece = (col % page_rows) // quarter
+        own_quarter = jnp.zeros_like(col)
+        for number, value in enumerate(piece_quarter):
+            own_quarter = jnp.where(piece == number, value, own_quarter)
+        position = page * page_rows + own_quarter * quarter + col % quarter
         return position < length
 
+    half = span_count * pair_count
     for head in range(kv_local):
-        lanes = pl.ds(head * HEAD_DIM, HEAD_DIM)
+        lanes = pl.ds(pl.multiple_of(side * kv_local * HEAD_DIM + head * HEAD_DIM, HEAD_DIM), HEAD_DIM)
         q_all = jnp.concatenate(
             [q_ref[:, pl.ds((head * group + g) * HEAD_DIM, HEAD_DIM)] for g in range(group)], axis=0
         )
@@ -158,16 +172,18 @@
         def page_part(page, part):
             distance, slot = page_distance[page], page_slot[page]
             pieces = []
-            for shift in range(tensor_count):
-                piece = chunk_refs[shift][slot, part, :, lanes]
-                for d in range(2, span_count + 1):
-                    other = chunk_refs[(d - 1) * tensor_count + shift][slot, part, :, lanes]
-                    piece = jnp.where(distance == d, other, piece)
-                pieces.append(piece)
+            for shift in range(pair_count):
+                for origin in (0, half):
+                    piece = chunk_refs[origin + shift][slot, part, :, lanes]
+                    for d in range(2, span_count + 1):
+                        other = chunk_refs[origin + (d - 1) * pair_count + shift][slot, part, :, lanes]
+                        piece = jnp.where(distance == d, other, piece)
+                    pieces.append(piece)
             return jnp.concatenate(pieces, axis=0)
 
-        keys = [suf_ref[0, :, lanes]]
-        vals = [suf_ref[1, :, lanes]]
+        suffix_lanes = pl.ds(head * HEAD_DIM, HEAD_DIM)
+        keys = [suf_ref[0, :, suffix_lanes]]
+        vals = [suf_ref[1, :, suffix_lanes]]
         masks = [causal]
         join = 2 if page_count % 2 == 0 else 1
         for page in range(0, page_count, join):
@@ -206,7 +222,7 @@
 def attend(q, suf, offsets, prefix_len, chunks, span_count, tensor_count):
     rows, width = q.shape
     page_count = offsets.shape[1]
-    chunk_keys = chunks[0].shape[0] * chunks[0].shape[2] * tensor_count // chunks[0].shape[0]
+    chunk_keys = chunks[0].shape[2] * tensor_count
     keys_total = suf.shape[1] + page_count * chunk_keys
     flops = 4 * rows * width * keys_total
     nbytes = 2 * (q.size * 2 + suf.size + sum(c.size for c in chunks))

time: 61.9 us -> 63.7 us (1.029)
  the two profiles are of different devices: /device:TPU:1 before, /device:TPU:13 now
where the time goes in v19:
time: 63.7 us; the launch traced here: 63.4 us
  starting transfers between devices  37.3 us (59%)
  Pallas kernels  14.5 us (23%)
  waiting for transfers between devices  10.9 us (17%)
  local copies, waits for them, and re-layouts  0.66 us (1%)
    ppermute x6, starting transfers between devices, on_device(): arrivals = arrivals + [lax.ppermute(a, 'tensor', swap) for a in arrivals]  28.3 us
    ppermute x6, waiting for transfers between devices, on_device(): lax.ppermute(payload[(distance - 1) * pair_count + shift], ('replica', 't...  9.44 us
    ppermute x6, starting transfers between devices, on_device(): lax.ppermute(payload[(distance - 1) * pair_count + shift], ('replica', 't...  8.96 us
    pallas_call x1, Pallas kernels, attend(): pl.pallas_call(functools.partial(attention_kernel, span_count, tensor_cou...  8.27 us
    pallas_call x2, Pallas kernels, pack_pages(): pl.pallas_call(functools.partial(gather_kernel, first, last, slot_cap, te...  6.18 us
    ppermute x6, waiting for transfers between devices, on_device(): arrivals = arrivals + [lax.ppermute(a, 'tensor', swap) for a in arrivals]  1.42 us
  transfers between devices with their start and end apart: 12, of which 6 were waited for; matrix products, arithmetic and copies ran while one was open for 0% of the time, Pallas kernels for 5%

profile of v19, /device:TPU:13, one launch (start us, length us, event | category | flops | bytes accessed | tf_op | source)
XLA Modules:
  0.0 63.4 jit_solution(9301363804114665563)
XLA Ops:
  0.0 2.7 %shard_map.64 = (bf16[4,2,32,512]{3,2,1,0:T(8,128)(2,1)}, bf16[4,2,32,512]{3,2,1,0:T(8,128)(2,1)}) custom-call(s32[4,8]{1,0:T(4,128)} %off_ref.5, s32[4,8]{1,0:T(4,128)} %slot_ref.3, bf16[12,2,32,1024]{3,2,1,0:T(8,128)(2,1)} %pool_hbm.3), custom_call_target="tpu_custom_call" | custom-call | bytes 1048576 | tf_op jit(solution)/shard_map/pallas_call | solution.py:83
  2.7 1.3 %collective-permute-start = (bf16[4,2,32,512]{3,2,1,0:T(8,128)(2,1)}, bf16[4,2,32,512]{3,2,1,0:T(8,128)(2,1)S(1)}, u32[]{:S(2)}, u32[]{:S(2)}) collective-permute-start(bf16[4,2,32,512]{3,2,1,0:T(8,128)(2,1)} %get-tuple-element.11), channel_id=1, source_target_pairs={{0,4},{1,5},{2,6},{3,7},{4,8},{5,9},{6,10},{7,11},{8,12},{9,13},{1... | collective-permute-start | bytes 786440 | tf_op jit(solution)/shard_map/ppermute | solution.py:115
  4.1 2.2 %collective-permute-start.1 = (bf16[4,2,32,512]{3,2,1,0:T(8,128)(2,1)}, bf16[4,2,32,512]{3,2,1,0:T(8,128)(2,1)S(1)}, u32[]{:S(2)}, u32[]{:S(2)}) collective-permute-start(bf16[4,2,32,512]{3,2,1,0:T(8,128)(2,1)} %get-tuple-element.12), channel_id=1, source_target_pairs={{0,6},{1,7},{2,4},{3,5},{4,10},{5,11},{6,8},{7,9},{8,14},{9,15},{1... | collective-permute-start | bytes 786440 | tf_op jit(solution)/shard_map/ppermute | solution.py:115
  6.3 3.5 %shard_map.65 = (bf16[4,2,32,512]{3,2,1,0:T(8,128)(2,1)}, bf16[4,2,32,512]{3,2,1,0:T(8,128)(2,1)}, bf16[4,2,32,512]{3,2,1,0:T(8,128)(2,1)}, bf16[4,2,32,512]{3,2,1,0:T(8,128)(2,1)}) custom-call(s32[4,8]{1,0:T(4,128)} %off_ref.5, s32[4,8]{1,0:T(4,128)} %slot_ref.3, bf16[12,2,32,1024]{3,2,1,0:T(8,128)(2,1)} %pool_hbm.3), custom_call_target="tpu_custom_call" | custom-call | bytes 2097152 | tf_op jit(solution)/shard_map/pallas_call | solution.py:83
  9.8 0.9 %collective-permute-start.2 = (bf16[4,2,32,512]{3,2,1,0:T(8,128)(2,1)}, bf16[4,2,32,512]{3,2,1,0:T(8,128)(2,1)S(1)}, u32[]{:S(2)}, u32[]{:S(2)}) collective-permute-start(bf16[4,2,32,512]{3,2,1,0:T(8,128)(2,1)} %get-tuple-element.13), channel_id=1, source_target_pairs={{0,8},{1,9},{2,10},{3,11},{4,12},{5,13},{6,14},{7,15},{8,0},{9,1},... | collective-permute-start | bytes 786440 | tf_op jit(solution)/shard_map/ppermute | solution.py:115
  10.7 1.5 %collective-permute-start.3 = (bf16[4,2,32,512]{3,2,1,0:T(8,128)(2,1)}, bf16[4,2,32,512]{3,2,1,0:T(8,128)(2,1)S(1)}, u32[]{:S(2)}, u32[]{:S(2)}) collective-permute-start(bf16[4,2,32,512]{3,2,1,0:T(8,128)(2,1)} %get-tuple-element.14), channel_id=1, source_target_pairs={{0,10},{1,11},{2,8},{3,9},{4,14},{5,15},{6,12},{7,13},{8,2},{9,3},... | collective-permute-start | bytes 786440 | tf_op jit(solution)/shard_map/ppermute | solution.py:115
  12.2 0.0 collective-permute-start.4
  12.2 0.0 collective-permute-done.rest_0_
  12.2 3.0 %collective-permute-start.5 = (bf16[4,2,32,512]{3,2,1,0:T(8,128)(2,1)}, bf16[4,2,32,512]{3,2,1,0:T(8,128)(2,1)S(1)}, u32[]{:S(2)}, u32[]{:S(2)}) collective-permute-start(bf16[4,2,32,512]{3,2,1,0:T(8,128)(2,1)} %get-tuple-element.16), channel_id=1, source_target_pairs={{0,14},{1,15},{2,12},{3,13},{4,2},{5,3},{6,0},{7,1},{8,6},{9,7},{1... | collective-permute-start | bytes 786440 | tf_op jit(solution)/shard_map/ppermute | solution.py:115
  15.2 1.5 %collective-permute-done.1.rest_1_ = bf16[4,2,32,512]{3,2,1,0:T(8,128)(2,1)S(1)} collective-permute-done((bf16[4,2,32,512]{3,2,1,0:T(8,128)(2,1)}, bf16[4,2,32,512]{3,2,1,0:T(8,128)(2,1)S(1)}, u32[]{:S(2)}, u32[]{:S(2)}) %collective-permute-start.1) | collective-permute-done | bytes 262176 | tf_op jit(solution)/shard_map/ppermute | solution.py:115
  16.7 23.4 %collective-permute-start.6 = (bf16[4,2,32,512]{3,2,1,0:T(8,128)(2,1)S(1)}, bf16[4,2,32,512]{3,2,1,0:T(8,128)(2,1)S(1)}, u32[]{:S(2)}, u32[]{:S(2)}) collective-permute-start(bf16[4,2,32,512]{3,2,1,0:T(8,128)(2,1)S(1)} %collective-permute-done.rest_0_), channel_id=1, source_target_pairs={{0,1},{1,0},{2,3},{3,2},{4,5},{5,4},{6,7},{7,6},{8,9},{9,8},{10,11... | collective-permute-start | bytes 786440 | tf_op jit(solution)/shard_map/ppermute | solution.py:117
  40.2 2.9 %collective-permute-done.2.rest_2_ = bf16[4,2,32,512]{3,2,1,0:T(8,128)(2,1)S(1)} collective-permute-done((bf16[4,2,32,512]{3,2,1,0:T(8,128)(2,1)}, bf16[4,2,32,512]{3,2,1,0:T(8,128)(2,1)S(1)}, u32[]{:S(2)}, u32[]{:S(2)}) %collective-permute-start.2) | collective-permute-done | bytes 262176 | tf_op jit(solution)/shard_map/ppermute | solution.py:115
  43.1 2.7 %collective-permute-start.7 = (bf16[4,2,32,512]{3,2,1,0:T(8,128)(2,1)S(1)}, bf16[4,2,32,512]{3,2,1,0:T(8,128)(2,1)S(1)}, u32[]{:S(2)}, u32[]{:S(2)}) collective-permute-start(bf16[4,2,32,512]{3,2,1,0:T(8,128)(2,1)S(1)} %collective-permute-done.1.rest_1_), channel_id=1, source_target_pairs={{0,1},{1,0},{2,3},{3,2},{4,5},{5,4},{6,7},{7,6},{8,9},{9,8},{10,11... | collective-permute-start | bytes 786440 | tf_op jit(solution)/shard_map/ppermute | solution.py:117
  45.8 2.9 %collective-permute-done.3.rest_3_ = bf16[4,2,32,512]{3,2,1,0:T(8,128)(2,1)S(1)} collective-permute-done((bf16[4,2,32,512]{3,2,1,0:T(8,128)(2,1)}, bf16[4,2,32,512]{3,2,1,0:T(8,128)(2,1)S(1)}, u32[]{:S(2)}, u32[]{:S(2)}) %collective-permute-start.3) | collective-permute-done | bytes 262176 | tf_op jit(solution)/shard_map/ppermute | solution.py:115
  48.7 1.5 %collective-permute-start.8 = (bf16[4,2,32,512]{3,2,1,0:T(8,128)(2,1)S(1)}, bf16[4,2,32,512]{3,2,1,0:T(8,128)(2,1)S(1)}, u32[]{:S(2)}, u32[]{:S(2)}) collective-permute-start(bf16[4,2,32,512]{3,2,1,0:T(8,128)(2,1)S(1)} %collective-permute-done.2.rest_2_), channel_id=1, source_target_pairs={{0,1},{1,0},{2,3},{3,2},{4,5},{5,4},{6,7},{7,6},{8,9},{9,8},{10,11... | collective-permute-start | bytes 786440 | tf_op jit(solution)/shard_map/ppermute | solution.py:117
  50.2 0.0 collective-permute-done.4.rest_4_
  50.2 0.1 collective-permute-start.9
  50.3 2.0 %collective-permute-done.5.rest_5_ = bf16[4,2,32,512]{3,2,1,0:T(8,128)(2,1)S(1)} collective-permute-done((bf16[4,2,32,512]{3,2,1,0:T(8,128)(2,1)}, bf16[4,2,32,512]{3,2,1,0:T(8,128)(2,1)S(1)}, u32[]{:S(2)}, u32[]{:S(2)}) %collective-permute-start.5) | collective-permute-done | bytes 262176 | tf_op jit(solution)/shard_map/ppermute | solution.py:115
  52.4 0.5 collective-permute-start.10
  52.9 0.0 collective-permute-done.6.rest_6_
  52.9 0.1 collective-permute-start.11
  52.9 0.0 collective-permute-done.7.rest_7_
  53.0 0.0 collective-permute-done.8.rest_8_
  53.0 0.0 collective-permute-done.9.rest_9_
  53.0 0.0 copy-start.9
  53.0 1.0 %collective-permute-done.10.rest_10_ = bf16[4,2,32,512]{3,2,1,0:T(8,128)(2,1)S(1)} collective-permute-done((bf16[4,2,32,512]{3,2,1,0:T(8,128)(2,1)S(1)}, bf16[4,2,32,512]{3,2,1,0:T(8,128)(2,1)S(1)}, u32[]{:S(2)}, u32[]{:S(2)}) %collective-permute-start.10) | collective-permute-done | bytes 262176 | tf_op jit(solution)/shard_map/ppermute | solution.py:117
  54.0 0.4 collective-permute-done.11.rest_11_
  54.4 0.0 copy-done
  54.4 0.0 copy-done.2
  54.5 0.3 copy-done.10
  54.7 0.4 copy-done.11
  55.1 8.3 %shard_map.66 = bf16[128,2048]{1,0:T(8,128)(2,1)} custom-call(s32[4,8]{1,0:T(4,128)} %off_ref.5, s32[4]{0:T(128)} %len_ref.1, bf16[128,2048]{1,0:T(8,128)(2,1)} %bitcast.3, bf16[2,128,256]{2,1,0:T(8,128)(2,1)} %bitcast.4, bf16[4,2,32,512]{3,2,1,0:T(8,128)(2,1)} %copy-done, bf16[4,2,32,512]{3,2,1,0:T(8,128)(2,1)} %copy-done.1, ...), custom_call_target="tpu_custom_call" | custom-call | flops 1207959552 | bytes 4325376 | tf_op jit(solution)/shard_map/pallas_call | solution.py:239
  (19 shorter events, 0.0 us)
Async XLA Ops:
  2.7 9.4 %collective-permute-start = (bf16[4,2,32,512]{3,2,1,0:T(8,128)(2,1)}, bf16[4,2,32,512]{3,2,1,0:T(8,128)(2,1)S(1)}, u32[]{:S(2)}, u32[]{:S(2)}) collective-permute-start(bf16[4,2,32,512]{3,2,1,0:T(8,128)(2,1)} %get-tuple-element.11), channel_id=1, source_target_pairs={{0,4},{1,5},{2,6},{3,7},{4,8},{5,9},{6,10},{7,11},{8,12},{9,13},{1... | collective-permute-start | bytes 786440 | tf_op jit(solution)/shard_map/ppermute | solution.py:115
  4.1 12.6 %collective-permute-start.1 = (bf16[4,2,32,512]{3,2,1,0:T(8,128)(2,1)}, bf16[4,2,32,512]{3,2,1,0:T(8,128)(2,1)S(1)}, u32[]{:S(2)}, u32[]{:S(2)}) collective-permute-start(bf16[4,2,32,512]{3,2,1,0:T(8,128)(2,1)} %get-tuple-element.12), channel_id=1, source_target_pairs={{0,6},{1,7},{2,4},{3,5},{4,10},{5,11},{6,8},{7,9},{8,14},{9,15},{1... | collective-permute-start | bytes 786440 | tf_op jit(solution)/shard_map/ppermute | solution.py:115
  9.8 33.3 %collective-permute-start.2 = (bf16[4,2,32,512]{3,2,1,0:T(8,128)(2,1)}, bf16[4,2,32,512]{3,2,1,0:T(8,128)(2,1)S(1)}, u32[]{:S(2)}, u32[]{:S(2)}) collective-permute-start(bf16[4,2,32,512]{3,2,1,0:T(8,128)(2,1)} %get-tuple-element.13), channel_id=1, source_target_pairs={{0,8},{1,9},{2,10},{3,11},{4,12},{5,13},{6,14},{7,15},{8,0},{9,1},... | collective-permute-start | bytes 786440 | tf_op jit(solution)/shard_map/ppermute | solution.py:115
  10.7 38.0 %collective-permute-start.3 = (bf16[4,2,32,512]{3,2,1,0:T(8,128)(2,1)}, bf16[4,2,32,512]{3,2,1,0:T(8,128)(2,1)S(1)}, u32[]{:S(2)}, u32[]{:S(2)}) collective-permute-start(bf16[4,2,32,512]{3,2,1,0:T(8,128)(2,1)} %get-tuple-element.14), channel_id=1, source_target_pairs={{0,10},{1,11},{2,8},{3,9},{4,14},{5,15},{6,12},{7,13},{8,2},{9,3},... | collective-permute-start | bytes 786440 | tf_op jit(solution)/shard_map/ppermute | solution.py:115
  12.2 38.1 %collective-permute-start.4 = (bf16[4,2,32,512]{3,2,1,0:T(8,128)(2,1)}, bf16[4,2,32,512]{3,2,1,0:T(8,128)(2,1)S(1)}, u32[]{:S(2)}, u32[]{:S(2)}) collective-permute-start(bf16[4,2,32,512]{3,2,1,0:T(8,128)(2,1)} %get-tuple-element.15), channel_id=1, source_target_pairs={{0,12},{1,13},{2,14},{3,15},{4,0},{5,1},{6,2},{7,3},{8,4},{9,5},{1... | collective-permute-start | bytes 786440 | tf_op jit(solution)/shard_map/ppermute | solution.py:115
  12.2 42.2 %copy-start = (bf16[4,2,32,512]{3,2,1,0:T(8,128)(2,1)}, bf16[4,2,32,512]{3,2,1,0:T(8,128)(2,1)S(1)}, u32[]{:S(2)}) copy-start(bf16[4,2,32,512]{3,2,1,0:T(8,128)(2,1)S(1)} %collective-permute-done.rest_0_) | copy-start | bytes 786436
  12.2 40.2 %collective-permute-start.5 = (bf16[4,2,32,512]{3,2,1,0:T(8,128)(2,1)}, bf16[4,2,32,512]{3,2,1,0:T(8,128)(2,1)S(1)}, u32[]{:S(2)}, u32[]{:S(2)}) collective-permute-start(bf16[4,2,32,512]{3,2,1,0:T(8,128)(2,1)} %get-tuple-element.16), channel_id=1, source_target_pairs={{0,14},{1,15},{2,12},{3,13},{4,2},{5,3},{6,0},{7,1},{8,6},{9,7},{1... | collective-permute-start | bytes 786440 | tf_op jit(solution)/shard_map/ppermute | solution.py:115
  16.7 37.7 %copy-start.1 = (bf16[4,2,32,512]{3,2,1,0:T(8,128)(2,1)}, bf16[4,2,32,512]{3,2,1,0:T(8,128)(2,1)S(1)}, u32[]{:S(2)}) copy-start(bf16[4,2,32,512]{3,2,1,0:T(8,128)(2,1)S(1)} %collective-permute-done.1.rest_1_) | copy-start | bytes 786436
  16.7 36.1 %collective-permute-start.6 = (bf16[4,2,32,512]{3,2,1,0:T(8,128)(2,1)S(1)}, bf16[4,2,32,512]{3,2,1,0:T(8,128)(2,1)S(1)}, u32[]{:S(2)}, u32[]{:S(2)}) collective-permute-start(bf16[4,2,32,512]{3,2,1,0:T(8,128)(2,1)S(1)} %collective-permute-done.rest_0_), channel_id=1, source_target_pairs={{0,1},{1,0},{2,3},{3,2},{4,5},{5,4},{6,7},{7,6},{8,9},{9,8},{10,11... | collective-permute-start | bytes 786440 | tf_op jit(solution)/shard_map/ppermute | solution.py:117
  43.1 11.3 %copy-start.2 = (bf16[4,2,32,512]{3,2,1,0:T(8,128)(2,1)}, bf16[4,2,32,512]{3,2,1,0:T(8,128)(2,1)S(1)}, u32[]{:S(2)}) copy-start(bf16[4,2,32,512]{3,2,1,0:T(8,128)(2,1)S(1)} %collective-permute-done.2.rest_2_) | copy-start | bytes 786436
  43.1 9.9 %collective-permute-start.7 = (bf16[4,2,32,512]{3,2,1,0:T(8,128)(2,1)S(1)}, bf16[4,2,32,512]{3,2,1,0:T(8,128)(2,1)S(1)}, u32[]{:S(2)}, u32[]{:S(2)}) collective-permute-start(bf16[4,2,32,512]{3,2,1,0:T(8,128)(2,1)S(1)} %collective-permute-done.1.rest_1_), channel_id=1, source_target_pairs={{0,1},{1,0},{2,3},{3,2},{4,5},{5,4},{6,7},{7,6},{8,9},{9,8},{10,11... | collective-permute-start | bytes 786440 | tf_op jit(solution)/shard_map/ppermute | solution.py:117
  48.7 5.7 %copy-start.3 = (bf16[4,2,32,512]{3,2,1,0:T(8,128)(2,1)}, bf16[4,2,32,512]{3,2,1,0:T(8,128)(2,1)S(1)}, u32[]{:S(2)}) copy-start(bf16[4,2,32,512]{3,2,1,0:T(8,128)(2,1)S(1)} %collective-permute-done.3.rest_3_) | copy-start | bytes 786436
  48.7 4.3 %collective-permute-start.8 = (bf16[4,2,32,512]{3,2,1,0:T(8,128)(2,1)S(1)}, bf16[4,2,32,512]{3,2,1,0:T(8,128)(2,1)S(1)}, u32[]{:S(2)}, u32[]{:S(2)}) collective-permute-start(bf16[4,2,32,512]{3,2,1,0:T(8,128)(2,1)S(1)} %collective-permute-done.2.rest_2_), channel_id=1, source_target_pairs={{0,1},{1,0},{2,3},{3,2},{4,5},{5,4},{6,7},{7,6},{8,9},{9,8},{10,11... | collective-permute-start | bytes 786440 | tf_op jit(solution)/shard_map/ppermute | solution.py:117
  50.2 4.2 %copy-start.4 = (bf16[4,2,32,512]{3,2,1,0:T(8,128)(2,1)}, bf16[4,2,32,512]{3,2,1,0:T(8,128)(2,1)S(1)}, u32[]{:S(2)}) copy-start(bf16[4,2,32,512]{3,2,1,0:T(8,128)(2,1)S(1)} %collective-permute-done.4.rest_4_) | copy-start | bytes 786436
  50.2 2.7 %collective-permute-start.9 = (bf16[4,2,32,512]{3,2,1,0:T(8,128)(2,1)S(1)}, bf16[4,2,32,512]{3,2,1,0:T(8,128)(2,1)S(1)}, u32[]{:S(2)}, u32[]{:S(2)}) collective-permute-start(bf16[4,2,32,512]{3,2,1,0:T(8,128)(2,1)S(1)} %collective-permute-done.3.rest_3_), channel_id=1, source_target_pairs={{0,1},{1,0},{2,3},{3,2},{4,5},{5,4},{6,7},{7,6},{8,9},{9,8},{10,11... | collective-permute-start | bytes 786440 | tf_op jit(solution)/shard_map/ppermute | solution.py:117
  52.4 2.1 %copy-start.5 = (bf16[4,2,32,512]{3,2,1,0:T(8,128)(2,1)}, bf16[4,2,32,512]{3,2,1,0:T(8,128)(2,1)S(1)}, u32[]{:S(2)}) copy-start(bf16[4,2,32,512]{3,2,1,0:T(8,128)(2,1)S(1)} %collective-permute-done.5.rest_5_) | copy-start | bytes 786436
  52.4 1.7 %collective-permute-start.10 = (bf16[4,2,32,512]{3,2,1,0:T(8,128)(2,1)S(1)}, bf16[4,2,32,512]{3,2,1,0:T(8,128)(2,1)S(1)}, u32[]{:S(2)}, u32[]{:S(2)}) collective-permute-start(bf16[4,2,32,512]{3,2,1,0:T(8,128)(2,1)S(1)} %collective-permute-done.4.rest_4_), channel_id=1, source_target_pairs={{0,1},{1,0},{2,3},{3,2},{4,5},{5,4},{6,7},{7,6},{8,9},{9,8},{10,11... | collective-permute-start | bytes 786440 | tf_op jit(solution)/shard_map/ppermute | solution.py:117
  52.9 1.6 %copy-start.6 = (bf16[4,2,32,512]{3,2,1,0:T(8,128)(2,1)}, bf16[4,2,32,512]{3,2,1,0:T(8,128)(2,1)S(1)}, u32[]{:S(2)}) copy-start(bf16[4,2,32,512]{3,2,1,0:T(8,128)(2,1)S(1)} %collective-permute-done.6.rest_6_) | copy-start | bytes 786436
  52.9 1.5 %collective-permute-start.11 = (bf16[4,2,32,512]{3,2,1,0:T(8,128)(2,1)S(1)}, bf16[4,2,32,512]{3,2,1,0:T(8,128)(2,1)S(1)}, u32[]{:S(2)}, u32[]{:S(2)}) collective-permute-start(bf16[4,2,32,512]{3,2,1,0:T(8,128)(2,1)S(1)} %collective-permute-done.5.rest_5_), channel_id=1, source_target_pairs={{0,1},{1,0},{2,3},{3,2},{4,5},{5,4},{6,7},{7,6},{8,9},{9,8},{10,11... | collective-permute-start | bytes 786440 | tf_op jit(solution)/shard_map/ppermute | solution.py:117
  52.9 1.5 %copy-start.7 = (bf16[4,2,32,512]{3,2,1,0:T(8,128)(2,1)}, bf16[4,2,32,512]{3,2,1,0:T(8,128)(2,1)S(1)}, u32[]{:S(2)}) copy-start(bf16[4,2,32,512]{3,2,1,0:T(8,128)(2,1)S(1)} %collective-permute-done.7.rest_7_) | copy-start | bytes 786436
  53.0 1.5 %copy-start.8 = (bf16[4,2,32,512]{3,2,1,0:T(8,128)(2,1)}, bf16[4,2,32,512]{3,2,1,0:T(8,128)(2,1)S(1)}, u32[]{:S(2)}) copy-start(bf16[4,2,32,512]{3,2,1,0:T(8,128)(2,1)S(1)} %collective-permute-done.8.rest_8_) | copy-start | bytes 786436
  53.0 1.5 %copy-start.9 = (bf16[4,2,32,512]{3,2,1,0:T(8,128)(2,1)}, bf16[4,2,32,512]{3,2,1,0:T(8,128)(2,1)S(1)}, u32[]{:S(2)}) copy-start(bf16[4,2,32,512]{3,2,1,0:T(8,128)(2,1)S(1)} %collective-permute-done.9.rest_9_) | copy-start | bytes 786436
  54.0 0.7 %copy-start.10 = (bf16[4,2,32,512]{3,2,1,0:T(8,128)(2,1)}, bf16[4,2,32,512]{3,2,1,0:T(8,128)(2,1)S(1)}, u32[]{:S(2)}) copy-start(bf16[4,2,32,512]{3,2,1,0:T(8,128)(2,1)S(1)} %collective-permute-done.10.rest_10_) | copy-start | bytes 786436
  54.4 0.7 %copy-start.11 = (bf16[4,2,32,512]{3,2,1,0:T(8,128)(2,1)}, bf16[4,2,32,512]{3,2,1,0:T(8,128)(2,1)S(1)}, u32[]{:S(2)}) copy-start(bf16[4,2,32,512]{3,2,1,0:T(8,128)(2,1)S(1)} %collective-permute-done.11.rest_11_) | copy-start | bytes 786436

commit v20 on v18

--- a/solution.py
+++ b/solution.py
@@ -169,7 +169,7 @@
         keys = [suf_ref[0, :, lanes]]
         vals = [suf_ref[1, :, lanes]]
         masks = [causal]
-        join = 2 if page_count % 2 == 0 else 1
+        join = 4 if page_count % 4 == 0 else (2 if page_count % 2 == 0 else 1)
         for page in range(0, page_count, join):
             keys.append(jnp.concatenate([page_part(p, 0) for p in range(page, page + join)], axis=0))
             vals.append(jnp.concatenate([page_part(p, 1) for p in range(page, page + join)], axis=0))

time: 61.9 us -> 61.3 us (level)
  Pallas kernels: 13.9 us -> 13.1 us
  transfers between devices with their start and end apart: 12 -> 12, of which waited for: 3 -> 3; matrix products, arithmetic and copies ran while one was open for 0% -> 0% of each run, Pallas kernels for 6% -> 5%
where the time goes in v20:
time: 61.3 us; the launch traced here: 61 us
  starting transfers between devices  32.1 us (52%)
  waiting for transfers between devices  15.1 us (25%)
  Pallas kernels  13.1 us (21%)
    ppermute x12, starting transfers between devices, on_device(): lax.ppermute(payload[(distance - 1) * tensor_count + shift], ('replica',...  32.1 us
    ppermute x12, waiting for transfers between devices, on_device(): lax.ppermute(payload[(distance - 1) * tensor_count + shift], ('replica',...  15.1 us
    pallas_call x1, Pallas kernels, attend(): pl.pallas_call(functools.partial(attention_kernel, span_count, tensor_cou...  7.12 us
    pallas_call x2, Pallas kernels, pack_pages(): pl.pallas_call(functools.partial(gather_kernel, first, last, slot_cap, te...  6.01 us
  transfers between devices with their start and end apart: 12, of which 3 were waited for; matrix products, arithmetic and copies ran while one was open for 0% of the time, Pallas kernels for 5%

profile of v20, /device:TPU:1, one launch (start us, length us, event | category | flops | bytes accessed | tf_op | source)
XLA Modules:
  0.0 61.0 jit_solution(6072184832658486288)
XLA Ops:
  0.0 2.7 %shard_map.64 = (bf16[4,2,32,256]{3,2,1,0:T(8,128)(2,1)}, bf16[4,2,32,256]{3,2,1,0:T(8,128)(2,1)}, bf16[4,2,32,256]{3,2,1,0:T(8,128)(2,1)}, bf16[4,2,32,256]{3,2,1,0:T(8,128)(2,1)}) custom-call(s32[4,8]{1,0:T(4,128)} %off_ref.5, s32[4,8]{1,0:T(4,128)} %slot_ref.3, bf16[12,2,32,1024]{3,2,1,0:T(8,128)(2,1)} %pool_hbm.3), custom_call_target="tpu_custom_call" | custom-call | bytes 1048576 | tf_op jit(solution)/shard_map/pallas_call | solution.py:82
  2.8 2.2 %collective-permute-start = (bf16[4,2,32,256]{3,2,1,0:T(8,128)(2,1)}, bf16[4,2,32,256]{3,2,1,0:T(8,128)(2,1)S(1)}, u32[]{:S(2)}, u32[]{:S(2)}) collective-permute-start(bf16[4,2,32,256]{3,2,1,0:T(8,128)(2,1)} %get-tuple-element.17), channel_id=1, source_target_pairs={{0,4},{1,5},{2,6},{3,7},{4,8},{5,9},{6,10},{7,11},{8,12},{9,13},{1... | collective-permute-start | bytes 393224 | tf_op jit(solution)/shard_map/ppermute | solution.py:112
  4.9 3.1 %collective-permute-start.1 = (bf16[4,2,32,256]{3,2,1,0:T(8,128)(2,1)}, bf16[4,2,32,256]{3,2,1,0:T(8,128)(2,1)S(1)}, u32[]{:S(2)}, u32[]{:S(2)}) collective-permute-start(bf16[4,2,32,256]{3,2,1,0:T(8,128)(2,1)} %get-tuple-element.18), channel_id=1, source_target_pairs={{0,5},{1,6},{2,7},{3,4},{4,9},{5,10},{6,11},{7,8},{8,13},{9,14},{1... | collective-permute-start | bytes 393224 | tf_op jit(solution)/shard_map/ppermute | solution.py:112
  8.0 1.3 %collective-permute-start.2 = (bf16[4,2,32,256]{3,2,1,0:T(8,128)(2,1)}, bf16[4,2,32,256]{3,2,1,0:T(8,128)(2,1)S(1)}, u32[]{:S(2)}, u32[]{:S(2)}) collective-permute-start(bf16[4,2,32,256]{3,2,1,0:T(8,128)(2,1)} %get-tuple-element.19), channel_id=1, source_target_pairs={{0,6},{1,7},{2,4},{3,5},{4,10},{5,11},{6,8},{7,9},{8,14},{9,15},{1... | collective-permute-start | bytes 393224 | tf_op jit(solution)/shard_map/ppermute | solution.py:112
  9.3 0.3 collective-permute-start.3
  9.6 3.3 %shard_map.65 = (bf16[4,2,32,256]{3,2,1,0:T(8,128)(2,1)}, bf16[4,2,32,256]{3,2,1,0:T(8,128)(2,1)}, bf16[4,2,32,256]{3,2,1,0:T(8,128)(2,1)}, bf16[4,2,32,256]{3,2...) custom-call(s32[4,8]{1,0:T(4,128)} %off_ref.5, ...), custom_call_target="tpu_custom_call" | custom-call | bytes 2097152 | tf_op jit(solution)/shard_map/pallas_call | solution.py:82
  12.9 2.0 %collective-permute-start.4 = (bf16[4,2,32,256]{3,2,1,0:T(8,128)(2,1)}, bf16[4,2,32,256]{3,2,1,0:T(8,128)(2,1)S(1)}, u32[]{:S(2)}, u32[]{:S(2)}) collective-permute-start(bf16[4,2,32,256]{3,2,1,0:T(8,128)(2,1)} %get-tuple-element.21), channel_id=1, source_target_pairs={{0,8},{1,9},{2,10},{3,11},{4,12},{5,13},{6,14},{7,15},{8,0},{9,1},... | collective-permute-start | bytes 393224 | tf_op jit(solution)/shard_map/ppermute | solution.py:112
  14.9 0.0 collective-permute-done.rest_0_
  14.9 1.6 %collective-permute-start.5 = (bf16[4,2,32,256]{3,2,1,0:T(8,128)(2,1)}, bf16[4,2,32,256]{3,2,1,0:T(8,128)(2,1)S(1)}, u32[]{:S(2)}, u32[]{:S(2)}) collective-permute-start(bf16[4,2,32,256]{3,2,1,0:T(8,128)(2,1)} %get-tuple-element.22), channel_id=1, source_target_pairs={{0,9},{1,10},{2,11},{3,8},{4,13},{5,14},{6,15},{7,12},{8,1},{9,2},... | collective-permute-start | bytes 393224 | tf_op jit(solution)/shard_map/ppermute | solution.py:112
  16.5 0.0 collective-permute-done.1.rest_1_
  16.5 3.4 %collective-permute-start.6 = (bf16[4,2,32,256]{3,2,1,0:T(8,128)(2,1)}, bf16[4,2,32,256]{3,2,1,0:T(8,128)(2,1)S(1)}, u32[]{:S(2)}, u32[]{:S(2)}) collective-permute-start(bf16[4,2,32,256]{3,2,1,0:T(8,128)(2,1)} %get-tuple-element.23), channel_id=1, source_target_pairs={{0,10},{1,11},{2,8},{3,9},{4,14},{5,15},{6,12},{7,13},{8,2},{9,3},... | collective-permute-start | bytes 393224 | tf_op jit(solution)/shard_map/ppermute | solution.py:112
  19.9 0.0 collective-permute-done.2.rest_2_
  19.9 0.0 collective-permute-start.7
  19.9 1.2 %collective-permute-done.3.rest_3_ = bf16[4,2,32,256]{3,2,1,0:T(8,128)(2,1)S(1)} collective-permute-done((bf16[4,2,32,256]{3,2,1,0:T(8,128)(2,1)}, bf16[4,2,32,256]{3,2,1,0:T(8,128)(2,1)S(1)}, u32[]{:S(2)}, u32[]{:S(2)}) %collective-permute-start.3) | collective-permute-done | bytes 131104 | tf_op jit(solution)/shard_map/ppermute | solution.py:112
  21.2 0.8 %collective-permute-start.8 = (bf16[4,2,32,256]{3,2,1,0:T(8,128)(2,1)}, bf16[4,2,32,256]{3,2,1,0:T(8,128)(2,1)S(1)}, u32[]{:S(2)}, u32[]{:S(2)}) collective-permute-start(bf16[4,2,32,256]{3,2,1,0:T(8,128)(2,1)} %get-tuple-element.25), channel_id=1, source_target_pairs={{0,12},{1,13},{2,14},{3,15},{4,0},{5,1},{6,2},{7,3},{8,4},{9,5},{1... | collective-permute-start | bytes 393224 | tf_op jit(solution)/shard_map/ppermute | solution.py:112
  22.0 11.6 %collective-permute-done.4.rest_4_ = bf16[4,2,32,256]{3,2,1,0:T(8,128)(2,1)S(1)} collective-permute-done((bf16[4,2,32,256]{3,2,1,0:T(8,128)(2,1)}, bf16[4,2,32,256]{3,2,1,0:T(8,128)(2,1)S(1)}, u32[]{:S(2)}, u32[]{:S(2)}) %collective-permute-start.4) | collective-permute-done | bytes 131104 | tf_op jit(solution)/shard_map/ppermute | solution.py:112
  33.6 6.2 %collective-permute-start.9 = (bf16[4,2,32,256]{3,2,1,0:T(8,128)(2,1)}, bf16[4,2,32,256]{3,2,1,0:T(8,128)(2,1)S(1)}, u32[]{:S(2)}, u32[]{:S(2)}) collective-permute-start(bf16[4,2,32,256]{3,2,1,0:T(8,128)(2,1)} %get-tuple-element.26), channel_id=1, source_target_pairs={{0,13},{1,14},{2,15},{3,12},{4,1},{5,2},{6,3},{7,0},{8,5},{9,6},{1... | collective-permute-start | bytes 393224 | tf_op jit(solution)/shard_map/ppermute | solution.py:112
  39.8 0.0 collective-permute-done.5.rest_5_
  39.8 2.5 %collective-permute-start.10 = (bf16[4,2,32,256]{3,2,1,0:T(8,128)(2,1)}, bf16[4,2,32,256]{3,2,1,0:T(8,128)(2,1)S(1)}, u32[]{:S(2)}, u32[]{:S(2)}) collective-permute-start(bf16[4,2,32,256]{3,2,1,0:T(8,128)(2,1)} %get-tuple-element.27), channel_id=1, source_target_pairs={{0,14},{1,15},{2,12},{3,13},{4,2},{5,3},{6,0},{7,1},{8,6},{9,7},{1... | collective-permute-start | bytes 393224 | tf_op jit(solution)/shard_map/ppermute | solution.py:112
  42.3 0.0 collective-permute-done.6.rest_6_
  42.3 8.7 %collective-permute-start.11 = (bf16[4,2,32,256]{3,2,1,0:T(8,128)(2,1)}, bf16[4,2,32,256]{3,2,1,0:T(8,128)(2,1)S(1)}, u32[]{:S(2)}, u32[]{:S(2)}) collective-permute-start(bf16[4,2,32,256]{3,2,1,0:T(8,128)(2,1)} %get-tuple-element.28), channel_id=1, source_target_pairs={{0,15},{1,12},{2,13},{3,14},{4,3},{5,0},{6,1},{7,2},{8,7},{9,4},{1... | collective-permute-start | bytes 393224 | tf_op jit(solution)/shard_map/ppermute | solution.py:112
  51.0 0.0 collective-permute-done.7.rest_7_
  51.0 0.0 collective-permute-done.8.rest_8_
  51.0 0.0 collective-permute-done.9.rest_9_
  51.0 0.0 collective-permute-done.10.rest_10_
  51.0 0.0 copy-start.10
  51.1 2.2 %collective-permute-done.11.rest_11_ = bf16[4,2,32,256]{3,2,1,0:T(8,128)(2,1)S(1)} collective-permute-done((bf16[4,2,32,256]{3,2,1,0:T(8,128)(2,1)}, bf16[4,2,32,256]{3,2,1,0:T(8,128)(2,1)S(1)}, u32[]{:S(2)}, u32[]{:S(2)}) %collective-permute-start.11) | collective-permute-done | bytes 131104 | tf_op jit(solution)/shard_map/ppermute | solution.py:112
  53.3 0.0 copy-done.3
  53.3 0.0 copy-done.4
  53.3 0.0 copy-done.5
  53.4 0.6 copy-done.11
  53.9 7.1 %shard_map.66 = bf16[128,2048]{1,0:T(8,128)(2,1)} custom-call(s32[4,8]{1,0:T(4,128)} %off_ref.5, s32[4]{0:T(128)} %len_ref.1, bf16[128,2048]{1,0:T(8,128)(2,1)} %bitcast.3, bf16[2,128,256]{2,1,0:T(8,128)(2,1)} %bitcast.4, bf16[4,2,32,256]{3,2,1,0:T(8,128)(2,1)} %copy-done, bf16[4,2,32,256]{3,2,1,0:T(8,128)(2,1)} %copy-done.1, ...), custom_call_target="tpu_custom_call" | custom-call | flops 1207959552 | bytes 2752512 | tf_op jit(solution)/shard_map/pallas_call | solution.py:223
  (19 shorter events, 0.0 us)
Async XLA Ops:
  2.8 12.1 %collective-permute-start = (bf16[4,2,32,256]{3,2,1,0:T(8,128)(2,1)}, bf16[4,2,32,256]{3,2,1,0:T(8,128)(2,1)S(1)}, u32[]{:S(2)}, u32[]{:S(2)}) collective-permute-start(bf16[4,2,32,256]{3,2,1,0:T(8,128)(2,1)} %get-tuple-element.17), channel_id=1, source_target_pairs={{0,4},{1,5},{2,6},{3,7},{4,8},{5,9},{6,10},{7,11},{8,12},{9,13},{1... | collective-permute-start | bytes 393224 | tf_op jit(solution)/shard_map/ppermute | solution.py:112
  4.9 11.6 %collective-permute-start.1 = (bf16[4,2,32,256]{3,2,1,0:T(8,128)(2,1)}, bf16[4,2,32,256]{3,2,1,0:T(8,128)(2,1)S(1)}, u32[]{:S(2)}, u32[]{:S(2)}) collective-permute-start(bf16[4,2,32,256]{3,2,1,0:T(8,128)(2,1)} %get-tuple-element.18), channel_id=1, source_target_pairs={{0,5},{1,6},{2,7},{3,4},{4,9},{5,10},{6,11},{7,8},{8,13},{9,14},{1... | collective-permute-start | bytes 393224 | tf_op jit(solution)/shard_map/ppermute | solution.py:112
  8.0 11.9 %collective-permute-start.2 = (bf16[4,2,32,256]{3,2,1,0:T(8,128)(2,1)}, bf16[4,2,32,256]{3,2,1,0:T(8,128)(2,1)S(1)}, u32[]{:S(2)}, u32[]{:S(2)}) collective-permute-start(bf16[4,2,32,256]{3,2,1,0:T(8,128)(2,1)} %get-tuple-element.19), channel_id=1, source_target_pairs={{0,6},{1,7},{2,4},{3,5},{4,10},{5,11},{6,8},{7,9},{8,14},{9,15},{1... | collective-permute-start | bytes 393224 | tf_op jit(solution)/shard_map/ppermute | solution.py:112
  9.3 11.9 %collective-permute-start.3 = (bf16[4,2,32,256]{3,2,1,0:T(8,128)(2,1)}, bf16[4,2,32,256]{3,2,1,0:T(8,128)(2,1)S(1)}, u32[]{:S(2)}, u32[]{:S(2)}) collective-permute-start(bf16[4,2,32,256]{3,2,1,0:T(8,128)(2,1)} %get-tuple-element.20), channel_id=1, source_target_pairs={{0,7},{1,4},{2,5},{3,6},{4,11},{5,8},{6,9},{7,10},{8,15},{9,12},{1... | collective-permute-start | bytes 393224 | tf_op jit(solution)/shard_map/ppermute | solution.py:112
  12.9 20.7 %collective-permute-start.4 = (bf16[4,2,32,256]{3,2,1,0:T(8,128)(2,1)}, bf16[4,2,32,256]{3,2,1,0:T(8,128)(2,1)S(1)}, u32[]{:S(2)}, u32[]{:S(2)}) collective-permute-start(bf16[4,2,32,256]{3,2,1,0:T(8,128)(2,1)} %get-tuple-element.21), channel_id=1, source_target_pairs={{0,8},{1,9},{2,10},{3,11},{4,12},{5,13},{6,14},{7,15},{8,0},{9,1},... | collective-permute-start | bytes 393224 | tf_op jit(solution)/shard_map/ppermute | solution.py:112
  14.9 38.4 %copy-start = (bf16[4,2,32,256]{3,2,1,0:T(8,128)(2,1)}, bf16[4,2,32,256]{3,2,1,0:T(8,128)(2,1)S(1)}, u32[]{:S(2)}) copy-start(bf16[4,2,32,256]{3,2,1,0:T(8,128)(2,1)S(1)} %collective-permute-done.rest_0_) | copy-start | bytes 393220
  14.9 24.9 %collective-permute-start.5 = (bf16[4,2,32,256]{3,2,1,0:T(8,128)(2,1)}, bf16[4,2,32,256]{3,2,1,0:T(8,128)(2,1)S(1)}, u32[]{:S(2)}, u32[]{:S(2)}) collective-permute-start(bf16[4,2,32,256]{3,2,1,0:T(8,128)(2,1)} %get-tuple-element.22), channel_id=1, source_target_pairs={{0,9},{1,10},{2,11},{3,8},{4,13},{5,14},{6,15},{7,12},{8,1},{9,2},... | collective-permute-start | bytes 393224 | tf_op jit(solution)/shard_map/ppermute | solution.py:112
  16.5 36.8 %copy-start.1 = (bf16[4,2,32,256]{3,2,1,0:T(8,128)(2,1)}, bf16[4,2,32,256]{3,2,1,0:T(8,128)(2,1)S(1)}, u32[]{:S(2)}) copy-start(bf16[4,2,32,256]{3,2,1,0:T(8,128)(2,1)S(1)} %collective-permute-done.1.rest_1_) | copy-start | bytes 393220
  16.5 25.8 %collective-permute-start.6 = (bf16[4,2,32,256]{3,2,1,0:T(8,128)(2,1)}, bf16[4,2,32,256]{3,2,1,0:T(8,128)(2,1)S(1)}, u32[]{:S(2)}, u32[]{:S(2)}) collective-permute-start(bf16[4,2,32,256]{3,2,1,0:T(8,128)(2,1)} %get-tuple-element.23), channel_id=1, source_target_pairs={{0,10},{1,11},{2,8},{3,9},{4,14},{5,15},{6,12},{7,13},{8,2},{9,3},... | collective-permute-start | bytes 393224 | tf_op jit(solution)/shard_map/ppermute | solution.py:112
  19.9 33.4 %copy-start.2 = (bf16[4,2,32,256]{3,2,1,0:T(8,128)(2,1)}, bf16[4,2,32,256]{3,2,1,0:T(8,128)(2,1)S(1)}, u32[]{:S(2)}) copy-start(bf16[4,2,32,256]{3,2,1,0:T(8,128)(2,1)S(1)} %collective-permute-done.2.rest_2_) | copy-start | bytes 393220
  19.9 31.1 %collective-permute-start.7 = (bf16[4,2,32,256]{3,2,1,0:T(8,128)(2,1)}, bf16[4,2,32,256]{3,2,1,0:T(8,128)(2,1)S(1)}, u32[]{:S(2)}, u32[]{:S(2)}) collective-permute-start(bf16[4,2,32,256]{3,2,1,0:T(8,128)(2,1)} %get-tuple-element.24), channel_id=1, source_target_pairs={{0,11},{1,8},{2,9},{3,10},{4,15},{5,12},{6,13},{7,14},{8,3},{9,0},... | collective-permute-start | bytes 393224 | tf_op jit(solution)/shard_map/ppermute | solution.py:112
  21.1 32.1 %copy-start.3 = (bf16[4,2,32,256]{3,2,1,0:T(8,128)(2,1)}, bf16[4,2,32,256]{3,2,1,0:T(8,128)(2,1)S(1)}, u32[]{:S(2)}) copy-start(bf16[4,2,32,256]{3,2,1,0:T(8,128)(2,1)S(1)} %collective-permute-done.3.rest_3_) | copy-start | bytes 393220
  21.2 29.9 %collective-permute-start.8 = (bf16[4,2,32,256]{3,2,1,0:T(8,128)(2,1)}, bf16[4,2,32,256]{3,2,1,0:T(8,128)(2,1)S(1)}, u32[]{:S(2)}, u32[]{:S(2)}) collective-permute-start(bf16[4,2,32,256]{3,2,1,0:T(8,128)(2,1)} %get-tuple-element.25), channel_id=1, source_target_pairs={{0,12},{1,13},{2,14},{3,15},{4,0},{5,1},{6,2},{7,3},{8,4},{9,5},{1... | collective-permute-start | bytes 393224 | tf_op jit(solution)/shard_map/ppermute | solution.py:112
  33.6 19.7 %copy-start.4 = (bf16[4,2,32,256]{3,2,1,0:T(8,128)(2,1)}, bf16[4,2,32,256]{3,2,1,0:T(8,128)(2,1)S(1)}, u32[]{:S(2)}) copy-start(bf16[4,2,32,256]{3,2,1,0:T(8,128)(2,1)S(1)} %collective-permute-done.4.rest_4_) | copy-start | bytes 393220
  33.6 17.4 %collective-permute-start.9 = (bf16[4,2,32,256]{3,2,1,0:T(8,128)(2,1)}, bf16[4,2,32,256]{3,2,1,0:T(8,128)(2,1)S(1)}, u32[]{:S(2)}, u32[]{:S(2)}) collective-permute-start(bf16[4,2,32,256]{3,2,1,0:T(8,128)(2,1)} %get-tuple-element.26), channel_id=1, source_target_pairs={{0,13},{1,14},{2,15},{3,12},{4,1},{5,2},{6,3},{7,0},{8,5},{9,6},{1... | collective-permute-start | bytes 393224 | tf_op jit(solution)/shard_map/ppermute | solution.py:112
  39.8 13.5 %copy-start.5 = (bf16[4,2,32,256]{3,2,1,0:T(8,128)(2,1)}, bf16[4,2,32,256]{3,2,1,0:T(8,128)(2,1)S(1)}, u32[]{:S(2)}) copy-start(bf16[4,2,32,256]{3,2,1,0:T(8,128)(2,1)S(1)} %collective-permute-done.5.rest_5_) | copy-start | bytes 393220
  39.8 11.3 %collective-permute-start.10 = (bf16[4,2,32,256]{3,2,1,0:T(8,128)(2,1)}, bf16[4,2,32,256]{3,2,1,0:T(8,128)(2,1)S(1)}, u32[]{:S(2)}, u32[]{:S(2)}) collective-permute-start(bf16[4,2,32,256]{3,2,1,0:T(8,128)(2,1)} %get-tuple-element.27), channel_id=1, source_target_pairs={{0,14},{1,15},{2,12},{3,13},{4,2},{5,3},{6,0},{7,1},{8,6},{9,7},{1... | collective-permute-start | bytes 393224 | tf_op jit(solution)/shard_map/ppermute | solution.py:112
  42.3 11.0 %copy-start.6 = (bf16[4,2,32,256]{3,2,1,0:T(8,128)(2,1)}, bf16[4,2,32,256]{3,2,1,0:T(8,128)(2,1)S(1)}, u32[]{:S(2)}) copy-start(bf16[4,2,32,256]{3,2,1,0:T(8,128)(2,1)S(1)} %collective-permute-done.6.rest_6_) | copy-start | bytes 393220
  42.3 11.0 %collective-permute-start.11 = (bf16[4,2,32,256]{3,2,1,0:T(8,128)(2,1)}, bf16[4,2,32,256]{3,2,1,0:T(8,128)(2,1)S(1)}, u32[]{:S(2)}, u32[]{:S(2)}) collective-permute-start(bf16[4,2,32,256]{3,2,1,0:T(8,128)(2,1)} %get-tuple-element.28), channel_id=1, source_target_pairs={{0,15},{1,12},{2,13},{3,14},{4,3},{5,0},{6,1},{7,2},{8,7},{9,4},{1... | collective-permute-start | bytes 393224 | tf_op jit(solution)/shard_map/ppermute | solution.py:112
  51.0 2.3 %copy-start.7 = (bf16[4,2,32,256]{3,2,1,0:T(8,128)(2,1)}, bf16[4,2,32,256]{3,2,1,0:T(8,128)(2,1)S(1)}, u32[]{:S(2)}) copy-start(bf16[4,2,32,256]{3,2,1,0:T(8,128)(2,1)S(1)} %collective-permute-done.7.rest_7_) | copy-start | bytes 393220
  51.0 2.3 %copy-start.8 = (bf16[4,2,32,256]{3,2,1,0:T(8,128)(2,1)}, bf16[4,2,32,256]{3,2,1,0:T(8,128)(2,1)S(1)}, u32[]{:S(2)}) copy-start(bf16[4,2,32,256]{3,2,1,0:T(8,128)(2,1)S(1)} %collective-permute-done.8.rest_8_) | copy-start | bytes 393220
  51.0 2.3 %copy-start.9 = (bf16[4,2,32,256]{3,2,1,0:T(8,128)(2,1)}, bf16[4,2,32,256]{3,2,1,0:T(8,128)(2,1)S(1)}, u32[]{:S(2)}) copy-start(bf16[4,2,32,256]{3,2,1,0:T(8,128)(2,1)S(1)} %collective-permute-done.9.rest_9_) | copy-start | bytes 393220
  51.0 2.3 %copy-start.10 = (bf16[4,2,32,256]{3,2,1,0:T(8,128)(2,1)}, bf16[4,2,32,256]{3,2,1,0:T(8,128)(2,1)S(1)}, u32[]{:S(2)}) copy-start(bf16[4,2,32,256]{3,2,1,0:T(8,128)(2,1)S(1)} %collective-permute-done.10.rest_10_) | copy-start | bytes 393220
  53.3 0.6 %copy-start.11 = (bf16[4,2,32,256]{3,2,1,0:T(8,128)(2,1)}, bf16[4,2,32,256]{3,2,1,0:T(8,128)(2,1)S(1)}, u32[]{:S(2)}) copy-start(bf16[4,2,32,256]{3,2,1,0:T(8,128)(2,1)S(1)} %collective-permute-done.11.rest_11_) | copy-start | bytes 393220

commit v21 on v20

--- a/solution.py
+++ b/solution.py
@@ -169,7 +169,7 @@
         keys = [suf_ref[0, :, lanes]]
         vals = [suf_ref[1, :, lanes]]
         masks = [causal]
-        join = 4 if page_count % 4 == 0 else (2 if page_count % 2 == 0 else 1)
+        join = page_count
         for page in range(0, page_count, join):
             keys.append(jnp.concatenate([page_part(p, 0) for p in range(page, page + join)], axis=0))
             vals.append(jnp.concatenate([page_part(p, 1) for p in range(page, page + join)], axis=0))

time: 61.3 us -> 61.7 us (level)
  no operation moved by 1% of the time
where the time goes in v21:
time: 61.7 us; the launch traced here: 61.4 us
  starting transfers between devices  31.8 us (52%)
  waiting for transfers between devices  15.4 us (25%)
  Pallas kernels  13.5 us (22%)
    ppermute x12, starting transfers between devices, on_device(): lax.ppermute(payload[(distance - 1) * tensor_count + shift], ('replica',...  31.8 us
    ppermute x12, waiting for transfers between devices, on_device(): lax.ppermute(payload[(distance - 1) * tensor_count + shift], ('replica',...  15.4 us
    pallas_call x1, Pallas kernels, attend(): pl.pallas_call(functools.partial(attention_kernel, span_count, tensor_cou...  7.53 us
    pallas_call x2, Pallas kernels, pack_pages(): pl.pallas_call(functools.partial(gather_kernel, first, last, slot_cap, te...  6.01 us
  transfers between devices with their start and end apart: 12, of which 3 were waited for; matrix products, arithmetic and copies ran while one was open for 0% of the time, Pallas kernels for 5%

profile of v21, /device:TPU:1, one launch (start us, length us, event | category | flops | bytes accessed | tf_op | source)
XLA Modules:
  0.0 61.4 jit_solution(14823746899763174591)
XLA Ops:
  0.0 2.7 %shard_map.64 = (bf16[4,2,32,256]{3,2,1,0:T(8,128)(2,1)}, bf16[4,2,32,256]{3,2,1,0:T(8,128)(2,1)}, bf16[4,2,32,256]{3,2,1,0:T(8,128)(2,1)}, bf16[4,2,32,256]{3,2,1,0:T(8,128)(2,1)}) custom-call(s32[4,8]{1,0:T(4,128)} %off_ref.5, s32[4,8]{1,0:T(4,128)} %slot_ref.3, bf16[12,2,32,1024]{3,2,1,0:T(8,128)(2,1)} %pool_hbm.3), custom_call_target="tpu_custom_call" | custom-call | bytes 1048576 | tf_op jit(solution)/shard_map/pallas_call | solution.py:82
  2.8 2.2 %collective-permute-start = (bf16[4,2,32,256]{3,2,1,0:T(8,128)(2,1)}, bf16[4,2,32,256]{3,2,1,0:T(8,128)(2,1)S(1)}, u32[]{:S(2)}, u32[]{:S(2)}) collective-permute-start(bf16[4,2,32,256]{3,2,1,0:T(8,128)(2,1)} %get-tuple-element.17), channel_id=1, source_target_pairs={{0,4},{1,5},{2,6},{3,7},{4,8},{5,9},{6,10},{7,11},{8,12},{9,13},{1... | collective-permute-start | bytes 393224 | tf_op jit(solution)/shard_map/ppermute | solution.py:112
  4.9 3.1 %collective-permute-start.1 = (bf16[4,2,32,256]{3,2,1,0:T(8,128)(2,1)}, bf16[4,2,32,256]{3,2,1,0:T(8,128)(2,1)S(1)}, u32[]{:S(2)}, u32[]{:S(2)}) collective-permute-start(bf16[4,2,32,256]{3,2,1,0:T(8,128)(2,1)} %get-tuple-element.18), channel_id=1, source_target_pairs={{0,5},{1,6},{2,7},{3,4},{4,9},{5,10},{6,11},{7,8},{8,13},{9,14},{1... | collective-permute-start | bytes 393224 | tf_op jit(solution)/shard_map/ppermute | solution.py:112
  8.0 1.3 %collective-permute-start.2 = (bf16[4,2,32,256]{3,2,1,0:T(8,128)(2,1)}, bf16[4,2,32,256]{3,2,1,0:T(8,128)(2,1)S(1)}, u32[]{:S(2)}, u32[]{:S(2)}) collective-permute-start(bf16[4,2,32,256]{3,2,1,0:T(8,128)(2,1)} %get-tuple-element.19), channel_id=1, source_target_pairs={{0,6},{1,7},{2,4},{3,5},{4,10},{5,11},{6,8},{7,9},{8,14},{9,15},{1... | collective-permute-start | bytes 393224 | tf_op jit(solution)/shard_map/ppermute | solution.py:112
  9.3 0.3 collective-permute-start.3
  9.6 3.3 %shard_map.65 = (bf16[4,2,32,256]{3,2,1,0:T(8,128)(2,1)}, bf16[4,2,32,256]{3,2,1,0:T(8,128)(2,1)}, bf16[4,2,32,256]{3,2,1,0:T(8,128)(2,1)}, bf16[4,2,32,256]{3,2...) custom-call(s32[4,8]{1,0:T(4,128)} %off_ref.5, ...), custom_call_target="tpu_custom_call" | custom-call | bytes 2097152 | tf_op jit(solution)/shard_map/pallas_call | solution.py:82
  12.9 1.7 %collective-permute-start.4 = (bf16[4,2,32,256]{3,2,1,0:T(8,128)(2,1)}, bf16[4,2,32,256]{3,2,1,0:T(8,128)(2,1)S(1)}, u32[]{:S(2)}, u32[]{:S(2)}) collective-permute-start(bf16[4,2,32,256]{3,2,1,0:T(8,128)(2,1)} %get-tuple-element.21), channel_id=1, source_target_pairs={{0,8},{1,9},{2,10},{3,11},{4,12},{5,13},{6,14},{7,15},{8,0},{9,1},... | collective-permute-start | bytes 393224 | tf_op jit(solution)/shard_map/ppermute | solution.py:112
  14.6 0.0 collective-permute-done.rest_0_
  14.6 1.9 %collective-permute-start.5 = (bf16[4,2,32,256]{3,2,1,0:T(8,128)(2,1)}, bf16[4,2,32,256]{3,2,1,0:T(8,128)(2,1)S(1)}, u32[]{:S(2)}, u32[]{:S(2)}) collective-permute-start(bf16[4,2,32,256]{3,2,1,0:T(8,128)(2,1)} %get-tuple-element.22), channel_id=1, source_target_pairs={{0,9},{1,10},{2,11},{3,8},{4,13},{5,14},{6,15},{7,12},{8,1},{9,2},... | collective-permute-start | bytes 393224 | tf_op jit(solution)/shard_map/ppermute | solution.py:112
  16.5 0.0 collective-permute-done.1.rest_1_
  16.5 3.1 %collective-permute-start.6 = (bf16[4,2,32,256]{3,2,1,0:T(8,128)(2,1)}, bf16[4,2,32,256]{3,2,1,0:T(8,128)(2,1)S(1)}, u32[]{:S(2)}, u32[]{:S(2)}) collective-permute-start(bf16[4,2,32,256]{3,2,1,0:T(8,128)(2,1)} %get-tuple-element.23), channel_id=1, source_target_pairs={{0,10},{1,11},{2,8},{3,9},{4,14},{5,15},{6,12},{7,13},{8,2},{9,3},... | collective-permute-start | bytes 393224 | tf_op jit(solution)/shard_map/ppermute | solution.py:112
  19.6 0.0 collective-permute-done.2.rest_2_
  19.6 0.0 collective-permute-start.7
  19.6 1.5 %collective-permute-done.3.rest_3_ = bf16[4,2,32,256]{3,2,1,0:T(8,128)(2,1)S(1)} collective-permute-done((bf16[4,2,32,256]{3,2,1,0:T(8,128)(2,1)}, bf16[4,2,32,256]{3,2,1,0:T(8,128)(2,1)S(1)}, u32[]{:S(2)}, u32[]{:S(2)}) %collective-permute-start.3) | collective-permute-done | bytes 131104 | tf_op jit(solution)/shard_map/ppermute | solution.py:112
  21.2 0.8 %collective-permute-start.8 = (bf16[4,2,32,256]{3,2,1,0:T(8,128)(2,1)}, bf16[4,2,32,256]{3,2,1,0:T(8,128)(2,1)S(1)}, u32[]{:S(2)}, u32[]{:S(2)}) collective-permute-start(bf16[4,2,32,256]{3,2,1,0:T(8,128)(2,1)} %get-tuple-element.25), channel_id=1, source_target_pairs={{0,12},{1,13},{2,14},{3,15},{4,0},{5,1},{6,2},{7,3},{8,4},{9,5},{1... | collective-permute-start | bytes 393224 | tf_op jit(solution)/shard_map/ppermute | solution.py:112
  22.0 11.6 %collective-permute-done.4.rest_4_ = bf16[4,2,32,256]{3,2,1,0:T(8,128)(2,1)S(1)} collective-permute-done((bf16[4,2,32,256]{3,2,1,0:T(8,128)(2,1)}, bf16[4,2,32,256]{3,2,1,0:T(8,128)(2,1)S(1)}, u32[]{:S(2)}, u32[]{:S(2)}) %collective-permute-start.4) | collective-permute-done | bytes 131104 | tf_op jit(solution)/shard_map/ppermute | solution.py:112
  33.6 6.2 %collective-permute-start.9 = (bf16[4,2,32,256]{3,2,1,0:T(8,128)(2,1)}, bf16[4,2,32,256]{3,2,1,0:T(8,128)(2,1)S(1)}, u32[]{:S(2)}, u32[]{:S(2)}) collective-permute-start(bf16[4,2,32,256]{3,2,1,0:T(8,128)(2,1)} %get-tuple-element.26), channel_id=1, source_target_pairs={{0,13},{1,14},{2,15},{3,12},{4,1},{5,2},{6,3},{7,0},{8,5},{9,6},{1... | collective-permute-start | bytes 393224 | tf_op jit(solution)/shard_map/ppermute | solution.py:112
  39.8 0.0 collective-permute-done.5.rest_5_
  39.8 2.5 %collective-permute-start.10 = (bf16[4,2,32,256]{3,2,1,0:T(8,128)(2,1)}, bf16[4,2,32,256]{3,2,1,0:T(8,128)(2,1)S(1)}, u32[]{:S(2)}, u32[]{:S(2)}) collective-permute-start(bf16[4,2,32,256]{3,2,1,0:T(8,128)(2,1)} %get-tuple-element.27), channel_id=1, source_target_pairs={{0,14},{1,15},{2,12},{3,13},{4,2},{5,3},{6,0},{7,1},{8,6},{9,7},{1... | collective-permute-start | bytes 393224 | tf_op jit(solution)/shard_map/ppermute | solution.py:112
  42.3 0.0 collective-permute-done.6.rest_6_
  42.3 8.7 %collective-permute-start.11 = (bf16[4,2,32,256]{3,2,1,0:T(8,128)(2,1)}, bf16[4,2,32,256]{3,2,1,0:T(8,128)(2,1)S(1)}, u32[]{:S(2)}, u32[]{:S(2)}) collective-permute-start(bf16[4,2,32,256]{3,2,1,0:T(8,128)(2,1)} %get-tuple-element.28), channel_id=1, source_target_pairs={{0,15},{1,12},{2,13},{3,14},{4,3},{5,0},{6,1},{7,2},{8,7},{9,4},{1... | collective-permute-start | bytes 393224 | tf_op jit(solution)/shard_map/ppermute | solution.py:112
  51.0 0.0 collective-permute-done.7.rest_7_
  51.0 0.0 collective-permute-done.8.rest_8_
  51.0 0.0 collective-permute-done.9.rest_9_
  51.0 0.0 copy-start.9
  51.0 0.0 collective-permute-done.10.rest_10_
  51.1 2.2 %collective-permute-done.11.rest_11_ = bf16[4,2,32,256]{3,2,1,0:T(8,128)(2,1)S(1)} collective-permute-done((bf16[4,2,32,256]{3,2,1,0:T(8,128)(2,1)}, bf16[4,2,32,256]{3,2,1,0:T(8,128)(2,1)S(1)}, u32[]{:S(2)}, u32[]{:S(2)}) %collective-permute-start.11) | collective-permute-done | bytes 131104 | tf_op jit(solution)/shard_map/ppermute | solution.py:112
  53.3 0.0 copy-done.2
  53.3 0.0 copy-done.3
  53.3 0.0 copy-done.4
  53.4 0.6 copy-done.11
  53.9 7.5 %shard_map.66 = bf16[128,2048]{1,0:T(8,128)(2,1)} custom-call(s32[4,8]{1,0:T(4,128)} %off_ref.5, s32[4]{0:T(128)} %len_ref.1, bf16[128,2048]{1,0:T(8,128)(2,1)} %bitcast.3, bf16[2,128,256]{2,1,0:T(8,128)(2,1)} %bitcast.4, bf16[4,2,32,256]{3,2,1,0:T(8,128)(2,1)} %copy-done, bf16[4,2,32,256]{3,2,1,0:T(8,128)(2,1)} %copy-done.1, ...), custom_call_target="tpu_custom_call" | custom-call | flops 1207959552 | bytes 2752512 | tf_op jit(solution)/shard_map/pallas_call | solution.py:223
  (19 shorter events, 0.0 us)
Async XLA Ops:
  2.8 11.9 %collective-permute-start = (bf16[4,2,32,256]{3,2,1,0:T(8,128)(2,1)}, bf16[4,2,32,256]{3,2,1,0:T(8,128)(2,1)S(1)}, u32[]{:S(2)}, u32[]{:S(2)}) collective-permute-start(bf16[4,2,32,256]{3,2,1,0:T(8,128)(2,1)} %get-tuple-element.17), channel_id=1, source_target_pairs={{0,4},{1,5},{2,6},{3,7},{4,8},{5,9},{6,10},{7,11},{8,12},{9,13},{1... | collective-permute-start | bytes 393224 | tf_op jit(solution)/shard_map/ppermute | solution.py:112
  4.9 11.6 %collective-permute-start.1 = (bf16[4,2,32,256]{3,2,1,0:T(8,128)(2,1)}, bf16[4,2,32,256]{3,2,1,0:T(8,128)(2,1)S(1)}, u32[]{:S(2)}, u32[]{:S(2)}) collective-permute-start(bf16[4,2,32,256]{3,2,1,0:T(8,128)(2,1)} %get-tuple-element.18), channel_id=1, source_target_pairs={{0,5},{1,6},{2,7},{3,4},{4,9},{5,10},{6,11},{7,8},{8,13},{9,14},{1... | collective-permute-start | bytes 393224 | tf_op jit(solution)/shard_map/ppermute | solution.py:112
  8.0 11.6 %collective-permute-start.2 = (bf16[4,2,32,256]{3,2,1,0:T(8,128)(2,1)}, bf16[4,2,32,256]{3,2,1,0:T(8,128)(2,1)S(1)}, u32[]{:S(2)}, u32[]{:S(2)}) collective-permute-start(bf16[4,2,32,256]{3,2,1,0:T(8,128)(2,1)} %get-tuple-element.19), channel_id=1, source_target_pairs={{0,6},{1,7},{2,4},{3,5},{4,10},{5,11},{6,8},{7,9},{8,14},{9,15},{1... | collective-permute-start | bytes 393224 | tf_op jit(solution)/shard_map/ppermute | solution.py:112
  9.3 11.9 %collective-permute-start.3 = (bf16[4,2,32,256]{3,2,1,0:T(8,128)(2,1)}, bf16[4,2,32,256]{3,2,1,0:T(8,128)(2,1)S(1)}, u32[]{:S(2)}, u32[]{:S(2)}) collective-permute-start(bf16[4,2,32,256]{3,2,1,0:T(8,128)(2,1)} %get-tuple-element.20), channel_id=1, source_target_pairs={{0,7},{1,4},{2,5},{3,6},{4,11},{5,8},{6,9},{7,10},{8,15},{9,12},{1... | collective-permute-start | bytes 393224 | tf_op jit(solution)/shard_map/ppermute | solution.py:112
  12.9 20.7 %collective-permute-start.4 = (bf16[4,2,32,256]{3,2,1,0:T(8,128)(2,1)}, bf16[4,2,32,256]{3,2,1,0:T(8,128)(2,1)S(1)}, u32[]{:S(2)}, u32[]{:S(2)}) collective-permute-start(bf16[4,2,32,256]{3,2,1,0:T(8,128)(2,1)} %get-tuple-element.21), channel_id=1, source_target_pairs={{0,8},{1,9},{2,10},{3,11},{4,12},{5,13},{6,14},{7,15},{8,0},{9,1},... | collective-permute-start | bytes 393224 | tf_op jit(solution)/shard_map/ppermute | solution.py:112
  14.6 38.7 %copy-start = (bf16[4,2,32,256]{3,2,1,0:T(8,128)(2,1)}, bf16[4,2,32,256]{3,2,1,0:T(8,128)(2,1)S(1)}, u32[]{:S(2)}) copy-start(bf16[4,2,32,256]{3,2,1,0:T(8,128)(2,1)S(1)} %collective-permute-done.rest_0_) | copy-start | bytes 393220
  14.6 25.2 %collective-permute-start.5 = (bf16[4,2,32,256]{3,2,1,0:T(8,128)(2,1)}, bf16[4,2,32,256]{3,2,1,0:T(8,128)(2,1)S(1)}, u32[]{:S(2)}, u32[]{:S(2)}) collective-permute-start(bf16[4,2,32,256]{3,2,1,0:T(8,128)(2,1)} %get-tuple-element.22), channel_id=1, source_target_pairs={{0,9},{1,10},{2,11},{3,8},{4,13},{5,14},{6,15},{7,12},{8,1},{9,2},... | collective-permute-start | bytes 393224 | tf_op jit(solution)/shard_map/ppermute | solution.py:112
  16.5 36.8 %copy-start.1 = (bf16[4,2,32,256]{3,2,1,0:T(8,128)(2,1)}, bf16[4,2,32,256]{3,2,1,0:T(8,128)(2,1)S(1)}, u32[]{:S(2)}) copy-start(bf16[4,2,32,256]{3,2,1,0:T(8,128)(2,1)S(1)} %collective-permute-done.1.rest_1_) | copy-start | bytes 393220
  16.5 25.8 %collective-permute-start.6 = (bf16[4,2,32,256]{3,2,1,0:T(8,128)(2,1)}, bf16[4,2,32,256]{3,2,1,0:T(8,128)(2,1)S(1)}, u32[]{:S(2)}, u32[]{:S(2)}) collective-permute-start(bf16[4,2,32,256]{3,2,1,0:T(8,128)(2,1)} %get-tuple-element.23), channel_id=1, source_target_pairs={{0,10},{1,11},{2,8},{3,9},{4,14},{5,15},{6,12},{7,13},{8,2},{9,3},... | collective-permute-start | bytes 393224 | tf_op jit(solution)/shard_map/ppermute | solution.py:112
  19.6 33.6 %copy-start.2 = (bf16[4,2,32,256]{3,2,1,0:T(8,128)(2,1)}, bf16[4,2,32,256]{3,2,1,0:T(8,128)(2,1)S(1)}, u32[]{:S(2)}) copy-start(bf16[4,2,32,256]{3,2,1,0:T(8,128)(2,1)S(1)} %collective-permute-done.2.rest_2_) | copy-start | bytes 393220
  19.6 31.4 %collective-permute-start.7 = (bf16[4,2,32,256]{3,2,1,0:T(8,128)(2,1)}, bf16[4,2,32,256]{3,2,1,0:T(8,128)(2,1)S(1)}, u32[]{:S(2)}, u32[]{:S(2)}) collective-permute-start(bf16[4,2,32,256]{3,2,1,0:T(8,128)(2,1)} %get-tuple-element.24), channel_id=1, source_target_pairs={{0,11},{1,8},{2,9},{3,10},{4,15},{5,12},{6,13},{7,14},{8,3},{9,0},... | collective-permute-start | bytes 393224 | tf_op jit(solution)/shard_map/ppermute | solution.py:112
  21.1 32.1 %copy-start.3 = (bf16[4,2,32,256]{3,2,1,0:T(8,128)(2,1)}, bf16[4,2,32,256]{3,2,1,0:T(8,128)(2,1)S(1)}, u32[]{:S(2)}) copy-start(bf16[4,2,32,256]{3,2,1,0:T(8,128)(2,1)S(1)} %collective-permute-done.3.rest_3_) | copy-start | bytes 393220
  21.2 29.9 %collective-permute-start.8 = (bf16[4,2,32,256]{3,2,1,0:T(8,128)(2,1)}, bf16[4,2,32,256]{3,2,1,0:T(8,128)(2,1)S(1)}, u32[]{:S(2)}, u32[]{:S(2)}) collective-permute-start(bf16[4,2,32,256]{3,2,1,0:T(8,128)(2,1)} %get-tuple-element.25), channel_id=1, source_target_pairs={{0,12},{1,13},{2,14},{3,15},{4,0},{5,1},{6,2},{7,3},{8,4},{9,5},{1... | collective-permute-start | bytes 393224 | tf_op jit(solution)/shard_map/ppermute | solution.py:112
  33.6 19.7 %copy-start.4 = (bf16[4,2,32,256]{3,2,1,0:T(8,128)(2,1)}, bf16[4,2,32,256]{3,2,1,0:T(8,128)(2,1)S(1)}, u32[]{:S(2)}) copy-start(bf16[4,2,32,256]{3,2,1,0:T(8,128)(2,1)S(1)} %collective-permute-done.4.rest_4_) | copy-start | bytes 393220
  33.6 17.4 %collective-permute-start.9 = (bf16[4,2,32,256]{3,2,1,0:T(8,128)(2,1)}, bf16[4,2,32,256]{3,2,1,0:T(8,128)(2,1)S(1)}, u32[]{:S(2)}, u32[]{:S(2)}) collective-permute-start(bf16[4,2,32,256]{3,2,1,0:T(8,128)(2,1)} %get-tuple-element.26), channel_id=1, source_target_pairs={{0,13},{1,14},{2,15},{3,12},{4,1},{5,2},{6,3},{7,0},{8,5},{9,6},{1... | collective-permute-start | bytes 393224 | tf_op jit(solution)/shard_map/ppermute | solution.py:112
  39.8 13.5 %copy-start.5 = (bf16[4,2,32,256]{3,2,1,0:T(8,128)(2,1)}, bf16[4,2,32,256]{3,2,1,0:T(8,128)(2,1)S(1)}, u32[]{:S(2)}) copy-start(bf16[4,2,32,256]{3,2,1,0:T(8,128)(2,1)S(1)} %collective-permute-done.5.rest_5_) | copy-start | bytes 393220
  39.8 11.3 %collective-permute-start.10 = (bf16[4,2,32,256]{3,2,1,0:T(8,128)(2,1)}, bf16[4,2,32,256]{3,2,1,0:T(8,128)(2,1)S(1)}, u32[]{:S(2)}, u32[]{:S(2)}) collective-permute-start(bf16[4,2,32,256]{3,2,1,0:T(8,128)(2,1)} %get-tuple-element.27), channel_id=1, source_target_pairs={{0,14},{1,15},{2,12},{3,13},{4,2},{5,3},{6,0},{7,1},{8,6},{9,7},{1... | collective-permute-start | bytes 393224 | tf_op jit(solution)/shard_map/ppermute | solution.py:112
  42.3 11.0 %copy-start.6 = (bf16[4,2,32,256]{3,2,1,0:T(8,128)(2,1)}, bf16[4,2,32,256]{3,2,1,0:T(8,128)(2,1)S(1)}, u32[]{:S(2)}) copy-start(bf16[4,2,32,256]{3,2,1,0:T(8,128)(2,1)S(1)} %collective-permute-done.6.rest_6_) | copy-start | bytes 393220
  42.3 11.0 %collective-permute-start.11 = (bf16[4,2,32,256]{3,2,1,0:T(8,128)(2,1)}, bf16[4,2,32,256]{3,2,1,0:T(8,128)(2,1)S(1)}, u32[]{:S(2)}, u32[]{:S(2)}) collective-permute-start(bf16[4,2,32,256]{3,2,1,0:T(8,128)(2,1)} %get-tuple-element.28), channel_id=1, source_target_pairs={{0,15},{1,12},{2,13},{3,14},{4,3},{5,0},{6,1},{7,2},{8,7},{9,4},{1... | collective-permute-start | bytes 393224 | tf_op jit(solution)/shard_map/ppermute | solution.py:112
  51.0 2.3 %copy-start.7 = (bf16[4,2,32,256]{3,2,1,0:T(8,128)(2,1)}, bf16[4,2,32,256]{3,2,1,0:T(8,128)(2,1)S(1)}, u32[]{:S(2)}) copy-start(bf16[4,2,32,256]{3,2,1,0:T(8,128)(2,1)S(1)} %collective-permute-done.7.rest_7_) | copy-start | bytes 393220
  51.0 2.3 %copy-start.8 = (bf16[4,2,32,256]{3,2,1,0:T(8,128)(2,1)}, bf16[4,2,32,256]{3,2,1,0:T(8,128)(2,1)S(1)}, u32[]{:S(2)}) copy-start(bf16[4,2,32,256]{3,2,1,0:T(8,128)(2,1)S(1)} %collective-permute-done.8.rest_8_) | copy-start | bytes 393220
  51.0 2.3 %copy-start.9 = (bf16[4,2,32,256]{3,2,1,0:T(8,128)(2,1)}, bf16[4,2,32,256]{3,2,1,0:T(8,128)(2,1)S(1)}, u32[]{:S(2)}) copy-start(bf16[4,2,32,256]{3,2,1,0:T(8,128)(2,1)S(1)} %collective-permute-done.9.rest_9_) | copy-start | bytes 393220
  51.0 2.3 %copy-start.10 = (bf16[4,2,32,256]{3,2,1,0:T(8,128)(2,1)}, bf16[4,2,32,256]{3,2,1,0:T(8,128)(2,1)S(1)}, u32[]{:S(2)}) copy-start(bf16[4,2,32,256]{3,2,1,0:T(8,128)(2,1)S(1)} %collective-permute-done.10.rest_10_) | copy-start | bytes 393220
  53.3 0.6 %copy-start.11 = (bf16[4,2,32,256]{3,2,1,0:T(8,128)(2,1)}, bf16[4,2,32,256]{3,2,1,0:T(8,128)(2,1)S(1)}, u32[]{:S(2)}) copy-start(bf16[4,2,32,256]{3,2,1,0:T(8,128)(2,1)S(1)} %collective-permute-done.11.rest_11_) | copy-start | bytes 393220

commit v22 on v20

--- a/solution.py
+++ b/solution.py
@@ -174,6 +174,10 @@
             keys.append(jnp.concatenate([page_part(p, 0) for p in range(page, page + join)], axis=0))
             vals.append(jnp.concatenate([page_part(p, 1) for p in range(page, page + join)], axis=0))
             masks.append(page_mask(page, join))
+        keys = keys[1:-1] + [jnp.concatenate([keys[-1], keys[0]], axis=0)]
+        vals = vals[1:-1] + [jnp.concatenate([vals[-1], vals[0]], axis=0)]
+        last_mask = jnp.broadcast_to(masks[-1], (causal.shape[0], masks[-1].shape[1]))
+        masks = masks[1:-1] + [jnp.concatenate([last_mask, causal], axis=1)]
         scores = []
         for key, mask in zip(keys, masks):
             s = lax.dot_general(q_all, key, dims, preferred_element_type=jnp.float32)

time: 61.3 us -> 61.4 us (level)
  no operation moved by 1% of the time
where the time goes in v22:
time: 61.4 us; the launch traced here: 61.1 us
  starting transfers between devices  32 us (52%)
  waiting for transfers between devices  15.2 us (25%)
  Pallas kernels  13.2 us (21%)
    ppermute x12, starting transfers between devices, on_device(): lax.ppermute(payload[(distance - 1) * tensor_count + shift], ('replica',...  32 us
    ppermute x12, waiting for transfers between devices, on_device(): lax.ppermute(payload[(distance - 1) * tensor_count + shift], ('replica',...  15.2 us
    pallas_call x1, Pallas kernels, attend(): pl.pallas_call(functools.partial(attention_kernel, span_count, tensor_cou...  7.16 us
    pallas_call x2, Pallas kernels, pack_pages(): pl.pallas_call(functools.partial(gather_kernel, first, last, slot_cap, te...  6.01 us
  transfers between devices with their start and end apart: 12, of which 3 were waited for; matrix products, arithmetic and copies ran while one was open for 0% of the time, Pallas kernels for 5%

profile of v22, /device:TPU:1, one launch (start us, length us, event | category | flops | bytes accessed | tf_op | source)
XLA Modules:
  0.0 61.1 jit_solution(14196032028280460812)
XLA Ops:
  0.0 2.7 %shard_map.64 = (bf16[4,2,32,256]{3,2,1,0:T(8,128)(2,1)}, bf16[4,2,32,256]{3,2,1,0:T(8,128)(2,1)}, bf16[4,2,32,256]{3,2,1,0:T(8,128)(2,1)}, bf16[4,2,32,256]{3,2,1,0:T(8,128)(2,1)}) custom-call(s32[4,8]{1,0:T(4,128)} %off_ref.5, s32[4,8]{1,0:T(4,128)} %slot_ref.3, bf16[12,2,32,1024]{3,2,1,0:T(8,128)(2,1)} %pool_hbm.3), custom_call_target="tpu_custom_call" | custom-call | bytes 1048576 | tf_op jit(solution)/shard_map/pallas_call | solution.py:82
  2.8 2.2 %collective-permute-start = (bf16[4,2,32,256]{3,2,1,0:T(8,128)(2,1)}, bf16[4,2,32,256]{3,2,1,0:T(8,128)(2,1)S(1)}, u32[]{:S(2)}, u32[]{:S(2)}) collective-permute-start(bf16[4,2,32,256]{3,2,1,0:T(8,128)(2,1)} %get-tuple-element.17), channel_id=1, source_target_pairs={{0,4},{1,5},{2,6},{3,7},{4,8},{5,9},{6,10},{7,11},{8,12},{9,13},{1... | collective-permute-start | bytes 393224 | tf_op jit(solution)/shard_map/ppermute | solution.py:112
  4.9 3.1 %collective-permute-start.1 = (bf16[4,2,32,256]{3,2,1,0:T(8,128)(2,1)}, bf16[4,2,32,256]{3,2,1,0:T(8,128)(2,1)S(1)}, u32[]{:S(2)}, u32[]{:S(2)}) collective-permute-start(bf16[4,2,32,256]{3,2,1,0:T(8,128)(2,1)} %get-tuple-element.18), channel_id=1, source_target_pairs={{0,5},{1,6},{2,7},{3,4},{4,9},{5,10},{6,11},{7,8},{8,13},{9,14},{1... | collective-permute-start | bytes 393224 | tf_op jit(solution)/shard_map/ppermute | solution.py:112
  8.0 1.2 %collective-permute-start.2 = (bf16[4,2,32,256]{3,2,1,0:T(8,128)(2,1)}, bf16[4,2,32,256]{3,2,1,0:T(8,128)(2,1)S(1)}, u32[]{:S(2)}, u32[]{:S(2)}) collective-permute-start(bf16[4,2,32,256]{3,2,1,0:T(8,128)(2,1)} %get-tuple-element.19), channel_id=1, source_target_pairs={{0,6},{1,7},{2,4},{3,5},{4,10},{5,11},{6,8},{7,9},{8,14},{9,15},{1... | collective-permute-start | bytes 393224 | tf_op jit(solution)/shard_map/ppermute | solution.py:112
  9.3 0.3 collective-permute-start.3
  9.6 3.3 %shard_map.65 = (bf16[4,2,32,256]{3,2,1,0:T(8,128)(2,1)}, bf16[4,2,32,256]{3,2,1,0:T(8,128)(2,1)}, bf16[4,2,32,256]{3,2,1,0:T(8,128)(2,1)}, bf16[4,2,32,256]{3,2...) custom-call(s32[4,8]{1,0:T(4,128)} %off_ref.5, ...), custom_call_target="tpu_custom_call" | custom-call | bytes 2097152 | tf_op jit(solution)/shard_map/pallas_call | solution.py:82
  12.9 1.8 %collective-permute-start.4 = (bf16[4,2,32,256]{3,2,1,0:T(8,128)(2,1)}, bf16[4,2,32,256]{3,2,1,0:T(8,128)(2,1)S(1)}, u32[]{:S(2)}, u32[]{:S(2)}) collective-permute-start(bf16[4,2,32,256]{3,2,1,0:T(8,128)(2,1)} %get-tuple-element.21), channel_id=1, source_target_pairs={{0,8},{1,9},{2,10},{3,11},{4,12},{5,13},{6,14},{7,15},{8,0},{9,1},... | collective-permute-start | bytes 393224 | tf_op jit(solution)/shard_map/ppermute | solution.py:112
  14.7 0.0 collective-permute-done.rest_0_
  14.7 1.8 %collective-permute-start.5 = (bf16[4,2,32,256]{3,2,1,0:T(8,128)(2,1)}, bf16[4,2,32,256]{3,2,1,0:T(8,128)(2,1)S(1)}, u32[]{:S(2)}, u32[]{:S(2)}) collective-permute-start(bf16[4,2,32,256]{3,2,1,0:T(8,128)(2,1)} %get-tuple-element.22), channel_id=1, source_target_pairs={{0,9},{1,10},{2,11},{3,8},{4,13},{5,14},{6,15},{7,12},{8,1},{9,2},... | collective-permute-start | bytes 393224 | tf_op jit(solution)/shard_map/ppermute | solution.py:112
  16.5 0.0 collective-permute-done.1.rest_1_
  16.5 3.2 %collective-permute-start.6 = (bf16[4,2,32,256]{3,2,1,0:T(8,128)(2,1)}, bf16[4,2,32,256]{3,2,1,0:T(8,128)(2,1)S(1)}, u32[]{:S(2)}, u32[]{:S(2)}) collective-permute-start(bf16[4,2,32,256]{3,2,1,0:T(8,128)(2,1)} %get-tuple-element.23), channel_id=1, source_target_pairs={{0,10},{1,11},{2,8},{3,9},{4,14},{5,15},{6,12},{7,13},{8,2},{9,3},... | collective-permute-start | bytes 393224 | tf_op jit(solution)/shard_map/ppermute | solution.py:112
  19.7 0.0 collective-permute-done.2.rest_2_
  19.7 0.0 collective-permute-start.7
  19.7 1.4 %collective-permute-done.3.rest_3_ = bf16[4,2,32,256]{3,2,1,0:T(8,128)(2,1)S(1)} collective-permute-done((bf16[4,2,32,256]{3,2,1,0:T(8,128)(2,1)}, bf16[4,2,32,256]{3,2,1,0:T(8,128)(2,1)S(1)}, u32[]{:S(2)}, u32[]{:S(2)}) %collective-permute-start.3) | collective-permute-done | bytes 131104 | tf_op jit(solution)/shard_map/ppermute | solution.py:112
  21.2 0.8 %collective-permute-start.8 = (bf16[4,2,32,256]{3,2,1,0:T(8,128)(2,1)}, bf16[4,2,32,256]{3,2,1,0:T(8,128)(2,1)S(1)}, u32[]{:S(2)}, u32[]{:S(2)}) collective-permute-start(bf16[4,2,32,256]{3,2,1,0:T(8,128)(2,1)} %get-tuple-element.25), channel_id=1, source_target_pairs={{0,12},{1,13},{2,14},{3,15},{4,0},{5,1},{6,2},{7,3},{8,4},{9,5},{1... | collective-permute-start | bytes 393224 | tf_op jit(solution)/shard_map/ppermute | solution.py:112
  22.0 11.6 %collective-permute-done.4.rest_4_ = bf16[4,2,32,256]{3,2,1,0:T(8,128)(2,1)S(1)} collective-permute-done((bf16[4,2,32,256]{3,2,1,0:T(8,128)(2,1)}, bf16[4,2,32,256]{3,2,1,0:T(8,128)(2,1)S(1)}, u32[]{:S(2)}, u32[]{:S(2)}) %collective-permute-start.4) | collective-permute-done | bytes 131104 | tf_op jit(solution)/shard_map/ppermute | solution.py:112
  33.6 6.2 %collective-permute-start.9 = (bf16[4,2,32,256]{3,2,1,0:T(8,128)(2,1)}, bf16[4,2,32,256]{3,2,1,0:T(8,128)(2,1)S(1)}, u32[]{:S(2)}, u32[]{:S(2)}) collective-permute-start(bf16[4,2,32,256]{3,2,1,0:T(8,128)(2,1)} %get-tuple-element.26), channel_id=1, source_target_pairs={{0,13},{1,14},{2,15},{3,12},{4,1},{5,2},{6,3},{7,0},{8,5},{9,6},{1... | collective-permute-start | bytes 393224 | tf_op jit(solution)/shard_map/ppermute | solution.py:112
  39.8 0.0 collective-permute-done.5.rest_5_
  39.8 2.5 %collective-permute-start.10 = (bf16[4,2,32,256]{3,2,1,0:T(8,128)(2,1)}, bf16[4,2,32,256]{3,2,1,0:T(8,128)(2,1)S(1)}, u32[]{:S(2)}, u32[]{:S(2)}) collective-permute-start(bf16[4,2,32,256]{3,2,1,0:T(8,128)(2,1)} %get-tuple-element.27), channel_id=1, source_target_pairs={{0,14},{1,15},{2,12},{3,13},{4,2},{5,3},{6,0},{7,1},{8,6},{9,7},{1... | collective-permute-start | bytes 393224 | tf_op jit(solution)/shard_map/ppermute | solution.py:112
  42.4 0.0 collective-permute-done.6.rest_6_
  42.4 8.7 %collective-permute-start.11 = (bf16[4,2,32,256]{3,2,1,0:T(8,128)(2,1)}, bf16[4,2,32,256]{3,2,1,0:T(8,128)(2,1)S(1)}, u32[]{:S(2)}, u32[]{:S(2)}) collective-permute-start(bf16[4,2,32,256]{3,2,1,0:T(8,128)(2,1)} %get-tuple-element.28), channel_id=1, source_target_pairs={{0,15},{1,12},{2,13},{3,14},{4,3},{5,0},{6,1},{7,2},{8,7},{9,4},{1... | collective-permute-start | bytes 393224 | tf_op jit(solution)/shard_map/ppermute | solution.py:112
  51.1 0.0 collective-permute-done.7.rest_7_
  51.1 0.0 collective-permute-done.8.rest_8_
  51.1 0.0 copy-start.8
  51.1 0.0 collective-permute-done.9.rest_9_
  51.1 0.0 copy-start.9
  51.1 0.0 collective-permute-done.10.rest_10_
  51.1 0.0 copy-start.10
  51.1 2.2 %collective-permute-done.11.rest_11_ = bf16[4,2,32,256]{3,2,1,0:T(8,128)(2,1)S(1)} collective-permute-done((bf16[4,2,32,256]{3,2,1,0:T(8,128)(2,1)}, bf16[4,2,32,256]{3,2,1,0:T(8,128)(2,1)S(1)}, u32[]{:S(2)}, u32[]{:S(2)}) %collective-permute-start.11) | collective-permute-done | bytes 131104 | tf_op jit(solution)/shard_map/ppermute | solution.py:112
  53.3 0.0 copy-done.2
  53.4 0.6 copy-done.11
  54.0 7.2 %shard_map.66 = bf16[128,2048]{1,0:T(8,128)(2,1)} custom-call(s32[4,8]{1,0:T(4,128)} %off_ref.5, s32[4]{0:T(128)} %len_ref.1, bf16[128,2048]{1,0:T(8,128)(2,1)} %bitcast.3, bf16[2,128,256]{2,1,0:T(8,128)(2,1)} %bitcast.4, bf16[4,2,32,256]{3,2,1,0:T(8,128)(2,1)} %copy-done, bf16[4,2,32,256]{3,2,1,0:T(8,128)(2,1)} %copy-done.1, ...), custom_call_target="tpu_custom_call" | custom-call | flops 1207959552 | bytes 2752512 | tf_op jit(solution)/shard_map/pallas_call | solution.py:227
  (19 shorter events, 0.0 us)
Async XLA Ops:
  2.8 12.0 %collective-permute-start = (bf16[4,2,32,256]{3,2,1,0:T(8,128)(2,1)}, bf16[4,2,32,256]{3,2,1,0:T(8,128)(2,1)S(1)}, u32[]{:S(2)}, u32[]{:S(2)}) collective-permute-start(bf16[4,2,32,256]{3,2,1,0:T(8,128)(2,1)} %get-tuple-element.17), channel_id=1, source_target_pairs={{0,4},{1,5},{2,6},{3,7},{4,8},{5,9},{6,10},{7,11},{8,12},{9,13},{1... | collective-permute-start | bytes 393224 | tf_op jit(solution)/shard_map/ppermute | solution.py:112
  4.9 11.6 %collective-permute-start.1 = (bf16[4,2,32,256]{3,2,1,0:T(8,128)(2,1)}, bf16[4,2,32,256]{3,2,1,0:T(8,128)(2,1)S(1)}, u32[]{:S(2)}, u32[]{:S(2)}) collective-permute-start(bf16[4,2,32,256]{3,2,1,0:T(8,128)(2,1)} %get-tuple-element.18), channel_id=1, source_target_pairs={{0,5},{1,6},{2,7},{3,4},{4,9},{5,10},{6,11},{7,8},{8,13},{9,14},{1... | collective-permute-start | bytes 393224 | tf_op jit(solution)/shard_map/ppermute | solution.py:112
  8.0 11.7 %collective-permute-start.2 = (bf16[4,2,32,256]{3,2,1,0:T(8,128)(2,1)}, bf16[4,2,32,256]{3,2,1,0:T(8,128)(2,1)S(1)}, u32[]{:S(2)}, u32[]{:S(2)}) collective-permute-start(bf16[4,2,32,256]{3,2,1,0:T(8,128)(2,1)} %get-tuple-element.19), channel_id=1, source_target_pairs={{0,6},{1,7},{2,4},{3,5},{4,10},{5,11},{6,8},{7,9},{8,14},{9,15},{1... | collective-permute-start | bytes 393224 | tf_op jit(solution)/shard_map/ppermute | solution.py:112
  9.3 11.9 %collective-permute-start.3 = (bf16[4,2,32,256]{3,2,1,0:T(8,128)(2,1)}, bf16[4,2,32,256]{3,2,1,0:T(8,128)(2,1)S(1)}, u32[]{:S(2)}, u32[]{:S(2)}) collective-permute-start(bf16[4,2,32,256]{3,2,1,0:T(8,128)(2,1)} %get-tuple-element.20), channel_id=1, source_target_pairs={{0,7},{1,4},{2,5},{3,6},{4,11},{5,8},{6,9},{7,10},{8,15},{9,12},{1... | collective-permute-start | bytes 393224 | tf_op jit(solution)/shard_map/ppermute | solution.py:112
  12.9 20.7 %collective-permute-start.4 = (bf16[4,2,32,256]{3,2,1,0:T(8,128)(2,1)}, bf16[4,2,32,256]{3,2,1,0:T(8,128)(2,1)S(1)}, u32[]{:S(2)}, u32[]{:S(2)}) collective-permute-start(bf16[4,2,32,256]{3,2,1,0:T(8,128)(2,1)} %get-tuple-element.21), channel_id=1, source_target_pairs={{0,8},{1,9},{2,10},{3,11},{4,12},{5,13},{6,14},{7,15},{8,0},{9,1},... | collective-permute-start | bytes 393224 | tf_op jit(solution)/shard_map/ppermute | solution.py:112
  14.7 38.6 %copy-start = (bf16[4,2,32,256]{3,2,1,0:T(8,128)(2,1)}, bf16[4,2,32,256]{3,2,1,0:T(8,128)(2,1)S(1)}, u32[]{:S(2)}) copy-start(bf16[4,2,32,256]{3,2,1,0:T(8,128)(2,1)S(1)} %collective-permute-done.rest_0_) | copy-start | bytes 393220
  14.7 25.1 %collective-permute-start.5 = (bf16[4,2,32,256]{3,2,1,0:T(8,128)(2,1)}, bf16[4,2,32,256]{3,2,1,0:T(8,128)(2,1)S(1)}, u32[]{:S(2)}, u32[]{:S(2)}) collective-permute-start(bf16[4,2,32,256]{3,2,1,0:T(8,128)(2,1)} %get-tuple-element.22), channel_id=1, source_target_pairs={{0,9},{1,10},{2,11},{3,8},{4,13},{5,14},{6,15},{7,12},{8,1},{9,2},... | collective-permute-start | bytes 393224 | tf_op jit(solution)/shard_map/ppermute | solution.py:112
  16.5 36.8 %copy-start.1 = (bf16[4,2,32,256]{3,2,1,0:T(8,128)(2,1)}, bf16[4,2,32,256]{3,2,1,0:T(8,128)(2,1)S(1)}, u32[]{:S(2)}) copy-start(bf16[4,2,32,256]{3,2,1,0:T(8,128)(2,1)S(1)} %collective-permute-done.1.rest_1_) | copy-start | bytes 393220
  16.5 25.9 %collective-permute-start.6 = (bf16[4,2,32,256]{3,2,1,0:T(8,128)(2,1)}, bf16[4,2,32,256]{3,2,1,0:T(8,128)(2,1)S(1)}, u32[]{:S(2)}, u32[]{:S(2)}) collective-permute-start(bf16[4,2,32,256]{3,2,1,0:T(8,128)(2,1)} %get-tuple-element.23), channel_id=1, source_target_pairs={{0,10},{1,11},{2,8},{3,9},{4,14},{5,15},{6,12},{7,13},{8,2},{9,3},... | collective-permute-start | bytes 393224 | tf_op jit(solution)/shard_map/ppermute | solution.py:112
  19.7 33.6 %copy-start.2 = (bf16[4,2,32,256]{3,2,1,0:T(8,128)(2,1)}, bf16[4,2,32,256]{3,2,1,0:T(8,128)(2,1)S(1)}, u32[]{:S(2)}) copy-start(bf16[4,2,32,256]{3,2,1,0:T(8,128)(2,1)S(1)} %collective-permute-done.2.rest_2_) | copy-start | bytes 393220
  19.7 31.3 %collective-permute-start.7 = (bf16[4,2,32,256]{3,2,1,0:T(8,128)(2,1)}, bf16[4,2,32,256]{3,2,1,0:T(8,128)(2,1)S(1)}, u32[]{:S(2)}, u32[]{:S(2)}) collective-permute-start(bf16[4,2,32,256]{3,2,1,0:T(8,128)(2,1)} %get-tuple-element.24), channel_id=1, source_target_pairs={{0,11},{1,8},{2,9},{3,10},{4,15},{5,12},{6,13},{7,14},{8,3},{9,0},... | collective-permute-start | bytes 393224 | tf_op jit(solution)/shard_map/ppermute | solution.py:112
  21.1 32.2 %copy-start.3 = (bf16[4,2,32,256]{3,2,1,0:T(8,128)(2,1)}, bf16[4,2,32,256]{3,2,1,0:T(8,128)(2,1)S(1)}, u32[]{:S(2)}) copy-start(bf16[4,2,32,256]{3,2,1,0:T(8,128)(2,1)S(1)} %collective-permute-done.3.rest_3_) | copy-start | bytes 393220
  21.2 29.9 %collective-permute-start.8 = (bf16[4,2,32,256]{3,2,1,0:T(8,128)(2,1)}, bf16[4,2,32,256]{3,2,1,0:T(8,128)(2,1)S(1)}, u32[]{:S(2)}, u32[]{:S(2)}) collective-permute-start(bf16[4,2,32,256]{3,2,1,0:T(8,128)(2,1)} %get-tuple-element.25), channel_id=1, source_target_pairs={{0,12},{1,13},{2,14},{3,15},{4,0},{5,1},{6,2},{7,3},{8,4},{9,5},{1... | collective-permute-start | bytes 393224 | tf_op jit(solution)/shard_map/ppermute | solution.py:112
  33.6 19.8 %copy-start.4 = (bf16[4,2,32,256]{3,2,1,0:T(8,128)(2,1)}, bf16[4,2,32,256]{3,2,1,0:T(8,128)(2,1)S(1)}, u32[]{:S(2)}) copy-start(bf16[4,2,32,256]{3,2,1,0:T(8,128)(2,1)S(1)} %collective-permute-done.4.rest_4_) | copy-start | bytes 393220
  33.6 17.5 %collective-permute-start.9 = (bf16[4,2,32,256]{3,2,1,0:T(8,128)(2,1)}, bf16[4,2,32,256]{3,2,1,0:T(8,128)(2,1)S(1)}, u32[]{:S(2)}, u32[]{:S(2)}) collective-permute-start(bf16[4,2,32,256]{3,2,1,0:T(8,128)(2,1)} %get-tuple-element.26), channel_id=1, source_target_pairs={{0,13},{1,14},{2,15},{3,12},{4,1},{5,2},{6,3},{7,0},{8,5},{9,6},{1... | collective-permute-start | bytes 393224 | tf_op jit(solution)/shard_map/ppermute | solution.py:112
  39.8 13.5 %copy-start.5 = (bf16[4,2,32,256]{3,2,1,0:T(8,128)(2,1)}, bf16[4,2,32,256]{3,2,1,0:T(8,128)(2,1)S(1)}, u32[]{:S(2)}) copy-start(bf16[4,2,32,256]{3,2,1,0:T(8,128)(2,1)S(1)} %collective-permute-done.5.rest_5_) | copy-start | bytes 393220
  39.8 11.3 %collective-permute-start.10 = (bf16[4,2,32,256]{3,2,1,0:T(8,128)(2,1)}, bf16[4,2,32,256]{3,2,1,0:T(8,128)(2,1)S(1)}, u32[]{:S(2)}, u32[]{:S(2)}) collective-permute-start(bf16[4,2,32,256]{3,2,1,0:T(8,128)(2,1)} %get-tuple-element.27), channel_id=1, source_target_pairs={{0,14},{1,15},{2,12},{3,13},{4,2},{5,3},{6,0},{7,1},{8,6},{9,7},{1... | collective-permute-start | bytes 393224 | tf_op jit(solution)/shard_map/ppermute | solution.py:112
  42.4 11.0 %copy-start.6 = (bf16[4,2,32,256]{3,2,1,0:T(8,128)(2,1)}, bf16[4,2,32,256]{3,2,1,0:T(8,128)(2,1)S(1)}, u32[]{:S(2)}) copy-start(bf16[4,2,32,256]{3,2,1,0:T(8,128)(2,1)S(1)} %collective-permute-done.6.rest_6_) | copy-start | bytes 393220
  42.4 11.0 %collective-permute-start.11 = (bf16[4,2,32,256]{3,2,1,0:T(8,128)(2,1)}, bf16[4,2,32,256]{3,2,1,0:T(8,128)(2,1)S(1)}, u32[]{:S(2)}, u32[]{:S(2)}) collective-permute-start(bf16[4,2,32,256]{3,2,1,0:T(8,128)(2,1)} %get-tuple-element.28), channel_id=1, source_target_pairs={{0,15},{1,12},{2,13},{3,14},{4,3},{5,0},{6,1},{7,2},{8,7},{9,4},{1... | collective-permute-start | bytes 393224 | tf_op jit(solution)/shard_map/ppermute | solution.py:112
  51.1 2.3 %copy-start.7 = (bf16[4,2,32,256]{3,2,1,0:T(8,128)(2,1)}, bf16[4,2,32,256]{3,2,1,0:T(8,128)(2,1)S(1)}, u32[]{:S(2)}) copy-start(bf16[4,2,32,256]{3,2,1,0:T(8,128)(2,1)S(1)} %collective-permute-done.7.rest_7_) | copy-start | bytes 393220
  51.1 2.3 %copy-start.8 = (bf16[4,2,32,256]{3,2,1,0:T(8,128)(2,1)}, bf16[4,2,32,256]{3,2,1,0:T(8,128)(2,1)S(1)}, u32[]{:S(2)}) copy-start(bf16[4,2,32,256]{3,2,1,0:T(8,128)(2,1)S(1)} %collective-permute-done.8.rest_8_) | copy-start | bytes 393220
  51.1 2.3 %copy-start.9 = (bf16[4,2,32,256]{3,2,1,0:T(8,128)(2,1)}, bf16[4,2,32,256]{3,2,1,0:T(8,128)(2,1)S(1)}, u32[]{:S(2)}) copy-start(bf16[4,2,32,256]{3,2,1,0:T(8,128)(2,1)S(1)} %collective-permute-done.9.rest_9_) | copy-start | bytes 393220
  51.1 2.3 %copy-start.10 = (bf16[4,2,32,256]{3,2,1,0:T(8,128)(2,1)}, bf16[4,2,32,256]{3,2,1,0:T(8,128)(2,1)S(1)}, u32[]{:S(2)}) copy-start(bf16[4,2,32,256]{3,2,1,0:T(8,128)(2,1)S(1)} %collective-permute-done.10.rest_10_) | copy-start | bytes 393220
  53.3 0.6 %copy-start.11 = (bf16[4,2,32,256]{3,2,1,0:T(8,128)(2,1)}, bf16[4,2,32,256]{3,2,1,0:T(8,128)(2,1)S(1)}, u32[]{:S(2)}) copy-start(bf16[4,2,32,256]{3,2,1,0:T(8,128)(2,1)S(1)} %collective-permute-done.11.rest_11_) | copy-start | bytes 393220

commit v23 on v22

--- a/solution.py
+++ b/solution.py
@@ -97,9 +97,10 @@
     slot_cap = (page_count + span_count - 1) // span_count + 1
     distances = jnp.arange(1, span_count + 1, dtype=jnp.int32)
 
-    payload = pack_pages(page_pool, offsets, slots, 1, 1, slot_cap, tensor_count)
-    if span_count > 1:
-        payload = payload + pack_pages(page_pool, offsets, slots, 2, span_count, slot_cap, tensor_count)
+    lead = min(2, span_count)
+    payload = pack_pages(page_pool, offsets, slots, 1, lead, slot_cap, tensor_count)
+    if span_count > lead:
+        payload = payload + pack_pages(page_pool, offsets, slots, lead + 1, span_count, slot_cap, tensor_count)
 
     arrivals = []
     for distance in range(1, span_count + 1):

time: 61.4 us -> 62.3 us (1.015)
  waiting for transfers between devices: 15.2 us -> 23.1 us
  starting transfers between devices: 32 us -> 25.1 us
    ppermute x12, waiting for transfers between devices: 15.2 us -> 23.1 us  [on_device(): lax.ppermute(payload[(distance - 1) * tensor_count + shift], ('replica',...]
    ppermute x12, starting transfers between devices: 32 us -> 25.1 us  [on_device(): lax.ppermute(payload[(distance - 1) * tensor_count + shift], ('replica',...]
  transfers between devices with their start and end apart: 12 -> 12, of which waited for: 3 -> 7; matrix products, arithmetic and copies ran while one was open for 0% -> 0% of each run, Pallas kernels for 5% -> 5%
where the time goes in v23:
time: 62.3 us; the launch traced here: 62 us
  starting transfers between devices  25.1 us (40%)
  waiting for transfers between devices  23.1 us (37%)
  Pallas kernels  13.2 us (21%)
    ppermute x12, starting transfers between devices, on_device(): lax.ppermute(payload[(distance - 1) * tensor_count + shift], ('replica',...  25.1 us
    ppermute x12, waiting for transfers between devices, on_device(): lax.ppermute(payload[(distance - 1) * tensor_count + shift], ('replica',...  23.1 us
    pallas_call x1, Pallas kernels, attend(): pl.pallas_call(functools.partial(attention_kernel, span_count, tensor_cou...  7.16 us
    pallas_call x2, Pallas kernels, pack_pages(): pl.pallas_call(functools.partial(gather_kernel, first, last, slot_cap, te...  6 us
  transfers between devices with their start and end apart: 12, of which 7 were waited for; matrix products, arithmetic and copies ran while one was open for 0% of the time, Pallas kernels for 5%

profile of v23, /device:TPU:1, one launch (start us, length us, event | category | flops | bytes accessed | tf_op | source)
XLA Modules:
  0.0 62.0 jit_solution(11421892211831275662)
XLA Ops:
  0.0 2.8 %shard_map.65 = (bf16[4,2,32,256]{3,2,1,0:T(8,128)(2,1)}, bf16[4,2,32,256]{3,2,1,0:T(8,128)(2,1)}, bf16[4,2,32,256]{3,2,1,0:T(8,128)(2,1)}, bf16[4,2,32,256]{3,2,1,0:T(8,128)(2,1)}) custom-call(s32[4,8]{1,0:T(4,128)} %off_ref.5, s32[4,8]{1,0:T(4,128)} %slot_ref.3, bf16[12,2,32,1024]{3,2,1,0:T(8,128)(2,1)} %pool_hbm.3), custom_call_target="tpu_custom_call" | custom-call | bytes 1048576 | tf_op jit(solution)/shard_map/pallas_call | solution.py:82
  2.8 4.2 %collective-permute-start.8 = (bf16[4,2,32,256]{3,2,1,0:T(8,128)(2,1)}, bf16[4,2,32,256]{3,2,1,0:T(8,128)(2,1)S(1)}, u32[]{:S(2)}, u32[]{:S(2)}) collective-permute-start(bf16[4,2,32,256]{3,2,1,0:T(8,128)(2,1)} %get-tuple-element.25), channel_id=1, source_target_pairs={{0,12},{1,13},{2,14},{3,15},{4,0},{5,1},{6,2},{7,3},{8,4},{9,5},{1... | collective-permute-start | bytes 393224 | tf_op jit(solution)/shard_map/ppermute | solution.py:113
  7.0 2.0 %collective-permute-start.9 = (bf16[4,2,32,256]{3,2,1,0:T(8,128)(2,1)}, bf16[4,2,32,256]{3,2,1,0:T(8,128)(2,1)S(1)}, u32[]{:S(2)}, u32[]{:S(2)}) collective-permute-start(bf16[4,2,32,256]{3,2,1,0:T(8,128)(2,1)} %get-tuple-element.26), channel_id=1, source_target_pairs={{0,13},{1,14},{2,15},{3,12},{4,1},{5,2},{6,3},{7,0},{8,5},{9,6},{1... | collective-permute-start | bytes 393224 | tf_op jit(solution)/shard_map/ppermute | solution.py:113
  9.0 0.1 collective-permute-start.10
  9.1 0.3 collective-permute-start.11
  9.4 3.2 %shard_map.64 = (bf16[4,2,32,256]{3,2,1,0:T(8,128)(2,1)}, bf16[4,2,32,256]{3,2,1,0:T(8,128)(2,1)}, bf16[4,2,32,256]{3,2,1,0:T(8,128)(2,1)}, bf16[4,2,32,256]{3,2...) custom-call(s32[4,8]{1,0:T(4,128)} %off_ref.5, ...), custom_call_target="tpu_custom_call" | custom-call | bytes 2097152 | tf_op jit(solution)/shard_map/pallas_call | solution.py:82
  12.6 1.4 %collective-permute-start = (bf16[4,2,32,256]{3,2,1,0:T(8,128)(2,1)}, bf16[4,2,32,256]{3,2,1,0:T(8,128)(2,1)S(1)}, u32[]{:S(2)}, u32[]{:S(2)}) collective-permute-start(bf16[4,2,32,256]{3,2,1,0:T(8,128)(2,1)} %get-tuple-element.17), channel_id=1, source_target_pairs={{0,4},{1,5},{2,6},{3,7},{4,8},{5,9},{6,10},{7,11},{8,12},{9,13},{1... | collective-permute-start | bytes 393224 | tf_op jit(solution)/shard_map/ppermute | solution.py:113
  14.1 0.0 collective-permute-done.8.rest_8_
  14.1 2.6 %collective-permute-start.1 = (bf16[4,2,32,256]{3,2,1,0:T(8,128)(2,1)}, bf16[4,2,32,256]{3,2,1,0:T(8,128)(2,1)S(1)}, u32[]{:S(2)}, u32[]{:S(2)}) collective-permute-start(bf16[4,2,32,256]{3,2,1,0:T(8,128)(2,1)} %get-tuple-element.18), channel_id=1, source_target_pairs={{0,5},{1,6},{2,7},{3,4},{4,9},{5,10},{6,11},{7,8},{8,13},{9,14},{1... | collective-permute-start | bytes 393224 | tf_op jit(solution)/shard_map/ppermute | solution.py:113
  16.7 0.0 collective-permute-done.9.rest_9_
  16.7 2.2 %collective-permute-start.2 = (bf16[4,2,32,256]{3,2,1,0:T(8,128)(2,1)}, bf16[4,2,32,256]{3,2,1,0:T(8,128)(2,1)S(1)}, u32[]{:S(2)}, u32[]{:S(2)}) collective-permute-start(bf16[4,2,32,256]{3,2,1,0:T(8,128)(2,1)} %get-tuple-element.19), channel_id=1, source_target_pairs={{0,6},{1,7},{2,4},{3,5},{4,10},{5,11},{6,8},{7,9},{8,14},{9,15},{1... | collective-permute-start | bytes 393224 | tf_op jit(solution)/shard_map/ppermute | solution.py:113
  18.8 0.0 collective-permute-done.10.rest_10_
  18.8 0.0 collective-permute-start.3
  18.8 0.5 collective-permute-done.11.rest_11_
  19.3 3.6 %collective-permute-start.4 = (bf16[4,2,32,256]{3,2,1,0:T(8,128)(2,1)}, bf16[4,2,32,256]{3,2,1,0:T(8,128)(2,1)S(1)}, u32[]{:S(2)}, u32[]{:S(2)}) collective-permute-start(bf16[4,2,32,256]{3,2,1,0:T(8,128)(2,1)} %get-tuple-element.21), channel_id=1, source_target_pairs={{0,8},{1,9},{2,10},{3,11},{4,12},{5,13},{6,14},{7,15},{8,0},{9,1},... | collective-permute-start | bytes 393224 | tf_op jit(solution)/shard_map/ppermute | solution.py:113
  22.9 0.0 collective-permute-done.rest_0_
  22.9 3.2 %collective-permute-start.5 = (bf16[4,2,32,256]{3,2,1,0:T(8,128)(2,1)}, bf16[4,2,32,256]{3,2,1,0:T(8,128)(2,1)S(1)}, u32[]{:S(2)}, u32[]{:S(2)}) collective-permute-start(bf16[4,2,32,256]{3,2,1,0:T(8,128)(2,1)} %get-tuple-element.22), channel_id=1, source_target_pairs={{0,9},{1,10},{2,11},{3,8},{4,13},{5,14},{6,15},{7,12},{8,1},{9,2},... | collective-permute-start | bytes 393224 | tf_op jit(solution)/shard_map/ppermute | solution.py:113
  26.1 0.2 collective-permute-done.1.rest_1_
  26.3 2.4 %collective-permute-start.6 = (bf16[4,2,32,256]{3,2,1,0:T(8,128)(2,1)}, bf16[4,2,32,256]{3,2,1,0:T(8,128)(2,1)S(1)}, u32[]{:S(2)}, u32[]{:S(2)}) collective-permute-start(bf16[4,2,32,256]{3,2,1,0:T(8,128)(2,1)} %get-tuple-element.23), channel_id=1, source_target_pairs={{0,10},{1,11},{2,8},{3,9},{4,14},{5,15},{6,12},{7,13},{8,2},{9,3},... | collective-permute-start | bytes 393224 | tf_op jit(solution)/shard_map/ppermute | solution.py:113
  28.7 0.0 collective-permute-done.2.rest_2_
  28.7 3.1 %collective-permute-start.7 = (bf16[4,2,32,256]{3,2,1,0:T(8,128)(2,1)}, bf16[4,2,32,256]{3,2,1,0:T(8,128)(2,1)S(1)}, u32[]{:S(2)}, u32[]{:S(2)}) collective-permute-start(bf16[4,2,32,256]{3,2,1,0:T(8,128)(2,1)} %get-tuple-element.24), channel_id=1, source_target_pairs={{0,11},{1,8},{2,9},{3,10},{4,15},{5,12},{6,13},{7,14},{8,3},{9,0},... | collective-permute-start | bytes 393224 | tf_op jit(solution)/shard_map/ppermute | solution.py:113
  31.8 1.3 %collective-permute-done.3.rest_3_ = bf16[4,2,32,256]{3,2,1,0:T(8,128)(2,1)S(1)} collective-permute-done((bf16[4,2,32,256]{3,2,1,0:T(8,128)(2,1)}, bf16[4,2,32,256]{3,2,1,0:T(8,128)(2,1)S(1)}, u32[]{:S(2)}, u32[]{:S(2)}) %collective-permute-start.3) | collective-permute-done | bytes 131104 | tf_op jit(solution)/shard_map/ppermute | solution.py:113
  33.0 12.1 %collective-permute-done.4.rest_4_ = bf16[4,2,32,256]{3,2,1,0:T(8,128)(2,1)S(1)} collective-permute-done((bf16[4,2,32,256]{3,2,1,0:T(8,128)(2,1)}, bf16[4,2,32,256]{3,2,1,0:T(8,128)(2,1)S(1)}, u32[]{:S(2)}, u32[]{:S(2)}) %collective-permute-start.4) | collective-permute-done | bytes 131104 | tf_op jit(solution)/shard_map/ppermute | solution.py:113
  45.2 2.8 %collective-permute-done.5.rest_5_ = bf16[4,2,32,256]{3,2,1,0:T(8,128)(2,1)S(1)} collective-permute-done((bf16[4,2,32,256]{3,2,1,0:T(8,128)(2,1)}, bf16[4,2,32,256]{3,2,1,0:T(8,128)(2,1)S(1)}, u32[]{:S(2)}, u32[]{:S(2)}) %collective-permute-start.5) | collective-permute-done | bytes 131104 | tf_op jit(solution)/shard_map/ppermute | solution.py:113
  48.0 3.6 %collective-permute-done.6.rest_6_ = bf16[4,2,32,256]{3,2,1,0:T(8,128)(2,1)S(1)} collective-permute-done((bf16[4,2,32,256]{3,2,1,0:T(8,128)(2,1)}, bf16[4,2,32,256]{3,2,1,0:T(8,128)(2,1)S(1)}, u32[]{:S(2)}, u32[]{:S(2)}) %collective-permute-start.6) | collective-permute-done | bytes 131104 | tf_op jit(solution)/shard_map/ppermute | solution.py:113
  51.6 2.6 %collective-permute-done.7.rest_7_ = bf16[4,2,32,256]{3,2,1,0:T(8,128)(2,1)S(1)} collective-permute-done((bf16[4,2,32,256]{3,2,1,0:T(8,128)(2,1)}, bf16[4,2,32,256]{3,2,1,0:T(8,128)(2,1)S(1)}, u32[]{:S(2)}, u32[]{:S(2)}) %collective-permute-start.7) | collective-permute-done | bytes 131104 | tf_op jit(solution)/shard_map/ppermute | solution.py:113
  54.3 0.0 copy-done
  54.3 0.0 copy-done.1
  54.3 0.0 copy-done.2
  54.3 0.0 copy-done.3
  54.3 0.5 copy-done.11
  54.9 7.2 %shard_map.66 = bf16[128,2048]{1,0:T(8,128)(2,1)} custom-call(s32[4,8]{1,0:T(4,128)} %off_ref.5, s32[4]{0:T(128)} %len_ref.1, bf16[128,2048]{1,0:T(8,128)(2,1)} %bitcast.3, bf16[2,128,256]{2,1,0:T(8,128)(2,1)} %bitcast.4, bf16[4,2,32,256]{3,2,1,0:T(8,128)(2,1)} %copy-done.4, bf16[4,2,32,256]{3,2,1,0:T(8,128)(2,1)} %copy-done.5, ...), custom_call_target="tpu_custom_call" | custom-call | flops 1207959552 | bytes 2752512 | tf_op jit(solution)/shard_map/pallas_call | solution.py:228
  (19 shorter events, 0.0 us)
Async XLA Ops:
  2.8 11.3 %collective-permute-start.8 = (bf16[4,2,32,256]{3,2,1,0:T(8,128)(2,1)}, bf16[4,2,32,256]{3,2,1,0:T(8,128)(2,1)S(1)}, u32[]{:S(2)}, u32[]{:S(2)}) collective-permute-start(bf16[4,2,32,256]{3,2,1,0:T(8,128)(2,1)} %get-tuple-element.25), channel_id=1, source_target_pairs={{0,12},{1,13},{2,14},{3,15},{4,0},{5,1},{6,2},{7,3},{8,4},{9,5},{1... | collective-permute-start | bytes 393224 | tf_op jit(solution)/shard_map/ppermute | solution.py:113
  7.0 9.7 %collective-permute-start.9 = (bf16[4,2,32,256]{3,2,1,0:T(8,128)(2,1)}, bf16[4,2,32,256]{3,2,1,0:T(8,128)(2,1)S(1)}, u32[]{:S(2)}, u32[]{:S(2)}) collective-permute-start(bf16[4,2,32,256]{3,2,1,0:T(8,128)(2,1)} %get-tuple-element.26), channel_id=1, source_target_pairs={{0,13},{1,14},{2,15},{3,12},{4,1},{5,2},{6,3},{7,0},{8,5},{9,6},{1... | collective-permute-start | bytes 393224 | tf_op jit(solution)/shard_map/ppermute | solution.py:113
  9.0 9.8 %collective-permute-start.10 = (bf16[4,2,32,256]{3,2,1,0:T(8,128)(2,1)}, bf16[4,2,32,256]{3,2,1,0:T(8,128)(2,1)S(1)}, u32[]{:S(2)}, u32[]{:S(2)}) collective-permute-start(bf16[4,2,32,256]{3,2,1,0:T(8,128)(2,1)} %get-tuple-element.27), channel_id=1, source_target_pairs={{0,14},{1,15},{2,12},{3,13},{4,2},{5,3},{6,0},{7,1},{8,6},{9,7},{1... | collective-permute-start | bytes 393224 | tf_op jit(solution)/shard_map/ppermute | solution.py:113
  9.1 10.2 %collective-permute-start.11 = (bf16[4,2,32,256]{3,2,1,0:T(8,128)(2,1)}, bf16[4,2,32,256]{3,2,1,0:T(8,128)(2,1)S(1)}, u32[]{:S(2)}, u32[]{:S(2)}) collective-permute-start(bf16[4,2,32,256]{3,2,1,0:T(8,128)(2,1)} %get-tuple-element.28), channel_id=1, source_target_pairs={{0,15},{1,12},{2,13},{3,14},{4,3},{5,0},{6,1},{7,2},{8,7},{9,4},{1... | collective-permute-start | bytes 393224 | tf_op jit(solution)/shard_map/ppermute | solution.py:113
  12.6 10.3 %collective-permute-start = (bf16[4,2,32,256]{3,2,1,0:T(8,128)(2,1)}, bf16[4,2,32,256]{3,2,1,0:T(8,128)(2,1)S(1)}, u32[]{:S(2)}, u32[]{:S(2)}) collective-permute-start(bf16[4,2,32,256]{3,2,1,0:T(8,128)(2,1)} %get-tuple-element.17), channel_id=1, source_target_pairs={{0,4},{1,5},{2,6},{3,7},{4,8},{5,9},{6,10},{7,11},{8,12},{9,13},{1... | collective-permute-start | bytes 393224 | tf_op jit(solution)/shard_map/ppermute | solution.py:113
  14.1 40.2 %copy-start = (bf16[4,2,32,256]{3,2,1,0:T(8,128)(2,1)}, bf16[4,2,32,256]{3,2,1,0:T(8,128)(2,1)S(1)}, u32[]{:S(2)}) copy-start(bf16[4,2,32,256]{3,2,1,0:T(8,128)(2,1)S(1)} %collective-permute-done.8.rest_8_) | copy-start | bytes 393220
  14.1 12.2 %collective-permute-start.1 = (bf16[4,2,32,256]{3,2,1,0:T(8,128)(2,1)}, bf16[4,2,32,256]{3,2,1,0:T(8,128)(2,1)S(1)}, u32[]{:S(2)}, u32[]{:S(2)}) collective-permute-start(bf16[4,2,32,256]{3,2,1,0:T(8,128)(2,1)} %get-tuple-element.18), channel_id=1, source_target_pairs={{0,5},{1,6},{2,7},{3,4},{4,9},{5,10},{6,11},{7,8},{8,13},{9,14},{1... | collective-permute-start | bytes 393224 | tf_op jit(solution)/shard_map/ppermute | solution.py:113
  16.7 37.6 %copy-start.1 = (bf16[4,2,32,256]{3,2,1,0:T(8,128)(2,1)}, bf16[4,2,32,256]{3,2,1,0:T(8,128)(2,1)S(1)}, u32[]{:S(2)}) copy-start(bf16[4,2,32,256]{3,2,1,0:T(8,128)(2,1)S(1)} %collective-permute-done.9.rest_9_) | copy-start | bytes 393220
  16.7 12.0 %collective-permute-start.2 = (bf16[4,2,32,256]{3,2,1,0:T(8,128)(2,1)}, bf16[4,2,32,256]{3,2,1,0:T(8,128)(2,1)S(1)}, u32[]{:S(2)}, u32[]{:S(2)}) collective-permute-start(bf16[4,2,32,256]{3,2,1,0:T(8,128)(2,1)} %get-tuple-element.19), channel_id=1, source_target_pairs={{0,6},{1,7},{2,4},{3,5},{4,10},{5,11},{6,8},{7,9},{8,14},{9,15},{1... | collective-permute-start | bytes 393224 | tf_op jit(solution)/shard_map/ppermute | solution.py:113
  18.8 35.4 %copy-start.2 = (bf16[4,2,32,256]{3,2,1,0:T(8,128)(2,1)}, bf16[4,2,32,256]{3,2,1,0:T(8,128)(2,1)S(1)}, u32[]{:S(2)}) copy-start(bf16[4,2,32,256]{3,2,1,0:T(8,128)(2,1)S(1)} %collective-permute-done.10.rest_10_) | copy-start | bytes 393220
  18.8 14.2 %collective-permute-start.3 = (bf16[4,2,32,256]{3,2,1,0:T(8,128)(2,1)}, bf16[4,2,32,256]{3,2,1,0:T(8,128)(2,1)S(1)}, u32[]{:S(2)}, u32[]{:S(2)}) collective-permute-start(bf16[4,2,32,256]{3,2,1,0:T(8,128)(2,1)} %get-tuple-element.20), channel_id=1, source_target_pairs={{0,7},{1,4},{2,5},{3,6},{4,11},{5,8},{6,9},{7,10},{8,15},{9,12},{1... | collective-permute-start | bytes 393224 | tf_op jit(solution)/shard_map/ppermute | solution.py:113
  19.3 35.0 %copy-start.3 = (bf16[4,2,32,256]{3,2,1,0:T(8,128)(2,1)}, bf16[4,2,32,256]{3,2,1,0:T(8,128)(2,1)S(1)}, u32[]{:S(2)}) copy-start(bf16[4,2,32,256]{3,2,1,0:T(8,128)(2,1)S(1)} %collective-permute-done.11.rest_11_) | copy-start | bytes 393220
  19.3 25.9 %collective-permute-start.4 = (bf16[4,2,32,256]{3,2,1,0:T(8,128)(2,1)}, bf16[4,2,32,256]{3,2,1,0:T(8,128)(2,1)S(1)}, u32[]{:S(2)}, u32[]{:S(2)}) collective-permute-start(bf16[4,2,32,256]{3,2,1,0:T(8,128)(2,1)} %get-tuple-element.21), channel_id=1, source_target_pairs={{0,8},{1,9},{2,10},{3,11},{4,12},{5,13},{6,14},{7,15},{8,0},{9,1},... | collective-permute-start | bytes 393224 | tf_op jit(solution)/shard_map/ppermute | solution.py:113
  22.9 31.3 %copy-start.4 = (bf16[4,2,32,256]{3,2,1,0:T(8,128)(2,1)}, bf16[4,2,32,256]{3,2,1,0:T(8,128)(2,1)S(1)}, u32[]{:S(2)}) copy-start(bf16[4,2,32,256]{3,2,1,0:T(8,128)(2,1)S(1)} %collective-permute-done.rest_0_) | copy-start | bytes 393220
  22.9 25.1 %collective-permute-start.5 = (bf16[4,2,32,256]{3,2,1,0:T(8,128)(2,1)}, bf16[4,2,32,256]{3,2,1,0:T(8,128)(2,1)S(1)}, u32[]{:S(2)}, u32[]{:S(2)}) collective-permute-start(bf16[4,2,32,256]{3,2,1,0:T(8,128)(2,1)} %get-tuple-element.22), channel_id=1, source_target_pairs={{0,9},{1,10},{2,11},{3,8},{4,13},{5,14},{6,15},{7,12},{8,1},{9,2},... | collective-permute-start | bytes 393224 | tf_op jit(solution)/shard_map/ppermute | solution.py:113
  26.3 28.0 %copy-start.5 = (bf16[4,2,32,256]{3,2,1,0:T(8,128)(2,1)}, bf16[4,2,32,256]{3,2,1,0:T(8,128)(2,1)S(1)}, u32[]{:S(2)}) copy-start(bf16[4,2,32,256]{3,2,1,0:T(8,128)(2,1)S(1)} %collective-permute-done.1.rest_1_) | copy-start | bytes 393220
  26.3 25.3 %collective-permute-start.6 = (bf16[4,2,32,256]{3,2,1,0:T(8,128)(2,1)}, bf16[4,2,32,256]{3,2,1,0:T(8,128)(2,1)S(1)}, u32[]{:S(2)}, u32[]{:S(2)}) collective-permute-start(bf16[4,2,32,256]{3,2,1,0:T(8,128)(2,1)} %get-tuple-element.23), channel_id=1, source_target_pairs={{0,10},{1,11},{2,8},{3,9},{4,14},{5,15},{6,12},{7,13},{8,2},{9,3},... | collective-permute-start | bytes 393224 | tf_op jit(solution)/shard_map/ppermute | solution.py:113
  28.7 25.6 %copy-start.6 = (bf16[4,2,32,256]{3,2,1,0:T(8,128)(2,1)}, bf16[4,2,32,256]{3,2,1,0:T(8,128)(2,1)S(1)}, u32[]{:S(2)}) copy-start(bf16[4,2,32,256]{3,2,1,0:T(8,128)(2,1)S(1)} %collective-permute-done.2.rest_2_) | copy-start | bytes 393220
  28.7 25.6 %collective-permute-start.7 = (bf16[4,2,32,256]{3,2,1,0:T(8,128)(2,1)}, bf16[4,2,32,256]{3,2,1,0:T(8,128)(2,1)S(1)}, u32[]{:S(2)}, u32[]{:S(2)}) collective-permute-start(bf16[4,2,32,256]{3,2,1,0:T(8,128)(2,1)} %get-tuple-element.24), channel_id=1, source_target_pairs={{0,11},{1,8},{2,9},{3,10},{4,15},{5,12},{6,13},{7,14},{8,3},{9,0},... | collective-permute-start | bytes 393224 | tf_op jit(solution)/shard_map/ppermute | solution.py:113
  33.0 21.3 %copy-start.7 = (bf16[4,2,32,256]{3,2,1,0:T(8,128)(2,1)}, bf16[4,2,32,256]{3,2,1,0:T(8,128)(2,1)S(1)}, u32[]{:S(2)}) copy-start(bf16[4,2,32,256]{3,2,1,0:T(8,128)(2,1)S(1)} %collective-permute-done.3.rest_3_) | copy-start | bytes 393220
  45.2 9.1 %copy-start.8 = (bf16[4,2,32,256]{3,2,1,0:T(8,128)(2,1)}, bf16[4,2,32,256]{3,2,1,0:T(8,128)(2,1)S(1)}, u32[]{:S(2)}) copy-start(bf16[4,2,32,256]{3,2,1,0:T(8,128)(2,1)S(1)} %collective-permute-done.4.rest_4_) | copy-start | bytes 393220
  48.0 6.3 %copy-start.9 = (bf16[4,2,32,256]{3,2,1,0:T(8,128)(2,1)}, bf16[4,2,32,256]{3,2,1,0:T(8,128)(2,1)S(1)}, u32[]{:S(2)}) copy-start(bf16[4,2,32,256]{3,2,1,0:T(8,128)(2,1)S(1)} %collective-permute-done.5.rest_5_) | copy-start | bytes 393220
  51.6 2.7 %copy-start.10 = (bf16[4,2,32,256]{3,2,1,0:T(8,128)(2,1)}, bf16[4,2,32,256]{3,2,1,0:T(8,128)(2,1)S(1)}, u32[]{:S(2)}) copy-start(bf16[4,2,32,256]{3,2,1,0:T(8,128)(2,1)S(1)} %collective-permute-done.6.rest_6_) | copy-start | bytes 393220
  54.2 0.6 %copy-start.11 = (bf16[4,2,32,256]{3,2,1,0:T(8,128)(2,1)}, bf16[4,2,32,256]{3,2,1,0:T(8,128)(2,1)S(1)}, u32[]{:S(2)}) copy-start(bf16[4,2,32,256]{3,2,1,0:T(8,128)(2,1)S(1)} %collective-permute-done.7.rest_7_) | copy-start | bytes 393220
